TPU v7x, 32 devices: a whole 2x2x4 slice. The times are simulated.
32 devices in a mesh: pipe: 4 (over z), et: 8 (over y, x, core).
Axes of the slice: x: 2, y: 2, z: 4, core: 2. Of those that a mesh axis runs over, the one named last changes fastest.
Arguments:
- tokens: bfloat16 [4, 1024, 4096], P('pipe', 'et'), may hold values from -6 to 6
- gate_vals: bfloat16 [4, 1024, 2], P('pipe', 'et'), may hold values from 0.099609375 to 1
- expert_ids: int32 [4, 1024, 2], P('pipe', 'et'), may hold values from 0 to 7, as said below
- grad_out: bfloat16 [4, 1024, 4096], P('pipe', 'et'), may hold values from -6 to 6
- w_gate: bfloat16 [4, 2, 4096, 7168], P('pipe', None, None, 'et'), may hold values from -0.09375 to 0.09375
- w_up: bfloat16 [4, 2, 4096, 7168], P('pipe', None, None, 'et'), may hold values from -0.09375 to 0.09375
- w_down: bfloat16 [4, 2, 7168, 4096], P('pipe', None, 'et'), may hold values from -0.0625 to 0.0625
Outputs:
- moe_out: bfloat16 [4, 1024, 4096], P('pipe', 'et')
- prior_grads: bfloat16 [4, 1024, 4096], P('pipe', 'et')
Inputs may be any that keep to these rules, and one draw needn't show every extreme that they name: `expert_ids`: each row names 2 different experts. The rows of one device of one section name each of experts 0 to 1 at most 16 times, and for each of these experts there is a section in which every device's rows name it exactly 16 times.
All inputs are finite; a program needn't handle non-finite values.
Results may differ from a plain program's by a relative error of at most 0.012.
Values may be sent and summed in bfloat16 or wider, within the bound.
No kernel may reach another device: no remote copies, remote signals or barrier semaphores. Data moves between devices by JAX's collectives and lax.ppermute only.
A program may use at most 192 MiB of HBM per device.

v0:
```python
import jax
import jax.numpy as jnp
from jax import lax
from jax.sharding import PartitionSpec as P

E_WIN = 2
MOST = 16


def shifted(value, axis, steps):
    count = lax.axis_size(axis)
    first, last = (max(0, -steps), min(count, count - steps))
    return lax.ppermute(value, axis, [(source, source + steps) for source in range(first, last)])


def silu_parts(pre_gate):
    sigma = jax.nn.sigmoid(pre_gate)
    return (pre_gate * sigma, sigma * (1.0 + pre_gate * (1.0 - sigma)))


def slot_layout(routed, groups, slot_width):
    length = routed.shape[0] // groups
    flags = routed.reshape(groups, length)
    positions = jnp.cumsum(flags.astype(jnp.int32), axis=1, dtype=jnp.int32) - 1
    positions = positions + (jnp.arange(groups, dtype=jnp.int32) * slot_width)[:, None]
    targets = jnp.where(flags, positions, groups * slot_width).reshape(-1)
    sources = (
        jnp.zeros((groups * slot_width,), jnp.int32)
        .at[targets]
        .set(jnp.arange(groups * length, dtype=jnp.int32), mode="drop")
    )
    return (targets, sources)


def gate_of(route_rows, gate_rows, expert):
    matches = route_rows == expert
    routed = jnp.any(matches, axis=1)
    gate_val = jnp.sum(jnp.where(matches, gate_rows.astype(jnp.float32), 0.0), axis=1)
    return (routed, gate_val)


def unpack_slots(slot_sums, local_targets):
    padded = jnp.concatenate([slot_sums, jnp.zeros((1, slot_sums.shape[1]), jnp.float32)], axis=0)
    return padded[local_targets]


def per_device(tokens, gate_vals, expert_ids, grad_out, w_gate, w_up, w_down):
    local_rows = tokens[0]
    local_gates = gate_vals[0]
    local_routes = expert_ids[0]
    local_grads = grad_out[0]
    gate_mats = w_gate[0]
    up_mats = w_up[0]
    down_mats = w_down[0]
    n_shards = lax.axis_size("et")
    model_width = local_rows.shape[1]
    capacity = MOST * n_shards
    slot_width = 2 * MOST
    gathered_routes = lax.all_gather(local_routes, "et", axis=0, tiled=True)
    rows_in = []
    grads_in = []
    gates_in = []
    sources_in = []
    all_rows, all_gates, all_grads = (
        lax.all_gather(local_rows, "et", axis=0, tiled=True),
        lax.all_gather(local_gates, "et", axis=0, tiled=True),
        lax.all_gather(local_grads, "et", axis=0, tiled=True),
    )
    for expert in range(E_WIN):
        routed, gate_val = gate_of(gathered_routes, all_gates, expert)
        targets, sources = slot_layout(routed, 1, capacity)
        gates_in.append(jnp.zeros((capacity,), jnp.float32).at[targets].set(gate_val, mode="drop"))
        sources_in.append(sources)
        rows_in.append(all_rows[sources])
        grads_in.append(all_grads[sources])
    union_all = jnp.any(gathered_routes < E_WIN, axis=1)
    union_targets, union_sources = slot_layout(union_all, n_shards, slot_width)
    dest_in = [union_targets[sources] for sources in sources_in]
    buffer_rows = n_shards * slot_width
    local_targets, local_sources = slot_layout(jnp.any(local_routes < E_WIN, axis=1), 1, slot_width)
    out_part = jnp.zeros((buffer_rows, model_width), jnp.float32)
    stored = []
    for expert in range(E_WIN):
        pre_gate = jnp.dot(rows_in[expert], gate_mats[expert], preferred_element_type=jnp.float32)
        pre_up = jnp.dot(rows_in[expert], up_mats[expert], preferred_element_type=jnp.float32)
        activated, slopes = silu_parts(pre_gate)
        hidden = (activated * pre_up).astype(jnp.bfloat16)
        out_part = out_part.at[dest_in[expert]].add(
            gates_in[expert][:, None]
            * jnp.dot(hidden, down_mats[expert], preferred_element_type=jnp.float32),
            mode="drop",
        )
        stored.append((pre_up, activated, slopes))
    out_slot_sums = lax.psum_scatter(
        out_part.astype(jnp.bfloat16), "et", scatter_dimension=0, tiled=True
    ).astype(jnp.float32)
    out_share = unpack_slots(out_slot_sums, local_targets).astype(jnp.bfloat16)
    grad_part = jnp.zeros((buffer_rows, model_width), jnp.float32)
    for expert in range(E_WIN):
        pre_up, activated, slopes = stored[expert]
        d_hidden = gates_in[expert][:, None] * jnp.dot(
            grads_in[expert], down_mats[expert].T, preferred_element_type=jnp.float32
        )
        d_gate = (d_hidden * pre_up * slopes).astype(jnp.bfloat16)
        d_up = (d_hidden * activated).astype(jnp.bfloat16)
        grad_part = grad_part.at[dest_in[expert]].add(
            jnp.dot(d_gate, gate_mats[expert].T, preferred_element_type=jnp.float32)
            + jnp.dot(d_up, up_mats[expert].T, preferred_element_type=jnp.float32),
            mode="drop",
        )
    grad_slot_sums = lax.psum_scatter(
        grad_part.astype(jnp.bfloat16), "et", scatter_dimension=0, tiled=True
    ).astype(jnp.float32)
    grad_share = unpack_slots(grad_slot_sums, local_targets).astype(jnp.bfloat16)
    received = shifted(grad_share, "pipe", -1)
    return (out_share[None], received[None])


def solution(mesh):
    placed = (
        P("pipe", "et", None),
        P("pipe", "et", None),
        P("pipe", "et", None),
        P("pipe", "et", None),
        P("pipe", None, None, "et"),
        P("pipe", None, None, "et"),
        P("pipe", None, "et", None),
    )
    return jax.shard_map(
        per_device,
        mesh=mesh,
        in_specs=placed,
        out_specs=(P("pipe", "et", None), P("pipe", "et", None)),
        check_vma=False,
    )
```

profile of v0, /device:TPU:0, one launch (start us, length us, event | category | flops | bytes accessed | tf_op | source)
XLA Modules:
  0.0 286.6 jit_solution(2784781630595700271)
XLA Ops:
  8.7 10.5 %all-gather = s32[1,1024,2]{1,2,0:T(2,128)S(1)} all-gather(s32[1,128,2]{1,2,0:T(2,128)} %param.9), channel_id=2, replica_groups=mesh['pipe'=4,'et'=8] {'et'}, dimensions={1}, use_global_device_ids=true | all-gather | bytes 9216 | tf_op jit(solution)/shard_map/all_gather | solution.py:59
  31.9 8.6 %all-gather.1 = bf16[1,1024,2]{1,2,0:T(2,128)(2,1)S(1)} all-gather(bf16[1,128,2]{1,2,0:T(2,128)(2,1)} %param.8), channel_id=3, replica_groups=mesh['pipe'=4,'et'=8] {'et'}, dimensions={1}, use_global_device_ids=true | all-gather | bytes 4608 | tf_op jit(solution)/shard_map/all_gather | solution.py:66
  44.9 4.8 %scatter_custom_fusion.4 = f32[128]{0:T(128)S(1)} fusion(s32[1024]{0:T(1024)S(1)} %bitcast.89, f32[1024]{0:T(1024)S(1)} %get-tuple-element.2, f32[]{:T(128)} %constant.13.clone.1), kind=kCustom, calls=%fused_computation.111 | custom fusion | bytes 516 | tf_op jit(solution)/shard_map/scatter | solution.py:72
  49.9 17.2 %all-gather.7.cloned.1.call-done = bf16[1,1024,4096]{2,1,0:T(8,128)(2,1)} async-done(((bf16[1,128,4096]{2,1,0:T(8,128)(2,1)}), bf16[1,1024,4096]{2,1,0:T(8,128)(2,1)}) %all-gather.7.cloned.1.call-update) | async-done | bytes 8388624 | tf_op jit(solution)/shard_map/all_gather | solution.py:65
  67.1 6.7 %gather_fusion.1 = bf16[128,4096]{1,0:T(8,128)(2,1)S(1)} fusion(bf16[1024,4096]{1,0:T(8,128)(2,1)} %bitcast.80, s32[1024]{0:T(1024)S(1)} %pad_clamp_fusion.2), kind=kCustom, calls=%fused_computation.1 | custom fusion | bytes 2097664 | tf_op jit(solution)/shard_map/gather | solution.py:74
  73.7 7.3 %gather_fusion.3 = bf16[128,4096]{1,0:T(8,128)(2,1)S(1)} fusion(bf16[1024,4096]{1,0:T(8,128)(2,1)} %bitcast.81, s32[1024]{0:T(1024)S(1)} %pad_clamp_fusion.1), kind=kCustom, calls=%fused_computation.3 | custom fusion | bytes 2097664 | tf_op jit(solution)/shard_map/gather | solution.py:74
  85.6 5.3 %fusion.22 = f32[128,896]{1,0:T(8,128)} fusion(bf16[128,4096]{1,0:T(8,128)(2,1)S(1)} %gather_fusion.1, bf16[1,2,4096,896]{3,2,1,0:T(8,128)(2,1)} %param.11), kind=kOutput, calls=%fused_computation.38 | convolution fusion | flops 939524096 | bytes 8847360 | tf_op jit(solution)/shard_map/dot_general | solution.py:84
  96.7 26.7 %all-gather.9.cloned.1.call-done = bf16[1,1024,4096]{2,1,0:T(8,128)(2,1)} async-done(((bf16[1,128,4096]{2,1,0:T(8,128)(2,1)}), bf16[1,1024,4096]{2,1,0:T(8,128)(2,1)}) %all-gather.9.cloned.1.call-update) | async-done | bytes 8388624 | tf_op jit(solution)/shard_map/all_gather | solution.py:67
  123.4 6.8 %gather_fusion.5 = bf16[128,4096]{1,0:T(8,128)(2,1)S(1)} fusion(bf16[1024,4096]{1,0:T(8,128)(2,1)} %bitcast.78, s32[1024]{0:T(1024)S(1)} %pad_clamp_fusion.2), kind=kCustom, calls=%fused_computation.5 | custom fusion | bytes 2097664 | tf_op jit(solution)/shard_map/gather | solution.py:75
  130.2 6.7 %gather_fusion.6 = bf16[128,4096]{1,0:T(8,128)(2,1)S(1)} fusion(bf16[1024,4096]{1,0:T(8,128)(2,1)} %bitcast.79, s32[1024]{0:T(1024)S(1)} %pad_clamp_fusion.1), kind=kCustom, calls=%fused_computation.6 | custom fusion | bytes 2097664 | tf_op jit(solution)/shard_map/gather | solution.py:75
  136.9 5.6 %fusion.52 = f32[128,896]{1,0:T(8,128)S(1)} fusion(bf16[128,4096]{1,0:T(8,128)(2,1)S(1)} %gather_fusion.5, bf16[1,2,896,4096]{3,2,1,0:T(8,128)(2,1)} %param.13, f32[128]{0:T(128)S(1)} %scatter_custom_fusion.1), kind=kOutput, calls=%fused_computation.60 | convolution fusion | flops 939638784 | bytes 8847872 | tf_op jit(solution)/shard_map/dot_general | solution.py:101
  142.5 5.5 %fusion.16 = f32[128,4096]{1,0:T(8,128)S(1)} fusion(bf16[1,2,4096,896]{3,2,1,0:T(8,128)(2,1)} %param.12, f32[128,896]{1,0:T(8,128)S(1)} %fusion.52, f32[128,896]{1,0:T(8,128)S(1)} %copy-done.1), kind=kOutput, calls=%fused_computation.32 | convolution fusion | flops 940212224 | bytes 10354688 | tf_op jit(solution)/shard_map/dot_general | solution.py:108
  148.1 6.9 %fusion.36 = f32[128,4096]{1,0:T(8,128)} fusion(f32[128,4096]{1,0:T(8,128)S(1)} %fusion.16, bf16[1,2,4096,896]{3,2,1,0:T(8,128)(2,1)} %param.11, f32[128,896]{1,0:T(8,128)S(1)} %copy-done.1, f32[128,896]{1,0:T(8,128)S(1)} %fusion.52, f32[128,896]{1,0:T(8,128)S(1)} %fusion.18), kind=kOutput, calls=%fused_computation.52 | convolution fusion | flops 941195264 | bytes 12910592 | tf_op jit(solution)/shard_map/dot_general | solution.py:107
  155.0 6.6 %scatter_custom_fusion.6 = f32[256,4096]{1,0:T(8,128)} fusion(s32[128]{0:T(128)S(1)} %fusion.66, f32[128,4096]{1,0:T(8,128)} %fusion.36, f32[]{:T(128)} %constant.13.clone.1), kind=kCustom, calls=%fused_computation.56 | custom fusion | flops 524288 | bytes 4194816 | tf_op jit(solution)/shard_map/scatter-add | solution.py:106
  161.6 5.5 %fusion.55 = f32[128,896]{1,0:T(8,128)S(1)} fusion(bf16[128,4096]{1,0:T(8,128)(2,1)S(1)} %gather_fusion.6, bf16[1,2,896,4096]{3,2,1,0:T(8,128)(2,1)} %param.13, f32[128]{0:T(128)S(1)} %scatter_custom_fusion.4), kind=kOutput, calls=%fused_computation.61 | convolution fusion | flops 939638784 | bytes 8847872 | tf_op jit(solution)/shard_map/dot_general | solution.py:101
  167.1 5.5 %fusion.4 = f32[128,4096]{1,0:T(8,128)S(1)} fusion(bf16[1,2,4096,896]{3,2,1,0:T(8,128)(2,1)} %param.12, f32[128,896]{1,0:T(8,128)S(1)} %fusion.55, f32[128,896]{1,0:T(8,128)S(1)} %fusion.10), kind=kOutput, calls=%fused_computation.20 | convolution fusion | flops 940212224 | bytes 10354688 | tf_op jit(solution)/shard_map/dot_general | solution.py:108
  172.7 5.6 %fusion.42 = f32[128,4096]{1,0:T(8,128)S(1)} fusion(f32[128,4096]{1,0:T(8,128)S(1)} %fusion.4, bf16[1,2,4096,896]{3,2,1,0:T(8,128)(2,1)} %param.11, f32[128,896]{1,0:T(8,128)S(1)} %fusion.10, f32[128,896]{1,0:T(8,128)S(1)} %fusion.55, f32[128,896]{1,0:T(8,128)S(1)} %fusion.6), kind=kOutput, calls=%fused_computation.54 | convolution fusion | flops 941195264 | bytes 12910592 | tf_op jit(solution)/shard_map/dot_general | solution.py:107
  178.3 7.3 %scatter_fusion.1 = f32[256,4096]{1,0:T(8,128)} fusion(f32[256,4096]{1,0:T(8,128)} %scatter_custom_fusion.6, s32[128]{0:T(128)S(1)} %fusion.67, f32[128,4096]{1,0:T(8,128)S(1)} %fusion.42), kind=kCustom, calls=%fused_computation.15 | custom fusion | flops 524288 | bytes 6291968 | tf_op jit(solution)/shard_map/scatter-add | solution.py:106
  189.7 4.5 %fusion.39 = f32[128,4096]{1,0:T(8,128)S(1)} fusion(bf16[1,2,896,4096]{3,2,1,0:T(8,128)(2,1)} %param.13, f32[128]{0:T(128)S(1)} %scatter_custom_fusion.1, f32[128,896]{1,0:T(8,128)S(1)} %fusion.18, f32[128,896]{1,0:T(8,128)} %fusion.22), kind=kOutput, calls=%fused_computation.53 | convolution fusion | flops 940736512 | bytes 10355200 | tf_op jit(solution)/shard_map/dot_general | solution.py:90
  194.3 5.4 %scatter_custom_fusion.2 = f32[256,4096]{1,0:T(8,128)} fusion(s32[128]{0:T(128)S(1)} %fusion.66, f32[128,4096]{1,0:T(8,128)S(1)} %fusion.39, f32[]{:T(128)} %constant.13.clone.1), kind=kCustom, calls=%fused_computation.58 | custom fusion | flops 524288 | bytes 4194308 | tf_op jit(solution)/shard_map/scatter-add | solution.py:88
  199.6 4.7 %fusion.45 = f32[128,4096]{1,0:T(8,128)S(1)} fusion(bf16[1,2,896,4096]{3,2,1,0:T(8,128)(2,1)} %param.13, f32[128]{0:T(128)S(1)} %scatter_custom_fusion.4, f32[128,896]{1,0:T(8,128)S(1)} %fusion.6, f32[128,896]{1,0:T(8,128)S(1)} %fusion.10), kind=kOutput, calls=%fused_computation.55 | convolution fusion | flops 940736512 | bytes 10355200 | tf_op jit(solution)/shard_map/dot_general | solution.py:90
  204.3 7.3 %scatter_fusion = f32[256,4096]{1,0:T(8,128)} fusion(f32[256,4096]{1,0:T(8,128)} %scatter_custom_fusion.2, s32[128]{0:T(128)S(1)} %fusion.67, f32[128,4096]{1,0:T(8,128)S(1)} %fusion.45), kind=kCustom, calls=%fused_computation.13 | custom fusion | flops 524288 | bytes 6291968 | tf_op jit(solution)/shard_map/scatter-add | solution.py:88
  216.0 14.8 %reduce-scatter.5.cloned.1.call-done = bf16[32,4096]{1,0:T(8,128)(2,1)} async-done(((bf16[256,4096]{1,0:T(8,128)(2,1)}), bf16[32,4096]{1,0:T(8,128)(2,1)}) %reduce-scatter.5.cloned.1.call-update) | async-done | bytes 262160 | tf_op jit(solution)/shard_map/reduce_scatter | solution.py:111
  234.2 41.3 %reduce-scatter.3.cloned.1.call-done = bf16[32,4096]{1,0:T(8,128)(2,1)} async-done(((bf16[256,4096]{1,0:T(8,128)(2,1)}), bf16[32,4096]{1,0:T(8,128)(2,1)}) %reduce-scatter.3.cloned.1.call-update) | async-done | bytes 262160 | tf_op jit(solution)/shard_map/reduce_scatter | solution.py:94
  (74 shorter events, 45.1 us)
Async XLA Ops:
  7.2 59.9 %all-gather.7.cloned.1.call-start = ((), (), s32[]{:S(2)}) async-start(), calls=%async_computation.4 | async-start | bytes 9437184 | tf_op jit(solution)/shard_map/all_gather | solution.py:65
  7.9 115.5 %all-gather.9.cloned.1.call-start = ((), (), s32[]{:S(2)}) async-start(), calls=%async_computation.5 | async-start | bytes 9437184 | tf_op jit(solution)/shard_map/all_gather | solution.py:67
  8.6 222.1 %reduce-scatter.5.cloned.1.call-start = ((), (), s32[]{:S(2)}) async-start(), calls=%async_computation.3 | async-start | bytes 2359296 | tf_op jit(solution)/shard_map/reduce_scatter | solution.py:111
  81.1 14.3 %slice-start = ((s8[14680064]{0:T(1024)(128)(4,1)}), s8[4194304]{0:T(1024)(128)(4,1)S(1)}, s32[]{:S(2)}) async-start(s8[14680064]{0:T(1024)(128)(4,1)} %bitcast.97), calls=%async_computation.6 | async-start | bytes 8388608
  81.1 14.3 %slice-start.1 = ((s8[14680064]{0:T(1024)(128)(4,1)}), s8[4194304]{0:T(1024)(128)(4,1)S(1)}, s32[]{:S(2)}) async-start(s8[14680064]{0:T(1024)(128)(4,1)} %bitcast.97), calls=%async_computation.7 | async-start | bytes 8388608
  85.6 9.8 %slice-start.2 = ((s8[14680064]{0:T(1024)(128)(4,1)}), s8[4194304]{0:T(1024)(128)(4,1)S(1)}, s32[]{:S(2)}) async-start(s8[14680064]{0:T(1024)(128)(4,1)} %bitcast.97), calls=%async_computation.8 | async-start | bytes 8388608
  90.9 4.5 %slice-start.3 = ((s8[14680064]{0:T(1024)(128)(4,1)}), s8[2097152]{0:T(1024)(128)(4,1)S(1)}, s32[]{:S(2)}) async-start(s8[14680064]{0:T(1024)(128)(4,1)} %bitcast.97), calls=%async_computation.9 | async-start | bytes 4194304
  136.9 5.6 %copy-start.1 = (f32[128,896]{1,0:T(8,128)S(1)}, f32[128,896]{1,0:T(8,128)}, u32[]{:S(2)}) copy-start(f32[128,896]{1,0:T(8,128)} %fusion.22) | copy-start | bytes 1376260
  189.4 86.1 %reduce-scatter.3.cloned.1.call-start = ((), (), s32[]{:S(2)}) async-start(), calls=%async_computation.2 | async-start | bytes 2359296 | tf_op jit(solution)/shard_map/reduce_scatter | solution.py:94
  211.6 3.9 %copy-start = (s32[1,128,2]{1,2,0:T(2,128)S(1)}, s32[1,128,2]{1,2,0:T(2,128)}, u32[]{:S(2)}) copy-start(s32[1,128,2]{1,2,0:T(2,128)} %param.9) | copy-start | bytes 3076
  232.9 45.7 %collective-permute-start = (bf16[128,4096]{1,0:T(8,128)(2,1)S(1)}, bf16[128,4096]{1,0:T(8,128)(2,1)S(1)}, u32[]{:S(2)}, u32[]{:S(2)}) collective-permute-start(bf16[128,4096]{1,0:T(8,128)(2,1)S(1)} %gather_fusion.7), channel_id=1, source_target_pairs={{8,0},{16,8},{24,16},{9,1},{17,9},{25,17},{10,2},{18,10},{26,18},{... | collective-permute-start | bytes 3145736 | tf_op jit(solution)/shard_map/ppermute | solution.py:13
Sparse Core Ops, SparseCore 0:
  9.9 57.1 all-gather.6
  68.9 54.4 all-gather.8
  189.5 41.1 reduce-scatter.4
  234.2 41.2 reduce-scatter.2
where the time goes:
time: 292 us; the launch traced here: 287 us
  waiting for transfers between devices  101 us (35%)
  matrix products  59.4 us (20%)
  local copies, waits for them, and re-layouts  54.4 us (19%)
  other arithmetic  36.1 us (12%)
  blocking collectives  19.1 us (7%)
  between operations  14.6 us (5%)
    reduce_scatter x1, waiting for transfers between devices, per_device(): lax.psum_scatter(out_part.astype(jnp.bfloat16), 'et', scatter_dimension=0...  41.3 us
    all_gather x1, waiting for transfers between devices, per_device(): lax.all_gather(local_grads, 'et', axis=0, tiled=True)  26.7 us
    all_gather x1, waiting for transfers between devices, per_device(): lax.all_gather(local_rows, 'et', axis=0, tiled=True)  17.2 us
    reduce_scatter x1, waiting for transfers between devices, per_device(): lax.psum_scatter(grad_part.astype(jnp.bfloat16), 'et', scatter_dimension=...  14.8 us
    gather x2, local copies, waits for them, and re-layouts, per_device(): rows_in.append(all_rows[sources])  14 us
    scatter-add x2, other arithmetic, per_device(): grad_part.at[dest_in[expert]]  13.9 us
    gather x2, local copies, waits for them, and re-layouts, per_device(): grads_in.append(all_grads[sources])  13.5 us
    scatter-add x2, other arithmetic, per_device(): out_part.at[dest_in[expert]]  12.6 us
  transfers between devices with their start and end apart: 5, of which 4 were waited for; matrix products, arithmetic and copies ran while one was open for 29% of the time, Pallas kernels for 0%

commit v1 on v0

v1 whole, which is shorter than its diff:
```python
import jax
import jax.numpy as jnp
from jax import lax
from jax.sharding import PartitionSpec as P

E_WIN = 2
MOST = 16
TAIL = 128


def shifted(value, axis, steps):
    count = lax.axis_size(axis)
    first, last = (max(0, -steps), min(count, count - steps))
    return lax.ppermute(value, axis, [(source, source + steps) for source in range(first, last)])


def silu_parts(pre_gate):
    sigma = jax.nn.sigmoid(pre_gate)
    return (pre_gate * sigma, sigma * (1.0 + pre_gate * (1.0 - sigma)))


def local_slots(local_routes, local_gates):
    count = local_routes.shape[0]
    sources, weights, targets = [], [], []
    for expert in range(E_WIN):
        matches = local_routes == expert
        routed = jnp.any(matches, axis=1)
        gate_val = jnp.sum(jnp.where(matches, local_gates.astype(jnp.float32), 0.0), axis=1)
        positions = jnp.cumsum(routed.astype(jnp.int32), dtype=jnp.int32) - 1
        target = jnp.where(routed, positions, MOST)
        sources.append(
            jnp.zeros((MOST,), jnp.int32).at[target].set(jnp.arange(count, dtype=jnp.int32), mode="drop")
        )
        weights.append(jnp.zeros((MOST,), jnp.float32).at[target].set(gate_val, mode="drop"))
        targets.append(jnp.where(routed, positions + expert * MOST, E_WIN * MOST))
    return jnp.concatenate(sources), jnp.concatenate(weights), targets


def reduce_to_owner(parts, axis):
    n = lax.axis_size(axis)
    me = lax.axis_index(axis)
    total = jnp.take(parts, me, axis=0).astype(jnp.float32)
    for step in range(1, n):
        chunk = jnp.take(parts, (me + step) % n, axis=0)
        total = total + lax.ppermute(chunk, axis, [(s, (s + step) % n) for s in range(n)]).astype(jnp.float32)
    return total


def unpack(slot_sums, targets):
    padded = jnp.concatenate([slot_sums, jnp.zeros((1, slot_sums.shape[1]), jnp.float32)], axis=0)
    total = padded[targets[0]]
    for target in targets[1:]:
        total = total + padded[target]
    return total.astype(jnp.bfloat16)


def per_device(tokens, gate_vals, expert_ids, grad_out, w_gate, w_up, w_down):
    local_rows = tokens[0]
    local_grads = grad_out[0]
    gate_mats = w_gate[0]
    up_mats = w_up[0]
    down_mats = w_down[0]
    n = lax.axis_size("et")
    width = local_rows.shape[1]
    sources, weights, targets = local_slots(expert_ids[0], gate_vals[0])
    weight_cols = jnp.broadcast_to(weights.astype(jnp.bfloat16)[:, None], (E_WIN * MOST, TAIL))
    packed = jnp.concatenate([local_rows[sources], weight_cols], axis=1)
    all_rows = lax.all_gather(packed, "et", axis=0, tiled=True).reshape(n, E_WIN, MOST, width + TAIL)
    grads = lax.all_gather(local_grads[sources], "et", axis=0, tiled=True).reshape(n, E_WIN, MOST, width)
    outs = []
    stored = []
    for expert in range(E_WIN):
        rows = all_rows[:, expert, :, :width].reshape(n * MOST, width)
        gate_w = all_rows[:, expert, :, width].reshape(n * MOST, 1).astype(jnp.float32)
        pre_gate = jnp.dot(rows, gate_mats[expert], preferred_element_type=jnp.float32)
        pre_up = jnp.dot(rows, up_mats[expert], preferred_element_type=jnp.float32)
        activated, slopes = silu_parts(pre_gate)
        hidden = (activated * pre_up).astype(jnp.bfloat16)
        out_e = gate_w * jnp.dot(hidden, down_mats[expert], preferred_element_type=jnp.float32)
        outs.append(out_e.astype(jnp.bfloat16).reshape(n, MOST, width))
        stored.append((gate_w, pre_up, activated, slopes))
    out_parts = jnp.stack(outs, axis=1).reshape(n, E_WIN * MOST, width)
    out_share = unpack(reduce_to_owner(out_parts, "et"), targets)
    grad_outs = []
    for expert in range(E_WIN):
        gate_w, pre_up, activated, slopes = stored[expert]
        grad_rows = grads[:, expert].reshape(n * MOST, width)
        d_hidden = gate_w * lax.dot_general(
            grad_rows, down_mats[expert], (((1,), (1,)), ((), ())), preferred_element_type=jnp.float32
        )
        d_gate = (d_hidden * pre_up * slopes).astype(jnp.bfloat16)
        d_up = (d_hidden * activated).astype(jnp.bfloat16)
        grad_e = lax.dot_general(
            d_gate, gate_mats[expert], (((1,), (1,)), ((), ())), preferred_element_type=jnp.float32
        ) + lax.dot_general(d_up, up_mats[expert], (((1,), (1,)), ((), ())), preferred_element_type=jnp.float32)
        grad_outs.append(grad_e.astype(jnp.bfloat16).reshape(n, MOST, width))
    grad_parts = jnp.stack(grad_outs, axis=1).reshape(n, E_WIN * MOST, width)
    grad_share = unpack(reduce_to_owner(grad_parts, "et"), targets)
    received = shifted(grad_share, "pipe", -1)
    return (out_share[None], received[None])


def solution(mesh):
    placed = (
        P("pipe", "et", None),
        P("pipe", "et", None),
        P("pipe", "et", None),
        P("pipe", "et", None),
        P("pipe", None, None, "et"),
        P("pipe", None, None, "et"),
        P("pipe", None, "et", None),
    )
    return jax.shard_map(
        per_device,
        mesh=mesh,
        in_specs=placed,
        out_specs=(P("pipe", "et", None), P("pipe", "et", None)),
        check_vma=False,
    )
```

time: 292 us -> 226 us (0.77); the launches traced: 287 us -> 226 us
  local copies, waits for them, and re-layouts: 54.4 us -> 24.7 us
  starting transfers between devices: 1.7 us -> 25.9 us
  other arithmetic: 36.1 us -> 12.3 us
  blocking collectives: 19.1 us -> 0 us
  matrix products: 59.4 us -> 51.5 us
  waiting for transfers between devices: 101 us -> 96.6 us
    reduce_scatter x2 -> x0, waiting for transfers between devices: 56 us -> none  [the longest x1 41.3 us: per_device(): lax.psum_scatter(out_part.astype(jnp.bfloat16), 'et', scatter_dimension=0...]
    scatter-add x4 -> x0, other arithmetic: 26.6 us -> none  [the longest x2 13.9 us: per_device(): grad_part.at[dest_in[expert]]]
    ppermute x0 -> x14, waiting for transfers between devices: none -> 25.6 us  [reduce_to_owner(): lax.ppermute(chunk, axis, [(s, (s + step) % n) for s in range(n)])]
    ppermute x0 -> x14, starting transfers between devices: none -> 24.5 us  [reduce_to_owner(): lax.ppermute(chunk, axis, [(s, (s + step) % n) for s in range(n)])]
    gather x10 -> x6, local copies, waits for them, and re-layouts: 33 us -> 11.1 us  [the longest x2 5.12 us: unpack(): total = padded[targets[0]]]
    all_gather x2 -> x0, blocking collectives: 19.1 us -> none  [the longest x1 10.5 us: per_device(): gathered_routes = lax.all_gather(local_routes, 'et', axis=0, tiled=True)]
    ppermute x1, waiting for transfers between devices: 0.01 us -> 15.3 us  [shifted(): lax.ppermute(value, axis, [(source, source + steps) for source in range(f...]
    scatter x4, local copies, waits for them, and re-layouts: 17.7 us -> 4.08 us  [the longest x2 2.13 us: local_slots(): jnp.zeros((MOST,), jnp.float32).at[target].set(gate_val, mode='drop')]
  transfers between devices with their start and end apart: 5 -> 17, of which waited for: 4 -> 8; matrix products, arithmetic and copies ran while one was open for 29% -> 11% of each run, Pallas kernels for 0% -> 0%
where the time goes in v1:
time: 226 us
  waiting for transfers between devices  96.6 us (43%)
  matrix products  51.5 us (23%)
  starting transfers between devices  25.9 us (11%)
  local copies, waits for them, and re-layouts  24.7 us (11%)
  between operations  14.7 us (7%)
  other arithmetic  12.3 us (5%)
    all_gather x1, waiting for transfers between devices, per_device(): lax.all_gather(packed, 'et', axis=0, tiled=True)  29 us
    all_gather x1, waiting for transfers between devices, per_device(): lax.all_gather(local_grads[sources], 'et', axis=0, tiled=True)  26.7 us
    ppermute x14, waiting for transfers between devices, reduce_to_owner(): lax.ppermute(chunk, axis, [(s, (s + step) % n) for s in range(n)])  25.6 us
    ppermute x14, starting transfers between devices, reduce_to_owner(): lax.ppermute(chunk, axis, [(s, (s + step) % n) for s in range(n)])  24.5 us
    ppermute x1, waiting for transfers between devices, shifted(): lax.ppermute(value, axis, [(source, source + steps) for source in range(f...  15.3 us
    dot_general x2, matrix products, per_device(): lax.dot_general(grad_rows, down_mats[expert], (((1,), (1,)), ((), ())), p...  11.6 us
    dot_general x2, matrix products, per_device(): lax.dot_general(d_up, up_mats[expert], (((1,), (1,)), ((), ())), preferre...  11.4 us
    dot_general x2, matrix products, per_device(): jnp.dot(rows, gate_mats[expert], preferred_element_type=jnp.float32)  10 us
  transfers between devices with their start and end apart: 17, of which 8 were waited for; matrix products, arithmetic and copies ran while one was open for 11% of the time, Pallas kernels for 0%

profile of v1, /device:TPU:0, one launch (start us, length us, event | category | flops | bytes accessed | tf_op | source)
XLA Modules:
  0.0 225.7 jit_solution(14695361973196415061)
XLA Ops:
  16.7 26.7 %all-gather.6.cloned.1.call-done = bf16[256,4096]{1,0:T(8,128)(2,1)} async-done(((bf16[32,4096]{1,0:T(8,128)(2,1)}), bf16[256,4096]{1,0:T(8,128)(2,1)}) %all-gather.6.cloned.1.call-update) | async-done | bytes 2097168 | tf_op jit(solution)/shard_map/all_gather | solution.py:69
  45.2 29.0 %all-gather.4.cloned.1.call-done = bf16[256,4224]{1,0:T(8,128)(2,1)} async-done(((bf16[32,4224]{1,0:T(8,128)(2,1)}), bf16[256,4224]{1,0:T(8,128)(2,1)}) %all-gather.4.cloned.1.call-update) | async-done | bytes 2162704 | tf_op jit(solution)/shard_map/all_gather | solution.py:68
  76.7 4.7 %fusion.22 = f32[128,896]{1,0:T(8,128)S(1)} fusion(bf16[128,4096]{1,0:T(8,128)(2,1)S(1)} %bitcast.138, bf16[1,2,4096,896]{3,2,1,0:T(8,128)(2,1)} %param.13), kind=kOutput, calls=%fused_computation.32 | convolution fusion | flops 939524096 | bytes 8847360 | tf_op jit(solution)/shard_map/dot_general | solution.py:75
  84.1 5.3 %fusion.10 = f32[128,896]{1,0:T(8,128)} fusion(bf16[128,4096]{1,0:T(8,128)(2,1)S(1)} %bitcast.135, bf16[1,2,4096,896]{3,2,1,0:T(8,128)(2,1)} %param.13), kind=kOutput, calls=%fused_computation.20 | convolution fusion | flops 939524096 | bytes 8847360 | tf_op jit(solution)/shard_map/dot_general | solution.py:75
  91.7 5.7 %fusion.60 = f32[128,896]{1,0:T(8,128)S(1)} fusion(bf16[128,4096]{1,0:T(8,128)(2,1)S(1)} %bitcast.133, bf16[1,2,896,4096]{3,2,1,0:T(8,128)(2,1)} %param.15, f32[128]{0:T(128)S(1)} %reshape.453), kind=kOutput, calls=%fused_computation.58 | convolution fusion | flops 939638784 | bytes 8847872 | tf_op jit(solution)/shard_map/dot_general | solution.py:88
  97.4 5.7 %fusion.16 = f32[128,4096]{1,0:T(8,128)S(1)} fusion(bf16[1,2,4096,896]{3,2,1,0:T(8,128)(2,1)} %param.14, f32[128,896]{1,0:T(8,128)S(1)} %fusion.60, f32[128,896]{1,0:T(8,128)S(1)} %fusion.22), kind=kOutput, calls=%fused_computation.26 | convolution fusion | flops 940212224 | bytes 10354688 | tf_op jit(solution)/shard_map/dot_general | solution.py:95
  103.2 4.5 %fusion.54 = bf16[128,4096]{1,0:T(8,128)(2,1)S(1)} fusion(bf16[1,2,896,4096]{3,2,1,0:T(8,128)(2,1)} %param.15, f32[128]{0:T(128)S(1)} %reshape.453, f32[128,896]{1,0:T(8,128)S(1)} %fusion.18, f32[128,896]{1,0:T(8,128)S(1)} %fusion.22), kind=kOutput, calls=%fused_computation.52 | convolution fusion | flops 941260800 | bytes 9306624 | tf_op jit(solution)/shard_map/dot_general | solution.py:79
  107.7 3.6 %fusion.57 = bf16[128,4096]{1,0:T(8,128)(2,1)S(1)} fusion(f32[128,4096]{1,0:T(8,128)S(1)} %fusion.16, bf16[1,2,4096,896]{3,2,1,0:T(8,128)(2,1)S(1)} %bitcast.143, f32[128,896]{1,0:T(8,128)} %copy-done.8, f32[128,896]{1,0:T(8,128)S(1)} %fusion.60, f32[128,896]{1,0:T(8,128)} %copy-done.9), kind=kOutput, calls=%fused_computation.53 | convolution fusion | flops 941719552 | bytes 11862016 | tf_op jit(solution)/shard_map/dot_general | solution.py:93
  111.6 5.9 %fusion.63 = f32[128,896]{1,0:T(8,128)S(1)} fusion(bf16[128,4096]{1,0:T(8,128)(2,1)S(1)} %bitcast.132, bf16[1,2,896,4096]{3,2,1,0:T(8,128)(2,1)} %param.15, f32[128]{0:T(128)S(1)} %reshape.454), kind=kOutput, calls=%fused_computation.59 | convolution fusion | flops 939638784 | bytes 8847872 | tf_op jit(solution)/shard_map/dot_general | solution.py:88
  117.6 5.7 %fusion.4 = f32[128,4096]{1,0:T(8,128)S(1)} fusion(bf16[1,2,4096,896]{3,2,1,0:T(8,128)(2,1)} %param.14, f32[128,896]{1,0:T(8,128)S(1)} %fusion.63, f32[128,896]{1,0:T(8,128)S(1)} %copy-done.6), kind=kOutput, calls=%fused_computation.14 | convolution fusion | flops 940212224 | bytes 10354688 | tf_op jit(solution)/shard_map/dot_general | solution.py:95
  123.3 4.6 %fusion.48 = bf16[128,4096]{1,0:T(8,128)(2,1)S(1)} fusion(bf16[1,2,896,4096]{3,2,1,0:T(8,128)(2,1)} %param.15, f32[128]{0:T(128)S(1)} %reshape.454, f32[128,896]{1,0:T(8,128)S(1)} %copy-done.7, f32[128,896]{1,0:T(8,128)S(1)} %copy-done.6), kind=kOutput, calls=%fused_computation.50 | convolution fusion | flops 941260800 | bytes 9306624 | tf_op jit(solution)/shard_map/dot_general | solution.py:79
  127.9 2.5 %fusion.51 = bf16[128,4096]{1,0:T(8,128)(2,1)S(1)} fusion(f32[128,4096]{1,0:T(8,128)S(1)} %fusion.4, bf16[1,2,4096,896]{3,2,1,0:T(8,128)(2,1)S(1)} %bitcast.145, f32[128,896]{1,0:T(8,128)S(1)} %copy-done.6, f32[128,896]{1,0:T(8,128)S(1)} %fusion.63, f32[128,896]{1,0:T(8,128)S(1)} %copy-done.7), kind=kOutput, calls=%fused_computation.51 | convolution fusion | flops 941719552 | bytes 11862016 | tf_op jit(solution)/shard_map/dot_general | solution.py:93
  135.8 3.7 %collective-permute-done.10 = bf16[32,4096]{1,0:T(8,128)(2,1)S(1)} collective-permute-done((bf16[32,4096]{1,0:T(8,128)(2,1)S(1)}, bf16[32,4096]{1,0:T(8,128)(2,1)S(1)}, u32[]{:S(2)}, u32[]{:S(2)}) %collective-permute-start.10) | collective-permute-done | bytes 262176 | tf_op jit(solution)/shard_map/ppermute | solution.py:45
  139.5 12.7 %collective-permute-start.8 = (bf16[32,4096]{1,0:T(8,128)(2,1)S(1)}, bf16[32,4096]{1,0:T(8,128)(2,1)S(1)}, u32[]{:S(2)}, u32[]{:S(2)}) collective-permute-start(bf16[32,4096]{1,0:T(8,128)(2,1)S(1)} %get-tuple-element.32), channel_id=1, source_target_pairs={{0,2},{1,3},{2,4},{3,5},{4,6},{5,7},{6,0},{7,1},{8,10},{9,11},{10,... | collective-permute-start | bytes 786440 | tf_op jit(solution)/shard_map/ppermute | solution.py:45
  152.2 2.2 collective-permute-start.9
  159.7 18.1 %collective-permute-done.9 = bf16[32,4096]{1,0:T(8,128)(2,1)S(1)} collective-permute-done((bf16[32,4096]{1,0:T(8,128)(2,1)S(1)}, bf16[32,4096]{1,0:T(8,128)(2,1)S(1)}, u32[]{:S(2)}, u32[]{:S(2)}) %collective-permute-start.9) | collective-permute-done | bytes 262176 | tf_op jit(solution)/shard_map/ppermute | solution.py:45
  178.1 2.5 %gather_fusion.5 = f32[128,4096]{1,0:T(8,128)} fusion(f32[33,4096]{1,0:T(8,128)S(1)} %concatenate.49, s32[1024]{0:T(1024)S(1)} %pad_clamp_fusion), kind=kCustom, calls=%fused_computation.5 | custom fusion | bytes 4194816 | tf_op jit(solution)/shard_map/gather | solution.py:53
  180.6 2.6 %gather_fusion.4 = f32[128,4096]{1,0:T(8,128)} fusion(f32[33,4096]{1,0:T(8,128)S(1)} %concatenate.49, s32[1024]{0:T(1024)S(1)} %pad_clamp_fusion.1), kind=kCustom, calls=%fused_computation.4 | custom fusion | bytes 4194816 | tf_op jit(solution)/shard_map/gather | solution.py:51
  183.2 2.6 %collective-permute-start.6 = (bf16[32,4096]{1,0:T(8,128)(2,1)S(1)}, bf16[32,4096]{1,0:T(8,128)(2,1)S(1)}, u32[]{:S(2)}, u32[]{:S(2)}) collective-permute-start(bf16[32,4096]{1,0:T(8,128)(2,1)S(1)} %get-tuple-element.36), channel_id=1, source_target_pairs={{0,7},{1,0},{2,1},{3,2},{4,3},{5,4},{6,5},{7,6},{8,15},{9,8},{10,9... | collective-permute-start | bytes 786440 | tf_op jit(solution)/shard_map/ppermute | solution.py:45
  185.8 3.4 %add_convert_fusion = bf16[128,4096]{1,0:T(8,128)(2,1)} fusion(f32[128,4096]{1,0:T(8,128)} %gather_fusion.4, f32[128,4096]{1,0:T(8,128)} %gather_fusion.5), kind=kLoop, calls=%fused_computation.56 | loop fusion | flops 1048576 | bytes 5242880 | tf_op jit(solution)/shard_map/convert_element_type | solution.py:54
  195.6 2.6 %gather_fusion.1 = f32[128,4096]{1,0:T(8,128)} fusion(f32[33,4096]{1,0:T(8,128)S(1)} %concatenate.48, s32[1024]{0:T(1024)S(1)} %pad_clamp_fusion.1), kind=kCustom, calls=%fused_computation.1 | custom fusion | bytes 4194816 | tf_op jit(solution)/shard_map/gather | solution.py:51
  198.2 3.0 %fusion.66 = bf16[1,128,4096]{2,1,0:T(8,128)(2,1)} fusion(f32[128,4096]{1,0:T(8,128)} %gather_fusion.1, f32[128,4096]{1,0:T(8,128)S(1)} %gather_fusion.2), kind=kLoop, calls=%fused_computation.60 | loop fusion | flops 1048576 | bytes 5242880 | tf_op jit(solution)/shard_map/convert_element_type | solution.py:54
  201.2 15.3 %collective-permute-done.14 = bf16[128,4096]{1,0:T(8,128)(2,1)} collective-permute-done((bf16[128,4096]{1,0:T(8,128)(2,1)}, bf16[128,4096]{1,0:T(8,128)(2,1)}, u32[]{:S(2)}, u32[]{:S(2)}) %collective-permute-start.14) | collective-permute-done | bytes 1048608 | tf_op jit(solution)/shard_map/ppermute | solution.py:14
  216.6 2.3 %copy.32 = bf16[1,128,4096]{2,1,0:T(8,128)(2,1)} copy(bf16[1,128,4096]{2,1,0:T(8,128)(2,1)} %bitcast.42) | data formatting | bytes 2097152
  (114 shorter events, 36.1 us)
Async XLA Ops:
  7.2 36.2 %all-gather.6.cloned.1.call-start = ((), (), s32[]{:S(2)}) async-start(), calls=%async_computation.1 | async-start | bytes 2359296 | tf_op jit(solution)/shard_map/all_gather | solution.py:69
  12.7 61.4 %all-gather.4.cloned.1.call-start = ((), (), s32[]{:S(2)}) async-start(), calls=%async_computation | async-start | bytes 2433024 | tf_op jit(solution)/shard_map/all_gather | solution.py:68
  82.8 20.3 %copy-start.8 = (f32[128,896]{1,0:T(8,128)}, f32[128,896]{1,0:T(8,128)S(1)}, u32[]{:S(2)}) copy-start(f32[128,896]{1,0:T(8,128)S(1)} %fusion.22) | copy-start | bytes 1376260
  84.1 19.0 %copy-start.9 = (f32[128,896]{1,0:T(8,128)}, f32[128,896]{1,0:T(8,128)S(1)}, u32[]{:S(2)}) copy-start(f32[128,896]{1,0:T(8,128)S(1)} %fusion.18) | copy-start | bytes 1376260
  91.7 16.0 %slice-start = ((s8[14680064]{0:T(1024)(128)(4,1)}), s8[4194304]{0:T(1024)(128)(4,1)S(1)}, s32[]{:S(2)}) async-start(s8[14680064]{0:T(1024)(128)(4,1)} %bitcast.142), calls=%async_computation.2 | async-start | bytes 8388608
  91.7 16.0 %slice-start.1 = ((s8[14680064]{0:T(1024)(128)(4,1)}), s8[4194304]{0:T(1024)(128)(4,1)S(1)}, s32[]{:S(2)}) async-start(s8[14680064]{0:T(1024)(128)(4,1)} %bitcast.142), calls=%async_computation.3 | async-start | bytes 8388608
  111.6 16.2 %slice-start.4 = ((s8[14680064]{0:T(1024)(128)(4,1)}), s8[4194304]{0:T(1024)(128)(4,1)S(1)}, s32[]{:S(2)}) async-start(s8[14680064]{0:T(1024)(128)(4,1)} %bitcast.144), calls=%async_computation.6 | async-start | bytes 8388608
  111.6 16.2 %slice-start.5 = ((s8[14680064]{0:T(1024)(128)(4,1)}), s8[4194304]{0:T(1024)(128)(4,1)S(1)}, s32[]{:S(2)}) async-start(s8[14680064]{0:T(1024)(128)(4,1)} %bitcast.144), calls=%async_computation.7 | async-start | bytes 8388608
  131.0 8.5 %collective-permute-start.10 = (bf16[32,4096]{1,0:T(8,128)(2,1)S(1)}, bf16[32,4096]{1,0:T(8,128)(2,1)S(1)}, u32[]{:S(2)}, u32[]{:S(2)}) collective-permute-start(bf16[32,4096]{1,0:T(8,128)(2,1)S(1)} %get-tuple-element.30), channel_id=1, source_target_pairs={{0,4},{1,5},{2,6},{3,7},{4,0},{5,1},{6,2},{7,3},{8,12},{9,13},{10,... | collective-permute-start | bytes 786440 | tf_op jit(solution)/shard_map/ppermute | solution.py:45
  132.4 19.8 %collective-permute-start.11 = (bf16[32,4096]{1,0:T(8,128)(2,1)S(1)}, bf16[32,4096]{1,0:T(8,128)(2,1)S(1)}, u32[]{:S(2)}, u32[]{:S(2)}) collective-permute-start(bf16[32,4096]{1,0:T(8,128)(2,1)S(1)} %get-tuple-element.29), channel_id=1, source_target_pairs={{0,5},{1,6},{2,7},{3,0},{4,1},{5,2},{6,3},{7,4},{8,13},{9,14},{10,... | collective-permute-start | bytes 786440 | tf_op jit(solution)/shard_map/ppermute | solution.py:45
  132.7 22.9 %collective-permute-start.12 = (bf16[32,4096]{1,0:T(8,128)(2,1)S(1)}, bf16[32,4096]{1,0:T(8,128)(2,1)S(1)}, u32[]{:S(2)}, u32[]{:S(2)}) collective-permute-start(bf16[32,4096]{1,0:T(8,128)(2,1)S(1)} %get-tuple-element.28), channel_id=1, source_target_pairs={{0,6},{1,7},{2,0},{3,1},{4,2},{5,3},{6,4},{7,5},{8,14},{9,15},{10,... | collective-permute-start | bytes 786440 | tf_op jit(solution)/shard_map/ppermute | solution.py:45
  134.1 21.4 %collective-permute-start.13 = (bf16[32,4096]{1,0:T(8,128)(2,1)S(1)}, bf16[32,4096]{1,0:T(8,128)(2,1)S(1)}, u32[]{:S(2)}, u32[]{:S(2)}) collective-permute-start(bf16[32,4096]{1,0:T(8,128)(2,1)S(1)} %get-tuple-element.27), channel_id=1, source_target_pairs={{0,7},{1,0},{2,1},{3,2},{4,3},{5,4},{6,5},{7,6},{8,15},{9,8},{10,9... | collective-permute-start | bytes 786440 | tf_op jit(solution)/shard_map/ppermute | solution.py:45
  135.4 20.5 %collective-permute-start.7 = (bf16[32,4096]{1,0:T(8,128)(2,1)S(1)}, bf16[32,4096]{1,0:T(8,128)(2,1)S(1)}, u32[]{:S(2)}, u32[]{:S(2)}) collective-permute-start(bf16[32,4096]{1,0:T(8,128)(2,1)S(1)} %get-tuple-element.26), channel_id=1, source_target_pairs={{0,1},{1,2},{2,3},{3,4},{4,5},{5,6},{6,7},{7,0},{8,9},{9,10},{10,1... | collective-permute-start | bytes 786440 | tf_op jit(solution)/shard_map/ppermute | solution.py:45
  139.5 19.5 %collective-permute-start.8 = (bf16[32,4096]{1,0:T(8,128)(2,1)S(1)}, bf16[32,4096]{1,0:T(8,128)(2,1)S(1)}, u32[]{:S(2)}, u32[]{:S(2)}) collective-permute-start(bf16[32,4096]{1,0:T(8,128)(2,1)S(1)} %get-tuple-element.32), channel_id=1, source_target_pairs={{0,2},{1,3},{2,4},{3,5},{4,6},{5,7},{6,0},{7,1},{8,10},{9,11},{10,... | collective-permute-start | bytes 786440 | tf_op jit(solution)/shard_map/ppermute | solution.py:45
  152.2 25.5 %collective-permute-start.9 = (bf16[32,4096]{1,0:T(8,128)(2,1)S(1)}, bf16[32,4096]{1,0:T(8,128)(2,1)S(1)}, u32[]{:S(2)}, u32[]{:S(2)}) collective-permute-start(bf16[32,4096]{1,0:T(8,128)(2,1)S(1)} %get-tuple-element.31), channel_id=1, source_target_pairs={{0,3},{1,4},{2,5},{3,6},{4,7},{5,0},{6,1},{7,2},{8,11},{9,12},{10,... | collective-permute-start | bytes 786440 | tf_op jit(solution)/shard_map/ppermute | solution.py:45
  155.5 27.6 %collective-permute-start = (bf16[32,4096]{1,0:T(8,128)(2,1)}, bf16[32,4096]{1,0:T(8,128)(2,1)}, u32[]{:S(2)}, u32[]{:S(2)}) collective-permute-start(bf16[32,4096]{1,0:T(8,128)(2,1)} %get-tuple-element.35), channel_id=1, source_target_pairs={{0,1},{1,2},{2,3},{3,4},{4,5},{5,6},{6,7},{7,0},{8,9},{9,10},{10,1... | collective-permute-start | bytes 786440 | tf_op jit(solution)/shard_map/ppermute | solution.py:45
  155.5 27.6 %collective-permute-start.1 = (bf16[32,4096]{1,0:T(8,128)(2,1)}, bf16[32,4096]{1,0:T(8,128)(2,1)}, u32[]{:S(2)}, u32[]{:S(2)}) collective-permute-start(bf16[32,4096]{1,0:T(8,128)(2,1)} %get-tuple-element.41), channel_id=1, source_target_pairs={{0,2},{1,3},{2,4},{3,5},{4,6},{5,7},{6,0},{7,1},{8,10},{9,11},{10,... | collective-permute-start | bytes 786440 | tf_op jit(solution)/shard_map/ppermute | solution.py:45
  155.9 33.3 %collective-permute-start.2 = (bf16[32,4096]{1,0:T(8,128)(2,1)}, bf16[32,4096]{1,0:T(8,128)(2,1)}, u32[]{:S(2)}, u32[]{:S(2)}) collective-permute-start(bf16[32,4096]{1,0:T(8,128)(2,1)} %get-tuple-element.40), channel_id=1, source_target_pairs={{0,3},{1,4},{2,5},{3,6},{4,7},{5,0},{6,1},{7,2},{8,11},{9,12},{10,... | collective-permute-start | bytes 786440 | tf_op jit(solution)/shard_map/ppermute | solution.py:45
  159.0 31.5 %collective-permute-start.3 = (bf16[32,4096]{1,0:T(8,128)(2,1)}, bf16[32,4096]{1,0:T(8,128)(2,1)}, u32[]{:S(2)}, u32[]{:S(2)}) collective-permute-start(bf16[32,4096]{1,0:T(8,128)(2,1)} %get-tuple-element.39), channel_id=1, source_target_pairs={{0,4},{1,5},{2,6},{3,7},{4,0},{5,1},{6,2},{7,3},{8,12},{9,13},{10,... | collective-permute-start | bytes 786440 | tf_op jit(solution)/shard_map/ppermute | solution.py:45
  177.7 12.8 %collective-permute-start.4 = (bf16[32,4096]{1,0:T(8,128)(2,1)}, bf16[32,4096]{1,0:T(8,128)(2,1)}, u32[]{:S(2)}, u32[]{:S(2)}) collective-permute-start(bf16[32,4096]{1,0:T(8,128)(2,1)} %get-tuple-element.38), channel_id=1, source_target_pairs={{0,5},{1,6},{2,7},{3,0},{4,1},{5,2},{6,3},{7,4},{8,13},{9,14},{10,... | collective-permute-start | bytes 786440 | tf_op jit(solution)/shard_map/ppermute | solution.py:45
  183.2 8.6 %collective-permute-start.5 = (bf16[32,4096]{1,0:T(8,128)(2,1)S(1)}, bf16[32,4096]{1,0:T(8,128)(2,1)S(1)}, u32[]{:S(2)}, u32[]{:S(2)}) collective-permute-start(bf16[32,4096]{1,0:T(8,128)(2,1)S(1)} %get-tuple-element.37), channel_id=1, source_target_pairs={{0,6},{1,7},{2,0},{3,1},{4,2},{5,3},{6,4},{7,5},{8,14},{9,15},{10,... | collective-permute-start | bytes 786440 | tf_op jit(solution)/shard_map/ppermute | solution.py:45
  183.2 9.5 %collective-permute-start.6 = (bf16[32,4096]{1,0:T(8,128)(2,1)S(1)}, bf16[32,4096]{1,0:T(8,128)(2,1)S(1)}, u32[]{:S(2)}, u32[]{:S(2)}) collective-permute-start(bf16[32,4096]{1,0:T(8,128)(2,1)S(1)} %get-tuple-element.36), channel_id=1, source_target_pairs={{0,7},{1,0},{2,1},{3,2},{4,3},{5,4},{6,5},{7,6},{8,15},{9,8},{10,9... | collective-permute-start | bytes 786440 | tf_op jit(solution)/shard_map/ppermute | solution.py:45
  189.2 27.3 %collective-permute-start.14 = (bf16[128,4096]{1,0:T(8,128)(2,1)}, bf16[128,4096]{1,0:T(8,128)(2,1)}, u32[]{:S(2)}, u32[]{:S(2)}) collective-permute-start(bf16[128,4096]{1,0:T(8,128)(2,1)} %add_convert_fusion), channel_id=1, source_target_pairs={{8,0},{16,8},{24,16},{9,1},{17,9},{25,17},{10,2},{18,10},{26,18},{... | collective-permute-start | bytes 3145736 | tf_op jit(solution)/shard_map/ppermute | solution.py:14
  198.2 20.7 %copy-start.1 = (bf16[1,128,4096]{2,1,0:T(8,128)(2,1)S(1)}, bf16[1,128,4096]{2,1,0:T(8,128)(2,1)}, u32[]{:S(2)}) copy-start(bf16[1,128,4096]{2,1,0:T(8,128)(2,1)} %param.12) | copy-start | bytes 3145732
  (11 other events, 72.4 us)
Sparse Core Ops, SparseCore 0:
  12.8 30.5 all-gather.5
  45.9 28.1 all-gather.3

commit v2 on v1

--- a/solution.py
+++ b/solution.py
@@ -26,23 +26,30 @@
         matches = local_routes == expert
         routed = jnp.any(matches, axis=1)
         gate_val = jnp.sum(jnp.where(matches, local_gates.astype(jnp.float32), 0.0), axis=1)
-        positions = jnp.cumsum(routed.astype(jnp.int32), dtype=jnp.int32) - 1
+        positions = jnp.minimum(jnp.cumsum(routed.astype(jnp.int32), dtype=jnp.int32) - 1, MOST)
         target = jnp.where(routed, positions, MOST)
         sources.append(
             jnp.zeros((MOST,), jnp.int32).at[target].set(jnp.arange(count, dtype=jnp.int32), mode="drop")
         )
         weights.append(jnp.zeros((MOST,), jnp.float32).at[target].set(gate_val, mode="drop"))
-        targets.append(jnp.where(routed, positions + expert * MOST, E_WIN * MOST))
+        targets.append(jnp.where(routed & (positions < MOST), positions + expert * MOST, E_WIN * MOST))
     return jnp.concatenate(sources), jnp.concatenate(weights), targets
 
 
-def reduce_to_owner(parts, axis):
-    n = lax.axis_size(axis)
-    me = lax.axis_index(axis)
-    total = jnp.take(parts, me, axis=0).astype(jnp.float32)
-    for step in range(1, n):
+def reduce_to_previous(parts):
+    n = lax.axis_size("et")
+    stages = lax.axis_size("pipe")
+    me = lax.axis_index("et")
+    total = None
+    for step in range(n):
         chunk = jnp.take(parts, (me + step) % n, axis=0)
-        total = total + lax.ppermute(chunk, axis, [(s, (s + step) % n) for s in range(n)]).astype(jnp.float32)
+        pairs = [
+            (stage * n + source, (stage - 1) * n + (source + step) % n)
+            for stage in range(1, stages)
+            for source in range(n)
+        ]
+        moved = lax.ppermute(chunk, ("pipe", "et"), pairs).astype(jnp.float32)
+        total = moved if total is None else total + moved
     return total
 
 
@@ -63,16 +70,20 @@
     n = lax.axis_size("et")
     width = local_rows.shape[1]
     sources, weights, targets = local_slots(expert_ids[0], gate_vals[0])
+    next_routes = shifted(expert_ids[0], "pipe", -1)
+    next_targets = local_slots(next_routes, gate_vals[0])[2]
     weight_cols = jnp.broadcast_to(weights.astype(jnp.bfloat16)[:, None], (E_WIN * MOST, TAIL))
     packed = jnp.concatenate([local_rows[sources], weight_cols], axis=1)
     all_rows = lax.all_gather(packed, "et", axis=0, tiled=True).reshape(n, E_WIN, MOST, width + TAIL)
-    grads = lax.all_gather(local_grads[sources], "et", axis=0, tiled=True).reshape(n, E_WIN, MOST, width)
+    first_gate = jnp.dot(all_rows[:, 0, :, :width].reshape(n * MOST, width), gate_mats[0], preferred_element_type=jnp.float32)
+    grad_rows_local, first_gate = lax.optimization_barrier((local_grads[sources], first_gate))
+    grads = lax.all_gather(grad_rows_local, "et", axis=0, tiled=True).reshape(n, E_WIN, MOST, width)
     outs = []
     stored = []
     for expert in range(E_WIN):
         rows = all_rows[:, expert, :, :width].reshape(n * MOST, width)
         gate_w = all_rows[:, expert, :, width].reshape(n * MOST, 1).astype(jnp.float32)
-        pre_gate = jnp.dot(rows, gate_mats[expert], preferred_element_type=jnp.float32)
+        pre_gate = first_gate if expert == 0 else jnp.dot(rows, gate_mats[expert], preferred_element_type=jnp.float32)
         pre_up = jnp.dot(rows, up_mats[expert], preferred_element_type=jnp.float32)
         activated, slopes = silu_parts(pre_gate)
         hidden = (activated * pre_up).astype(jnp.bfloat16)
@@ -80,7 +91,8 @@
         outs.append(out_e.astype(jnp.bfloat16).reshape(n, MOST, width))
         stored.append((gate_w, pre_up, activated, slopes))
     out_parts = jnp.stack(outs, axis=1).reshape(n, E_WIN * MOST, width)
-    out_share = unpack(reduce_to_owner(out_parts, "et"), targets)
+    out_sums = lax.psum_scatter(out_parts.reshape(n * E_WIN * MOST, width), "et", scatter_dimension=0, tiled=True)
+    out_share = unpack(out_sums.astype(jnp.float32), targets)
     grad_outs = []
     for expert in range(E_WIN):
         gate_w, pre_up, activated, slopes = stored[expert]
@@ -95,8 +107,7 @@
         ) + lax.dot_general(d_up, up_mats[expert], (((1,), (1,)), ((), ())), preferred_element_type=jnp.float32)
         grad_outs.append(grad_e.astype(jnp.bfloat16).reshape(n, MOST, width))
     grad_parts = jnp.stack(grad_outs, axis=1).reshape(n, E_WIN * MOST, width)
-    grad_share = unpack(reduce_to_owner(grad_parts, "et"), targets)
-    received = shifted(grad_share, "pipe", -1)
+    received = unpack(reduce_to_previous(grad_parts), next_targets)
     return (out_share[None], received[None])
 
 

time: 226 us -> 191 us (0.85)
  waiting for transfers between devices: 96.6 us -> 78.8 us
  starting transfers between devices: 25.9 us -> 11.9 us
  matrix products: 51.5 us -> 46.7 us
    reduce_scatter x0 -> x1, waiting for transfers between devices: none -> 19.9 us  [per_device(): lax.psum_scatter(out_parts.reshape(n * E_WIN * MOST, width), 'et', scatte...]
    all_gather x1, waiting for transfers between devices: 26.7 us -> 8.29 us  [per_device(): lax.all_gather(grad_rows_local, 'et', axis=0, tiled=True)]
    ppermute x14 -> x8, starting transfers between devices: 24.5 us -> 10.3 us  [reduce_to_previous(): moved = lax.ppermute(chunk, ('pipe', 'et'), pairs).astype(jnp.float32)]
    ppermute x1, waiting for transfers between devices: 15.3 us -> 3.57 us  [shifted(): lax.ppermute(value, axis, [(source, source + steps) for source in range(f...]
    dot_general x2, matrix products: 9.09 us -> 2.6 us  [per_device(): jnp.dot(hidden, down_mats[expert], preferred_element_type=jnp.float32)]
    dot_general x2, matrix products: 3.34 us -> 9.35 us  [per_device(): pre_up = jnp.dot(rows, up_mats[expert], preferred_element_type=jnp.float32)]
    all_gather x1, waiting for transfers between devices: 29 us -> 23.4 us  [per_device(): lax.all_gather(packed, 'et', axis=0, tiled=True)]
    dot_general x2 -> x1, matrix products: 10 us -> 4.5 us  [per_device(): jnp.dot(rows, gate_mats[expert], preferred_element_type=jnp.float32)]
  transfers between devices with their start and end apart: 17 -> 12, of which waited for: 8 -> 9; matrix products, arithmetic and copies ran while one was open for 11% -> 31% of each run, Pallas kernels for 0% -> 0%
where the time goes in v2:
time: 191 us; the launch traced here: 189 us
  waiting for transfers between devices  78.8 us (41%)
  matrix products  46.7 us (24%)
  local copies, waits for them, and re-layouts  22.8 us (12%)
  between operations  14.6 us (8%)
  other arithmetic  13.8 us (7%)
  starting transfers between devices  11.9 us (6%)
    ppermute x8, waiting for transfers between devices, reduce_to_previous(): moved = lax.ppermute(chunk, ('pipe', 'et'), pairs).astype(jnp.float32)  23.6 us
    all_gather x1, waiting for transfers between devices, per_device(): lax.all_gather(packed, 'et', axis=0, tiled=True)  23.4 us
    reduce_scatter x1, waiting for transfers between devices, per_device(): lax.psum_scatter(out_parts.reshape(n * E_WIN * MOST, width), 'et', scatte...  19.9 us
    dot_general x2, matrix products, per_device(): lax.dot_general(d_up, up_mats[expert], (((1,), (1,)), ((), ())), preferre...  12 us
    ppermute x8, starting transfers between devices, reduce_to_previous(): moved = lax.ppermute(chunk, ('pipe', 'et'), pairs).astype(jnp.float32)  10.3 us
    dot_general x2, matrix products, per_device(): pre_up = jnp.dot(rows, up_mats[expert], preferred_element_type=jnp.float32)  9.35 us
    dot_general x2, matrix products, per_device(): lax.dot_general(grad_rows, down_mats[expert], (((1,), (1,)), ((), ())), p...  8.93 us
    all_gather x1, waiting for transfers between devices, per_device(): lax.all_gather(grad_rows_local, 'et', axis=0, tiled=True)  8.29 us
  transfers between devices with their start and end apart: 12, of which 9 were waited for; matrix products, arithmetic and copies ran while one was open for 31% of the time, Pallas kernels for 0%

profile of v2, /device:TPU:0, one launch (start us, length us, event | category | flops | bytes accessed | tf_op | source)
XLA Modules:
  0.0 188.6 jit_solution(3816019075428724777)
XLA Ops:
  18.6 3.6 %collective-permute-done.8 = s32[128,2]{0,1:T(2,128)S(1)} collective-permute-done((s32[128,2]{0,1:T(2,128)S(1)}, s32[128,2]{0,1:T(2,128)S(1)}, u32[]{:S(2)}, u32[]{:S(2)}) %collective-permute-start.8) | collective-permute-done | bytes 1056 | tf_op jit(solution)/shard_map/ppermute | solution.py:14
  23.3 23.4 %all-gather.3.cloned.1.call-done = bf16[256,4224]{1,0:T(8,128)(2,1)} async-done(((bf16[32,4224]{1,0:T(8,128)(2,1)}), bf16[256,4224]{1,0:T(8,128)(2,1)}) %all-gather.3.cloned.1.call-update) | async-done | bytes 2162704 | tf_op jit(solution)/shard_map/all_gather | solution.py:77
  48.4 4.3 %fusion.22 = f32[128,896]{1,0:T(8,128)S(1)} fusion(bf16[128,4096]{1,0:T(8,128)(2,1)S(1)} %bitcast.126, bf16[1,2,4096,896]{3,2,1,0:T(8,128)(2,1)} %param.13), kind=kOutput, calls=%fused_computation.32 | convolution fusion | flops 939524096 | bytes 8847360 | tf_op jit(solution)/shard_map/dot_general | solution.py:78
  54.2 4.5 %fusion.10 = f32[128,896]{1,0:T(8,128)S(1)} fusion(bf16[128,4096]{1,0:T(8,128)(2,1)S(1)} %bitcast.128, bf16[1,2,4096,896]{3,2,1,0:T(8,128)(2,1)} %param.13), kind=kOutput, calls=%fused_computation.20 | convolution fusion | flops 939524096 | bytes 8847360 | tf_op jit(solution)/shard_map/dot_general | solution.py:86
  58.7 4.8 %fusion.6 = f32[128,896]{1,0:T(8,128)S(1)} fusion(bf16[128,4096]{1,0:T(8,128)(2,1)S(1)} %bitcast.129, bf16[1,2,4096,896]{3,2,1,0:T(8,128)(2,1)} %param.14), kind=kOutput, calls=%fused_computation.16 | convolution fusion | flops 939524096 | bytes 8847360 | tf_op jit(solution)/shard_map/dot_general | solution.py:87
  63.6 4.6 %fusion.18 = f32[128,896]{1,0:T(8,128)S(1)} fusion(bf16[128,4096]{1,0:T(8,128)(2,1)S(1)} %bitcast.127, bf16[1,2,4096,896]{3,2,1,0:T(8,128)(2,1)} %param.14), kind=kOutput, calls=%fused_computation.28 | convolution fusion | flops 939524096 | bytes 8847360 | tf_op jit(solution)/shard_map/dot_general | solution.py:87
  72.5 8.3 %all-gather.5.cloned.1.call-done = bf16[256,4096]{1,0:T(8,128)(2,1)} async-done(((bf16[32,4096]{1,0:T(8,128)(2,1)}), bf16[256,4096]{1,0:T(8,128)(2,1)}) %all-gather.5.cloned.1.call-update) | async-done | bytes 2097168 | tf_op jit(solution)/shard_map/all_gather | solution.py:80
  82.7 5.7 %fusion.63 = f32[128,896]{1,0:T(8,128)S(1)} fusion(bf16[128,4096]{1,0:T(8,128)(2,1)S(1)} %bitcast.133, bf16[1,2,896,4096]{3,2,1,0:T(8,128)(2,1)} %param.15, f32[128]{0:T(128)S(1)} %reshape.478), kind=kOutput, calls=%fused_computation.59 | convolution fusion | flops 939638784 | bytes 8847872 | tf_op jit(solution)/shard_map/dot_general | solution.py:100
  88.5 6.0 %fusion.4 = f32[128,4096]{1,0:T(8,128)S(1)} fusion(bf16[1,2,4096,896]{3,2,1,0:T(8,128)(2,1)} %param.14, f32[128,896]{1,0:T(8,128)S(1)} %fusion.63, f32[128,896]{1,0:T(8,128)S(1)} %copy-done.5), kind=kOutput, calls=%fused_computation.14 | convolution fusion | flops 940212224 | bytes 10354688 | tf_op jit(solution)/shard_map/dot_general | solution.py:107
  94.6 3.2 %fusion.60 = f32[128,896]{1,0:T(8,128)} fusion(bf16[128,4096]{1,0:T(8,128)(2,1)S(1)} %bitcast.131, bf16[1,2,896,4096]{3,2,1,0:T(8,128)(2,1)S(1)} %bitcast.144, f32[128]{0:T(128)S(1)} %reshape.477), kind=kOutput, calls=%fused_computation.58 | convolution fusion | flops 939638784 | bytes 8847872 | tf_op jit(solution)/shard_map/dot_general | solution.py:100
  97.8 6.0 %fusion.16 = f32[128,4096]{1,0:T(8,128)S(1)} fusion(bf16[1,2,4096,896]{3,2,1,0:T(8,128)(2,1)} %param.14, f32[128,896]{1,0:T(8,128)} %fusion.60, f32[128,896]{1,0:T(8,128)S(1)} %fusion.22), kind=kOutput, calls=%fused_computation.26 | convolution fusion | flops 940212224 | bytes 10354688 | tf_op jit(solution)/shard_map/dot_general | solution.py:107
  103.9 2.5 %fusion.51 = bf16[128,4096]{1,0:T(8,128)(2,1)S(1)} fusion(f32[128,4096]{1,0:T(8,128)S(1)} %fusion.4, bf16[1,2,4096,896]{3,2,1,0:T(8,128)(2,1)S(1)} %bitcast.146, f32[128,896]{1,0:T(8,128)S(1)} %copy-done.6, f32[128,896]{1,0:T(8,128)S(1)} %copy-done.10, f32[128,896]{1,0:T(8,128)S(1)} %copy-done.8), kind=kOutput, calls=%fused_computation.51 | convolution fusion | flops 941719552 | bytes 11862016 | tf_op jit(solution)/shard_map/dot_general | solution.py:105
  106.4 2.5 %fusion.57 = bf16[128,4096]{1,0:T(8,128)(2,1)S(1)} fusion(f32[128,4096]{1,0:T(8,128)S(1)} %fusion.16, bf16[1,2,4096,896]{3,2,1,0:T(8,128)(2,1)S(1)} %bitcast.146, f32[128,896]{1,0:T(8,128)S(1)} %fusion.22, f32[128,896]{1,0:T(8,128)S(1)} %copy-done.11, f32[128,896]{1,0:T(8,128)S(1)} %fusion.18), kind=kOutput, calls=%fused_computation.53 | convolution fusion | flops 941719552 | bytes 11862016 | tf_op jit(solution)/shard_map/dot_general | solution.py:105
  114.4 19.9 %reduce-scatter.2.cloned.1.call-done = bf16[32,4096]{1,0:T(8,128)(2,1)} async-done(((bf16[256,4096]{1,0:T(8,128)(2,1)}), bf16[32,4096]{1,0:T(8,128)(2,1)}) %reduce-scatter.2.cloned.1.call-update) | async-done | bytes 262160 | tf_op jit(solution)/shard_map/reduce_scatter | solution.py:94
  136.6 2.6 %gather_fusion.3 = f32[128,4096]{1,0:T(8,128)} fusion(f32[33,4096]{1,0:T(8,128)S(1)} %pad_convert_fusion, s32[1024]{0:T(1024)S(1)} %pad_clamp_fusion.2), kind=kCustom, calls=%fused_computation.3 | custom fusion | bytes 4194816 | tf_op jit(solution)/shard_map/gather | solution.py:60
  145.7 2.8 %fusion.66 = bf16[1,128,4096]{2,1,0:T(8,128)(2,1)} fusion(f32[128,4096]{1,0:T(8,128)S(1)} %gather_fusion.2, f32[128,4096]{1,0:T(8,128)} %gather_fusion.3), kind=kLoop, calls=%fused_computation.60 | loop fusion | flops 1048576 | bytes 5242880 | tf_op jit(solution)/shard_map/convert_element_type | solution.py:61
  148.5 2.9 %collective-permute-done.4 = bf16[32,4096]{1,0:T(8,128)(2,1)S(1)} collective-permute-done((bf16[32,4096]{1,0:T(8,128)(2,1)}, bf16[32,4096]{1,0:T(8,128)(2,1)S(1)}, u32[]{:S(2)}, u32[]{:S(2)}) %collective-permute-start.4) | collective-permute-done | bytes 262176 | tf_op jit(solution)/shard_map/ppermute | solution.py:51
  151.4 3.8 %collective-permute-done.3 = bf16[32,4096]{1,0:T(8,128)(2,1)S(1)} collective-permute-done((bf16[32,4096]{1,0:T(8,128)(2,1)}, bf16[32,4096]{1,0:T(8,128)(2,1)S(1)}, u32[]{:S(2)}, u32[]{:S(2)}) %collective-permute-start.3) | collective-permute-done | bytes 262176 | tf_op jit(solution)/shard_map/ppermute | solution.py:51
  155.2 11.2 %collective-permute-done.2 = bf16[32,4096]{1,0:T(8,128)(2,1)S(1)} collective-permute-done((bf16[32,4096]{1,0:T(8,128)(2,1)}, bf16[32,4096]{1,0:T(8,128)(2,1)S(1)}, u32[]{:S(2)}, u32[]{:S(2)}) %collective-permute-start.2) | collective-permute-done | bytes 262176 | tf_op jit(solution)/shard_map/ppermute | solution.py:51
  166.4 3.8 %collective-permute-done.1 = bf16[32,4096]{1,0:T(8,128)(2,1)S(1)} collective-permute-done((bf16[32,4096]{1,0:T(8,128)(2,1)S(1)}, bf16[32,4096]{1,0:T(8,128)(2,1)S(1)}, u32[]{:S(2)}, u32[]{:S(2)}) %collective-permute-start.1) | collective-permute-done | bytes 262176 | tf_op jit(solution)/shard_map/ppermute | solution.py:51
  170.1 2.0 %collective-permute-done = bf16[32,4096]{1,0:T(8,128)(2,1)S(1)} collective-permute-done((bf16[32,4096]{1,0:T(8,128)(2,1)S(1)}, bf16[32,4096]{1,0:T(8,128)(2,1)S(1)}, u32[]{:S(2)}, u32[]{:S(2)}) %collective-permute-start) | collective-permute-done | bytes 262176 | tf_op jit(solution)/shard_map/ppermute | solution.py:51
  173.6 2.6 %gather_fusion.4 = f32[128,4096]{1,0:T(8,128)} fusion(f32[33,4096]{1,0:T(8,128)S(1)} %concatenate.52, s32[1024]{0:T(1024)S(1)} %pad_clamp_fusion.1), kind=kCustom, calls=%fused_computation.4 | custom fusion | bytes 4194816 | tf_op jit(solution)/shard_map/gather | solution.py:58
  176.1 2.5 %gather_fusion.5 = f32[128,4096]{1,0:T(8,128)} fusion(f32[33,4096]{1,0:T(8,128)S(1)} %concatenate.52, s32[1024]{0:T(1024)S(1)} %pad_clamp_fusion), kind=kCustom, calls=%fused_computation.5 | custom fusion | bytes 4194816 | tf_op jit(solution)/shard_map/gather | solution.py:60
  178.7 3.4 %fusion.67 = bf16[1,128,4096]{2,1,0:T(8,128)(2,1)} fusion(f32[128,4096]{1,0:T(8,128)} %gather_fusion.4, f32[128,4096]{1,0:T(8,128)} %gather_fusion.5), kind=kLoop, calls=%fused_computation.61 | loop fusion | flops 1048576 | bytes 5242880 | tf_op jit(solution)/shard_map/convert_element_type | solution.py:61
  (127 shorter events, 37.3 us)
Async XLA Ops:
  7.2 8.5 %copy-start.3 = (s32[1,128,2]{1,2,0:T(2,128)S(1)}, s32[1,128,2]{1,2,0:T(2,128)}, u32[]{:S(2)}) copy-start(s32[1,128,2]{1,2,0:T(2,128)} %param.11) | copy-start | bytes 3076
  7.2 9.9 %copy-start.2 = (bf16[1,128,4096]{2,1,0:T(8,128)(2,1)S(1)}, bf16[1,128,4096]{2,1,0:T(8,128)(2,1)}, u32[]{:S(2)}) copy-start(bf16[1,128,4096]{2,1,0:T(8,128)(2,1)} %param.12) | copy-start | bytes 3145732
  7.2 39.4 %all-gather.3.cloned.1.call-start = ((), (), s32[]{:S(2)}) async-start(), calls=%async_computation.1 | async-start | bytes 2433024 | tf_op jit(solution)/shard_map/all_gather | solution.py:77
  15.6 65.2 %all-gather.5.cloned.1.call-start = ((), (), s32[]{:S(2)}) async-start(), calls=%async_computation.3 | async-start | bytes 2359296 | tf_op jit(solution)/shard_map/all_gather | solution.py:80
  15.7 6.5 %collective-permute-start.8 = (s32[128,2]{0,1:T(2,128)S(1)}, s32[128,2]{0,1:T(2,128)S(1)}, u32[]{:S(2)}, u32[]{:S(2)}) collective-permute-start(s32[128,2]{0,1:T(2,128)S(1)} %bitcast.140), channel_id=1, source_target_pairs={{8,0},{16,8},{24,16},{9,1},{17,9},{25,17},{10,2},{18,10},{26,18},{... | collective-permute-start | bytes 3080 | tf_op jit(solution)/shard_map/ppermute | solution.py:14
  52.7 81.6 %reduce-scatter.2.cloned.1.call-start = ((), (), s32[]{:S(2)}) async-start(), calls=%async_computation.2 | async-start | bytes 2359296 | tf_op jit(solution)/shard_map/reduce_scatter | solution.py:94
  54.2 13.9 %slice-start = ((s8[14680064]{0:T(1024)(128)(4,1)}), s8[4194304]{0:T(1024)(128)(4,1)S(1)}, s32[]{:S(2)}) async-start(s8[14680064]{0:T(1024)(128)(4,1)} %bitcast.141), calls=%async_computation.4 | async-start | bytes 8388608
  54.2 13.9 %slice-start.1 = ((s8[14680064]{0:T(1024)(128)(4,1)}), s8[4194304]{0:T(1024)(128)(4,1)S(1)}, s32[]{:S(2)}) async-start(s8[14680064]{0:T(1024)(128)(4,1)} %bitcast.141), calls=%async_computation.5 | async-start | bytes 8388608
  58.7 9.4 %copy-start.4 = (f32[128,896]{1,0:T(8,128)}, f32[128,896]{1,0:T(8,128)S(1)}, u32[]{:S(2)}) copy-start(f32[128,896]{1,0:T(8,128)S(1)} %fusion.10) | copy-start | bytes 1376260
  58.7 9.4 %slice-start.2 = ((s8[14680064]{0:T(1024)(128)(4,1)}), s8[4194304]{0:T(1024)(128)(4,1)S(1)}, s32[]{:S(2)}) async-start(s8[14680064]{0:T(1024)(128)(4,1)} %bitcast.141), calls=%async_computation.6 | async-start | bytes 8388608
  80.8 13.7 %slice-start.4 = ((s8[14680064]{0:T(1024)(128)(4,1)}), s8[2097152]{0:T(1024)(128)(4,1)S(1)}, s32[]{:S(2)}) async-start(s8[14680064]{0:T(1024)(128)(4,1)} %bitcast.143), calls=%async_computation.8 | async-start | bytes 4194304
  82.7 11.8 %slice-start.5 = ((s8[14680064]{0:T(1024)(128)(4,1)}), s8[4194304]{0:T(1024)(128)(4,1)S(1)}, s32[]{:S(2)}) async-start(s8[14680064]{0:T(1024)(128)(4,1)} %bitcast.143), calls=%async_computation.9 | async-start | bytes 8388608
  82.7 11.8 %slice-start.6 = ((s8[14680064]{0:T(1024)(128)(4,1)}), s8[4194304]{0:T(1024)(128)(4,1)S(1)}, s32[]{:S(2)}) async-start(s8[14680064]{0:T(1024)(128)(4,1)} %bitcast.143), calls=%async_computation.10 | async-start | bytes 8388608
  88.4 15.4 %slice-start.8 = ((s8[14680064]{0:T(1024)(128)(4,1)}), s8[2097152]{0:T(1024)(128)(4,1)S(1)}, s32[]{:S(2)}) async-start(s8[14680064]{0:T(1024)(128)(4,1)} %bitcast.145), calls=%async_computation.12 | async-start | bytes 4194304
  88.4 15.4 %slice-start.9 = ((s8[14680064]{0:T(1024)(128)(4,1)}), s8[4194304]{0:T(1024)(128)(4,1)S(1)}, s32[]{:S(2)}) async-start(s8[14680064]{0:T(1024)(128)(4,1)} %bitcast.145), calls=%async_computation.13 | async-start | bytes 8388608
  94.6 9.3 %slice-start.10 = ((s8[14680064]{0:T(1024)(128)(4,1)}), s8[4194304]{0:T(1024)(128)(4,1)S(1)}, s32[]{:S(2)}) async-start(s8[14680064]{0:T(1024)(128)(4,1)} %bitcast.145), calls=%async_computation.14 | async-start | bytes 8388608
  110.6 31.2 %collective-permute-start.7 = (bf16[32,4096]{1,0:T(8,128)(2,1)}, bf16[32,4096]{1,0:T(8,128)(2,1)}, u32[]{:S(2)}, u32[]{:S(2)}) collective-permute-start(bf16[32,4096]{1,0:T(8,128)(2,1)} %get-tuple-element.33), channel_id=1, source_target_pairs={{8,7},{9,0},{10,1},{11,2},{12,3},{13,4},{14,5},{15,6},{16,15},{17,... | collective-permute-start | bytes 786440 | tf_op jit(solution)/shard_map/ppermute | solution.py:51
  111.8 31.3 %collective-permute-start.6 = (bf16[32,4096]{1,0:T(8,128)(2,1)}, bf16[32,4096]{1,0:T(8,128)(2,1)}, u32[]{:S(2)}, u32[]{:S(2)}) collective-permute-start(bf16[32,4096]{1,0:T(8,128)(2,1)} %get-tuple-element.34), channel_id=1, source_target_pairs={{8,6},{9,7},{10,0},{11,1},{12,2},{13,3},{14,4},{15,5},{16,14},{17,... | collective-permute-start | bytes 786440 | tf_op jit(solution)/shard_map/ppermute | solution.py:51
  113.1 31.3 %collective-permute-start.5 = (bf16[32,4096]{1,0:T(8,128)(2,1)}, bf16[32,4096]{1,0:T(8,128)(2,1)}, u32[]{:S(2)}, u32[]{:S(2)}) collective-permute-start(bf16[32,4096]{1,0:T(8,128)(2,1)} %get-tuple-element.35), channel_id=1, source_target_pairs={{8,5},{9,6},{10,7},{11,0},{12,1},{13,2},{14,3},{15,4},{16,13},{17,... | collective-permute-start | bytes 786440 | tf_op jit(solution)/shard_map/ppermute | solution.py:51
  139.2 12.2 %collective-permute-start.4 = (bf16[32,4096]{1,0:T(8,128)(2,1)}, bf16[32,4096]{1,0:T(8,128)(2,1)S(1)}, u32[]{:S(2)}, u32[]{:S(2)}) collective-permute-start(bf16[32,4096]{1,0:T(8,128)(2,1)} %get-tuple-element.36), channel_id=1, source_target_pairs={{8,4},{9,5},{10,6},{11,7},{12,0},{13,1},{14,2},{15,3},{16,12},{17,... | collective-permute-start | bytes 786440 | tf_op jit(solution)/shard_map/ppermute | solution.py:51
  140.5 14.7 %collective-permute-start.3 = (bf16[32,4096]{1,0:T(8,128)(2,1)}, bf16[32,4096]{1,0:T(8,128)(2,1)S(1)}, u32[]{:S(2)}, u32[]{:S(2)}) collective-permute-start(bf16[32,4096]{1,0:T(8,128)(2,1)} %get-tuple-element.37), channel_id=1, source_target_pairs={{8,3},{9,4},{10,5},{11,6},{12,7},{13,0},{14,1},{15,2},{16,11},{17,... | collective-permute-start | bytes 786440 | tf_op jit(solution)/shard_map/ppermute | solution.py:51
  141.8 24.6 %collective-permute-start.2 = (bf16[32,4096]{1,0:T(8,128)(2,1)}, bf16[32,4096]{1,0:T(8,128)(2,1)S(1)}, u32[]{:S(2)}, u32[]{:S(2)}) collective-permute-start(bf16[32,4096]{1,0:T(8,128)(2,1)} %get-tuple-element.38), channel_id=1, source_target_pairs={{8,2},{9,3},{10,4},{11,5},{12,6},{13,7},{14,0},{15,1},{16,10},{17,... | collective-permute-start | bytes 786440 | tf_op jit(solution)/shard_map/ppermute | solution.py:51
  143.1 27.0 %collective-permute-start.1 = (bf16[32,4096]{1,0:T(8,128)(2,1)S(1)}, bf16[32,4096]{1,0:T(8,128)(2,1)S(1)}, u32[]{:S(2)}, u32[]{:S(2)}) collective-permute-start(bf16[32,4096]{1,0:T(8,128)(2,1)S(1)} %get-tuple-element.39), channel_id=1, source_target_pairs={{8,1},{9,2},{10,3},{11,4},{12,5},{13,6},{14,7},{15,0},{16,9},{17,1... | collective-permute-start | bytes 786440 | tf_op jit(solution)/shard_map/ppermute | solution.py:51
  144.4 27.7 %collective-permute-start = (bf16[32,4096]{1,0:T(8,128)(2,1)S(1)}, bf16[32,4096]{1,0:T(8,128)(2,1)S(1)}, u32[]{:S(2)}, u32[]{:S(2)}) collective-permute-start(bf16[32,4096]{1,0:T(8,128)(2,1)S(1)} %get-tuple-element.32), channel_id=1, source_target_pairs={{8,0},{9,1},{10,2},{11,3},{12,4},{13,5},{14,6},{15,7},{16,8},{17,9... | collective-permute-start | bytes 786440 | tf_op jit(solution)/shard_map/ppermute | solution.py:51
  (12 other events, 66.8 us)
Sparse Core Ops, SparseCore 0:
  15.7 30.8 all-gather.2
  52.9 27.9 all-gather.4
  84.1 50.1 reduce-scatter.1

commit v3 on v2

--- a/solution.py
+++ b/solution.py
@@ -20,20 +20,21 @@
 
 
 def local_slots(local_routes, local_gates):
-    count = local_routes.shape[0]
-    sources, weights, targets = [], [], []
+    slot_ids = jnp.arange(MOST, dtype=jnp.int32)[:, None]
+    selects, weights = [], []
     for expert in range(E_WIN):
         matches = local_routes == expert
         routed = jnp.any(matches, axis=1)
         gate_val = jnp.sum(jnp.where(matches, local_gates.astype(jnp.float32), 0.0), axis=1)
-        positions = jnp.minimum(jnp.cumsum(routed.astype(jnp.int32), dtype=jnp.int32) - 1, MOST)
-        target = jnp.where(routed, positions, MOST)
-        sources.append(
-            jnp.zeros((MOST,), jnp.int32).at[target].set(jnp.arange(count, dtype=jnp.int32), mode="drop")
-        )
-        weights.append(jnp.zeros((MOST,), jnp.float32).at[target].set(gate_val, mode="drop"))
-        targets.append(jnp.where(routed & (positions < MOST), positions + expert * MOST, E_WIN * MOST))
-    return jnp.concatenate(sources), jnp.concatenate(weights), targets
+        positions = jnp.cumsum(routed.astype(jnp.int32), dtype=jnp.int32) - 1
+        select = routed[None, :] & (positions[None, :] == slot_ids)
+        selects.append(select)
+        weights.append(jnp.sum(jnp.where(select, gate_val[None, :], 0.0), axis=1))
+    return jnp.concatenate(selects, axis=0), jnp.concatenate(weights)
+
+
+def pick_rows(select, rows):
+    return jnp.dot(select.astype(rows.dtype), rows, preferred_element_type=jnp.float32).astype(rows.dtype)
 
 
 def reduce_to_previous(parts):
@@ -53,12 +54,14 @@
     return total
 
 
-def unpack(slot_sums, targets):
-    padded = jnp.concatenate([slot_sums, jnp.zeros((1, slot_sums.shape[1]), jnp.float32)], axis=0)
-    total = padded[targets[0]]
-    for target in targets[1:]:
-        total = total + padded[target]
-    return total.astype(jnp.bfloat16)
+def unpack(slot_sums, select):
+    return lax.dot_general(
+        select.astype(jnp.float32),
+        slot_sums,
+        (((0,), (0,)), ((), ())),
+        precision=lax.Precision.HIGHEST,
+        preferred_element_type=jnp.float32,
+    ).astype(jnp.bfloat16)
 
 
 def per_device(tokens, gate_vals, expert_ids, grad_out, w_gate, w_up, w_down):
@@ -69,14 +72,14 @@
     down_mats = w_down[0]
     n = lax.axis_size("et")
     width = local_rows.shape[1]
-    sources, weights, targets = local_slots(expert_ids[0], gate_vals[0])
+    select, weights = local_slots(expert_ids[0], gate_vals[0])
     next_routes = shifted(expert_ids[0], "pipe", -1)
-    next_targets = local_slots(next_routes, gate_vals[0])[2]
+    next_select = local_slots(next_routes, gate_vals[0])[0]
     weight_cols = jnp.broadcast_to(weights.astype(jnp.bfloat16)[:, None], (E_WIN * MOST, TAIL))
-    packed = jnp.concatenate([local_rows[sources], weight_cols], axis=1)
+    packed = jnp.concatenate([pick_rows(select, local_rows), weight_cols], axis=1)
     all_rows = lax.all_gather(packed, "et", axis=0, tiled=True).reshape(n, E_WIN, MOST, width + TAIL)
     first_gate = jnp.dot(all_rows[:, 0, :, :width].reshape(n * MOST, width), gate_mats[0], preferred_element_type=jnp.float32)
-    grad_rows_local, first_gate = lax.optimization_barrier((local_grads[sources], first_gate))
+    grad_rows_local, first_gate = lax.optimization_barrier((pick_rows(select, local_grads), first_gate))
     grads = lax.all_gather(grad_rows_local, "et", axis=0, tiled=True).reshape(n, E_WIN, MOST, width)
     outs = []
     stored = []
@@ -92,7 +95,7 @@
         stored.append((gate_w, pre_up, activated, slopes))
     out_parts = jnp.stack(outs, axis=1).reshape(n, E_WIN * MOST, width)
     out_sums = lax.psum_scatter(out_parts.reshape(n * E_WIN * MOST, width), "et", scatter_dimension=0, tiled=True)
-    out_share = unpack(out_sums.astype(jnp.float32), targets)
+    out_share = unpack(out_sums.astype(jnp.float32), select)
     grad_outs = []
     for expert in range(E_WIN):
         gate_w, pre_up, activated, slopes = stored[expert]
@@ -107,7 +110,7 @@
         ) + lax.dot_general(d_up, up_mats[expert], (((1,), (1,)), ((), ())), preferred_element_type=jnp.float32)
         grad_outs.append(grad_e.astype(jnp.bfloat16).reshape(n, MOST, width))
     grad_parts = jnp.stack(grad_outs, axis=1).reshape(n, E_WIN * MOST, width)
-    received = unpack(reduce_to_previous(grad_parts), next_targets)
+    received = unpack(reduce_to_previous(grad_parts), next_select)
     return (out_share[None], received[None])
 
 

time: 191 us -> 170 us (0.89)
  local copies, waits for them, and re-layouts: 22.8 us -> 6.47 us
  matrix products: 46.7 us -> 58 us
  waiting for transfers between devices: 78.8 us -> 70.6 us
  other arithmetic: 13.8 us -> 7.64 us
    reduce_scatter x1, waiting for transfers between devices: 19.9 us -> 0.02 us  [per_device(): lax.psum_scatter(out_parts.reshape(n * E_WIN * MOST, width), 'et', scatte...]
    ppermute x8, waiting for transfers between devices: 23.6 us -> 35.2 us  [reduce_to_previous(): moved = lax.ppermute(chunk, ('pipe', 'et'), pairs).astype(jnp.float32)]
    gather x6 -> x0, local copies, waits for them, and re-layouts: 11.1 us -> none  [the longest x2 5.1 us: unpack(): total = total + padded[target]]
    dot_general x0 -> x4, matrix products: none -> 8.13 us  [the longest x2 5.67 us: unpack(): lax.dot_general(select.astype(jnp.float32), slot_sums, (((0,), (0,)), (()...]
    convert_element_type x4, other arithmetic: 6.17 us -> 0.52 us  [local_slots(): positions = jnp.cumsum(routed.astype(jnp.int32), dtype=jnp.int32) - 1]
    scatter x4 -> x0, local copies, waits for them, and re-layouts: 3.91 us -> none  [the longest x2 1.96 us: local_slots(): jnp.zeros((MOST,), jnp.float32).at[target].set(gate_val, mode='drop')]
    dot_general x2, matrix products: 4.98 us -> 8.79 us  [per_device(): lax.dot_general(d_gate, gate_mats[expert], (((1,), (1,)), ((), ())), pref...]
    dot_general x2, matrix products: 12 us -> 8.64 us  [per_device(): lax.dot_general(d_up, up_mats[expert], (((1,), (1,)), ((), ())), preferre...]
  transfers between devices with their start and end apart: 12 -> 12, of which waited for: 9 -> 11; matrix products, arithmetic and copies ran while one was open for 31% -> 35% of each run, Pallas kernels for 0% -> 0%
where the time goes in v3:
time: 170 us; the launch traced here: 169 us
  waiting for transfers between devices  70.6 us (42%)
  matrix products  58 us (34%)
  between operations  14.5 us (9%)
  starting transfers between devices  11.9 us (7%)
  other arithmetic  7.64 us (4%)
  local copies, waits for them, and re-layouts  6.47 us (4%)
    ppermute x8, waiting for transfers between devices, reduce_to_previous(): moved = lax.ppermute(chunk, ('pipe', 'et'), pairs).astype(jnp.float32)  35.2 us
    all_gather x1, waiting for transfers between devices, per_device(): lax.all_gather(packed, 'et', axis=0, tiled=True)  23.8 us
    dot_general x2, matrix products, per_device(): lax.dot_general(grad_rows, down_mats[expert], (((1,), (1,)), ((), ())), p...  11.7 us
    ppermute x8, starting transfers between devices, reduce_to_previous(): moved = lax.ppermute(chunk, ('pipe', 'et'), pairs).astype(jnp.float32)  10.3 us
    dot_general x2, matrix products, per_device(): pre_up = jnp.dot(rows, up_mats[expert], preferred_element_type=jnp.float32)  9.34 us
    dot_general x2, matrix products, per_device(): lax.dot_general(d_gate, gate_mats[expert], (((1,), (1,)), ((), ())), pref...  8.79 us
    dot_general x2, matrix products, per_device(): lax.dot_general(d_up, up_mats[expert], (((1,), (1,)), ((), ())), preferre...  8.64 us
    all_gather x1, waiting for transfers between devices, per_device(): lax.all_gather(grad_rows_local, 'et', axis=0, tiled=True)  8.46 us
  transfers between devices with their start and end apart: 12, of which 11 were waited for; matrix products, arithmetic and copies ran while one was open for 35% of the time, Pallas kernels for 0%

profile of v3, /device:TPU:0, one launch (start us, length us, event | category | flops | bytes accessed | tf_op | source)
XLA Modules:
  0.0 169.1 jit_solution(12944403016185682323)
XLA Ops:
  12.3 2.2 %convolution_convert_fusion.2 = bf16[32,4096]{1,0:T(8,128)(2,1)} fusion(bf16[1,128,4096]{2,1,0:T(8,128)(2,1)} %param.12, pred[16,128]{1,0:T(8,128)(4,1)S(1)} %get-tuple-element.41, pred[16,128]{1,0:T(8,128)(4,1)S(1)} %get-tuple-element.40), kind=kOutput, calls=%fused_computation.48 | convolution fusion | flops 33689600 | bytes 1314816 | tf_op jit(solution)/shard_map/dot_general | solution.py:37
  14.5 3.0 %collective-permute-done = s32[128,2]{0,1:T(2,128)S(1)} collective-permute-done((s32[128,2]{0,1:T(2,128)}, s32[128,2]{0,1:T(2,128)S(1)}, u32[]{:S(2)}, u32[]{:S(2)}) %collective-permute-start) | collective-permute-done | bytes 1056 | tf_op jit(solution)/shard_map/ppermute | solution.py:14
  18.1 23.8 %all-gather.3.cloned.1.call-done = bf16[256,4224]{1,0:T(8,128)(2,1)} async-done(((bf16[32,4224]{1,0:T(8,128)(2,1)}), bf16[256,4224]{1,0:T(8,128)(2,1)}) %all-gather.3.cloned.1.call-update) | async-done | bytes 2162704 | tf_op jit(solution)/shard_map/all_gather | solution.py:80
  41.9 1.7 fusion.111
  43.6 4.3 %fusion.22 = f32[128,896]{1,0:T(8,128)S(1)} fusion(bf16[128,4096]{1,0:T(8,128)(2,1)S(1)} %bitcast.133, bf16[1,2,4096,896]{3,2,1,0:T(8,128)(2,1)} %param.13), kind=kOutput, calls=%fused_computation.22 | convolution fusion | flops 939524096 | bytes 8847360 | tf_op jit(solution)/shard_map/dot_general | solution.py:81
  49.4 4.5 %fusion.10 = f32[128,896]{1,0:T(8,128)S(1)} fusion(bf16[128,4096]{1,0:T(8,128)(2,1)S(1)} %bitcast.135, bf16[1,2,4096,896]{3,2,1,0:T(8,128)(2,1)} %param.13), kind=kOutput, calls=%fused_computation.10 | convolution fusion | flops 939524096 | bytes 8847360 | tf_op jit(solution)/shard_map/dot_general | solution.py:89
  54.0 4.8 %fusion.6 = f32[128,896]{1,0:T(8,128)S(1)} fusion(bf16[128,4096]{1,0:T(8,128)(2,1)S(1)} %bitcast.136, bf16[1,2,4096,896]{3,2,1,0:T(8,128)(2,1)} %param.14), kind=kOutput, calls=%fused_computation.6 | convolution fusion | flops 939524096 | bytes 8847360 | tf_op jit(solution)/shard_map/dot_general | solution.py:90
  58.8 4.6 %fusion.18 = f32[128,896]{1,0:T(8,128)S(1)} fusion(bf16[128,4096]{1,0:T(8,128)(2,1)S(1)} %bitcast.134, bf16[1,2,4096,896]{3,2,1,0:T(8,128)(2,1)} %param.14), kind=kOutput, calls=%fused_computation.18 | convolution fusion | flops 939524096 | bytes 8847360 | tf_op jit(solution)/shard_map/dot_general | solution.py:90
  67.6 8.5 %all-gather.5.cloned.1.call-done = bf16[256,4096]{1,0:T(8,128)(2,1)} async-done(((bf16[32,4096]{1,0:T(8,128)(2,1)}), bf16[256,4096]{1,0:T(8,128)(2,1)}) %all-gather.5.cloned.1.call-update) | async-done | bytes 2097168 | tf_op jit(solution)/shard_map/all_gather | solution.py:83
  77.8 5.7 %fusion.62 = f32[128,896]{1,0:T(8,128)S(1)} fusion(bf16[128,4096]{1,0:T(8,128)(2,1)S(1)} %bitcast.140, bf16[1,2,896,4096]{3,2,1,0:T(8,128)(2,1)} %param.15, f32[128]{0:T(128)S(1)} %reshape.300), kind=kOutput, calls=%fused_computation.52 | convolution fusion | flops 939638784 | bytes 8847872 | tf_op jit(solution)/shard_map/dot_general | solution.py:103
  83.5 6.0 %fusion.65 = f32[128,896]{1,0:T(8,128)S(1)} fusion(bf16[128,4096]{1,0:T(8,128)(2,1)S(1)} %bitcast.138, bf16[1,2,896,4096]{3,2,1,0:T(8,128)(2,1)} %param.15, f32[128]{0:T(128)S(1)} %reshape.301), kind=kOutput, calls=%fused_computation.53 | convolution fusion | flops 939638784 | bytes 8847872 | tf_op jit(solution)/shard_map/dot_general | solution.py:103
  89.5 6.0 %fusion.4 = f32[128,4096]{1,0:T(8,128)S(1)} fusion(bf16[1,2,4096,896]{3,2,1,0:T(8,128)(2,1)} %param.14, f32[128,896]{1,0:T(8,128)S(1)} %fusion.65, f32[128,896]{1,0:T(8,128)S(1)} %copy-done.7), kind=kOutput, calls=%fused_computation.4 | convolution fusion | flops 940212224 | bytes 10354688 | tf_op jit(solution)/shard_map/dot_general | solution.py:110
  95.6 2.7 %fusion.16 = f32[128,4096]{1,0:T(8,128)S(1)} fusion(bf16[1,2,4096,896]{3,2,1,0:T(8,128)(2,1)S(1)} %bitcast.147, f32[128,896]{1,0:T(8,128)S(1)} %fusion.62, f32[128,896]{1,0:T(8,128)S(1)} %fusion.22), kind=kOutput, calls=%fused_computation.16 | convolution fusion | flops 940212224 | bytes 10354688 | tf_op jit(solution)/shard_map/dot_general | solution.py:110
  98.3 6.3 %fusion.51 = bf16[128,4096]{1,0:T(8,128)(2,1)S(1)} fusion(f32[128,4096]{1,0:T(8,128)S(1)} %fusion.4, bf16[1,2,4096,896]{3,2,1,0:T(8,128)(2,1)} %param.13, f32[128,896]{1,0:T(8,128)S(1)} %copy-done.7, f32[128,896]{1,0:T(8,128)} %copy-done.11, f32[128,896]{1,0:T(8,128)} %copy-done.8), kind=kOutput, calls=%fused_computation.41 | convolution fusion | flops 941719552 | bytes 11862016 | tf_op jit(solution)/shard_map/dot_general | solution.py:108
  104.8 2.5 %fusion.57 = bf16[128,4096]{1,0:T(8,128)(2,1)S(1)} fusion(f32[128,4096]{1,0:T(8,128)S(1)} %fusion.16, bf16[1,2,4096,896]{3,2,1,0:T(8,128)(2,1)S(1)} %bitcast.149, f32[128,896]{1,0:T(8,128)S(1)} %copy-done.3, f32[128,896]{1,0:T(8,128)S(1)} %copy-done.10, f32[128,896]{1,0:T(8,128)S(1)} %copy-done.5), kind=kOutput, calls=%fused_computation.43 | convolution fusion | flops 941719552 | bytes 11862016 | tf_op jit(solution)/shard_map/dot_general | solution.py:108
  117.8 1.9 %collective-permute-done.1 = bf16[32,4096]{1,0:T(8,128)(2,1)S(1)} collective-permute-done((bf16[32,4096]{1,0:T(8,128)(2,1)}, bf16[32,4096]{1,0:T(8,128)(2,1)S(1)}, u32[]{:S(2)}, u32[]{:S(2)}) %collective-permute-start.1) | collective-permute-done | bytes 262176 | tf_op jit(solution)/shard_map/ppermute | solution.py:52
  120.9 3.0 %collective-permute-done.8 = bf16[32,4096]{1,0:T(8,128)(2,1)S(1)} collective-permute-done((bf16[32,4096]{1,0:T(8,128)(2,1)}, bf16[32,4096]{1,0:T(8,128)(2,1)S(1)}, u32[]{:S(2)}, u32[]{:S(2)}) %collective-permute-start.8) | collective-permute-done | bytes 262176 | tf_op jit(solution)/shard_map/ppermute | solution.py:52
  125.2 6.6 %collective-permute-done.7 = bf16[32,4096]{1,0:T(8,128)(2,1)S(1)} collective-permute-done((bf16[32,4096]{1,0:T(8,128)(2,1)S(1)}, bf16[32,4096]{1,0:T(8,128)(2,1)S(1)}, u32[]{:S(2)}, u32[]{:S(2)}) %collective-permute-start.7) | collective-permute-done | bytes 262176 | tf_op jit(solution)/shard_map/ppermute | solution.py:52
  133.1 2.4 %fusion.61 = bf16[1,128,4096]{2,1,0:T(8,128)(2,1)} fusion(bf16[32,4096]{1,0:T(8,128)(2,1)} %reduce-scatter.2.cloned.1.call-done, pred[16,128]{1,0:T(8,128)(4,1)S(1)} %get-tuple-element.41, pred[16,128]{1,0:T(8,128)(4,1)S(1)} %get-tuple-element.40), kind=kOutput, calls=%fused_computation.47 | convolution fusion | flops 34082816 | bytes 1314816 | tf_op jit(solution)/shard_map/dot_general | solution.py:58
  136.1 6.9 %collective-permute-done.5 = bf16[32,4096]{1,0:T(8,128)(2,1)} collective-permute-done((bf16[32,4096]{1,0:T(8,128)(2,1)S(1)}, bf16[32,4096]{1,0:T(8,128)(2,1)}, u32[]{:S(2)}, u32[]{:S(2)}) %collective-permute-start.5) | collective-permute-done | bytes 262176 | tf_op jit(solution)/shard_map/ppermute | solution.py:52
  143.0 4.2 %collective-permute-done.4 = bf16[32,4096]{1,0:T(8,128)(2,1)} collective-permute-done((bf16[32,4096]{1,0:T(8,128)(2,1)S(1)}, bf16[32,4096]{1,0:T(8,128)(2,1)}, u32[]{:S(2)}, u32[]{:S(2)}) %collective-permute-start.4) | collective-permute-done | bytes 262176 | tf_op jit(solution)/shard_map/ppermute | solution.py:52
  147.2 7.8 %collective-permute-done.3 = bf16[32,4096]{1,0:T(8,128)(2,1)} collective-permute-done((bf16[32,4096]{1,0:T(8,128)(2,1)S(1)}, bf16[32,4096]{1,0:T(8,128)(2,1)}, u32[]{:S(2)}, u32[]{:S(2)}) %collective-permute-start.3) | collective-permute-done | bytes 262176 | tf_op jit(solution)/shard_map/ppermute | solution.py:52
  155.0 4.3 %collective-permute-done.2 = bf16[32,4096]{1,0:T(8,128)(2,1)S(1)} collective-permute-done((bf16[32,4096]{1,0:T(8,128)(2,1)S(1)}, bf16[32,4096]{1,0:T(8,128)(2,1)S(1)}, u32[]{:S(2)}, u32[]{:S(2)}) %collective-permute-start.2) | collective-permute-done | bytes 262176 | tf_op jit(solution)/shard_map/ppermute | solution.py:52
  159.3 3.3 %fusion.60 = bf16[1,128,4096]{2,1,0:T(8,128)(2,1)} fusion(bf16[32,4096]{1,0:T(8,128)(2,1)S(1)} %collective-permute-done.8, bf16[32,4096]{1,0:T(8,128)(2,1)S(1)} %collective-permute-done.7, bf16[32,4096]{1,0:T(8,128)(2,1)} %collective-permute-done.6, bf16[32,4096]{1,0:T(8,128)(2,1)} %collective-permute-done.5, bf16[32,4096]{1,0:T(8,128)(2,1)} %collective-permute-done.4, ...), kind=kOutput, calls=%fused_computation.46 | convolution fusion | flops 203821056 | bytes 3149824 | tf_op jit(solution)/shard_map/dot_general | solution.py:58
  (105 shorter events, 27.9 us)
Async XLA Ops:
  7.2 34.7 %all-gather.3.cloned.1.call-start = ((), (), s32[]{:S(2)}) async-start(), calls=%async_computation.1 | async-start | bytes 2433024 | tf_op jit(solution)/shard_map/all_gather | solution.py:80
  10.9 65.2 %all-gather.5.cloned.1.call-start = ((), (), s32[]{:S(2)}) async-start(), calls=%async_computation.3 | async-start | bytes 2359296 | tf_op jit(solution)/shard_map/all_gather | solution.py:83
  10.9 6.7 %collective-permute-start = (s32[128,2]{0,1:T(2,128)}, s32[128,2]{0,1:T(2,128)S(1)}, u32[]{:S(2)}, u32[]{:S(2)}) collective-permute-start(s32[128,2]{0,1:T(2,128)} %bitcast.143), channel_id=1, source_target_pairs={{8,0},{16,8},{24,16},{9,1},{17,9},{25,17},{10,2},{18,10},{26,18},{... | collective-permute-start | bytes 3080 | tf_op jit(solution)/shard_map/ppermute | solution.py:14
  47.9 47.6 %copy-start.2 = (f32[128,896]{1,0:T(8,128)}, f32[128,896]{1,0:T(8,128)S(1)}, u32[]{:S(2)}) copy-start(f32[128,896]{1,0:T(8,128)S(1)} %fusion.22) | copy-start | bytes 1376260
  48.0 85.1 %reduce-scatter.2.cloned.1.call-start = ((), (), s32[]{:S(2)}) async-start(), calls=%async_computation.2 | async-start | bytes 2359296 | tf_op jit(solution)/shard_map/reduce_scatter | solution.py:97
  49.4 13.9 %slice-start = ((s8[14680064]{0:T(1024)(128)(4,1)}), s8[4194304]{0:T(1024)(128)(4,1)S(1)}, s32[]{:S(2)}) async-start(s8[14680064]{0:T(1024)(128)(4,1)} %bitcast.144), calls=%async_computation.4 | async-start | bytes 8388608
  49.4 13.9 %slice-start.1 = ((s8[14680064]{0:T(1024)(128)(4,1)}), s8[4194304]{0:T(1024)(128)(4,1)S(1)}, s32[]{:S(2)}) async-start(s8[14680064]{0:T(1024)(128)(4,1)} %bitcast.144), calls=%async_computation.5 | async-start | bytes 8388608
  54.0 9.4 %copy-start.6 = (f32[128,896]{1,0:T(8,128)}, f32[128,896]{1,0:T(8,128)S(1)}, u32[]{:S(2)}) copy-start(f32[128,896]{1,0:T(8,128)S(1)} %fusion.10) | copy-start | bytes 1376260
  54.0 9.4 %slice-start.2 = ((s8[14680064]{0:T(1024)(128)(4,1)}), s8[4194304]{0:T(1024)(128)(4,1)S(1)}, s32[]{:S(2)}) async-start(s8[14680064]{0:T(1024)(128)(4,1)} %bitcast.144), calls=%async_computation.6 | async-start | bytes 8388608
  77.7 17.8 %slice-start.4 = ((s8[14680064]{0:T(1024)(128)(4,1)}), s8[2097152]{0:T(1024)(128)(4,1)S(1)}, s32[]{:S(2)}) async-start(s8[14680064]{0:T(1024)(128)(4,1)} %bitcast.146), calls=%async_computation.8 | async-start | bytes 4194304
  77.8 17.8 %slice-start.5 = ((s8[14680064]{0:T(1024)(128)(4,1)}), s8[4194304]{0:T(1024)(128)(4,1)S(1)}, s32[]{:S(2)}) async-start(s8[14680064]{0:T(1024)(128)(4,1)} %bitcast.146), calls=%async_computation.9 | async-start | bytes 8388608
  83.4 12.1 %copy-start.9 = (f32[128,896]{1,0:T(8,128)}, f32[128,896]{1,0:T(8,128)S(1)}, u32[]{:S(2)}) copy-start(f32[128,896]{1,0:T(8,128)S(1)} %fusion.62) | copy-start | bytes 1376260
  83.5 12.1 %slice-start.6 = ((s8[14680064]{0:T(1024)(128)(4,1)}), s8[4194304]{0:T(1024)(128)(4,1)S(1)}, s32[]{:S(2)}) async-start(s8[14680064]{0:T(1024)(128)(4,1)} %bitcast.146), calls=%async_computation.10 | async-start | bytes 8388608
  89.5 15.2 %slice-start.8 = ((s8[14680064]{0:T(1024)(128)(4,1)}), s8[2097152]{0:T(1024)(128)(4,1)S(1)}, s32[]{:S(2)}) async-start(s8[14680064]{0:T(1024)(128)(4,1)} %bitcast.148), calls=%async_computation.12 | async-start | bytes 4194304
  89.5 15.2 %slice-start.9 = ((s8[14680064]{0:T(1024)(128)(4,1)}), s8[4194304]{0:T(1024)(128)(4,1)S(1)}, s32[]{:S(2)}) async-start(s8[14680064]{0:T(1024)(128)(4,1)} %bitcast.148), calls=%async_computation.13 | async-start | bytes 8388608
  104.7 57.8 %copy-start.1 = (bf16[1,128,4096]{2,1,0:T(8,128)(2,1)S(1)}, bf16[1,128,4096]{2,1,0:T(8,128)(2,1)}, u32[]{:S(2)}) copy-start(bf16[1,128,4096]{2,1,0:T(8,128)(2,1)} %param.9) | copy-start | bytes 3145732
  108.4 11.2 %collective-permute-start.1 = (bf16[32,4096]{1,0:T(8,128)(2,1)}, bf16[32,4096]{1,0:T(8,128)(2,1)S(1)}, u32[]{:S(2)}, u32[]{:S(2)}) collective-permute-start(bf16[32,4096]{1,0:T(8,128)(2,1)} %get-tuple-element.28), channel_id=1, source_target_pairs={{8,0},{9,1},{10,2},{11,3},{12,4},{13,5},{14,6},{15,7},{16,8},{17,9... | collective-permute-start | bytes 786440 | tf_op jit(solution)/shard_map/ppermute | solution.py:52
  109.7 14.2 %collective-permute-start.8 = (bf16[32,4096]{1,0:T(8,128)(2,1)}, bf16[32,4096]{1,0:T(8,128)(2,1)S(1)}, u32[]{:S(2)}, u32[]{:S(2)}) collective-permute-start(bf16[32,4096]{1,0:T(8,128)(2,1)} %get-tuple-element.29), channel_id=1, source_target_pairs={{8,7},{9,0},{10,1},{11,2},{12,3},{13,4},{14,5},{15,6},{16,15},{17,... | collective-permute-start | bytes 786440 | tf_op jit(solution)/shard_map/ppermute | solution.py:52
  111.0 20.8 %collective-permute-start.7 = (bf16[32,4096]{1,0:T(8,128)(2,1)S(1)}, bf16[32,4096]{1,0:T(8,128)(2,1)S(1)}, u32[]{:S(2)}, u32[]{:S(2)}) collective-permute-start(bf16[32,4096]{1,0:T(8,128)(2,1)S(1)} %get-tuple-element.30), channel_id=1, source_target_pairs={{8,6},{9,7},{10,0},{11,1},{12,2},{13,3},{14,4},{15,5},{16,14},{17,... | collective-permute-start | bytes 786440 | tf_op jit(solution)/shard_map/ppermute | solution.py:52
  115.2 21.0 %collective-permute-start.6 = (bf16[32,4096]{1,0:T(8,128)(2,1)S(1)}, bf16[32,4096]{1,0:T(8,128)(2,1)}, u32[]{:S(2)}, u32[]{:S(2)}) collective-permute-start(bf16[32,4096]{1,0:T(8,128)(2,1)S(1)} %get-tuple-element.31), channel_id=1, source_target_pairs={{8,5},{9,6},{10,7},{11,0},{12,1},{13,2},{14,3},{15,4},{16,13},{17,... | collective-permute-start | bytes 786440 | tf_op jit(solution)/shard_map/ppermute | solution.py:52
  116.5 26.6 %collective-permute-start.5 = (bf16[32,4096]{1,0:T(8,128)(2,1)S(1)}, bf16[32,4096]{1,0:T(8,128)(2,1)}, u32[]{:S(2)}, u32[]{:S(2)}) collective-permute-start(bf16[32,4096]{1,0:T(8,128)(2,1)S(1)} %get-tuple-element.32), channel_id=1, source_target_pairs={{8,4},{9,5},{10,6},{11,7},{12,0},{13,1},{14,2},{15,3},{16,12},{17,... | collective-permute-start | bytes 786440 | tf_op jit(solution)/shard_map/ppermute | solution.py:52
  119.6 27.6 %collective-permute-start.4 = (bf16[32,4096]{1,0:T(8,128)(2,1)S(1)}, bf16[32,4096]{1,0:T(8,128)(2,1)}, u32[]{:S(2)}, u32[]{:S(2)}) collective-permute-start(bf16[32,4096]{1,0:T(8,128)(2,1)S(1)} %get-tuple-element.33), channel_id=1, source_target_pairs={{8,3},{9,4},{10,5},{11,6},{12,7},{13,0},{14,1},{15,2},{16,11},{17,... | collective-permute-start | bytes 786440 | tf_op jit(solution)/shard_map/ppermute | solution.py:52
  123.9 31.1 %collective-permute-start.3 = (bf16[32,4096]{1,0:T(8,128)(2,1)S(1)}, bf16[32,4096]{1,0:T(8,128)(2,1)}, u32[]{:S(2)}, u32[]{:S(2)}) collective-permute-start(bf16[32,4096]{1,0:T(8,128)(2,1)S(1)} %get-tuple-element.34), channel_id=1, source_target_pairs={{8,2},{9,3},{10,4},{11,5},{12,6},{13,7},{14,0},{15,1},{16,10},{17,... | collective-permute-start | bytes 786440 | tf_op jit(solution)/shard_map/ppermute | solution.py:52
  131.8 27.5 %collective-permute-start.2 = (bf16[32,4096]{1,0:T(8,128)(2,1)S(1)}, bf16[32,4096]{1,0:T(8,128)(2,1)S(1)}, u32[]{:S(2)}, u32[]{:S(2)}) collective-permute-start(bf16[32,4096]{1,0:T(8,128)(2,1)S(1)} %get-tuple-element.35), channel_id=1, source_target_pairs={{8,1},{9,2},{10,3},{11,4},{12,5},{13,6},{14,7},{15,0},{16,9},{17,1... | collective-permute-start | bytes 786440 | tf_op jit(solution)/shard_map/ppermute | solution.py:52
  (12 other events, 67.4 us)
Sparse Core Ops, SparseCore 0:
  11.0 30.8 all-gather.2
  48.1 27.9 all-gather.4
  79.3 41.2 reduce-scatter.1

commit v4 on v3

--- a/solution.py
+++ b/solution.py
@@ -41,17 +41,24 @@
     n = lax.axis_size("et")
     stages = lax.axis_size("pipe")
     me = lax.axis_index("et")
-    total = None
-    for step in range(n):
-        chunk = jnp.take(parts, (me + step) % n, axis=0)
-        pairs = [
-            (stage * n + source, (stage - 1) * n + (source + step) % n)
-            for stage in range(1, stages)
-            for source in range(n)
-        ]
-        moved = lax.ppermute(chunk, ("pipe", "et"), pairs).astype(jnp.float32)
-        total = moved if total is None else total + moved
-    return total
+    held = parts
+    bit = 1
+    while 2 * bit < n:
+        halves = held.reshape((held.shape[0] // 2, 2) + held.shape[1:])
+        side = (me // bit) % 2
+        keep = jnp.take(halves, side, axis=1)
+        give = jnp.take(halves, 1 - side, axis=1)
+        got = lax.ppermute(give, "et", [(i, i ^ bit) for i in range(n)])
+        held = (keep.astype(jnp.float32) + got.astype(jnp.float32)).astype(jnp.bfloat16)
+        bit *= 2
+    side = (me // bit) % 2
+    keep = jnp.take(held, side, axis=0)
+    give = jnp.take(held, 1 - side, axis=0)
+    to_same = [(stage * n + i, (stage - 1) * n + i) for stage in range(1, stages) for i in range(n)]
+    to_other = [(stage * n + i, (stage - 1) * n + (i ^ bit)) for stage in range(1, stages) for i in range(n)]
+    first = lax.ppermute(keep, ("pipe", "et"), to_same)
+    second = lax.ppermute(give, ("pipe", "et"), to_other)
+    return first.astype(jnp.float32) + second.astype(jnp.float32)
 
 
 def unpack(slot_sums, select):

time: 170 us -> 172 us (1.012)
  starting transfers between devices: 11.9 us -> 5.97 us
  waiting for transfers between devices: 70.6 us -> 74.7 us
  matrix products: 58 us -> 60.9 us
    reduce_scatter x1, waiting for transfers between devices: 0.02 us -> 25.4 us  [per_device(): lax.psum_scatter(out_parts.reshape(n * E_WIN * MOST, width), 'et', scatte...]
    ppermute x8 -> x4, waiting for transfers between devices: 35.2 us -> 11.8 us  [the longest x2 11.8 us: reduce_to_previous(): got = lax.ppermute(give, 'et', [(i, i ^ bit) for i in range(n)])]
    ppermute x8 -> x4, starting transfers between devices: 10.3 us -> 4.38 us  [the longest x2 1.79 us: reduce_to_previous(): got = lax.ppermute(give, 'et', [(i, i ^ bit) for i in range(n)])]
    all_gather x1, waiting for transfers between devices: 23.8 us -> 28.8 us  [per_device(): lax.all_gather(packed, 'et', axis=0, tiled=True)]
    all_gather x1, waiting for transfers between devices: 8.46 us -> 4.79 us  [per_device(): lax.all_gather(grad_rows_local, 'et', axis=0, tiled=True)]
    convert_element_type x0 -> x2, other arithmetic: none -> 2.74 us  [reduce_to_previous(): (keep.astype(jnp.float32) + got.astype(jnp.float32)).astype(jnp.bfloat16)]
    dot_general x2, matrix products: 8.79 us -> 11.4 us  [per_device(): lax.dot_general(d_gate, gate_mats[expert], (((1,), (1,)), ((), ())), pref...]
    dot_general x2, matrix products: 2.62 us -> 4.71 us  [per_device(): jnp.dot(hidden, down_mats[expert], preferred_element_type=jnp.float32)]
  transfers between devices with their start and end apart: 12 -> 8, of which waited for: 11 -> 5; matrix products, arithmetic and copies ran while one was open for 35% -> 17% of each run, Pallas kernels for 0% -> 0%
where the time goes in v4:
time: 172 us
  waiting for transfers between devices  74.7 us (43%)
  matrix products  60.9 us (35%)
  between operations  14.4 us (8%)
  other arithmetic  9.23 us (5%)
  local copies, waits for them, and re-layouts  6.34 us (4%)
  starting transfers between devices  5.97 us (3%)
    all_gather x1, waiting for transfers between devices, per_device(): lax.all_gather(packed, 'et', axis=0, tiled=True)  28.8 us
    reduce_scatter x1, waiting for transfers between devices, per_device(): lax.psum_scatter(out_parts.reshape(n * E_WIN * MOST, width), 'et', scatte...  25.4 us
    ppermute x2, waiting for transfers between devices, reduce_to_previous(): got = lax.ppermute(give, 'et', [(i, i ^ bit) for i in range(n)])  11.8 us
    dot_general x2, matrix products, per_device(): lax.dot_general(d_gate, gate_mats[expert], (((1,), (1,)), ((), ())), pref...  11.4 us
    dot_general x2, matrix products, per_device(): lax.dot_general(grad_rows, down_mats[expert], (((1,), (1,)), ((), ())), p...  11.2 us
    dot_general x2, matrix products, per_device(): pre_up = jnp.dot(rows, up_mats[expert], preferred_element_type=jnp.float32)  9.45 us
    dot_general x2, matrix products, per_device(): lax.dot_general(d_up, up_mats[expert], (((1,), (1,)), ((), ())), preferre...  8.32 us
    all_gather x1, waiting for transfers between devices, per_device(): lax.all_gather(grad_rows_local, 'et', axis=0, tiled=True)  4.79 us
  transfers between devices with their start and end apart: 8, of which 5 were waited for; matrix products, arithmetic and copies ran while one was open for 17% of the time, Pallas kernels for 0%

profile of v4, /device:TPU:0, one launch (start us, length us, event | category | flops | bytes accessed | tf_op | source)
XLA Modules:
  0.0 171.5 jit_solution(4071523302199957610)
XLA Ops:
  10.9 2.2 %convolution_convert_fusion.2 = bf16[32,4096]{1,0:T(8,128)(2,1)} fusion(bf16[1,128,4096]{2,1,0:T(8,128)(2,1)} %param.16, pred[16,128]{1,0:T(8,128)(4,1)S(1)} %get-tuple-element.59, pred[16,128]{1,0:T(8,128)(4,1)S(1)} %get-tuple-element.58), kind=kOutput, calls=%fused_computation.48 | convolution fusion | flops 33689600 | bytes 1314816 | tf_op jit(solution)/shard_map/dot_general | solution.py:37
  13.1 28.8 %all-gather.3.cloned.1.call-done = bf16[256,4224]{1,0:T(8,128)(2,1)} async-done(((bf16[32,4224]{1,0:T(8,128)(2,1)}), bf16[256,4224]{1,0:T(8,128)(2,1)}) %all-gather.3.cloned.1.call-update) | async-done | bytes 2162704 | tf_op jit(solution)/shard_map/all_gather | solution.py:87
  41.9 1.7 %fusion.101 = (bf16[8,1,16,4096]{3,2,1,0:T(8,128)(2,1)S(1)}, bf16[8,1,16,4096]{3,2,1,0:T(8,128)(2,1)S(1)}) fusion(bf16[8,2,16,4224]{3,2,1,0:T(8,128)(2,1)} %bitcast.146), kind=kLoop, calls=%fused_computation.122 | loop fusion | bytes 4194304 | tf_op jit(solution)/shard_map/slice | solution.py:88
  43.6 4.3 %fusion.22 = f32[128,896]{1,0:T(8,128)S(1)} fusion(bf16[128,4096]{1,0:T(8,128)(2,1)S(1)} %bitcast.149, bf16[1,2,4096,896]{3,2,1,0:T(8,128)(2,1)} %param.17), kind=kOutput, calls=%fused_computation.22 | convolution fusion | flops 939524096 | bytes 8847360 | tf_op jit(solution)/shard_map/dot_general | solution.py:88
  49.7 3.9 %collective-permute-done = s32[128,2]{0,1:T(2,128)S(1)} collective-permute-done((s32[128,2]{0,1:T(2,128)S(1)}, s32[128,2]{0,1:T(2,128)S(1)}, u32[]{:S(2)}, u32[]{:S(2)}) %collective-permute-start) | collective-permute-done | bytes 1056 | tf_op jit(solution)/shard_map/ppermute | solution.py:14
  54.8 4.6 %fusion.10 = f32[128,896]{1,0:T(8,128)S(1)} fusion(bf16[128,4096]{1,0:T(8,128)(2,1)S(1)} %bitcast.151, bf16[1,2,4096,896]{3,2,1,0:T(8,128)(2,1)} %param.17), kind=kOutput, calls=%fused_computation.10 | convolution fusion | flops 939524096 | bytes 8847360 | tf_op jit(solution)/shard_map/dot_general | solution.py:96
  59.5 4.6 %fusion.6 = f32[128,896]{1,0:T(8,128)S(1)} fusion(bf16[128,4096]{1,0:T(8,128)(2,1)S(1)} %bitcast.152, bf16[1,2,4096,896]{3,2,1,0:T(8,128)(2,1)} %param.18), kind=kOutput, calls=%fused_computation.6 | convolution fusion | flops 939524096 | bytes 8847360 | tf_op jit(solution)/shard_map/dot_general | solution.py:97
  64.1 4.9 %fusion.18 = f32[128,896]{1,0:T(8,128)S(1)} fusion(bf16[128,4096]{1,0:T(8,128)(2,1)S(1)} %bitcast.150, bf16[1,2,4096,896]{3,2,1,0:T(8,128)(2,1)} %param.18), kind=kOutput, calls=%fused_computation.18 | convolution fusion | flops 939524096 | bytes 8847360 | tf_op jit(solution)/shard_map/dot_general | solution.py:97
  69.0 2.3 %fusion.48 = bf16[128,4096]{1,0:T(8,128)(2,1)} fusion(bf16[1,2,896,4096]{3,2,1,0:T(8,128)(2,1)S(1)} %bitcast.163, f32[128]{0:T(128)S(1)} %reshape.329, f32[128,896]{1,0:T(8,128)S(1)} %fusion.6, f32[128,896]{1,0:T(8,128)S(1)} %fusion.10), kind=kOutput, calls=%fused_computation.40 | convolution fusion | flops 941260800 | bytes 9306624 | tf_op jit(solution)/shard_map/dot_general | solution.py:100
  71.3 4.8 %all-gather.5.cloned.1.call-done = bf16[256,4096]{1,0:T(8,128)(2,1)} async-done(((bf16[32,4096]{1,0:T(8,128)(2,1)}), bf16[256,4096]{1,0:T(8,128)(2,1)}) %all-gather.5.cloned.1.call-update) | async-done | bytes 2097168 | tf_op jit(solution)/shard_map/all_gather | solution.py:90
  76.1 1.8 %fusion.103 = (bf16[8,1,16,4096]{3,2,1,0:T(8,128)(2,1)S(1)}, bf16[8,1,16,4096]{3,2,1,0:T(8,128)(2,1)S(1)}) fusion(bf16[8,2,16,4096]{3,2,1,0:T(8,128)(2,1)} %bitcast.148), kind=kLoop, calls=%fused_computation.124 | loop fusion | bytes 4194304 | tf_op jit(solution)/shard_map/slice | solution.py:109
  77.8 5.5 %fusion.65 = f32[128,896]{1,0:T(8,128)S(1)} fusion(bf16[128,4096]{1,0:T(8,128)(2,1)S(1)} %bitcast.156, bf16[1,2,896,4096]{3,2,1,0:T(8,128)(2,1)} %param.19, f32[128]{0:T(128)S(1)} %reshape.329), kind=kOutput, calls=%fused_computation.54 | convolution fusion | flops 939638784 | bytes 8847872 | tf_op jit(solution)/shard_map/dot_general | solution.py:110
  83.4 5.7 %fusion.4 = f32[128,4096]{1,0:T(8,128)S(1)} fusion(bf16[1,2,4096,896]{3,2,1,0:T(8,128)(2,1)} %param.18, f32[128,896]{1,0:T(8,128)S(1)} %fusion.65, f32[128,896]{1,0:T(8,128)S(1)} %copy-done.8), kind=kOutput, calls=%fused_computation.4 | convolution fusion | flops 940212224 | bytes 10354688 | tf_op jit(solution)/shard_map/dot_general | solution.py:117
  89.1 5.7 %fusion.51 = bf16[128,4096]{1,0:T(8,128)(2,1)S(1)} fusion(f32[128,4096]{1,0:T(8,128)S(1)} %fusion.4, bf16[1,2,4096,896]{3,2,1,0:T(8,128)(2,1)} %param.17, f32[128,896]{1,0:T(8,128)S(1)} %copy-done.8, f32[128,896]{1,0:T(8,128)S(1)} %fusion.65, f32[128,896]{1,0:T(8,128)S(1)} %copy-done.10), kind=kOutput, calls=%fused_computation.41 | convolution fusion | flops 941719552 | bytes 11862016 | tf_op jit(solution)/shard_map/dot_general | solution.py:115
  94.8 5.7 %fusion.62 = f32[128,896]{1,0:T(8,128)S(1)} fusion(bf16[128,4096]{1,0:T(8,128)(2,1)S(1)} %bitcast.154, bf16[1,2,896,4096]{3,2,1,0:T(8,128)(2,1)} %param.19, f32[128]{0:T(128)S(1)} %reshape.328), kind=kOutput, calls=%fused_computation.53 | convolution fusion | flops 939638784 | bytes 8847872 | tf_op jit(solution)/shard_map/dot_general | solution.py:110
  100.6 2.6 %fusion.16 = f32[128,4096]{1,0:T(8,128)S(1)} fusion(bf16[1,2,4096,896]{3,2,1,0:T(8,128)(2,1)S(1)} %bitcast.161, f32[128,896]{1,0:T(8,128)S(1)} %fusion.62, f32[128,896]{1,0:T(8,128)S(1)} %fusion.22), kind=kOutput, calls=%fused_computation.16 | convolution fusion | flops 940212224 | bytes 10354688 | tf_op jit(solution)/shard_map/dot_general | solution.py:117
  103.3 5.7 %fusion.57 = bf16[128,4096]{1,0:T(8,128)(2,1)S(1)} fusion(f32[128,4096]{1,0:T(8,128)S(1)} %fusion.16, bf16[1,2,4096,896]{3,2,1,0:T(8,128)(2,1)} %param.17, f32[128,896]{1,0:T(8,128)S(1)} %fusion.22, f32[128,896]{1,0:T(8,128)S(1)} %fusion.62, f32[128,896]{1,0:T(8,128)S(1)} %fusion.18), kind=kOutput, calls=%fused_computation.43 | convolution fusion | flops 941719552 | bytes 11862016 | tf_op jit(solution)/shard_map/dot_general | solution.py:115
  110.5 2.4 %fusion.54 = bf16[128,4096]{1,0:T(8,128)(2,1)S(1)} fusion(bf16[1,2,896,4096]{3,2,1,0:T(8,128)(2,1)S(1)} %bitcast.165, f32[128]{0:T(128)S(1)} %reshape.328, f32[128,896]{1,0:T(8,128)} %copy-done.6, f32[128,896]{1,0:T(8,128)} %copy-done.5), kind=kOutput, calls=%fused_computation.42 | convolution fusion | flops 941260800 | bytes 9306624 | tf_op jit(solution)/shard_map/dot_general | solution.py:100
  114.6 1.5 add_convert_fusion
  117.2 1.5 collective-permute-start.2
  119.5 11.8 %collective-permute-done.2 = bf16[2,32,4096]{2,1,0:T(8,128)(2,1)S(1)} collective-permute-done((bf16[2,32,4096]{2,1,0:T(8,128)(2,1)S(1)}, bf16[2,32,4096]{2,1,0:T(8,128)(2,1)S(1)}, u32[]{:S(2)}, u32[]{:S(2)}) %collective-permute-start.2) | collective-permute-done | bytes 524320 | tf_op jit(solution)/shard_map/ppermute | solution.py:51
  135.2 25.4 %reduce-scatter.2.cloned.1.call-done = bf16[32,4096]{1,0:T(8,128)(2,1)} async-done(((bf16[256,4096]{1,0:T(8,128)(2,1)}), bf16[32,4096]{1,0:T(8,128)(2,1)}) %reduce-scatter.2.cloned.1.call-update) | async-done | bytes 262160 | tf_op jit(solution)/shard_map/reduce_scatter | solution.py:104
  160.6 2.4 %fusion.61 = bf16[1,128,4096]{2,1,0:T(8,128)(2,1)} fusion(bf16[32,4096]{1,0:T(8,128)(2,1)} %reduce-scatter.2.cloned.1.call-done, pred[16,128]{1,0:T(8,128)(4,1)S(1)} %get-tuple-element.59, pred[16,128]{1,0:T(8,128)(4,1)S(1)} %get-tuple-element.58), kind=kOutput, calls=%fused_computation.47 | convolution fusion | flops 34082816 | bytes 1314816 | tf_op jit(solution)/shard_map/dot_general | solution.py:65
  163.0 2.0 %fusion.60 = bf16[1,128,4096]{2,1,0:T(8,128)(2,1)} fusion(bf16[32,4096]{1,0:T(8,128)(2,1)S(1)} %collective-permute-done.4, bf16[32,4096]{1,0:T(8,128)(2,1)S(1)} %collective-permute-done.3, pred[16,128]{1,0:T(8,128)(4,1)S(1)} %get-tuple-element.61, pred[16,128]{1,0:T(8,128)(4,1)S(1)} %get-tuple-element.60), kind=kOutput, calls=%fused_computation.46 | convolution fusion | flops 202248192 | bytes 1576960 | tf_op jit(solution)/shard_map/dot_general | solution.py:65
  (99 shorter events, 15.3 us)
Async XLA Ops:
  7.2 34.7 %all-gather.3.cloned.1.call-start = ((), (), s32[]{:S(2)}) async-start(), calls=%async_computation.1 | async-start | bytes 2433024 | tf_op jit(solution)/shard_map/all_gather | solution.py:87
  10.9 65.2 %all-gather.5.cloned.1.call-start = ((), (), s32[]{:S(2)}) async-start(), calls=%async_computation.3 | async-start | bytes 2359296 | tf_op jit(solution)/shard_map/all_gather | solution.py:90
  41.9 6.2 %copy-start.4 = (s32[1,128,2]{1,2,0:T(2,128)S(1)}, s32[1,128,2]{1,2,0:T(2,128)}, u32[]{:S(2)}) copy-start(s32[1,128,2]{1,2,0:T(2,128)} %param.15) | copy-start | bytes 3076
  48.0 55.2 %copy-start.5 = (f32[128,896]{1,0:T(8,128)}, f32[128,896]{1,0:T(8,128)S(1)}, u32[]{:S(2)}) copy-start(f32[128,896]{1,0:T(8,128)S(1)} %fusion.22) | copy-start | bytes 1376260
  48.0 112.6 %reduce-scatter.2.cloned.1.call-start = ((), (), s32[]{:S(2)}) async-start(), calls=%async_computation.2 | async-start | bytes 2359296 | tf_op jit(solution)/shard_map/reduce_scatter | solution.py:104
  48.1 5.5 %collective-permute-start = (s32[128,2]{0,1:T(2,128)S(1)}, s32[128,2]{0,1:T(2,128)S(1)}, u32[]{:S(2)}, u32[]{:S(2)}) collective-permute-start(s32[128,2]{0,1:T(2,128)S(1)} %bitcast.159), channel_id=1, source_target_pairs={{8,0},{16,8},{24,16},{9,1},{17,9},{25,17},{10,2},{18,10},{26,18},{... | collective-permute-start | bytes 3080 | tf_op jit(solution)/shard_map/ppermute | solution.py:14
  54.8 14.2 %slice-start.4 = ((s8[14680064]{0:T(1024)(128)(4,1)}), s8[4194304]{0:T(1024)(128)(4,1)S(1)}, s32[]{:S(2)}) async-start(s8[14680064]{0:T(1024)(128)(4,1)} %bitcast.162), calls=%async_computation.8 | async-start | bytes 8388608
  54.8 14.2 %slice-start.5 = ((s8[14680064]{0:T(1024)(128)(4,1)}), s8[4194304]{0:T(1024)(128)(4,1)S(1)}, s32[]{:S(2)}) async-start(s8[14680064]{0:T(1024)(128)(4,1)} %bitcast.162), calls=%async_computation.9 | async-start | bytes 8388608
  59.4 9.5 %copy-start.7 = (f32[128,896]{1,0:T(8,128)}, f32[128,896]{1,0:T(8,128)S(1)}, u32[]{:S(2)}) copy-start(f32[128,896]{1,0:T(8,128)S(1)} %fusion.10) | copy-start | bytes 1376260
  59.5 9.5 %slice-start.6 = ((s8[14680064]{0:T(1024)(128)(4,1)}), s8[4194304]{0:T(1024)(128)(4,1)S(1)}, s32[]{:S(2)}) async-start(s8[14680064]{0:T(1024)(128)(4,1)} %bitcast.162), calls=%async_computation.10 | async-start | bytes 8388608
  69.0 34.2 %copy-start.6 = (f32[128,896]{1,0:T(8,128)}, f32[128,896]{1,0:T(8,128)S(1)}, u32[]{:S(2)}) copy-start(f32[128,896]{1,0:T(8,128)S(1)} %fusion.18) | copy-start | bytes 1376260
  76.1 7.3 %copy-start.8 = (f32[128,896]{1,0:T(8,128)S(1)}, f32[128,896]{1,0:T(8,128)}, u32[]{:S(2)}) copy-start(f32[128,896]{1,0:T(8,128)} %copy-done.7) | copy-start | bytes 1376260
  83.4 17.1 %slice-start = ((s8[14680064]{0:T(1024)(128)(4,1)}), s8[4194304]{0:T(1024)(128)(4,1)S(1)}, s32[]{:S(2)}) async-start(s8[14680064]{0:T(1024)(128)(4,1)} %bitcast.160), calls=%async_computation.4 | async-start | bytes 8388608
  83.4 17.1 %slice-start.1 = ((s8[14680064]{0:T(1024)(128)(4,1)}), s8[4194304]{0:T(1024)(128)(4,1)S(1)}, s32[]{:S(2)}) async-start(s8[14680064]{0:T(1024)(128)(4,1)} %bitcast.160), calls=%async_computation.5 | async-start | bytes 8388608
  89.1 11.4 %slice-start.2 = ((s8[14680064]{0:T(1024)(128)(4,1)}), s8[4194304]{0:T(1024)(128)(4,1)S(1)}, s32[]{:S(2)}) async-start(s8[14680064]{0:T(1024)(128)(4,1)} %bitcast.160), calls=%async_computation.6 | async-start | bytes 8388608
  100.5 10.0 %slice-start.8 = ((s8[14680064]{0:T(1024)(128)(4,1)}), s8[2097152]{0:T(1024)(128)(4,1)S(1)}, s32[]{:S(2)}) async-start(s8[14680064]{0:T(1024)(128)(4,1)} %bitcast.164), calls=%async_computation.12 | async-start | bytes 4194304
  100.6 10.0 %slice-start.9 = ((s8[14680064]{0:T(1024)(128)(4,1)}), s8[4194304]{0:T(1024)(128)(4,1)S(1)}, s32[]{:S(2)}) async-start(s8[14680064]{0:T(1024)(128)(4,1)} %bitcast.164), calls=%async_computation.13 | async-start | bytes 8388608
  103.2 7.3 %slice-start.10 = ((s8[14680064]{0:T(1024)(128)(4,1)}), s8[4194304]{0:T(1024)(128)(4,1)S(1)}, s32[]{:S(2)}) async-start(s8[14680064]{0:T(1024)(128)(4,1)} %bitcast.164), calls=%async_computation.14 | async-start | bytes 8388608
  103.3 7.3 %slice-start.11 = ((s8[14680064]{0:T(1024)(128)(4,1)}), s8[4194304]{0:T(1024)(128)(4,1)S(1)}, s32[]{:S(2)}) async-start(s8[14680064]{0:T(1024)(128)(4,1)} %bitcast.164), calls=%async_computation.15 | async-start | bytes 8388608
  110.2 4.3 %collective-permute-start.1 = (bf16[4,32,4096]{2,1,0:T(8,128)(2,1)}, bf16[4,32,4096]{2,1,0:T(8,128)(2,1)}, u32[]{:S(2)}, u32[]{:S(2)}) collective-permute-start(bf16[4,32,4096]{2,1,0:T(8,128)(2,1)} %select_bitcast_fusion), channel_id=1, source_target_pairs={{0,1},{1,0},{2,3},{3,2},{4,5},{5,4},{6,7},{7,6},{8,9},{9,8},{10,11... | collective-permute-start | bytes 3145736 | tf_op jit(solution)/shard_map/ppermute | solution.py:51
  113.0 52.0 %copy-start.1 = (bf16[1,128,4096]{2,1,0:T(8,128)(2,1)S(1)}, bf16[1,128,4096]{2,1,0:T(8,128)(2,1)}, u32[]{:S(2)}) copy-start(bf16[1,128,4096]{2,1,0:T(8,128)(2,1)} %param.13) | copy-start | bytes 3145732
  117.2 14.1 %collective-permute-start.2 = (bf16[2,32,4096]{2,1,0:T(8,128)(2,1)S(1)}, bf16[2,32,4096]{2,1,0:T(8,128)(2,1)S(1)}, u32[]{:S(2)}, u32[]{:S(2)}) collective-permute-start(bf16[2,32,4096]{2,1,0:T(8,128)(2,1)S(1)} %select_bitcast_fusion.1), channel_id=1, source_target_pairs={{0,2},{1,3},{2,0},{3,1},{4,6},{5,7},{6,4},{7,5},{8,10},{9,11},{10,... | collective-permute-start | bytes 1572872 | tf_op jit(solution)/shard_map/ppermute | solution.py:51
  132.6 30.4 %collective-permute-start.3 = (bf16[32,4096]{1,0:T(8,128)(2,1)S(1)}, bf16[32,4096]{1,0:T(8,128)(2,1)S(1)}, u32[]{:S(2)}, u32[]{:S(2)}) collective-permute-start(bf16[32,4096]{1,0:T(8,128)(2,1)S(1)} %get-tuple-element.54), channel_id=1, source_target_pairs={{8,0},{9,1},{10,2},{11,3},{12,4},{13,5},{14,6},{15,7},{16,8},{17,9... | collective-permute-start | bytes 786440 | tf_op jit(solution)/shard_map/ppermute | solution.py:59
  133.9 29.1 %collective-permute-start.4 = (bf16[32,4096]{1,0:T(8,128)(2,1)S(1)}, bf16[32,4096]{1,0:T(8,128)(2,1)S(1)}, u32[]{:S(2)}, u32[]{:S(2)}) collective-permute-start(bf16[32,4096]{1,0:T(8,128)(2,1)S(1)} %get-tuple-element.55), channel_id=1, source_target_pairs={{8,4},{9,5},{10,6},{11,7},{12,0},{13,1},{14,2},{15,3},{16,12},{17,... | collective-permute-start | bytes 786440 | tf_op jit(solution)/shard_map/ppermute | solution.py:60
  (7 other events, 28.7 us)
Sparse Core Ops, SparseCore 0:
  11.0 30.8 all-gather.2
  48.1 27.8 all-gather.4
  114.7 45.8 reduce-scatter.1

commit v5 on v4

--- a/solution.py
+++ b/solution.py
@@ -37,9 +37,8 @@
     return jnp.dot(select.astype(rows.dtype), rows, preferred_element_type=jnp.float32).astype(rows.dtype)
 
 
-def reduce_to_previous(parts):
+def halve_over_et(parts):
     n = lax.axis_size("et")
-    stages = lax.axis_size("pipe")
     me = lax.axis_index("et")
     held = parts
     bit = 1
@@ -52,8 +51,20 @@
         held = (keep.astype(jnp.float32) + got.astype(jnp.float32)).astype(jnp.bfloat16)
         bit *= 2
     side = (me // bit) % 2
-    keep = jnp.take(held, side, axis=0)
-    give = jnp.take(held, 1 - side, axis=0)
+    return jnp.take(held, side, axis=0), jnp.take(held, 1 - side, axis=0), bit
+
+
+def reduce_to_owner(parts):
+    n = lax.axis_size("et")
+    keep, give, bit = halve_over_et(parts)
+    got = lax.ppermute(give, "et", [(i, i ^ bit) for i in range(n)])
+    return keep.astype(jnp.float32) + got.astype(jnp.float32)
+
+
+def reduce_to_previous(parts):
+    n = lax.axis_size("et")
+    stages = lax.axis_size("pipe")
+    keep, give, bit = halve_over_et(parts)
     to_same = [(stage * n + i, (stage - 1) * n + i) for stage in range(1, stages) for i in range(n)]
     to_other = [(stage * n + i, (stage - 1) * n + (i ^ bit)) for stage in range(1, stages) for i in range(n)]
     first = lax.ppermute(keep, ("pipe", "et"), to_same)
@@ -101,12 +112,13 @@
         outs.append(out_e.astype(jnp.bfloat16).reshape(n, MOST, width))
         stored.append((gate_w, pre_up, activated, slopes))
     out_parts = jnp.stack(outs, axis=1).reshape(n, E_WIN * MOST, width)
-    out_sums = lax.psum_scatter(out_parts.reshape(n * E_WIN * MOST, width), "et", scatter_dimension=0, tiled=True)
-    out_share = unpack(out_sums.astype(jnp.float32), select)
+    out_sums = reduce_to_owner(out_parts)
     grad_outs = []
     for expert in range(E_WIN):
         gate_w, pre_up, activated, slopes = stored[expert]
         grad_rows = grads[:, expert].reshape(n * MOST, width)
+        if expert == E_WIN - 1:
+            out_sums, grad_rows = lax.optimization_barrier((out_sums, grad_rows))
         d_hidden = gate_w * lax.dot_general(
             grad_rows, down_mats[expert], (((1,), (1,)), ((), ())), preferred_element_type=jnp.float32
         )
@@ -118,6 +130,7 @@
         grad_outs.append(grad_e.astype(jnp.bfloat16).reshape(n, MOST, width))
     grad_parts = jnp.stack(grad_outs, axis=1).reshape(n, E_WIN * MOST, width)
     received = unpack(reduce_to_previous(grad_parts), next_select)
+    out_share = unpack(out_sums, select)
     return (out_share[None], received[None])
 
 

time: 172 us -> 181 us (1.052)
  waiting for transfers between devices: 74.7 us -> 84.2 us
  matrix products: 60.9 us -> 57.7 us
  starting transfers between devices: 5.97 us -> 9.09 us
    ppermute x2 -> x5, waiting for transfers between devices: 11.8 us -> 40.6 us  [the longest x4 28.7 us: halve_over_et(): got = lax.ppermute(give, 'et', [(i, i ^ bit) for i in range(n)])]
    reduce_scatter x1 -> x0, waiting for transfers between devices: 25.4 us -> none  [per_device(): lax.psum_scatter(out_parts.reshape(n * E_WIN * MOST, width), 'et', scatte...]
    ppermute x1, waiting for transfers between devices: 0.01 us -> 7.36 us  [reduce_to_previous(): second = lax.ppermute(give, ('pipe', 'et'), to_other)]
    dot_general x2, matrix products: 4.71 us -> 8.79 us  [per_device(): jnp.dot(hidden, down_mats[expert], preferred_element_type=jnp.float32)]
    all_gather x1, waiting for transfers between devices: 4.79 us -> 1.24 us  [per_device(): lax.all_gather(grad_rows_local, 'et', axis=0, tiled=True)]
    dot_general x1, matrix products: 4.63 us -> 1.26 us  [per_device(): jnp.dot(rows, gate_mats[expert], preferred_element_type=jnp.float32)]
    ppermute x2 -> x5, starting transfers between devices: 1.79 us -> 5.15 us  [the longest x4 3.71 us: halve_over_et(): got = lax.ppermute(give, 'et', [(i, i ^ bit) for i in range(n)])]
    dot_general x2, matrix products: 8.32 us -> 11.4 us  [per_device(): lax.dot_general(d_up, up_mats[expert], (((1,), (1,)), ((), ())), preferre...]
  transfers between devices with their start and end apart: 8 -> 10, of which waited for: 5 -> 9; matrix products, arithmetic and copies ran while one was open for 17% -> 4% of each run, Pallas kernels for 0% -> 0%
where the time goes in v5:
time: 181 us; the launch traced here: 180 us
  waiting for transfers between devices  84.2 us (47%)
  matrix products  57.7 us (32%)
  between operations  14.6 us (8%)
  starting transfers between devices  9.09 us (5%)
  other arithmetic  7.69 us (4%)
  local copies, waits for them, and re-layouts  6.84 us (4%)
    all_gather x1, waiting for transfers between devices, per_device(): lax.all_gather(packed, 'et', axis=0, tiled=True)  28.8 us
    ppermute x4, waiting for transfers between devices, halve_over_et(): got = lax.ppermute(give, 'et', [(i, i ^ bit) for i in range(n)])  28.7 us
    ppermute x1, waiting for transfers between devices, reduce_to_owner(): got = lax.ppermute(give, 'et', [(i, i ^ bit) for i in range(n)])  11.9 us
    dot_general x2, matrix products, per_device(): lax.dot_general(d_up, up_mats[expert], (((1,), (1,)), ((), ())), preferre...  11.4 us
    dot_general x2, matrix products, per_device(): lax.dot_general(d_gate, gate_mats[expert], (((1,), (1,)), ((), ())), pref...  11.3 us
    dot_general x2, matrix products, per_device(): pre_up = jnp.dot(rows, up_mats[expert], preferred_element_type=jnp.float32)  9.14 us
    dot_general x2, matrix products, per_device(): jnp.dot(hidden, down_mats[expert], preferred_element_type=jnp.float32)  8.79 us
    dot_general x2, matrix products, per_device(): lax.dot_general(grad_rows, down_mats[expert], (((1,), (1,)), ((), ())), p...  8.11 us
  transfers between devices with their start and end apart: 10, of which 9 were waited for; matrix products, arithmetic and copies ran while one was open for 4% of the time, Pallas kernels for 0%

profile of v5, /device:TPU:0, one launch (start us, length us, event | category | flops | bytes accessed | tf_op | source)
XLA Modules:
  0.0 180.0 jit_solution(9951340757005002670)
XLA Ops:
  10.9 2.2 %convolution_convert_fusion.2 = bf16[32,4096]{1,0:T(8,128)(2,1)} fusion(bf16[1,128,4096]{2,1,0:T(8,128)(2,1)} %param.16, pred[16,128]{1,0:T(8,128)(4,1)S(1)} %get-tuple-element.63, pred[16,128]{1,0:T(8,128)(4,1)S(1)} %get-tuple-element.62), kind=kOutput, calls=%fused_computation.48 | convolution fusion | flops 33689600 | bytes 1314816 | tf_op jit(solution)/shard_map/dot_general | solution.py:37
  13.1 28.8 %all-gather.3.cloned.1.call-done = bf16[256,4224]{1,0:T(8,128)(2,1)} async-done(((bf16[32,4224]{1,0:T(8,128)(2,1)}), bf16[256,4224]{1,0:T(8,128)(2,1)}) %all-gather.3.cloned.1.call-update) | async-done | bytes 2162704 | tf_op jit(solution)/shard_map/all_gather | solution.py:98
  42.7 1.8 %fusion.103 = (bf16[8,1,16,4096]{3,2,1,0:T(8,128)(2,1)S(1)}, bf16[8,1,16,4096]{3,2,1,0:T(8,128)(2,1)S(1)}) fusion(bf16[8,2,16,4224]{3,2,1,0:T(8,128)(2,1)} %bitcast.179), kind=kLoop, calls=%fused_computation.132 | loop fusion | bytes 4194304 | tf_op jit(solution)/shard_map/slice | solution.py:99
  44.5 4.6 %fusion.6 = f32[128,896]{1,0:T(8,128)S(1)} fusion(bf16[128,4096]{1,0:T(8,128)(2,1)S(1)} %bitcast.186, bf16[1,2,4096,896]{3,2,1,0:T(8,128)(2,1)} %param.18), kind=kOutput, calls=%fused_computation.6 | convolution fusion | flops 939524096 | bytes 8847360 | tf_op jit(solution)/shard_map/dot_general | solution.py:108
  51.8 4.5 %fusion.18 = f32[128,896]{1,0:T(8,128)S(1)} fusion(bf16[128,4096]{1,0:T(8,128)(2,1)S(1)} %bitcast.183, bf16[1,2,4096,896]{3,2,1,0:T(8,128)(2,1)} %param.18), kind=kOutput, calls=%fused_computation.18 | convolution fusion | flops 939524096 | bytes 8847360 | tf_op jit(solution)/shard_map/dot_general | solution.py:108
  58.1 4.4 %fusion.48 = bf16[128,4096]{1,0:T(8,128)(2,1)S(1)} fusion(bf16[1,2,896,4096]{3,2,1,0:T(8,128)(2,1)} %param.19, f32[128]{0:T(128)S(1)} %reshape.397, f32[128,896]{1,0:T(8,128)S(1)} %fusion.6, f32[128,896]{1,0:T(8,128)S(1)} %fusion.10), kind=kOutput, calls=%fused_computation.40 | convolution fusion | flops 941260800 | bytes 9306624 | tf_op jit(solution)/shard_map/dot_general | solution.py:111
  62.5 4.4 %fusion.54 = bf16[128,4096]{1,0:T(8,128)(2,1)S(1)} fusion(bf16[1,2,896,4096]{3,2,1,0:T(8,128)(2,1)} %param.19, f32[128]{0:T(128)S(1)} %reshape.396, f32[128,896]{1,0:T(8,128)S(1)} %fusion.18, f32[128,896]{1,0:T(8,128)S(1)} %fusion.22), kind=kOutput, calls=%fused_computation.42 | convolution fusion | flops 941260800 | bytes 9306624 | tf_op jit(solution)/shard_map/dot_general | solution.py:111
  67.6 2.5 %collective-permute-done = bf16[4,32,4096]{2,1,0:T(8,128)(2,1)} collective-permute-done((bf16[4,32,4096]{2,1,0:T(8,128)(2,1)S(1)}, bf16[4,32,4096]{2,1,0:T(8,128)(2,1)}, u32[]{:S(2)}, u32[]{:S(2)}) %collective-permute-start) | collective-permute-done | bytes 1048608 | tf_op jit(solution)/shard_map/ppermute | solution.py:50
  70.1 1.5 add_convert_fusion.1
  73.3 15.4 %collective-permute-done.1 = bf16[2,32,4096]{2,1,0:T(8,128)(2,1)S(1)} collective-permute-done((bf16[2,32,4096]{2,1,0:T(8,128)(2,1)S(1)}, bf16[2,32,4096]{2,1,0:T(8,128)(2,1)S(1)}, u32[]{:S(2)}, u32[]{:S(2)}) %collective-permute-start.1) | collective-permute-done | bytes 524320 | tf_op jit(solution)/shard_map/ppermute | solution.py:50
  90.3 11.9 %collective-permute-done.2 = bf16[32,4096]{1,0:T(8,128)(2,1)S(1)} collective-permute-done((bf16[32,4096]{1,0:T(8,128)(2,1)S(1)}, bf16[32,4096]{1,0:T(8,128)(2,1)S(1)}, u32[]{:S(2)}, u32[]{:S(2)}) %collective-permute-start.2) | collective-permute-done | bytes 262176 | tf_op jit(solution)/shard_map/ppermute | solution.py:60
  103.6 1.8 fusion.105
  105.4 5.7 %fusion.65 = f32[128,896]{1,0:T(8,128)S(1)} fusion(bf16[128,4096]{1,0:T(8,128)(2,1)S(1)} %bitcast.188, bf16[1,2,896,4096]{3,2,1,0:T(8,128)(2,1)} %param.19, f32[128]{0:T(128)S(1)} %reshape.397), kind=kOutput, calls=%fused_computation.55 | convolution fusion | flops 939638784 | bytes 8847872 | tf_op jit(solution)/shard_map/dot_general | solution.py:122
  111.1 5.8 %fusion.4 = f32[128,4096]{1,0:T(8,128)S(1)} fusion(bf16[1,2,4096,896]{3,2,1,0:T(8,128)(2,1)} %param.18, f32[128,896]{1,0:T(8,128)S(1)} %fusion.65, f32[128,896]{1,0:T(8,128)S(1)} %copy-done.11), kind=kOutput, calls=%fused_computation.4 | convolution fusion | flops 940212224 | bytes 10354688 | tf_op jit(solution)/shard_map/dot_general | solution.py:129
  116.9 5.7 %fusion.51 = bf16[128,4096]{1,0:T(8,128)(2,1)S(1)} fusion(f32[128,4096]{1,0:T(8,128)S(1)} %fusion.4, bf16[1,2,4096,896]{3,2,1,0:T(8,128)(2,1)} %param.17, f32[128,896]{1,0:T(8,128)S(1)} %copy-done.11, f32[128,896]{1,0:T(8,128)S(1)} %fusion.65, f32[128,896]{1,0:T(8,128)S(1)} %copy-done.9), kind=kOutput, calls=%fused_computation.41 | convolution fusion | flops 941719552 | bytes 11862016 | tf_op jit(solution)/shard_map/dot_general | solution.py:127
  122.7 2.4 %fusion.62 = f32[128,896]{1,0:T(8,128)S(1)} fusion(bf16[128,4096]{1,0:T(8,128)(2,1)S(1)} %bitcast.182, bf16[1,2,896,4096]{3,2,1,0:T(8,128)(2,1)S(1)} %bitcast.193, f32[128]{0:T(128)S(1)} %reshape.396), kind=kOutput, calls=%fused_computation.54 | convolution fusion | flops 939638784 | bytes 8847872 | tf_op jit(solution)/shard_map/dot_general | solution.py:122
  125.2 5.6 %fusion.16 = f32[128,4096]{1,0:T(8,128)S(1)} fusion(bf16[1,2,4096,896]{3,2,1,0:T(8,128)(2,1)} %param.18, f32[128,896]{1,0:T(8,128)S(1)} %fusion.62, f32[128,896]{1,0:T(8,128)S(1)} %copy-done.7), kind=kOutput, calls=%fused_computation.16 | convolution fusion | flops 940212224 | bytes 10354688 | tf_op jit(solution)/shard_map/dot_general | solution.py:129
  130.8 5.6 %fusion.57 = bf16[128,4096]{1,0:T(8,128)(2,1)S(1)} fusion(f32[128,4096]{1,0:T(8,128)S(1)} %fusion.16, bf16[1,2,4096,896]{3,2,1,0:T(8,128)(2,1)} %param.17, f32[128,896]{1,0:T(8,128)S(1)} %copy-done.7, f32[128,896]{1,0:T(8,128)S(1)} %fusion.62, f32[128,896]{1,0:T(8,128)S(1)} %copy-done.5), kind=kOutput, calls=%fused_computation.43 | convolution fusion | flops 941719552 | bytes 11862016 | tf_op jit(solution)/shard_map/dot_general | solution.py:127
  138.3 4.2 %collective-permute-done.3 = s32[128,2]{0,1:T(2,128)S(1)} collective-permute-done((s32[128,2]{0,1:T(2,128)S(1)}, s32[128,2]{0,1:T(2,128)S(1)}, u32[]{:S(2)}, u32[]{:S(2)}) %collective-permute-start.3) | collective-permute-done | bytes 1056 | tf_op jit(solution)/shard_map/ppermute | solution.py:14
  145.2 10.8 %collective-permute-done.5 = bf16[2,32,4096]{2,1,0:T(8,128)(2,1)} collective-permute-done((bf16[2,32,4096]{2,1,0:T(8,128)(2,1)S(1)}, bf16[2,32,4096]{2,1,0:T(8,128)(2,1)}, u32[]{:S(2)}, u32[]{:S(2)}) %collective-permute-start.5) | collective-permute-done | bytes 524320 | tf_op jit(solution)/shard_map/ppermute | solution.py:50
  159.9 2.0 %fusion.60 = bf16[1,128,4096]{2,1,0:T(8,128)(2,1)} fusion(f32[32,4096]{1,0:T(8,128)S(1)} %convert_add_fusion, pred[16,128]{1,0:T(8,128)(4,1)S(1)} %get-tuple-element.63, pred[16,128]{1,0:T(8,128)(4,1)S(1)} %get-tuple-element.62), kind=kOutput, calls=%fused_computation.46 | convolution fusion | flops 201854976 | bytes 1576960 | tf_op jit(solution)/shard_map/dot_general | solution.py:76
  161.9 7.4 %collective-permute-done.7 = bf16[32,4096]{1,0:T(8,128)(2,1)S(1)} collective-permute-done((bf16[32,4096]{1,0:T(8,128)(2,1)S(1)}, bf16[32,4096]{1,0:T(8,128)(2,1)S(1)}, u32[]{:S(2)}, u32[]{:S(2)}) %collective-permute-start.7) | collective-permute-done | bytes 262176 | tf_op jit(solution)/shard_map/ppermute | solution.py:71
  169.2 1.9 %collective-permute-done.6 = bf16[32,4096]{1,0:T(8,128)(2,1)S(1)} collective-permute-done((bf16[32,4096]{1,0:T(8,128)(2,1)S(1)}, bf16[32,4096]{1,0:T(8,128)(2,1)S(1)}, u32[]{:S(2)}, u32[]{:S(2)}) %collective-permute-start.6) | collective-permute-done | bytes 262176 | tf_op jit(solution)/shard_map/ppermute | solution.py:70
  171.2 2.0 %fusion.61 = bf16[1,128,4096]{2,1,0:T(8,128)(2,1)} fusion(bf16[32,4096]{1,0:T(8,128)(2,1)S(1)} %collective-permute-done.7, bf16[32,4096]{1,0:T(8,128)(2,1)S(1)} %collective-permute-done.6, pred[16,128]{1,0:T(8,128)(4,1)S(1)} %get-tuple-element.65, pred[16,128]{1,0:T(8,128)(4,1)S(1)} %get-tuple-element.64), kind=kOutput, calls=%fused_computation.47 | convolution fusion | flops 202248192 | bytes 1576960 | tf_op jit(solution)/shard_map/dot_general | solution.py:76
  (92 shorter events, 22.6 us)
Async XLA Ops:
  7.2 34.7 %all-gather.3.cloned.1.call-start = ((), (), s32[]{:S(2)}) async-start(), calls=%async_computation | async-start | bytes 2433024 | tf_op jit(solution)/shard_map/all_gather | solution.py:98
  10.8 92.7 %all-gather.5.cloned.1.call-start = ((), (), s32[]{:S(2)}) async-start(), calls=%async_computation.1 | async-start | bytes 2359296 | tf_op jit(solution)/shard_map/all_gather | solution.py:101
  42.7 7.9 %copy-start.3 = (bf16[1,2,4096,896]{3,2,1,0:T(8,128)(2,1)S(1)}, bf16[1,2,4096,896]{3,2,1,0:T(8,128)(2,1)}, u32[]{:S(2)}) copy-start(bf16[1,2,4096,896]{3,2,1,0:T(8,128)(2,1)} %param.17) | copy-start | bytes 44040196
  50.6 7.5 %copy-start.8 = (f32[128,896]{1,0:T(8,128)}, f32[128,896]{1,0:T(8,128)S(1)}, u32[]{:S(2)}) copy-start(f32[128,896]{1,0:T(8,128)S(1)} %fusion.6) | copy-start | bytes 1376260
  51.8 6.3 %copy-start.10 = (f32[128,896]{1,0:T(8,128)}, f32[128,896]{1,0:T(8,128)S(1)}, u32[]{:S(2)}) copy-start(f32[128,896]{1,0:T(8,128)S(1)} %fusion.10) | copy-start | bytes 1376260
  56.4 6.2 %copy-start.4 = (f32[128,896]{1,0:T(8,128)}, f32[128,896]{1,0:T(8,128)S(1)}, u32[]{:S(2)}) copy-start(f32[128,896]{1,0:T(8,128)S(1)} %fusion.18) | copy-start | bytes 1376260
  57.6 9.3 %copy-start.6 = (f32[128,896]{1,0:T(8,128)}, f32[128,896]{1,0:T(8,128)S(1)}, u32[]{:S(2)}) copy-start(f32[128,896]{1,0:T(8,128)S(1)} %fusion.22) | copy-start | bytes 1376260
  67.3 2.9 %collective-permute-start = (bf16[4,32,4096]{2,1,0:T(8,128)(2,1)S(1)}, bf16[4,32,4096]{2,1,0:T(8,128)(2,1)}, u32[]{:S(2)}, u32[]{:S(2)}) collective-permute-start(bf16[4,32,4096]{2,1,0:T(8,128)(2,1)S(1)} %select_bitcast_fusion.1), channel_id=1, source_target_pairs={{0,1},{1,0},{2,3},{3,2},{4,5},{5,4},{6,7},{7,6},{8,9},{9,8},{10,11... | collective-permute-start | bytes 3145736 | tf_op jit(solution)/shard_map/ppermute | solution.py:50
  71.7 17.0 %collective-permute-start.1 = (bf16[2,32,4096]{2,1,0:T(8,128)(2,1)S(1)}, bf16[2,32,4096]{2,1,0:T(8,128)(2,1)S(1)}, u32[]{:S(2)}, u32[]{:S(2)}) collective-permute-start(bf16[2,32,4096]{2,1,0:T(8,128)(2,1)S(1)} %select_bitcast_fusion.3), channel_id=1, source_target_pairs={{0,2},{1,3},{2,0},{3,1},{4,6},{5,7},{6,4},{7,5},{8,10},{9,11},{10,... | collective-permute-start | bytes 1572872 | tf_op jit(solution)/shard_map/ppermute | solution.py:50
  88.9 13.4 %collective-permute-start.2 = (bf16[32,4096]{1,0:T(8,128)(2,1)S(1)}, bf16[32,4096]{1,0:T(8,128)(2,1)S(1)}, u32[]{:S(2)}, u32[]{:S(2)}) collective-permute-start(bf16[32,4096]{1,0:T(8,128)(2,1)S(1)} %select_bitcast_fusion.6), channel_id=1, source_target_pairs={{0,4},{1,5},{2,6},{3,7},{4,0},{5,1},{6,2},{7,3},{8,12},{9,13},{10,... | collective-permute-start | bytes 786440 | tf_op jit(solution)/shard_map/ppermute | solution.py:60
  103.6 7.5 %copy-start.11 = (f32[128,896]{1,0:T(8,128)S(1)}, f32[128,896]{1,0:T(8,128)}, u32[]{:S(2)}) copy-start(f32[128,896]{1,0:T(8,128)} %copy-done.10) | copy-start | bytes 1376260
  105.3 17.3 %slice-start = ((s8[14680064]{0:T(1024)(128)(4,1)}), s8[4194304]{0:T(1024)(128)(4,1)S(1)}, s32[]{:S(2)}) async-start(s8[14680064]{0:T(1024)(128)(4,1)} %bitcast.192), calls=%async_computation.2 | async-start | bytes 8388608
  105.4 17.3 %slice-start.1 = ((s8[14680064]{0:T(1024)(128)(4,1)}), s8[4194304]{0:T(1024)(128)(4,1)S(1)}, s32[]{:S(2)}) async-start(s8[14680064]{0:T(1024)(128)(4,1)} %bitcast.192), calls=%async_computation.3 | async-start | bytes 8388608
  111.1 5.9 %copy-start.9 = (f32[128,896]{1,0:T(8,128)S(1)}, f32[128,896]{1,0:T(8,128)}, u32[]{:S(2)}) copy-start(f32[128,896]{1,0:T(8,128)} %copy-done.8) | copy-start | bytes 1376260
  111.1 11.6 %slice-start.2 = ((s8[14680064]{0:T(1024)(128)(4,1)}), s8[4194304]{0:T(1024)(128)(4,1)S(1)}, s32[]{:S(2)}) async-start(s8[14680064]{0:T(1024)(128)(4,1)} %bitcast.192), calls=%async_computation.4 | async-start | bytes 8388608
  116.9 5.8 %slice-start.3 = ((s8[14680064]{0:T(1024)(128)(4,1)}), s8[2097152]{0:T(1024)(128)(4,1)S(1)}, s32[]{:S(2)}) async-start(s8[14680064]{0:T(1024)(128)(4,1)} %bitcast.192), calls=%async_computation.5 | async-start | bytes 4194304
  125.2 5.6 %copy-start.5 = (f32[128,896]{1,0:T(8,128)S(1)}, f32[128,896]{1,0:T(8,128)}, u32[]{:S(2)}) copy-start(f32[128,896]{1,0:T(8,128)} %copy-done.4) | copy-start | bytes 1376260
  130.8 6.3 %copy-start.2 = (s32[1,128,2]{1,2,0:T(2,128)S(1)}, s32[1,128,2]{1,2,0:T(2,128)}, u32[]{:S(2)}) copy-start(s32[1,128,2]{1,2,0:T(2,128)} %param.15) | copy-start | bytes 3076
  136.3 36.8 %copy-start.1 = (bf16[1,128,4096]{2,1,0:T(8,128)(2,1)S(1)}, bf16[1,128,4096]{2,1,0:T(8,128)(2,1)}, u32[]{:S(2)}) copy-start(bf16[1,128,4096]{2,1,0:T(8,128)(2,1)} %param.13) | copy-start | bytes 3145732
  136.7 5.8 %collective-permute-start.4 = (bf16[4,32,4096]{2,1,0:T(8,128)(2,1)S(1)}, bf16[4,32,4096]{2,1,0:T(8,128)(2,1)S(1)}, u32[]{:S(2)}, u32[]{:S(2)}) collective-permute-start(bf16[4,32,4096]{2,1,0:T(8,128)(2,1)S(1)} %select_bitcast_fusion), channel_id=1, source_target_pairs={{0,1},{1,0},{2,3},{3,2},{4,5},{5,4},{6,7},{7,6},{8,9},{9,8},{10,11... | collective-permute-start | bytes 3145736 | tf_op jit(solution)/shard_map/ppermute | solution.py:50
  137.0 5.5 %collective-permute-start.3 = (s32[128,2]{0,1:T(2,128)S(1)}, s32[128,2]{0,1:T(2,128)S(1)}, u32[]{:S(2)}, u32[]{:S(2)}) collective-permute-start(s32[128,2]{0,1:T(2,128)S(1)} %bitcast.191), channel_id=1, source_target_pairs={{8,0},{16,8},{24,16},{9,1},{17,9},{25,17},{10,2},{18,10},{26,18},{... | collective-permute-start | bytes 3080 | tf_op jit(solution)/shard_map/ppermute | solution.py:14
  142.9 13.1 %collective-permute-start.5 = (bf16[2,32,4096]{2,1,0:T(8,128)(2,1)S(1)}, bf16[2,32,4096]{2,1,0:T(8,128)(2,1)}, u32[]{:S(2)}, u32[]{:S(2)}) collective-permute-start(bf16[2,32,4096]{2,1,0:T(8,128)(2,1)S(1)} %select_bitcast_fusion.2), channel_id=1, source_target_pairs={{0,2},{1,3},{2,0},{3,1},{4,6},{5,7},{6,4},{7,5},{8,10},{9,11},{10,... | collective-permute-start | bytes 1572872 | tf_op jit(solution)/shard_map/ppermute | solution.py:50
  157.3 12.0 %collective-permute-start.7 = (bf16[32,4096]{1,0:T(8,128)(2,1)S(1)}, bf16[32,4096]{1,0:T(8,128)(2,1)S(1)}, u32[]{:S(2)}, u32[]{:S(2)}) collective-permute-start(bf16[32,4096]{1,0:T(8,128)(2,1)S(1)} %get-tuple-element.59), channel_id=1, source_target_pairs={{8,4},{9,5},{10,6},{11,7},{12,0},{13,1},{14,2},{15,3},{16,12},{17,... | collective-permute-start | bytes 786440 | tf_op jit(solution)/shard_map/ppermute | solution.py:71
  158.6 12.6 %collective-permute-start.6 = (bf16[32,4096]{1,0:T(8,128)(2,1)S(1)}, bf16[32,4096]{1,0:T(8,128)(2,1)S(1)}, u32[]{:S(2)}, u32[]{:S(2)}) collective-permute-start(bf16[32,4096]{1,0:T(8,128)(2,1)S(1)} %get-tuple-element.58), channel_id=1, source_target_pairs={{8,0},{9,1},{10,2},{11,3},{12,4},{13,5},{14,6},{15,7},{16,8},{17,9... | collective-permute-start | bytes 786440 | tf_op jit(solution)/shard_map/ppermute | solution.py:70
  (2 other events, 5.1 us)
Sparse Core Ops, SparseCore 0:
  11.0 30.8 all-gather.2
  67.7 35.8 all-gather.4

commit v6 on v5

--- a/solution.py
+++ b/solution.py
@@ -94,17 +94,16 @@
     next_routes = shifted(expert_ids[0], "pipe", -1)
     next_select = local_slots(next_routes, gate_vals[0])[0]
     weight_cols = jnp.broadcast_to(weights.astype(jnp.bfloat16)[:, None], (E_WIN * MOST, TAIL))
-    packed = jnp.concatenate([pick_rows(select, local_rows), weight_cols], axis=1)
-    all_rows = lax.all_gather(packed, "et", axis=0, tiled=True).reshape(n, E_WIN, MOST, width + TAIL)
-    first_gate = jnp.dot(all_rows[:, 0, :, :width].reshape(n * MOST, width), gate_mats[0], preferred_element_type=jnp.float32)
-    grad_rows_local, first_gate = lax.optimization_barrier((pick_rows(select, local_grads), first_gate))
-    grads = lax.all_gather(grad_rows_local, "et", axis=0, tiled=True).reshape(n, E_WIN, MOST, width)
+    packed = jnp.concatenate(
+        [pick_rows(select, local_rows), pick_rows(select, local_grads), weight_cols], axis=1
+    )
+    gathered = lax.all_gather(packed, "et", axis=0, tiled=True).reshape(n, E_WIN, MOST, 2 * width + TAIL)
     outs = []
     stored = []
     for expert in range(E_WIN):
-        rows = all_rows[:, expert, :, :width].reshape(n * MOST, width)
-        gate_w = all_rows[:, expert, :, width].reshape(n * MOST, 1).astype(jnp.float32)
-        pre_gate = first_gate if expert == 0 else jnp.dot(rows, gate_mats[expert], preferred_element_type=jnp.float32)
+        rows = gathered[:, expert, :, :width].reshape(n * MOST, width)
+        gate_w = gathered[:, expert, :, 2 * width].reshape(n * MOST, 1).astype(jnp.float32)
+        pre_gate = jnp.dot(rows, gate_mats[expert], preferred_element_type=jnp.float32)
         pre_up = jnp.dot(rows, up_mats[expert], preferred_element_type=jnp.float32)
         activated, slopes = silu_parts(pre_gate)
         hidden = (activated * pre_up).astype(jnp.bfloat16)
@@ -116,9 +115,7 @@
     grad_outs = []
     for expert in range(E_WIN):
         gate_w, pre_up, activated, slopes = stored[expert]
-        grad_rows = grads[:, expert].reshape(n * MOST, width)
-        if expert == E_WIN - 1:
-            out_sums, grad_rows = lax.optimization_barrier((out_sums, grad_rows))
+        grad_rows = gathered[:, expert, :, width : 2 * width].reshape(n * MOST, width)
         d_hidden = gate_w * lax.dot_general(
             grad_rows, down_mats[expert], (((1,), (1,)), ((), ())), preferred_element_type=jnp.float32
         )
@@ -129,6 +126,7 @@
         ) + lax.dot_general(d_up, up_mats[expert], (((1,), (1,)), ((), ())), preferred_element_type=jnp.float32)
         grad_outs.append(grad_e.astype(jnp.bfloat16).reshape(n, MOST, width))
     grad_parts = jnp.stack(grad_outs, axis=1).reshape(n, E_WIN * MOST, width)
+    out_sums, grad_parts = lax.optimization_barrier((out_sums, grad_parts))
     received = unpack(reduce_to_previous(grad_parts), next_select)
     out_share = unpack(out_sums, select)
     return (out_share[None], received[None])

time: 181 us -> 168 us (0.928)
  waiting for transfers between devices: 84.2 us -> 78.3 us
  matrix products: 57.7 us -> 52 us
    all_gather x1, waiting for transfers between devices: 28.8 us -> 39.7 us  [per_device(): lax.all_gather(packed, 'et', axis=0, tiled=True)]
    ppermute x4, waiting for transfers between devices: 28.7 us -> 18 us  [halve_over_et(): got = lax.ppermute(give, 'et', [(i, i ^ bit) for i in range(n)])]
    ppermute x1, waiting for transfers between devices: 11.9 us -> 6.13 us  [reduce_to_owner(): got = lax.ppermute(give, 'et', [(i, i ^ bit) for i in range(n)])]
    dot_general x2, matrix products: 8.11 us -> 4.87 us  [per_device(): lax.dot_general(grad_rows, down_mats[expert], (((1,), (1,)), ((), ())), p...]
    dot_general x2, matrix products: 9.14 us -> 6.48 us  [per_device(): pre_up = jnp.dot(rows, up_mats[expert], preferred_element_type=jnp.float32)]
    dot_general x1 -> x2, matrix products: 1.26 us -> 3.33 us  [per_device(): jnp.dot(rows, gate_mats[expert], preferred_element_type=jnp.float32)]
    slice x3 -> x2, local copies, waits for them, and re-layouts: 4.36 us -> 3.88 us  [the longest x1 2.95 us: per_device(): grad_rows = gathered[:, expert, :, width:2 * width].reshape(n * MOST, width)]
  transfers between devices with their start and end apart: 10 -> 9, of which waited for: 9 -> 7; matrix products, arithmetic and copies ran while one was open for 4% -> 18% of each run, Pallas kernels for 0% -> 0%
where the time goes in v6:
time: 168 us; the launch traced here: 167 us
  waiting for transfers between devices  78.3 us (47%)
  matrix products  52 us (31%)
  between operations  14.6 us (9%)
  starting transfers between devices  8.75 us (5%)
  local copies, waits for them, and re-layouts  6.88 us (4%)
  other arithmetic  6.58 us (4%)
    all_gather x1, waiting for transfers between devices, per_device(): lax.all_gather(packed, 'et', axis=0, tiled=True)  39.7 us
    ppermute x4, waiting for transfers between devices, halve_over_et(): got = lax.ppermute(give, 'et', [(i, i ^ bit) for i in range(n)])  18 us
    dot_general x2, matrix products, per_device(): lax.dot_general(d_up, up_mats[expert], (((1,), (1,)), ((), ())), preferre...  11.2 us
    dot_general x2, matrix products, per_device(): lax.dot_general(d_gate, gate_mats[expert], (((1,), (1,)), ((), ())), pref...  11.2 us
    dot_general x2, matrix products, per_device(): jnp.dot(hidden, down_mats[expert], preferred_element_type=jnp.float32)  9.21 us
    ppermute x1, waiting for transfers between devices, reduce_to_previous(): second = lax.ppermute(give, ('pipe', 'et'), to_other)  7.42 us
    dot_general x2, matrix products, per_device(): pre_up = jnp.dot(rows, up_mats[expert], preferred_element_type=jnp.float32)  6.48 us
    ppermute x1, waiting for transfers between devices, reduce_to_owner(): got = lax.ppermute(give, 'et', [(i, i ^ bit) for i in range(n)])  6.13 us
  transfers between devices with their start and end apart: 9, of which 7 were waited for; matrix products, arithmetic and copies ran while one was open for 18% of the time, Pallas kernels for 0%

profile of v6, /device:TPU:0, one launch (start us, length us, event | category | flops | bytes accessed | tf_op | source)
XLA Modules:
  0.0 167.1 jit_solution(3968941739426077450)
XLA Ops:
  9.8 1.5 convolution_convert_fusion.3
  12.6 39.7 %all-gather.2.cloned.1.call-done = bf16[256,8320]{1,0:T(8,128)(2,1)} async-done(((bf16[32,8320]{1,0:T(8,128)(2,1)}), bf16[256,8320]{1,0:T(8,128)(2,1)}) %all-gather.2.cloned.1.call-update) | async-done | bytes 4259856 | tf_op jit(solution)/shard_map/all_gather | solution.py:100
  53.3 2.9 %fusion.103 = (bf16[8,1,16,4096]{3,2,1,0:T(8,128)(2,1)S(1)}, bf16[8,1,16,4096]{3,2,1,0:T(8,128)(2,1)S(1)}, bf16[8,1,16,4096]{3,2,1,0:T(8,128)(2,1)S(1)}, bf16[8,1,16,4096]{3,2,1,0:T(8,128)(2,1)S(1)}) fusion(bf16[8,2,16,8320]{3,2,1,0:T(8,128)(2,1)} %bitcast.175), kind=kLoop, calls=%fused_computation.132 | loop fusion | bytes 8388608 | tf_op jit(solution)/shard_map/slice | solution.py:118
  56.2 5.2 %fusion.6 = f32[128,896]{1,0:T(8,128)S(1)} fusion(bf16[128,4096]{1,0:T(8,128)(2,1)S(1)} %bitcast.188, bf16[1,2,4096,896]{3,2,1,0:T(8,128)(2,1)} %param.18), kind=kOutput, calls=%fused_computation.6 | convolution fusion | flops 939524096 | bytes 8847360 | tf_op jit(solution)/shard_map/dot_general | solution.py:107
  61.4 2.1 %fusion.10 = f32[128,896]{1,0:T(8,128)} fusion(bf16[128,4096]{1,0:T(8,128)(2,1)S(1)} %bitcast.189, bf16[1,2,4096,896]{3,2,1,0:T(8,128)(2,1)S(1)} %copy-done.3), kind=kOutput, calls=%fused_computation.10 | convolution fusion | flops 939524096 | bytes 8847360 | tf_op jit(solution)/shard_map/dot_general | solution.py:106
  68.5 4.7 %fusion.48 = bf16[128,4096]{1,0:T(8,128)(2,1)S(1)} fusion(bf16[1,2,896,4096]{3,2,1,0:T(8,128)(2,1)} %param.19, f32[128]{0:T(128)S(1)} %reshape.401, f32[128,896]{1,0:T(8,128)S(1)} %fusion.6, f32[128,896]{1,0:T(8,128)} %fusion.10), kind=kOutput, calls=%fused_computation.40 | convolution fusion | flops 941260800 | bytes 9306624 | tf_op jit(solution)/shard_map/dot_general | solution.py:110
  73.2 4.5 %fusion.54 = bf16[128,4096]{1,0:T(8,128)(2,1)S(1)} fusion(bf16[1,2,896,4096]{3,2,1,0:T(8,128)(2,1)} %param.19, f32[128]{0:T(128)S(1)} %reshape.400, f32[128,896]{1,0:T(8,128)S(1)} %fusion.18, f32[128,896]{1,0:T(8,128)S(1)} %fusion.22), kind=kOutput, calls=%fused_computation.42 | convolution fusion | flops 941260800 | bytes 9306624 | tf_op jit(solution)/shard_map/dot_general | solution.py:110
  78.4 2.4 %fusion.65 = f32[128,896]{1,0:T(8,128)S(1)} fusion(bf16[128,4096]{1,0:T(8,128)(2,1)S(1)} %bitcast.185, bf16[1,2,896,4096]{3,2,1,0:T(8,128)(2,1)S(1)} %bitcast.192, f32[128]{0:T(128)S(1)} %reshape.401), kind=kOutput, calls=%fused_computation.55 | convolution fusion | flops 939638784 | bytes 8847872 | tf_op jit(solution)/shard_map/dot_general | solution.py:119
  80.9 5.7 %fusion.4 = f32[128,4096]{1,0:T(8,128)S(1)} fusion(bf16[1,2,4096,896]{3,2,1,0:T(8,128)(2,1)} %param.18, f32[128,896]{1,0:T(8,128)S(1)} %fusion.65, f32[128,896]{1,0:T(8,128)S(1)} %copy-done.4), kind=kOutput, calls=%fused_computation.4 | convolution fusion | flops 940212224 | bytes 10354688 | tf_op jit(solution)/shard_map/dot_general | solution.py:126
  86.6 2.4 %fusion.62 = f32[128,896]{1,0:T(8,128)S(1)} fusion(bf16[128,4096]{1,0:T(8,128)(2,1)S(1)} %bitcast.184, bf16[1,2,896,4096]{3,2,1,0:T(8,128)(2,1)S(1)} %bitcast.192, f32[128]{0:T(128)S(1)} %reshape.400), kind=kOutput, calls=%fused_computation.54 | convolution fusion | flops 939638784 | bytes 8847872 | tf_op jit(solution)/shard_map/dot_general | solution.py:119
  89.0 5.5 %fusion.16 = f32[128,4096]{1,0:T(8,128)S(1)} fusion(bf16[1,2,4096,896]{3,2,1,0:T(8,128)(2,1)} %param.18, f32[128,896]{1,0:T(8,128)S(1)} %fusion.62, f32[128,896]{1,0:T(8,128)S(1)} %fusion.22), kind=kOutput, calls=%fused_computation.16 | convolution fusion | flops 940212224 | bytes 10354688 | tf_op jit(solution)/shard_map/dot_general | solution.py:126
  94.5 5.6 %fusion.51 = bf16[128,4096]{1,0:T(8,128)(2,1)S(1)} fusion(f32[128,4096]{1,0:T(8,128)S(1)} %fusion.4, bf16[1,2,4096,896]{3,2,1,0:T(8,128)(2,1)} %param.17, f32[128,896]{1,0:T(8,128)S(1)} %copy-done.4, f32[128,896]{1,0:T(8,128)S(1)} %fusion.65, f32[128,896]{1,0:T(8,128)S(1)} %fusion.6), kind=kOutput, calls=%fused_computation.41 | convolution fusion | flops 941719552 | bytes 11862016 | tf_op jit(solution)/shard_map/dot_general | solution.py:124
  100.5 1.5 collective-permute-start.1
  102.1 5.6 %fusion.57 = bf16[128,4096]{1,0:T(8,128)(2,1)S(1)} fusion(f32[128,4096]{1,0:T(8,128)S(1)} %fusion.16, bf16[1,2,4096,896]{3,2,1,0:T(8,128)(2,1)} %param.17, f32[128,896]{1,0:T(8,128)S(1)} %fusion.22, f32[128,896]{1,0:T(8,128)S(1)} %fusion.62, f32[128,896]{1,0:T(8,128)S(1)} %fusion.18), kind=kOutput, calls=%fused_computation.43 | convolution fusion | flops 941719552 | bytes 11862016 | tf_op jit(solution)/shard_map/dot_general | solution.py:124
  107.7 7.0 %collective-permute-done.1 = bf16[2,32,4096]{2,1,0:T(8,128)(2,1)S(1)} collective-permute-done((bf16[2,32,4096]{2,1,0:T(8,128)(2,1)S(1)}, bf16[2,32,4096]{2,1,0:T(8,128)(2,1)S(1)}, u32[]{:S(2)}, u32[]{:S(2)}) %collective-permute-start.1) | collective-permute-done | bytes 524320 | tf_op jit(solution)/shard_map/ppermute | solution.py:50
  114.9 1.4 collective-permute-start.2
  116.5 6.1 %collective-permute-done.2 = bf16[32,4096]{1,0:T(8,128)(2,1)S(1)} collective-permute-done((bf16[32,4096]{1,0:T(8,128)(2,1)S(1)}, bf16[32,4096]{1,0:T(8,128)(2,1)S(1)}, u32[]{:S(2)}, u32[]{:S(2)}) %collective-permute-start.2) | collective-permute-done | bytes 262176 | tf_op jit(solution)/shard_map/ppermute | solution.py:60
  124.2 4.2 %collective-permute-done.3 = s32[128,2]{0,1:T(2,128)S(1)} collective-permute-done((s32[128,2]{0,1:T(2,128)S(1)}, s32[128,2]{0,1:T(2,128)S(1)}, u32[]{:S(2)}, u32[]{:S(2)}) %collective-permute-start.3) | collective-permute-done | bytes 1056 | tf_op jit(solution)/shard_map/ppermute | solution.py:14
  128.8 1.5 collective-permute-start.5
  131.1 11.0 %collective-permute-done.5 = bf16[2,32,4096]{2,1,0:T(8,128)(2,1)} collective-permute-done((bf16[2,32,4096]{2,1,0:T(8,128)(2,1)S(1)}, bf16[2,32,4096]{2,1,0:T(8,128)(2,1)}, u32[]{:S(2)}, u32[]{:S(2)}) %collective-permute-start.5) | collective-permute-done | bytes 524320 | tf_op jit(solution)/shard_map/ppermute | solution.py:50
  146.0 2.0 %fusion.60 = bf16[1,128,4096]{2,1,0:T(8,128)(2,1)} fusion(f32[32,4096]{1,0:T(8,128)S(1)} %convert_add_fusion, pred[16,128]{1,0:T(8,128)(4,1)S(1)} %get-tuple-element.59, pred[16,128]{1,0:T(8,128)(4,1)S(1)} %get-tuple-element.58), kind=kOutput, calls=%fused_computation.46 | convolution fusion | flops 201854976 | bytes 1576960 | tf_op jit(solution)/shard_map/dot_general | solution.py:76
  148.0 7.4 %collective-permute-done.7 = bf16[32,4096]{1,0:T(8,128)(2,1)S(1)} collective-permute-done((bf16[32,4096]{1,0:T(8,128)(2,1)S(1)}, bf16[32,4096]{1,0:T(8,128)(2,1)S(1)}, u32[]{:S(2)}, u32[]{:S(2)}) %collective-permute-start.7) | collective-permute-done | bytes 262176 | tf_op jit(solution)/shard_map/ppermute | solution.py:71
  155.4 2.9 %collective-permute-done.6 = bf16[32,4096]{1,0:T(8,128)(2,1)S(1)} collective-permute-done((bf16[32,4096]{1,0:T(8,128)(2,1)S(1)}, bf16[32,4096]{1,0:T(8,128)(2,1)S(1)}, u32[]{:S(2)}, u32[]{:S(2)}) %collective-permute-start.6) | collective-permute-done | bytes 262176 | tf_op jit(solution)/shard_map/ppermute | solution.py:70
  158.3 2.0 %fusion.61 = bf16[1,128,4096]{2,1,0:T(8,128)(2,1)} fusion(bf16[32,4096]{1,0:T(8,128)(2,1)S(1)} %collective-permute-done.7, bf16[32,4096]{1,0:T(8,128)(2,1)S(1)} %collective-permute-done.6, pred[16,128]{1,0:T(8,128)(4,1)S(1)} %get-tuple-element.61, pred[16,128]{1,0:T(8,128)(4,1)S(1)} %get-tuple-element.60), kind=kOutput, calls=%fused_computation.47 | convolution fusion | flops 202248192 | bytes 1576960 | tf_op jit(solution)/shard_map/dot_general | solution.py:76
  (83 shorter events, 17.7 us)
Async XLA Ops:
  7.2 2.4 %copy-start = (bf16[1,128,4096]{2,1,0:T(8,128)(2,1)S(1)}, bf16[1,128,4096]{2,1,0:T(8,128)(2,1)}, u32[]{:S(2)}) copy-start(bf16[1,128,4096]{2,1,0:T(8,128)(2,1)} %param.16) | copy-start | bytes 3145732
  7.2 45.1 %all-gather.2.cloned.1.call-start = ((), (), s32[]{:S(2)}) async-start(), calls=%async_computation | async-start | bytes 4792320 | tf_op jit(solution)/shard_map/all_gather | solution.py:100
  52.3 9.1 %copy-start.3 = (bf16[1,2,4096,896]{3,2,1,0:T(8,128)(2,1)S(1)}, bf16[1,2,4096,896]{3,2,1,0:T(8,128)(2,1)}, u32[]{:S(2)}) copy-start(bf16[1,2,4096,896]{3,2,1,0:T(8,128)(2,1)} %param.17) | copy-start | bytes 44040196
  53.2 10.3 %slice-start.4 = ((s8[14680064]{0:T(1024)(128)(4,1)}), s8[4194304]{0:T(1024)(128)(4,1)S(1)}, s32[]{:S(2)}) async-start(s8[14680064]{0:T(1024)(128)(4,1)} %bitcast.193), calls=%async_computation.5 | async-start | bytes 8388608
  53.2 10.3 %slice-start.5 = ((s8[14680064]{0:T(1024)(128)(4,1)}), s8[4194304]{0:T(1024)(128)(4,1)S(1)}, s32[]{:S(2)}) async-start(s8[14680064]{0:T(1024)(128)(4,1)} %bitcast.193), calls=%async_computation.6 | async-start | bytes 8388608
  56.2 8.7 %slice-start.6 = ((s8[14680064]{0:T(1024)(128)(4,1)}), s8[4194304]{0:T(1024)(128)(4,1)S(1)}, s32[]{:S(2)}) async-start(s8[14680064]{0:T(1024)(128)(4,1)} %bitcast.193), calls=%async_computation.7 | async-start | bytes 8388608
  61.4 4.0 %slice-start.7 = ((s8[14680064]{0:T(1024)(128)(4,1)}), s8[2097152]{0:T(1024)(128)(4,1)S(1)}, s32[]{:S(2)}) async-start(s8[14680064]{0:T(1024)(128)(4,1)} %bitcast.193), calls=%async_computation.8 | async-start | bytes 4194304
  68.5 9.9 %slice-start = ((s8[14680064]{0:T(1024)(128)(4,1)}), s8[4194304]{0:T(1024)(128)(4,1)S(1)}, s32[]{:S(2)}) async-start(s8[14680064]{0:T(1024)(128)(4,1)} %bitcast.191), calls=%async_computation.1 | async-start | bytes 8388608
  68.5 9.9 %slice-start.1 = ((s8[14680064]{0:T(1024)(128)(4,1)}), s8[4194304]{0:T(1024)(128)(4,1)S(1)}, s32[]{:S(2)}) async-start(s8[14680064]{0:T(1024)(128)(4,1)} %bitcast.191), calls=%async_computation.2 | async-start | bytes 8388608
  73.2 5.2 %slice-start.2 = ((s8[14680064]{0:T(1024)(128)(4,1)}), s8[4194304]{0:T(1024)(128)(4,1)S(1)}, s32[]{:S(2)}) async-start(s8[14680064]{0:T(1024)(128)(4,1)} %bitcast.191), calls=%async_computation.3 | async-start | bytes 8388608
  73.2 5.2 %slice-start.3 = ((s8[14680064]{0:T(1024)(128)(4,1)}), s8[2097152]{0:T(1024)(128)(4,1)S(1)}, s32[]{:S(2)}) async-start(s8[14680064]{0:T(1024)(128)(4,1)} %bitcast.191), calls=%async_computation.4 | async-start | bytes 4194304
  77.9 2.9 %copy-start.4 = (f32[128,896]{1,0:T(8,128)S(1)}, f32[128,896]{1,0:T(8,128)}, u32[]{:S(2)}) copy-start(f32[128,896]{1,0:T(8,128)} %fusion.10) | copy-start | bytes 1376260
  78.1 22.0 %collective-permute-start = (bf16[4,32,4096]{2,1,0:T(8,128)(2,1)S(1)}, bf16[4,32,4096]{2,1,0:T(8,128)(2,1)S(1)}, u32[]{:S(2)}, u32[]{:S(2)}) collective-permute-start(bf16[4,32,4096]{2,1,0:T(8,128)(2,1)S(1)} %select_bitcast_fusion.1), channel_id=1, source_target_pairs={{0,1},{1,0},{2,3},{3,2},{4,5},{5,4},{6,7},{7,6},{8,9},{9,8},{10,11... | collective-permute-start | bytes 3145736 | tf_op jit(solution)/shard_map/ppermute | solution.py:50
  100.5 14.1 %collective-permute-start.1 = (bf16[2,32,4096]{2,1,0:T(8,128)(2,1)S(1)}, bf16[2,32,4096]{2,1,0:T(8,128)(2,1)S(1)}, u32[]{:S(2)}, u32[]{:S(2)}) collective-permute-start(bf16[2,32,4096]{2,1,0:T(8,128)(2,1)S(1)} %select_bitcast_fusion.3), channel_id=1, source_target_pairs={{0,2},{1,3},{2,0},{3,1},{4,6},{5,7},{6,4},{7,5},{8,10},{9,11},{10,... | collective-permute-start | bytes 1572872 | tf_op jit(solution)/shard_map/ppermute | solution.py:50
  107.7 15.2 %copy-start.2 = (s32[1,128,2]{1,2,0:T(2,128)S(1)}, s32[1,128,2]{1,2,0:T(2,128)}, u32[]{:S(2)}) copy-start(s32[1,128,2]{1,2,0:T(2,128)} %param.15) | copy-start | bytes 3076
  114.9 7.7 %collective-permute-start.2 = (bf16[32,4096]{1,0:T(8,128)(2,1)S(1)}, bf16[32,4096]{1,0:T(8,128)(2,1)S(1)}, u32[]{:S(2)}, u32[]{:S(2)}) collective-permute-start(bf16[32,4096]{1,0:T(8,128)(2,1)S(1)} %select_bitcast_fusion.6), channel_id=1, source_target_pairs={{0,4},{1,5},{2,6},{3,7},{4,0},{5,1},{6,2},{7,3},{8,12},{9,13},{10,... | collective-permute-start | bytes 786440 | tf_op jit(solution)/shard_map/ppermute | solution.py:60
  116.3 44.0 %copy-start.1 = (bf16[1,128,4096]{2,1,0:T(8,128)(2,1)S(1)}, bf16[1,128,4096]{2,1,0:T(8,128)(2,1)}, u32[]{:S(2)}) copy-start(bf16[1,128,4096]{2,1,0:T(8,128)(2,1)} %param.16) | copy-start | bytes 3145732
  122.8 5.6 %collective-permute-start.4 = (bf16[4,32,4096]{2,1,0:T(8,128)(2,1)S(1)}, bf16[4,32,4096]{2,1,0:T(8,128)(2,1)S(1)}, u32[]{:S(2)}, u32[]{:S(2)}) collective-permute-start(bf16[4,32,4096]{2,1,0:T(8,128)(2,1)S(1)} %select_bitcast_fusion), channel_id=1, source_target_pairs={{0,1},{1,0},{2,3},{3,2},{4,5},{5,4},{6,7},{7,6},{8,9},{9,8},{10,11... | collective-permute-start | bytes 3145736 | tf_op jit(solution)/shard_map/ppermute | solution.py:50
  122.9 5.5 %collective-permute-start.3 = (s32[128,2]{0,1:T(2,128)S(1)}, s32[128,2]{0,1:T(2,128)S(1)}, u32[]{:S(2)}, u32[]{:S(2)}) collective-permute-start(s32[128,2]{0,1:T(2,128)S(1)} %bitcast.190), channel_id=1, source_target_pairs={{8,0},{16,8},{24,16},{9,1},{17,9},{25,17},{10,2},{18,10},{26,18},{... | collective-permute-start | bytes 3080 | tf_op jit(solution)/shard_map/ppermute | solution.py:14
  128.8 13.3 %collective-permute-start.5 = (bf16[2,32,4096]{2,1,0:T(8,128)(2,1)S(1)}, bf16[2,32,4096]{2,1,0:T(8,128)(2,1)}, u32[]{:S(2)}, u32[]{:S(2)}) collective-permute-start(bf16[2,32,4096]{2,1,0:T(8,128)(2,1)S(1)} %select_bitcast_fusion.2), channel_id=1, source_target_pairs={{0,2},{1,3},{2,0},{3,1},{4,6},{5,7},{6,4},{7,5},{8,10},{9,11},{10,... | collective-permute-start | bytes 1572872 | tf_op jit(solution)/shard_map/ppermute | solution.py:50
  143.4 12.0 %collective-permute-start.7 = (bf16[32,4096]{1,0:T(8,128)(2,1)S(1)}, bf16[32,4096]{1,0:T(8,128)(2,1)S(1)}, u32[]{:S(2)}, u32[]{:S(2)}) collective-permute-start(bf16[32,4096]{1,0:T(8,128)(2,1)S(1)} %get-tuple-element.55), channel_id=1, source_target_pairs={{8,4},{9,5},{10,6},{11,7},{12,0},{13,1},{14,2},{15,3},{16,12},{17,... | collective-permute-start | bytes 786440 | tf_op jit(solution)/shard_map/ppermute | solution.py:71
  144.7 13.6 %collective-permute-start.6 = (bf16[32,4096]{1,0:T(8,128)(2,1)S(1)}, bf16[32,4096]{1,0:T(8,128)(2,1)S(1)}, u32[]{:S(2)}, u32[]{:S(2)}) collective-permute-start(bf16[32,4096]{1,0:T(8,128)(2,1)S(1)} %get-tuple-element.54), channel_id=1, source_target_pairs={{8,0},{9,1},{10,2},{11,3},{12,4},{13,5},{14,6},{15,7},{16,8},{17,9... | collective-permute-start | bytes 786440 | tf_op jit(solution)/shard_map/ppermute | solution.py:70
Sparse Core Ops, SparseCore 0:
  12.6 39.6 all-gather.1

commit v7 on v6

--- a/solution.py
+++ b/solution.py
@@ -1,6 +1,8 @@
 import jax
 import jax.numpy as jnp
 from jax import lax
+from jax.experimental import pallas as pl
+from jax.experimental.pallas import tpu as pltpu
 from jax.sharding import PartitionSpec as P
 
 E_WIN = 2
@@ -82,6 +84,75 @@
     ).astype(jnp.bfloat16)
 
 
+def _expert_body(x_ref, g_ref, w_ref, wg_ref, wu_ref, wd_ref, out_ref, grad_ref, out_acc, grad_acc):
+    step = pl.program_id(1)
+    rows = x_ref.shape[0] * x_ref.shape[1]
+    width = x_ref.shape[2]
+
+    @pl.when(step == 0)
+    def _():
+        out_acc[...] = jnp.zeros_like(out_acc)
+        grad_acc[...] = jnp.zeros_like(grad_acc)
+
+    x = x_ref[...].reshape(rows, width)
+    g = g_ref[...].reshape(rows, width)
+    gate_w = w_ref[...].reshape(rows, w_ref.shape[2])[:, 0:1].astype(jnp.float32)
+    wg = wg_ref[...]
+    wu = wu_ref[...]
+    wd = wd_ref[...]
+    pre_gate = jnp.dot(x, wg, preferred_element_type=jnp.float32)
+    pre_up = jnp.dot(x, wu, preferred_element_type=jnp.float32)
+    d_hidden = gate_w * lax.dot_general(g, wd, (((1,), (1,)), ((), ())), preferred_element_type=jnp.float32)
+    sigma = jax.nn.sigmoid(pre_gate)
+    activated = pre_gate * sigma
+    slopes = sigma * (1.0 + pre_gate * (1.0 - sigma))
+    hidden = (activated * pre_up).astype(jnp.bfloat16)
+    out_acc[...] += jnp.dot(hidden, wd, preferred_element_type=jnp.float32)
+    d_gate = (d_hidden * pre_up * slopes).astype(jnp.bfloat16)
+    d_up = (d_hidden * activated).astype(jnp.bfloat16)
+    grad_acc[...] += lax.dot_general(
+        d_gate, wg, (((1,), (1,)), ((), ())), preferred_element_type=jnp.float32
+    ) + lax.dot_general(d_up, wu, (((1,), (1,)), ((), ())), preferred_element_type=jnp.float32)
+
+    @pl.when(step == pl.num_programs(1) - 1)
+    def _():
+        out_ref[...] = (gate_w * out_acc[...]).astype(out_ref.dtype).reshape(out_ref.shape)
+        grad_ref[...] = grad_acc[...].astype(grad_ref.dtype).reshape(grad_ref.shape)
+
+
+def expert_pass(gathered, gate_mats, up_mats, down_mats):
+    n, experts, most, packed_width = gathered.shape
+    width = gate_mats.shape[1]
+    shard = gate_mats.shape[2]
+    tile = 128 if shard % 128 == 0 else shard
+    steps = shard // tile
+    rows = n * most
+    return pl.pallas_call(
+        _expert_body,
+        grid=(experts, steps),
+        in_specs=[
+            pl.BlockSpec((n, None, most, width), lambda e, f: (0, e, 0, 0)),
+            pl.BlockSpec((n, None, most, width), lambda e, f: (0, e, 0, 1)),
+            pl.BlockSpec((n, None, most, TAIL), lambda e, f: (0, e, 0, 2 * width // TAIL)),
+            pl.BlockSpec((None, width, tile), lambda e, f: (e, 0, f)),
+            pl.BlockSpec((None, width, tile), lambda e, f: (e, 0, f)),
+            pl.BlockSpec((None, tile, width), lambda e, f: (e, f, 0)),
+        ],
+        out_specs=[
+            pl.BlockSpec((n, None, most, width), lambda e, f: (0, e, 0, 0)),
+            pl.BlockSpec((n, None, most, width), lambda e, f: (0, e, 0, 0)),
+        ],
+        out_shape=[
+            jax.ShapeDtypeStruct((n, experts, most, width), jnp.bfloat16),
+            jax.ShapeDtypeStruct((n, experts, most, width), jnp.bfloat16),
+        ],
+        scratch_shapes=[pltpu.VMEM((rows, width), jnp.float32), pltpu.VMEM((rows, width), jnp.float32)],
+        compiler_params=pltpu.CompilerParams(
+            dimension_semantics=("arbitrary", "arbitrary"), vmem_limit_bytes=100 * 1024 * 1024
+        ),
+    )(gathered, gathered, gathered, gate_mats, up_mats, down_mats)
+
+
 def per_device(tokens, gate_vals, expert_ids, grad_out, w_gate, w_up, w_down):
     local_rows = tokens[0]
     local_grads = grad_out[0]
@@ -98,36 +169,9 @@
         [pick_rows(select, local_rows), pick_rows(select, local_grads), weight_cols], axis=1
     )
     gathered = lax.all_gather(packed, "et", axis=0, tiled=True).reshape(n, E_WIN, MOST, 2 * width + TAIL)
-    outs = []
-    stored = []
-    for expert in range(E_WIN):
-        rows = gathered[:, expert, :, :width].reshape(n * MOST, width)
-        gate_w = gathered[:, expert, :, 2 * width].reshape(n * MOST, 1).astype(jnp.float32)
-        pre_gate = jnp.dot(rows, gate_mats[expert], preferred_element_type=jnp.float32)
-        pre_up = jnp.dot(rows, up_mats[expert], preferred_element_type=jnp.float32)
-        activated, slopes = silu_parts(pre_gate)
-        hidden = (activated * pre_up).astype(jnp.bfloat16)
-        out_e = gate_w * jnp.dot(hidden, down_mats[expert], preferred_element_type=jnp.float32)
-        outs.append(out_e.astype(jnp.bfloat16).reshape(n, MOST, width))
-        stored.append((gate_w, pre_up, activated, slopes))
-    out_parts = jnp.stack(outs, axis=1).reshape(n, E_WIN * MOST, width)
-    out_sums = reduce_to_owner(out_parts)
-    grad_outs = []
-    for expert in range(E_WIN):
-        gate_w, pre_up, activated, slopes = stored[expert]
-        grad_rows = gathered[:, expert, :, width : 2 * width].reshape(n * MOST, width)
-        d_hidden = gate_w * lax.dot_general(
-            grad_rows, down_mats[expert], (((1,), (1,)), ((), ())), preferred_element_type=jnp.float32
-        )
-        d_gate = (d_hidden * pre_up * slopes).astype(jnp.bfloat16)
-        d_up = (d_hidden * activated).astype(jnp.bfloat16)
-        grad_e = lax.dot_general(
-            d_gate, gate_mats[expert], (((1,), (1,)), ((), ())), preferred_element_type=jnp.float32
-        ) + lax.dot_general(d_up, up_mats[expert], (((1,), (1,)), ((), ())), preferred_element_type=jnp.float32)
-        grad_outs.append(grad_e.astype(jnp.bfloat16).reshape(n, MOST, width))
-    grad_parts = jnp.stack(grad_outs, axis=1).reshape(n, E_WIN * MOST, width)
-    out_sums, grad_parts = lax.optimization_barrier((out_sums, grad_parts))
-    received = unpack(reduce_to_previous(grad_parts), next_select)
+    out_parts, grad_parts = expert_pass(gathered, gate_mats, up_mats, down_mats)
+    out_sums = reduce_to_owner(out_parts.reshape(n, E_WIN * MOST, width))
+    received = unpack(reduce_to_previous(grad_parts.reshape(n, E_WIN * MOST, width)), next_select)
     out_share = unpack(out_sums, select)
     return (out_share[None], received[None])
 

time: 168 us -> 141 us (0.84)
  matrix products: 52 us -> 5.76 us
  Pallas kernels: 0 us -> 32.6 us
  waiting for transfers between devices: 78.3 us -> 71.4 us
  local copies, waits for them, and re-layouts: 6.88 us -> 0.58 us
    dot_general x12 -> x0, matrix products: 46.3 us -> none  [the longest x2 11.2 us: per_device(): lax.dot_general(d_up, up_mats[expert], (((1,), (1,)), ((), ())), preferre...]
    pallas_call x0 -> x1, Pallas kernels: none -> 32.6 us  [expert_pass(): pl.pallas_call(_expert_body, grid=(experts, steps), in_specs=[pl.BlockSpe...]
    all_gather x1, waiting for transfers between devices: 39.7 us -> 32.8 us  [per_device(): lax.all_gather(packed, 'et', axis=0, tiled=True)]
    ppermute x1, waiting for transfers between devices: 6.13 us -> 0.01 us  [reduce_to_owner(): got = lax.ppermute(give, 'et', [(i, i ^ bit) for i in range(n)])]
    ppermute x4, waiting for transfers between devices: 18 us -> 22.3 us  [halve_over_et(): got = lax.ppermute(give, 'et', [(i, i ^ bit) for i in range(n)])]
    slice x2 -> x0, local copies, waits for them, and re-layouts: 3.88 us -> none  [the longest x1 2.95 us: per_device(): grad_rows = gathered[:, expert, :, width:2 * width].reshape(n * MOST, width)]
    select_n x4, other arithmetic: 0.35 us -> 2.69 us  [halve_over_et(): give = jnp.take(halves, 1 - side, axis=1)]
    unnamed x28 -> x20, local copies, waits for them, and re-layouts: 2.29 us -> 0.05 us
  transfers between devices with their start and end apart: 9 -> 9, of which waited for: 7 -> 7; matrix products, arithmetic and copies ran while one was open for 18% -> 3% of each run, Pallas kernels for 0% -> 0%
where the time goes in v7:
time: 141 us
  waiting for transfers between devices  71.4 us (51%)
  Pallas kernels  32.6 us (23%)
  between operations  14.4 us (10%)
  starting transfers between devices  8.3 us (6%)
  other arithmetic  7.98 us (6%)
  matrix products  5.76 us (4%)
    all_gather x1, waiting for transfers between devices, per_device(): lax.all_gather(packed, 'et', axis=0, tiled=True)  32.8 us
    pallas_call x1, Pallas kernels, expert_pass(): pl.pallas_call(_expert_body, grid=(experts, steps), in_specs=[pl.BlockSpe...  32.6 us
    ppermute x4, waiting for transfers between devices, halve_over_et(): got = lax.ppermute(give, 'et', [(i, i ^ bit) for i in range(n)])  22.3 us
    ppermute x1, waiting for transfers between devices, reduce_to_previous(): second = lax.ppermute(give, ('pipe', 'et'), to_other)  7.38 us
    ppermute x1, waiting for transfers between devices, shifted(): lax.ppermute(value, axis, [(source, source + steps) for source in range(f...  5.06 us
    dot_general x2, matrix products, unpack(): lax.dot_general(select.astype(jnp.float32), slot_sums, (((0,), (0,)), (()...  4 us
    ppermute x1, waiting for transfers between devices, reduce_to_previous(): first = lax.ppermute(keep, ('pipe', 'et'), to_same)  3.83 us
    ppermute x4, starting transfers between devices, halve_over_et(): got = lax.ppermute(give, 'et', [(i, i ^ bit) for i in range(n)])  3 us
  transfers between devices with their start and end apart: 9, of which 7 were waited for; matrix products, arithmetic and copies ran while one was open for 3% of the time, Pallas kernels for 0%

profile of v7, /device:TPU:0, one launch (start us, length us, event | category | flops | bytes accessed | tf_op | source)
XLA Modules:
  0.0 141.0 jit_solution(5823656623864702912)
XLA Ops:
  7.2 0.8 fusion.29
  8.0 0.7 fusion.27
  9.6 1.5 %convolution_convert_fusion.2 = bf16[32,4096]{1,0:T(8,128)(2,1)S(1)} fusion(bf16[1,128,4096]{2,1,0:T(8,128)(2,1)} %param.16, pred[16,128]{1,0:T(8,128)(4,1)S(1)} %get-tuple-element.53, pred[16,128]{1,0:T(8,128)(4,1)S(1)} %get-tuple-element.52), kind=kOutput, calls=%fused_computation.4 | convolution fusion | flops 33689600 | bytes 1314816 | tf_op jit(solution)/shard_map/dot_general | solution.py:39
  11.7 0.8 pad_maximum_fusion
  12.5 1.3 collective-permute-start.3
  13.9 5.1 %collective-permute-done.3 = s32[128,2]{0,1:T(2,128)S(1)} collective-permute-done((s32[128,2]{0,1:T(2,128)S(1)}, s32[128,2]{0,1:T(2,128)S(1)}, u32[]{:S(2)}, u32[]{:S(2)}) %collective-permute-start.3) | collective-permute-done | bytes 1056 | tf_op jit(solution)/shard_map/ppermute | solution.py:16
  19.0 0.6 compare_reduce_fusion.1
  19.6 32.8 %all-gather.2.cloned.1.call-done = bf16[256,8320]{1,0:T(8,128)(2,1)} async-done(((bf16[32,8320]{1,0:T(8,128)(2,1)}), bf16[256,8320]{1,0:T(8,128)(2,1)}) %all-gather.2.cloned.1.call-update) | async-done | bytes 4259856 | tf_op jit(solution)/shard_map/all_gather | solution.py:171
  52.4 32.6 %shard_map.86 = (bf16[8,2,16,4096]{3,2,1,0:T(8,128)(2,1)}, bf16[8,2,16,4096]{3,2,1,0:T(8,128)(2,1)}) custom-call(bf16[8,2,16,8320]{3,2,1,0:T(8,128)(2,1)} %bitcast.94, bf16[8,2,16,8320]{3,2,1,0:T(8,128)(2,1)} %bitcast.95, bf16[8,2,16,8320]{3,2,1,0:T(8,128)(2,1)} %bitcast.96, bf16[2,4096,896]{2,1,0:T(8,128)(2,1)} %bitcast.97, bf16[2,4096,896]{2,1,0:T(8,128)(2,1)} %bitcast.98, ...), custom_call_target="tpu_custom_call" | custom-call | tf_op jit(solution)/shard_map/pallas_call | solution.py:130
  85.0 2.5 %select_bitcast_fusion.1 = bf16[4,32,4096]{2,1,0:T(8,128)(2,1)} fusion(bf16[4,2,32,4096]{3,2,1,0:T(8,128)(2,1)} %bitcast.106, s32[]{:T(128)S(6)} %select_n.113, pred[]{:T(512)S(6)} %and.107), kind=kLoop, calls=%fused_computation.15 | loop fusion | flops 524288 | bytes 2097157 | tf_op jit(solution)/shard_map/jit(_take)/select_n | solution.py:51
  88.6 0.3 collective-permute-start.4
  88.9 1.4 collective-permute-done
  90.3 0.3 add_convert_fusion.1
  90.7 1.5 %collective-permute-start.1 = (bf16[2,32,4096]{2,1,0:T(8,128)(2,1)S(1)}, bf16[2,32,4096]{2,1,0:T(8,128)(2,1)S(1)}, u32[]{:S(2)}, u32[]{:S(2)}) collective-permute-start(bf16[2,32,4096]{2,1,0:T(8,128)(2,1)S(1)} %select_bitcast_fusion.3), channel_id=1, source_target_pairs={{0,2},{1,3},{2,0},{3,1},{4,6},{5,7},{6,4},{7,5},{8,10},{9,11},{10,... | collective-permute-start | bytes 1572872 | tf_op jit(solution)/shard_map/ppermute | solution.py:52
  92.6 0.9 collective-permute-start.5
  93.5 12.0 %collective-permute-done.1 = bf16[2,32,4096]{2,1,0:T(8,128)(2,1)S(1)} collective-permute-done((bf16[2,32,4096]{2,1,0:T(8,128)(2,1)S(1)}, bf16[2,32,4096]{2,1,0:T(8,128)(2,1)S(1)}, u32[]{:S(2)}, u32[]{:S(2)}) %collective-permute-start.1) | collective-permute-done | bytes 524320 | tf_op jit(solution)/shard_map/ppermute | solution.py:52
  105.7 1.4 collective-permute-start.2
  107.1 9.0 %collective-permute-done.5 = bf16[2,32,4096]{2,1,0:T(8,128)(2,1)S(1)} collective-permute-done((bf16[2,32,4096]{2,1,0:T(8,128)(2,1)S(1)}, bf16[2,32,4096]{2,1,0:T(8,128)(2,1)S(1)}, u32[]{:S(2)}, u32[]{:S(2)}) %collective-permute-start.5) | collective-permute-done | bytes 524320 | tf_op jit(solution)/shard_map/ppermute | solution.py:52
  116.3 1.3 collective-permute-start.7
  117.6 1.3 collective-permute-start.6
  119.0 2.0 %fusion = bf16[1,128,4096]{2,1,0:T(8,128)(2,1)} fusion(bf16[32,4096]{1,0:T(8,128)(2,1)S(1)} %collective-permute-done.2, bf16[2,32,4096]{2,1,0:T(8,128)(2,1)S(1)} %add_convert_fusion.3, s32[]{:T(128)S(6)} %select_n.119, pred[]{:T(512)S(6)} %and.110, pred[16,128]{1,0:T(8,128)(4,1)S(1)} %copy-done.6, pred[16,128]{1,0:T(8,128)(4,1)S(1)} %copy-done.4), kind=kOutput, calls=%fused_computation.2 | convolution fusion | flops 202379264 | bytes 1576965 | tf_op jit(solution)/shard_map/dot_general | solution.py:78
  121.0 7.4 %collective-permute-done.7 = bf16[32,4096]{1,0:T(8,128)(2,1)S(1)} collective-permute-done((bf16[32,4096]{1,0:T(8,128)(2,1)S(1)}, bf16[32,4096]{1,0:T(8,128)(2,1)S(1)}, u32[]{:S(2)}, u32[]{:S(2)}) %collective-permute-start.7) | collective-permute-done | bytes 262176 | tf_op jit(solution)/shard_map/ppermute | solution.py:73
  128.3 3.8 %collective-permute-done.6 = bf16[32,4096]{1,0:T(8,128)(2,1)S(1)} collective-permute-done((bf16[32,4096]{1,0:T(8,128)(2,1)S(1)}, bf16[32,4096]{1,0:T(8,128)(2,1)S(1)}, u32[]{:S(2)}, u32[]{:S(2)}) %collective-permute-start.6) | collective-permute-done | bytes 262176 | tf_op jit(solution)/shard_map/ppermute | solution.py:72
  132.2 2.0 %fusion.1 = bf16[1,128,4096]{2,1,0:T(8,128)(2,1)} fusion(bf16[32,4096]{1,0:T(8,128)(2,1)S(1)} %collective-permute-done.7, bf16[32,4096]{1,0:T(8,128)(2,1)S(1)} %collective-permute-done.6, pred[16,128]{1,0:T(8,128)(4,1)S(1)} %get-tuple-element.55, pred[16,128]{1,0:T(8,128)(4,1)S(1)} %get-tuple-element.54), kind=kOutput, calls=%fused_computation.3 | convolution fusion | flops 202248192 | bytes 1576960 | tf_op jit(solution)/shard_map/dot_general | solution.py:78
  (55 shorter events, 3.4 us)
Async XLA Ops:
  7.2 3.9 %copy-start.2 = (bf16[1,128,4096]{2,1,0:T(8,128)(2,1)S(1)}, bf16[1,128,4096]{2,1,0:T(8,128)(2,1)}, u32[]{:S(2)}) copy-start(bf16[1,128,4096]{2,1,0:T(8,128)(2,1)} %param.13) | copy-start | bytes 3145732
  7.2 45.2 %all-gather.2.cloned.1.call-start = ((), (), s32[]{:S(2)}) async-start(), calls=%async_computation | async-start | bytes 4792320 | tf_op jit(solution)/shard_map/all_gather | solution.py:171
  9.5 1.8 %copy-start.3 = (pred[16,128]{1,0:T(8,128)(4,1)}, pred[16,128]{1,0:T(8,128)(4,1)S(1)}, u32[]{:S(2)}) copy-start(pred[16,128]{1,0:T(8,128)(4,1)S(1)} %get-tuple-element.52) | copy-start | bytes 6148
  9.5 1.8 %copy-start.5 = (pred[16,128]{1,0:T(8,128)(4,1)}, pred[16,128]{1,0:T(8,128)(4,1)S(1)}, u32[]{:S(2)}) copy-start(pred[16,128]{1,0:T(8,128)(4,1)S(1)} %get-tuple-element.53) | copy-start | bytes 6148
  9.6 3.0 %copy-start.7 = (s32[1,128,2]{1,2,0:T(2,128)S(1)}, s32[1,128,2]{1,2,0:T(2,128)}, u32[]{:S(2)}) copy-start(s32[1,128,2]{1,2,0:T(2,128)} %param.15) | copy-start | bytes 3076
  12.5 6.5 %collective-permute-start.3 = (s32[128,2]{0,1:T(2,128)S(1)}, s32[128,2]{0,1:T(2,128)S(1)}, u32[]{:S(2)}, u32[]{:S(2)}) collective-permute-start(s32[128,2]{0,1:T(2,128)S(1)} %bitcast.108), channel_id=1, source_target_pairs={{8,0},{16,8},{24,16},{9,1},{17,9},{25,17},{10,2},{18,10},{26,18},{... | collective-permute-start | bytes 3080 | tf_op jit(solution)/shard_map/ppermute | solution.py:16
  85.0 2.7 %copy-start.8 = (pred[128]{0:T(512)(128)(4,1)S(1)}, pred[128]{0:T(512)(128)(4,1)}, u32[]{:S(2)}) copy-start(pred[128]{0:T(512)(128)(4,1)} %get-tuple-element.44) | copy-start | bytes 388
  85.0 3.0 %copy-start.9 = (pred[128]{0:T(512)(128)(4,1)S(1)}, pred[128]{0:T(512)(128)(4,1)}, u32[]{:S(2)}) copy-start(pred[128]{0:T(512)(128)(4,1)} %get-tuple-element.45) | copy-start | bytes 388
  85.0 3.5 %copy-start = (bf16[8,2,16,4096]{3,2,1,0:T(8,128)(2,1)S(1)}, bf16[8,2,16,4096]{3,2,1,0:T(8,128)(2,1)}, u32[]{:S(2)}) copy-start(bf16[8,2,16,4096]{3,2,1,0:T(8,128)(2,1)} %get-tuple-element.8) | copy-start | bytes 6291460
  87.4 2.9 %collective-permute-start = (bf16[4,32,4096]{2,1,0:T(8,128)(2,1)}, bf16[4,32,4096]{2,1,0:T(8,128)(2,1)S(1)}, u32[]{:S(2)}, u32[]{:S(2)}) collective-permute-start(bf16[4,32,4096]{2,1,0:T(8,128)(2,1)} %select_bitcast_fusion.1), channel_id=1, source_target_pairs={{0,1},{1,0},{2,3},{3,2},{4,5},{5,4},{6,7},{7,6},{8,9},{9,8},{10,11... | collective-permute-start | bytes 3145736 | tf_op jit(solution)/shard_map/ppermute | solution.py:52
  88.3 2.0 %copy-start.1 = (bf16[8,2,16,4096]{3,2,1,0:T(8,128)(2,1)S(1)}, bf16[8,2,16,4096]{3,2,1,0:T(8,128)(2,1)}, u32[]{:S(2)}) copy-start(bf16[8,2,16,4096]{3,2,1,0:T(8,128)(2,1)} %get-tuple-element.7) | copy-start | bytes 6291460
  88.6 3.6 %collective-permute-start.4 = (bf16[4,32,4096]{2,1,0:T(8,128)(2,1)S(1)}, bf16[4,32,4096]{2,1,0:T(8,128)(2,1)S(1)}, u32[]{:S(2)}, u32[]{:S(2)}) collective-permute-start(bf16[4,32,4096]{2,1,0:T(8,128)(2,1)S(1)} %select_bitcast_fusion), channel_id=1, source_target_pairs={{0,1},{1,0},{2,3},{3,2},{4,5},{5,4},{6,7},{7,6},{8,9},{9,8},{10,11... | collective-permute-start | bytes 3145736 | tf_op jit(solution)/shard_map/ppermute | solution.py:52
  90.7 14.8 %collective-permute-start.1 = (bf16[2,32,4096]{2,1,0:T(8,128)(2,1)S(1)}, bf16[2,32,4096]{2,1,0:T(8,128)(2,1)S(1)}, u32[]{:S(2)}, u32[]{:S(2)}) collective-permute-start(bf16[2,32,4096]{2,1,0:T(8,128)(2,1)S(1)} %select_bitcast_fusion.3), channel_id=1, source_target_pairs={{0,2},{1,3},{2,0},{3,1},{4,6},{5,7},{6,4},{7,5},{8,10},{9,11},{10,... | collective-permute-start | bytes 1572872 | tf_op jit(solution)/shard_map/ppermute | solution.py:52
  92.6 26.3 %copy-start.4 = (pred[16,128]{1,0:T(8,128)(4,1)S(1)}, pred[16,128]{1,0:T(8,128)(4,1)}, u32[]{:S(2)}) copy-start(pred[16,128]{1,0:T(8,128)(4,1)} %copy-done.3) | copy-start | bytes 6148
  92.6 26.3 %copy-start.6 = (pred[16,128]{1,0:T(8,128)(4,1)S(1)}, pred[16,128]{1,0:T(8,128)(4,1)}, u32[]{:S(2)}) copy-start(pred[16,128]{1,0:T(8,128)(4,1)} %copy-done.5) | copy-start | bytes 6148
  92.6 23.4 %collective-permute-start.5 = (bf16[2,32,4096]{2,1,0:T(8,128)(2,1)S(1)}, bf16[2,32,4096]{2,1,0:T(8,128)(2,1)S(1)}, u32[]{:S(2)}, u32[]{:S(2)}) collective-permute-start(bf16[2,32,4096]{2,1,0:T(8,128)(2,1)S(1)} %select_bitcast_fusion.2), channel_id=1, source_target_pairs={{0,2},{1,3},{2,0},{3,1},{4,6},{5,7},{6,4},{7,5},{8,10},{9,11},{10,... | collective-permute-start | bytes 1572872 | tf_op jit(solution)/shard_map/ppermute | solution.py:52
  105.7 13.2 %collective-permute-start.2 = (bf16[32,4096]{1,0:T(8,128)(2,1)S(1)}, bf16[32,4096]{1,0:T(8,128)(2,1)S(1)}, u32[]{:S(2)}, u32[]{:S(2)}) collective-permute-start(bf16[32,4096]{1,0:T(8,128)(2,1)S(1)} %select_bitcast_fusion.6), channel_id=1, source_target_pairs={{0,4},{1,5},{2,6},{3,7},{4,0},{5,1},{6,2},{7,3},{8,12},{9,13},{10,... | collective-permute-start | bytes 786440 | tf_op jit(solution)/shard_map/ppermute | solution.py:62
  116.3 12.0 %collective-permute-start.7 = (bf16[32,4096]{1,0:T(8,128)(2,1)S(1)}, bf16[32,4096]{1,0:T(8,128)(2,1)S(1)}, u32[]{:S(2)}, u32[]{:S(2)}) collective-permute-start(bf16[32,4096]{1,0:T(8,128)(2,1)S(1)} %get-tuple-element.49), channel_id=1, source_target_pairs={{8,4},{9,5},{10,6},{11,7},{12,0},{13,1},{14,2},{15,3},{16,12},{17,... | collective-permute-start | bytes 786440 | tf_op jit(solution)/shard_map/ppermute | solution.py:73
  117.6 14.6 %collective-permute-start.6 = (bf16[32,4096]{1,0:T(8,128)(2,1)S(1)}, bf16[32,4096]{1,0:T(8,128)(2,1)S(1)}, u32[]{:S(2)}, u32[]{:S(2)}) collective-permute-start(bf16[32,4096]{1,0:T(8,128)(2,1)S(1)} %get-tuple-element.48), channel_id=1, source_target_pairs={{8,0},{9,1},{10,2},{11,3},{12,4},{13,5},{14,6},{15,7},{16,8},{17,9... | collective-permute-start | bytes 786440 | tf_op jit(solution)/shard_map/ppermute | solution.py:72
Sparse Core Ops, SparseCore 0:
  12.6 39.6 all-gather.1

commit v8 on v7

--- a/solution.py
+++ b/solution.py
@@ -39,34 +39,47 @@
     return jnp.dot(select.astype(rows.dtype), rows, preferred_element_type=jnp.float32).astype(rows.dtype)
 
 
-def halve_over_et(parts):
+def halve_over_et(parts, order, hook):
     n = lax.axis_size("et")
     me = lax.axis_index("et")
+    remaining = sorted(order)
     held = parts
-    bit = 1
-    while 2 * bit < n:
-        halves = held.reshape((held.shape[0] // 2, 2) + held.shape[1:])
+    for bit in order[:-1]:
+        lower = 1 << remaining.index(bit)
+        count = held.shape[0]
+        halves = held.reshape((count // (2 * lower), 2, lower) + held.shape[1:])
         side = (me // bit) % 2
-        keep = jnp.take(halves, side, axis=1)
-        give = jnp.take(halves, 1 - side, axis=1)
+        keep = jnp.take(halves, side, axis=1).reshape((count // 2,) + held.shape[1:])
+        give = jnp.take(halves, 1 - side, axis=1).reshape((count // 2,) + held.shape[1:])
         got = lax.ppermute(give, "et", [(i, i ^ bit) for i in range(n)])
         held = (keep.astype(jnp.float32) + got.astype(jnp.float32)).astype(jnp.bfloat16)
-        bit *= 2
+        held = hook(held)
+        hook = lambda value: value
+        remaining.remove(bit)
+    bit = order[-1]
     side = (me // bit) % 2
     return jnp.take(held, side, axis=0), jnp.take(held, 1 - side, axis=0), bit
 
 
-def reduce_to_owner(parts):
-    n = lax.axis_size("et")
-    keep, give, bit = halve_over_et(parts)
+def round_order(n, early):
+    bits = [1 << k for k in range(n.bit_length() - 1)]
+    head = bits[:-1]
+    if early in head:
+        head = [early] + [bit for bit in head if bit != early]
+    return head + bits[-1:]
+
+
+def reduce_to_owner(parts, order, hook):
+    n = lax.axis_size("et")
+    keep, give, bit = halve_over_et(parts, order, hook)
     got = lax.ppermute(give, "et", [(i, i ^ bit) for i in range(n)])
     return keep.astype(jnp.float32) + got.astype(jnp.float32)
 
 
-def reduce_to_previous(parts):
+def reduce_to_previous(parts, order, hook):
     n = lax.axis_size("et")
     stages = lax.axis_size("pipe")
-    keep, give, bit = halve_over_et(parts)
+    keep, give, bit = halve_over_et(parts, order, hook)
     to_same = [(stage * n + i, (stage - 1) * n + i) for stage in range(1, stages) for i in range(n)]
     to_other = [(stage * n + i, (stage - 1) * n + (i ^ bit)) for stage in range(1, stages) for i in range(n)]
     first = lax.ppermute(keep, ("pipe", "et"), to_same)
@@ -120,7 +133,7 @@
         grad_ref[...] = grad_acc[...].astype(grad_ref.dtype).reshape(grad_ref.shape)
 
 
-def expert_pass(gathered, gate_mats, up_mats, down_mats):
+def expert_pass(gathered, gate_mats, up_mats, down_mats, expert):
     n, experts, most, packed_width = gathered.shape
     width = gate_mats.shape[1]
     shard = gate_mats.shape[2]
@@ -129,26 +142,31 @@
     rows = n * most
     return pl.pallas_call(
         _expert_body,
-        grid=(experts, steps),
+        grid=(1, steps),
         in_specs=[
-            pl.BlockSpec((n, None, most, width), lambda e, f: (0, e, 0, 0)),
-            pl.BlockSpec((n, None, most, width), lambda e, f: (0, e, 0, 1)),
-            pl.BlockSpec((n, None, most, TAIL), lambda e, f: (0, e, 0, 2 * width // TAIL)),
-            pl.BlockSpec((None, width, tile), lambda e, f: (e, 0, f)),
-            pl.BlockSpec((None, width, tile), lambda e, f: (e, 0, f)),
-            pl.BlockSpec((None, tile, width), lambda e, f: (e, f, 0)),
+            pl.BlockSpec((n, None, most, width), lambda e, f: (0, expert, 0, 0)),
+            pl.BlockSpec((n, None, most, width), lambda e, f: (0, expert, 0, 1)),
+            pl.BlockSpec((n, None, most, TAIL), lambda e, f: (0, expert, 0, 2 * width // TAIL)),
+            pl.BlockSpec((None, width, tile), lambda e, f: (expert, 0, f)),
+            pl.BlockSpec((None, width, tile), lambda e, f: (expert, 0, f)),
+            pl.BlockSpec((None, tile, width), lambda e, f: (expert, f, 0)),
         ],
         out_specs=[
-            pl.BlockSpec((n, None, most, width), lambda e, f: (0, e, 0, 0)),
-            pl.BlockSpec((n, None, most, width), lambda e, f: (0, e, 0, 0)),
+            pl.BlockSpec((n, most, width), lambda e, f: (0, 0, 0)),
+            pl.BlockSpec((n, most, width), lambda e, f: (0, 0, 0)),
         ],
         out_shape=[
-            jax.ShapeDtypeStruct((n, experts, most, width), jnp.bfloat16),
-            jax.ShapeDtypeStruct((n, experts, most, width), jnp.bfloat16),
+            jax.ShapeDtypeStruct((n, most, width), jnp.bfloat16),
+            jax.ShapeDtypeStruct((n, most, width), jnp.bfloat16),
         ],
         scratch_shapes=[pltpu.VMEM((rows, width), jnp.float32), pltpu.VMEM((rows, width), jnp.float32)],
         compiler_params=pltpu.CompilerParams(
             dimension_semantics=("arbitrary", "arbitrary"), vmem_limit_bytes=100 * 1024 * 1024
+        ),
+        cost_estimate=pl.CostEstimate(
+            flops=12 * rows * width * shard,
+            transcendentals=rows * shard,
+            bytes_accessed=6 * width * shard + 8 * rows * width,
         ),
     )(gathered, gathered, gathered, gate_mats, up_mats, down_mats)
 
@@ -169,10 +187,19 @@
         [pick_rows(select, local_rows), pick_rows(select, local_grads), weight_cols], axis=1
     )
     gathered = lax.all_gather(packed, "et", axis=0, tiled=True).reshape(n, E_WIN, MOST, 2 * width + TAIL)
-    out_parts, grad_parts = expert_pass(gathered, gate_mats, up_mats, down_mats)
-    out_sums = reduce_to_owner(out_parts.reshape(n, E_WIN * MOST, width))
-    received = unpack(reduce_to_previous(grad_parts.reshape(n, E_WIN * MOST, width)), next_select)
-    out_share = unpack(out_sums, select)
+    out_sums, grad_sums = [], []
+    same = lambda value: value
+    for expert in range(E_WIN):
+        out_part, grad_part = expert_pass(gathered, gate_mats, up_mats, down_mats, expert)
+        if out_sums:
+            out_sums, grad_sums, out_part, grad_part = lax.optimization_barrier(
+                (out_sums, grad_sums, out_part, grad_part)
+            )
+        order = round_order(n, 2 if expert + 1 < E_WIN else 1)
+        out_sums.append(reduce_to_owner(out_part, order, same))
+        grad_sums.append(reduce_to_previous(grad_part, order, same))
+    out_share = unpack(jnp.concatenate(out_sums, axis=0), select)
+    received = unpack(jnp.concatenate(grad_sums, axis=0), next_select)
     return (out_share[None], received[None])
 
 

time: 141 us -> 149 us (1.057)
  starting transfers between devices: 8.3 us -> 14.1 us
  waiting for transfers between devices: 71.4 us -> 66.1 us
  other arithmetic: 7.98 us -> 11.2 us
  Pallas kernels: 32.6 us -> 35.6 us
    ppermute x4 -> x8, waiting for transfers between devices: 22.3 us -> 16.7 us  [halve_over_et(): got = lax.ppermute(give, 'et', [(i, i ^ bit) for i in range(n)])]
    ppermute x1 -> x2, waiting for transfers between devices: 3.83 us -> 7.39 us  [reduce_to_previous(): first = lax.ppermute(keep, ('pipe', 'et'), to_same)]
    pallas_call x1 -> x2, Pallas kernels: 32.6 us -> 35.6 us  [expert_pass(): pl.pallas_call(_expert_body, grid=(1, steps), in_specs=[pl.BlockSpec((n,...]
    ppermute x1 -> x2, waiting for transfers between devices: 7.38 us -> 4.62 us  [reduce_to_previous(): second = lax.ppermute(give, ('pipe', 'et'), to_other)]
    ppermute x4 -> x8, starting transfers between devices: 3 us -> 5.41 us  [halve_over_et(): got = lax.ppermute(give, 'et', [(i, i ^ bit) for i in range(n)])]
    convert_element_type x4 -> x8, other arithmetic: 0.94 us -> 3.13 us  [halve_over_et(): (keep.astype(jnp.float32) + got.astype(jnp.float32)).astype(jnp.bfloat16)]
    all_gather x1, waiting for transfers between devices: 32.8 us -> 30.9 us  [per_device(): lax.all_gather(packed, 'et', axis=0, tiled=True)]
    select_n x4 -> x2, other arithmetic: 2.69 us -> 3.44 us  [halve_over_et(): jnp.take(halves, side, axis=1).reshape((count // 2,) + held.shape[1:])]
  transfers between devices with their start and end apart: 9 -> 16, of which waited for: 7 -> 11; matrix products, arithmetic and copies ran while one was open for 3% -> 6% of each run, Pallas kernels for 0% -> 12%
where the time goes in v8:
time: 149 us; the launch traced here: 148 us
  waiting for transfers between devices  66.1 us (44%)
  Pallas kernels  35.6 us (24%)
  between operations  14.6 us (10%)
  starting transfers between devices  14.1 us (9%)
  other arithmetic  11.2 us (8%)
  matrix products  5.75 us (4%)
    pallas_call x2, Pallas kernels, expert_pass(): pl.pallas_call(_expert_body, grid=(1, steps), in_specs=[pl.BlockSpec((n,...  35.6 us
    all_gather x1, waiting for transfers between devices, per_device(): lax.all_gather(packed, 'et', axis=0, tiled=True)  30.9 us
    ppermute x8, waiting for transfers between devices, halve_over_et(): got = lax.ppermute(give, 'et', [(i, i ^ bit) for i in range(n)])  16.7 us
    ppermute x2, waiting for transfers between devices, reduce_to_previous(): first = lax.ppermute(keep, ('pipe', 'et'), to_same)  7.39 us
    ppermute x8, starting transfers between devices, halve_over_et(): got = lax.ppermute(give, 'et', [(i, i ^ bit) for i in range(n)])  5.41 us
    ppermute x1, waiting for transfers between devices, shifted(): lax.ppermute(value, axis, [(source, source + steps) for source in range(f...  5.05 us
    ppermute x2, waiting for transfers between devices, reduce_to_previous(): second = lax.ppermute(give, ('pipe', 'et'), to_other)  4.62 us
    dot_general x2, matrix products, unpack(): lax.dot_general(select.astype(jnp.float32), slot_sums, (((0,), (0,)), (()...  3.99 us
  transfers between devices with their start and end apart: 16, of which 11 were waited for; matrix products, arithmetic and copies ran while one was open for 6% of the time, Pallas kernels for 12%

profile of v8, /device:TPU:0, one launch (start us, length us, event | category | flops | bytes accessed | tf_op | source)
XLA Modules:
  0.0 148.5 jit_solution(14841372435653033522)
XLA Ops:
  8.9 1.5 %convolution_convert_fusion.3 = bf16[32,4096]{1,0:T(8,128)(2,1)S(1)} fusion(bf16[1,128,4096]{2,1,0:T(8,128)(2,1)} %param.15, pred[16,128]{1,0:T(8,128)(4,1)S(1)} %get-tuple-element.83, pred[16,128]{1,0:T(8,128)(4,1)S(1)} %get-tuple-element.82), kind=kOutput, calls=%fused_computation.5 | convolution fusion | flops 33689600 | bytes 1314816 | tf_op jit(solution)/shard_map/dot_general | solution.py:39
  11.8 1.3 collective-permute-start.10
  13.3 5.1 %collective-permute-done.10 = s32[128,2]{0,1:T(2,128)S(1)} collective-permute-done((s32[128,2]{0,1:T(2,128)S(1)}, s32[128,2]{0,1:T(2,128)S(1)}, u32[]{:S(2)}, u32[]{:S(2)}) %collective-permute-start.10) | collective-permute-done | bytes 1056 | tf_op jit(solution)/shard_map/ppermute | solution.py:16
  20.8 30.9 %all-gather.2.cloned.1.call-done = bf16[256,8320]{1,0:T(8,128)(2,1)} async-done(((bf16[32,8320]{1,0:T(8,128)(2,1)}), bf16[256,8320]{1,0:T(8,128)(2,1)}) %all-gather.2.cloned.1.call-update) | async-done | bytes 4259856 | tf_op jit(solution)/shard_map/all_gather | solution.py:189
  51.7 17.8 %shard_map.86 = (bf16[8,16,4096]{2,1,0:T(8,128)(2,1)}, bf16[8,16,4096]{2,1,0:T(8,128)(2,1)}) custom-call(bf16[8,2,16,8320]{3,2,1,0:T(8,128)(2,1)} %bitcast.189, bf16[8,2,16,8320]{3,2,1,0:T(8,128)(2,1)} %bitcast.190, bf16[8,2,16,8320]{3,2,1,0:T(8,128)(2,1)} %bitcast.191, bf16[2,4096,896]{2,1,0:T(8,128)(2,1)} %bitcast.195, bf16[2,4096,896]{2,1,0:T(8,128)(2,1)} %bitcast.197, ...), custom_call_target="tpu_custom_call" | custom-call | flops 5637144576 | bytes 26214400 | tf_op jit(solution)/shard_map/pallas_call | solution.py:143
  69.5 2.4 %dynamic-slice_select_fusion.1 = (bf16[2,1,2,16,4096]{4,3,2,1,0:T(8,128)(2,1)}, bf16[2,1,2,16,4096]{4,3,2,1,0:T(8,128)(2,1)}) fusion(bf16[2,2,2,16,4096]{4,3,2,1,0:T(8,128)(2,1)} %bitcast.210, s32[]{:T(128)S(6)} %select_n.193, pred[]{:T(512)S(6)} %and.144, s32[]{:T(128)S(6)} %select_n.195, pred[]{:T(512)S(6)} %and.145), kind=kLoop, calls=%fused_computation.40 | loop fusion | flops 524288 | bytes 2097162 | tf_op jit(solution)/shard_map/jit(_take)/select_n | solution.py:52
  71.9 1.5 collective-permute-start.3
  75.0 17.8 %shard_map.87 = (bf16[8,16,4096]{2,1,0:T(8,128)(2,1)}, bf16[8,16,4096]{2,1,0:T(8,128)(2,1)}) custom-call(bf16[8,2,16,8320]{3,2,1,0:T(8,128)(2,1)} %bitcast.192, bf16[8,2,16,8320]{3,2,1,0:T(8,128)(2,1)} %bitcast.193, bf16[8,2,16,8320]{3,2,1,0:T(8,128)(2,1)} %bitcast.194, bf16[2,4096,896]{2,1,0:T(8,128)(2,1)} %bitcast.196, bf16[2,4096,896]{2,1,0:T(8,128)(2,1)} %bitcast.198, ...), custom_call_target="tpu_custom_call" | custom-call | flops 5637144576 | bytes 26214400 | tf_op jit(solution)/shard_map/pallas_call | solution.py:143
  92.8 4.7 %collective-permute-done = bf16[4,16,4096]{2,1,0:T(8,128)(2,1)} collective-permute-done((bf16[4,16,4096]{2,1,0:T(8,128)(2,1)}, bf16[4,16,4096]{2,1,0:T(8,128)(2,1)}, u32[]{:S(2)}, u32[]{:S(2)}) %collective-permute-start) | collective-permute-done | bytes 524320 | tf_op jit(solution)/shard_map/ppermute | solution.py:54
  97.5 1.3 fusion.5
  100.9 1.4 collective-permute-start.2
  102.4 1.3 collective-permute-start.5
  103.7 1.3 collective-permute-start.6
  105.0 1.4 collective-permute-done.2
  106.5 4.1 %collective-permute-done.5 = bf16[16,4096]{1,0:T(8,128)(2,1)S(1)} collective-permute-done((bf16[16,4096]{1,0:T(8,128)(2,1)S(1)}, bf16[16,4096]{1,0:T(8,128)(2,1)S(1)}, u32[]{:S(2)}, u32[]{:S(2)}) %collective-permute-start.5) | collective-permute-done | bytes 131104 | tf_op jit(solution)/shard_map/ppermute | solution.py:85
  110.5 2.8 %collective-permute-done.6 = bf16[16,4096]{1,0:T(8,128)(2,1)S(1)} collective-permute-done((bf16[16,4096]{1,0:T(8,128)(2,1)S(1)}, bf16[16,4096]{1,0:T(8,128)(2,1)S(1)}, u32[]{:S(2)}, u32[]{:S(2)}) %collective-permute-start.6) | collective-permute-done | bytes 131104 | tf_op jit(solution)/shard_map/ppermute | solution.py:86
  116.6 1.4 collective-permute-start.12
  118.0 6.8 %collective-permute-done.8 = bf16[2,16,4096]{2,1,0:T(8,128)(2,1)S(1)} collective-permute-done((bf16[2,16,4096]{2,1,0:T(8,128)(2,1)S(1)}, bf16[2,16,4096]{2,1,0:T(8,128)(2,1)S(1)}, u32[]{:S(2)}, u32[]{:S(2)}) %collective-permute-start.8) | collective-permute-done | bytes 262176 | tf_op jit(solution)/shard_map/ppermute | solution.py:54
  125.7 3.9 %collective-permute-done.12 = bf16[2,16,4096]{2,1,0:T(8,128)(2,1)S(1)} collective-permute-done((bf16[2,16,4096]{2,1,0:T(8,128)(2,1)S(1)}, bf16[2,16,4096]{2,1,0:T(8,128)(2,1)S(1)}, u32[]{:S(2)}, u32[]{:S(2)}) %collective-permute-start.12) | collective-permute-done | bytes 262176 | tf_op jit(solution)/shard_map/ppermute | solution.py:54
  129.7 1.3 collective-permute-start.13
  132.4 2.0 %fusion = bf16[1,128,4096]{2,1,0:T(8,128)(2,1)} fusion(f32[16,4096]{1,0:T(8,128)S(1)} %convert_add_fusion.9, f32[16,4096]{1,0:T(8,128)S(1)} %convert_add_fusion.11, pred[16,128]{1,0:T(8,128)(4,1)S(1)} %copy-done.8, pred[16,128]{1,0:T(8,128)(4,1)S(1)} %copy-done.6), kind=kOutput, calls=%fused_computation.2 | convolution fusion | flops 201986048 | bytes 1576960 | tf_op jit(solution)/shard_map/dot_general | solution.py:91
  134.4 3.3 %collective-permute-done.13 = bf16[16,4096]{1,0:T(8,128)(2,1)S(1)} collective-permute-done((bf16[16,4096]{1,0:T(8,128)(2,1)S(1)}, bf16[16,4096]{1,0:T(8,128)(2,1)S(1)}, u32[]{:S(2)}, u32[]{:S(2)}) %collective-permute-start.13) | collective-permute-done | bytes 131104 | tf_op jit(solution)/shard_map/ppermute | solution.py:85
  137.7 1.8 %collective-permute-done.14 = bf16[16,4096]{1,0:T(8,128)(2,1)S(1)} collective-permute-done((bf16[16,4096]{1,0:T(8,128)(2,1)S(1)}, bf16[16,4096]{1,0:T(8,128)(2,1)S(1)}, u32[]{:S(2)}, u32[]{:S(2)}) %collective-permute-start.14) | collective-permute-done | bytes 131104 | tf_op jit(solution)/shard_map/ppermute | solution.py:86
  139.6 2.0 %fusion.1 = bf16[1,128,4096]{2,1,0:T(8,128)(2,1)} fusion(f32[16,4096]{1,0:T(8,128)S(1)} %convert_add_fusion.8, f32[16,4096]{1,0:T(8,128)S(1)} %convert_add_fusion.10, pred[16,128]{1,0:T(8,128)(4,1)S(1)} %get-tuple-element.85, pred[16,128]{1,0:T(8,128)(4,1)S(1)} %get-tuple-element.84), kind=kOutput, calls=%fused_computation.3 | convolution fusion | flops 201986048 | bytes 1576960 | tf_op jit(solution)/shard_map/dot_general | solution.py:91
  (98 shorter events, 14.8 us)
Async XLA Ops:
  7.2 44.5 %all-gather.2.cloned.1.call-start = ((), (), s32[]{:S(2)}) async-start(), calls=%async_computation | async-start | bytes 4792320 | tf_op jit(solution)/shard_map/all_gather | solution.py:189
  11.8 6.5 %collective-permute-start.10 = (s32[128,2]{0,1:T(2,128)S(1)}, s32[128,2]{0,1:T(2,128)S(1)}, u32[]{:S(2)}, u32[]{:S(2)}) collective-permute-start(s32[128,2]{0,1:T(2,128)S(1)} %bitcast.215), channel_id=1, source_target_pairs={{8,0},{16,8},{24,16},{9,1},{17,9},{25,17},{10,2},{18,10},{26,18},{... | collective-permute-start | bytes 3080 | tf_op jit(solution)/shard_map/ppermute | solution.py:16
  71.9 27.1 %collective-permute-start.3 = (bf16[4,16,4096]{2,1,0:T(8,128)(2,1)}, bf16[4,16,4096]{2,1,0:T(8,128)(2,1)}, u32[]{:S(2)}, u32[]{:S(2)}) collective-permute-start(bf16[4,16,4096]{2,1,0:T(8,128)(2,1)} %bitcast.27), channel_id=1, source_target_pairs={{0,2},{1,3},{2,0},{3,1},{4,6},{5,7},{6,4},{7,5},{8,10},{9,11},{10,... | collective-permute-start | bytes 1572872 | tf_op jit(solution)/shard_map/ppermute | solution.py:54
  74.4 23.1 %collective-permute-start = (bf16[4,16,4096]{2,1,0:T(8,128)(2,1)}, bf16[4,16,4096]{2,1,0:T(8,128)(2,1)}, u32[]{:S(2)}, u32[]{:S(2)}) collective-permute-start(bf16[4,16,4096]{2,1,0:T(8,128)(2,1)} %bitcast.15), channel_id=1, source_target_pairs={{0,2},{1,3},{2,0},{3,1},{4,6},{5,7},{6,4},{7,5},{8,10},{9,11},{10,... | collective-permute-start | bytes 1572872 | tf_op jit(solution)/shard_map/ppermute | solution.py:54
  98.9 1.9 %collective-permute-start.1 = (bf16[2,16,4096]{2,1,0:T(8,128)(2,1)S(1)}, bf16[2,16,4096]{2,1,0:T(8,128)(2,1)S(1)}, u32[]{:S(2)}, u32[]{:S(2)}) collective-permute-start(bf16[2,16,4096]{2,1,0:T(8,128)(2,1)S(1)} %select_bitcast_fusion.1), channel_id=1, source_target_pairs={{0,1},{1,0},{2,3},{3,2},{4,5},{5,4},{6,7},{7,6},{8,9},{9,8},{10,11... | collective-permute-start | bytes 786440 | tf_op jit(solution)/shard_map/ppermute | solution.py:54
  100.1 13.2 %copy-start.4 = (bf16[8,16,4096]{2,1,0:T(8,128)(2,1)S(1)}, bf16[8,16,4096]{2,1,0:T(8,128)(2,1)}, u32[]{:S(2)}) copy-start(bf16[8,16,4096]{2,1,0:T(8,128)(2,1)} %get-tuple-element.19) | copy-start | bytes 3145732
  100.2 13.3 %copy-start.10 = (s32[128]{0:T(128)S(1)}, s32[128]{0:T(128)}, u32[]{:S(2)}) copy-start(s32[128]{0:T(128)} %add_reduce_fusion) | copy-start | bytes 1540
  100.2 13.3 %copy-start.11 = (s32[128]{0:T(128)S(1)}, s32[128]{0:T(128)}, u32[]{:S(2)}) copy-start(s32[128]{0:T(128)} %add_reduce_fusion.1) | copy-start | bytes 1540
  100.2 13.3 %copy-start.13 = (pred[128]{0:T(512)(128)(4,1)S(1)}, pred[128]{0:T(512)(128)(4,1)}, u32[]{:S(2)}) copy-start(pred[128]{0:T(512)(128)(4,1)} %copy-done.12) | copy-start | bytes 388
  100.2 13.3 %copy-start.15 = (pred[128]{0:T(512)(128)(4,1)S(1)}, pred[128]{0:T(512)(128)(4,1)}, u32[]{:S(2)}) copy-start(pred[128]{0:T(512)(128)(4,1)} %copy-done.14) | copy-start | bytes 388
  100.2 13.3 %copy-start.3 = (bf16[8,16,4096]{2,1,0:T(8,128)(2,1)S(1)}, bf16[8,16,4096]{2,1,0:T(8,128)(2,1)}, u32[]{:S(2)}) copy-start(bf16[8,16,4096]{2,1,0:T(8,128)(2,1)} %get-tuple-element.21) | copy-start | bytes 3145732
  100.3 2.0 %collective-permute-start.4 = (bf16[2,16,4096]{2,1,0:T(8,128)(2,1)S(1)}, bf16[2,16,4096]{2,1,0:T(8,128)(2,1)S(1)}, u32[]{:S(2)}, u32[]{:S(2)}) collective-permute-start(bf16[2,16,4096]{2,1,0:T(8,128)(2,1)S(1)} %select_bitcast_fusion), channel_id=1, source_target_pairs={{0,1},{1,0},{2,3},{3,2},{4,5},{5,4},{6,7},{7,6},{8,9},{9,8},{10,11... | collective-permute-start | bytes 786440 | tf_op jit(solution)/shard_map/ppermute | solution.py:54
  100.9 5.5 %collective-permute-start.2 = (bf16[16,4096]{1,0:T(8,128)(2,1)S(1)}, bf16[16,4096]{1,0:T(8,128)(2,1)S(1)}, u32[]{:S(2)}, u32[]{:S(2)}) collective-permute-start(bf16[16,4096]{1,0:T(8,128)(2,1)S(1)} %select_bitcast_fusion.7), channel_id=1, source_target_pairs={{0,4},{1,5},{2,6},{3,7},{4,0},{5,1},{6,2},{7,3},{8,12},{9,13},{10,... | collective-permute-start | bytes 393224 | tf_op jit(solution)/shard_map/ppermute | solution.py:75
  102.4 8.1 %collective-permute-start.5 = (bf16[16,4096]{1,0:T(8,128)(2,1)S(1)}, bf16[16,4096]{1,0:T(8,128)(2,1)S(1)}, u32[]{:S(2)}, u32[]{:S(2)}) collective-permute-start(bf16[16,4096]{1,0:T(8,128)(2,1)S(1)} %get-tuple-element.78), channel_id=1, source_target_pairs={{8,0},{9,1},{10,2},{11,3},{12,4},{13,5},{14,6},{15,7},{16,8},{17,9... | collective-permute-start | bytes 393224 | tf_op jit(solution)/shard_map/ppermute | solution.py:85
  103.7 9.6 %collective-permute-start.6 = (bf16[16,4096]{1,0:T(8,128)(2,1)S(1)}, bf16[16,4096]{1,0:T(8,128)(2,1)S(1)}, u32[]{:S(2)}, u32[]{:S(2)}) collective-permute-start(bf16[16,4096]{1,0:T(8,128)(2,1)S(1)} %get-tuple-element.79), channel_id=1, source_target_pairs={{8,4},{9,5},{10,6},{11,7},{12,0},{13,1},{14,2},{15,3},{16,12},{17,... | collective-permute-start | bytes 393224 | tf_op jit(solution)/shard_map/ppermute | solution.py:86
  113.4 2.0 %collective-permute-start.7 = (bf16[4,16,4096]{2,1,0:T(8,128)(2,1)S(1)}, bf16[4,16,4096]{2,1,0:T(8,128)(2,1)S(1)}, u32[]{:S(2)}, u32[]{:S(2)}) collective-permute-start(bf16[4,16,4096]{2,1,0:T(8,128)(2,1)S(1)} %fusion.16), channel_id=1, source_target_pairs={{0,1},{1,0},{2,3},{3,2},{4,5},{5,4},{6,7},{7,6},{8,9},{9,8},{10,11... | collective-permute-start | bytes 1572872 | tf_op jit(solution)/shard_map/ppermute | solution.py:54
  113.6 2.8 %collective-permute-start.11 = (bf16[4,16,4096]{2,1,0:T(8,128)(2,1)S(1)}, bf16[4,16,4096]{2,1,0:T(8,128)(2,1)S(1)}, u32[]{:S(2)}, u32[]{:S(2)}) collective-permute-start(bf16[4,16,4096]{2,1,0:T(8,128)(2,1)S(1)} %fusion.14), channel_id=1, source_target_pairs={{0,1},{1,0},{2,3},{3,2},{4,5},{5,4},{6,7},{7,6},{8,9},{9,8},{10,11... | collective-permute-start | bytes 1572872 | tf_op jit(solution)/shard_map/ppermute | solution.py:54
  115.6 9.2 %collective-permute-start.8 = (bf16[2,16,4096]{2,1,0:T(8,128)(2,1)S(1)}, bf16[2,16,4096]{2,1,0:T(8,128)(2,1)S(1)}, u32[]{:S(2)}, u32[]{:S(2)}) collective-permute-start(bf16[2,16,4096]{2,1,0:T(8,128)(2,1)S(1)} %fusion.24), channel_id=1, source_target_pairs={{0,2},{1,3},{2,0},{3,1},{4,6},{5,7},{6,4},{7,5},{8,10},{9,11},{10,... | collective-permute-start | bytes 786440 | tf_op jit(solution)/shard_map/ppermute | solution.py:54
  116.5 15.9 %copy-start.6 = (pred[16,128]{1,0:T(8,128)(4,1)S(1)}, pred[16,128]{1,0:T(8,128)(4,1)}, u32[]{:S(2)}) copy-start(pred[16,128]{1,0:T(8,128)(4,1)} %copy-done.5) | copy-start | bytes 6148
  116.6 15.9 %copy-start.8 = (pred[16,128]{1,0:T(8,128)(4,1)S(1)}, pred[16,128]{1,0:T(8,128)(4,1)}, u32[]{:S(2)}) copy-start(pred[16,128]{1,0:T(8,128)(4,1)} %copy-done.7) | copy-start | bytes 6148
  116.6 13.0 %collective-permute-start.12 = (bf16[2,16,4096]{2,1,0:T(8,128)(2,1)S(1)}, bf16[2,16,4096]{2,1,0:T(8,128)(2,1)S(1)}, u32[]{:S(2)}, u32[]{:S(2)}) collective-permute-start(bf16[2,16,4096]{2,1,0:T(8,128)(2,1)S(1)} %fusion.22), channel_id=1, source_target_pairs={{0,2},{1,3},{2,0},{3,1},{4,6},{5,7},{6,4},{7,5},{8,10},{9,11},{10,... | collective-permute-start | bytes 786440 | tf_op jit(solution)/shard_map/ppermute | solution.py:54
  124.9 7.4 %collective-permute-start.9 = (bf16[16,4096]{1,0:T(8,128)(2,1)S(1)}, bf16[16,4096]{1,0:T(8,128)(2,1)S(1)}, u32[]{:S(2)}, u32[]{:S(2)}) collective-permute-start(bf16[16,4096]{1,0:T(8,128)(2,1)S(1)} %select_bitcast_fusion.4), channel_id=1, source_target_pairs={{0,4},{1,5},{2,6},{3,7},{4,0},{5,1},{6,2},{7,3},{8,12},{9,13},{10,... | collective-permute-start | bytes 393224 | tf_op jit(solution)/shard_map/ppermute | solution.py:75
  129.7 8.0 %collective-permute-start.13 = (bf16[16,4096]{1,0:T(8,128)(2,1)S(1)}, bf16[16,4096]{1,0:T(8,128)(2,1)S(1)}, u32[]{:S(2)}, u32[]{:S(2)}) collective-permute-start(bf16[16,4096]{1,0:T(8,128)(2,1)S(1)} %get-tuple-element.76), channel_id=1, source_target_pairs={{8,0},{9,1},{10,2},{11,3},{12,4},{13,5},{14,6},{15,7},{16,8},{17,9... | collective-permute-start | bytes 393224 | tf_op jit(solution)/shard_map/ppermute | solution.py:85
  131.0 8.5 %collective-permute-start.14 = (bf16[16,4096]{1,0:T(8,128)(2,1)S(1)}, bf16[16,4096]{1,0:T(8,128)(2,1)S(1)}, u32[]{:S(2)}, u32[]{:S(2)}) collective-permute-start(bf16[16,4096]{1,0:T(8,128)(2,1)S(1)} %get-tuple-element.77), channel_id=1, source_target_pairs={{8,4},{9,5},{10,6},{11,7},{12,0},{13,1},{14,2},{15,3},{16,12},{17,... | collective-permute-start | bytes 393224 | tf_op jit(solution)/shard_map/ppermute | solution.py:86
  (9 other events, 25.2 us)
Sparse Core Ops, SparseCore 0:
  12.0 39.6 all-gather.1

commit v9 on v7

--- a/solution.py
+++ b/solution.py
@@ -39,21 +39,27 @@
     return jnp.dot(select.astype(rows.dtype), rows, preferred_element_type=jnp.float32).astype(rows.dtype)
 
 
+def gather_over_et(packed):
+    n = lax.axis_size("et")
+    held = packed[None]
+    bit = 1
+    while bit < n:
+        got = lax.ppermute(held, "et", [(i, i ^ bit) for i in range(n)])
+        held = jnp.concatenate([held, got], axis=0)
+        bit *= 2
+    return held
+
+
 def halve_over_et(parts):
     n = lax.axis_size("et")
-    me = lax.axis_index("et")
     held = parts
     bit = 1
     while 2 * bit < n:
         halves = held.reshape((held.shape[0] // 2, 2) + held.shape[1:])
-        side = (me // bit) % 2
-        keep = jnp.take(halves, side, axis=1)
-        give = jnp.take(halves, 1 - side, axis=1)
-        got = lax.ppermute(give, "et", [(i, i ^ bit) for i in range(n)])
-        held = (keep.astype(jnp.float32) + got.astype(jnp.float32)).astype(jnp.bfloat16)
+        got = lax.ppermute(halves[:, 1], "et", [(i, i ^ bit) for i in range(n)])
+        held = (halves[:, 0].astype(jnp.float32) + got.astype(jnp.float32)).astype(jnp.bfloat16)
         bit *= 2
-    side = (me // bit) % 2
-    return jnp.take(held, side, axis=0), jnp.take(held, 1 - side, axis=0), bit
+    return held[0], held[1], bit
 
 
 def reduce_to_owner(parts):
@@ -168,7 +174,7 @@
     packed = jnp.concatenate(
         [pick_rows(select, local_rows), pick_rows(select, local_grads), weight_cols], axis=1
     )
-    gathered = lax.all_gather(packed, "et", axis=0, tiled=True).reshape(n, E_WIN, MOST, 2 * width + TAIL)
+    gathered = gather_over_et(packed).reshape(n, E_WIN, MOST, 2 * width + TAIL)
     out_parts, grad_parts = expert_pass(gathered, gate_mats, up_mats, down_mats)
     out_sums = reduce_to_owner(out_parts.reshape(n, E_WIN * MOST, width))
     received = unpack(reduce_to_previous(grad_parts.reshape(n, E_WIN * MOST, width)), next_select)

time: 141 us -> 167 us (1.18)
  waiting for transfers between devices: 71.4 us -> 101 us
  between operations: 14.4 us -> 1 us
  starting transfers between devices: 8.3 us -> 13.9 us
  local copies, waits for them, and re-layouts: 0.58 us -> 2.81 us
  other arithmetic: 7.98 us -> 10.2 us
    ppermute x4 -> x7, waiting for transfers between devices: 22.3 us -> 85.5 us  [the longest x3 63.9 us: gather_over_et(): got = lax.ppermute(held, 'et', [(i, i ^ bit) for i in range(n)])]
    all_gather x1 -> x0, waiting for transfers between devices: 32.8 us -> none  [per_device(): lax.all_gather(packed, 'et', axis=0, tiled=True)]
    ppermute x4 -> x7, starting transfers between devices: 3 us -> 8.49 us  [the longest x3 5.21 us: gather_over_et(): got = lax.ppermute(held, 'et', [(i, i ^ bit) for i in range(n)])]
    concatenate x0 -> x3, other arithmetic: none -> 5.22 us  [gather_over_et(): held = jnp.concatenate([held, got], axis=0)]
    select_n x6 -> x0, other arithmetic: 2.78 us -> none  [the longest x4 2.69 us: halve_over_et(): give = jnp.take(halves, 1 - side, axis=1)]
  transfers between devices with their start and end apart: 9 -> 11, of which waited for: 7 -> 9; matrix products, arithmetic and copies ran while one was open for 3% -> 3% of each run, Pallas kernels for 0% -> 0%
where the time goes in v9:
time: 167 us
  waiting for transfers between devices  101 us (60%)
  Pallas kernels  32.6 us (20%)
  starting transfers between devices  13.9 us (8%)
  other arithmetic  10.2 us (6%)
  matrix products  5.75 us (3%)
  local copies, waits for them, and re-layouts  2.81 us (2%)
    ppermute x3, waiting for transfers between devices, gather_over_et(): got = lax.ppermute(held, 'et', [(i, i ^ bit) for i in range(n)])  63.9 us
    pallas_call x1, Pallas kernels, expert_pass(): pl.pallas_call(_expert_body, grid=(experts, steps), in_specs=[pl.BlockSpe...  32.6 us
    ppermute x4, waiting for transfers between devices, halve_over_et(): got = lax.ppermute(halves[:, 1], 'et', [(i, i ^ bit) for i in range(n)])  21.6 us
    ppermute x1, waiting for transfers between devices, reduce_to_previous(): second = lax.ppermute(give, ('pipe', 'et'), to_other)  7.36 us
    concatenate x3, other arithmetic, gather_over_et(): held = jnp.concatenate([held, got], axis=0)  5.22 us
    ppermute x3, starting transfers between devices, gather_over_et(): got = lax.ppermute(held, 'et', [(i, i ^ bit) for i in range(n)])  5.21 us
    ppermute x1, waiting for transfers between devices, shifted(): lax.ppermute(value, axis, [(source, source + steps) for source in range(f...  4.16 us
    dot_general x2, matrix products, unpack(): lax.dot_general(select.astype(jnp.float32), slot_sums, (((0,), (0,)), (()...  4 us
  transfers between devices with their start and end apart: 11, of which 9 were waited for; matrix products, arithmetic and copies ran while one was open for 3% of the time, Pallas kernels for 0%

profile of v9, /device:TPU:0, one launch (start us, length us, event | category | flops | bytes accessed | tf_op | source)
XLA Modules:
  0.0 167.2 jit_solution(13855511540096974766)
XLA Ops:
  2.3 1.5 convolution_convert_fusion.3
  5.0 1.5 collective-permute-done
  6.7 2.9 %collective-permute-start.1 = (bf16[2,32,8320]{2,1,0:T(8,128)(2,1)S(1)}, bf16[2,32,8320]{2,1,0:T(8,128)(2,1)S(1)}, u32[]{:S(2)}, u32[]{:S(2)}) collective-permute-start(bf16[2,32,8320]{2,1,0:T(8,128)(2,1)S(1)} %pad_maximum_fusion.2), channel_id=1, source_target_pairs={{0,2},{1,3},{2,0},{3,1},{4,6},{5,7},{6,4},{7,5},{8,10},{9,11},{10,... | collective-permute-start | bytes 3194888 | tf_op jit(solution)/shard_map/ppermute | solution.py:47
  9.6 23.8 %collective-permute-done.1 = bf16[2,32,8320]{2,1,0:T(8,128)(2,1)S(1)} collective-permute-done((bf16[2,32,8320]{2,1,0:T(8,128)(2,1)S(1)}, bf16[2,32,8320]{2,1,0:T(8,128)(2,1)S(1)}, u32[]{:S(2)}, u32[]{:S(2)}) %collective-permute-start.1) | collective-permute-done | bytes 1064992 | tf_op jit(solution)/shard_map/ppermute | solution.py:47
  33.4 1.6 pad_maximum_fusion.1
  35.0 1.8 %collective-permute-start.2 = (bf16[4,32,8320]{2,1,0:T(8,128)(2,1)}, bf16[4,32,8320]{2,1,0:T(8,128)(2,1)}, u32[]{:S(2)}, u32[]{:S(2)}) collective-permute-start(bf16[4,32,8320]{2,1,0:T(8,128)(2,1)} %pad_maximum_fusion.1), channel_id=1, source_target_pairs={{0,4},{1,5},{2,6},{3,7},{4,0},{5,1},{6,2},{7,3},{8,12},{9,13},{10,... | collective-permute-start | bytes 6389768 | tf_op jit(solution)/shard_map/ppermute | solution.py:47
  36.8 1.3 collective-permute-start.6
  38.1 4.2 %collective-permute-done.6 = s32[128,2]{0,1:T(2,128)S(1)} collective-permute-done((s32[128,2]{0,1:T(2,128)S(1)}, s32[128,2]{0,1:T(2,128)S(1)}, u32[]{:S(2)}, u32[]{:S(2)}) %collective-permute-start.6) | collective-permute-done | bytes 1056 | tf_op jit(solution)/shard_map/ppermute | solution.py:16
  44.7 38.5 %collective-permute-done.2 = bf16[4,32,8320]{2,1,0:T(8,128)(2,1)} collective-permute-done((bf16[4,32,8320]{2,1,0:T(8,128)(2,1)}, bf16[4,32,8320]{2,1,0:T(8,128)(2,1)}, u32[]{:S(2)}, u32[]{:S(2)}) %collective-permute-start.2) | collective-permute-done | bytes 2129952 | tf_op jit(solution)/shard_map/ppermute | solution.py:47
  83.2 3.5 %pad_maximum_fusion.x_ref.g_ref.w_ref = bf16[8,2,16,8320]{3,2,1,0:T(8,128)(2,1)} fusion(bf16[4,2,16,8320]{3,2,1,0:T(8,128)(2,1)} %bitcast.11, bf16[2,2,16,8320]{3,2,1,0:T(8,128)(2,1)S(1)} %bitcast.92, bf16[1,2,16,8320]{3,2,1,0:T(8,128)(2,1)S(1)} %bitcast.91, bf16[1,2,16,8320]{3,2,1,0:T(8,128)(2,1)S(1)} %bitcast.97), kind=kLoop, calls=%fused_computation.6 | loop fusion | flops 6389760 | bytes 8519680 | tf_op jit(solution)/shard_map/concatenate | solution.py:48
  86.7 32.6 %shard_map.86 = (bf16[8,2,16,4096]{3,2,1,0:T(8,128)(2,1)}, bf16[8,2,16,4096]{3,2,1,0:T(8,128)(2,1)}) custom-call(bf16[8,2,16,8320]{3,2,1,0:T(8,128)(2,1)} %pad_maximum_fusion.x_ref.g_ref.w_ref, bf16[8,2,16,8320]{3,2,1,0:T(8,128)(2,1)} %pad_maximum_fusion.x_ref.g_ref.w_ref, bf16[8,2,16,8320]{3,2,1,0:T(8,128)(2,1)} %pad_maximum_fusion.x_ref.g_ref.w_ref, ...), custom_call_target="tpu_custom_call" | custom-call | tf_op jit(solution)/shard_map/pallas_call | solution.py:136
  119.3 1.4 slice_bitcast_fusion.2
  122.5 1.0 collective-permute-done.3
  123.8 1.5 collective-permute-start.4
  125.6 1.2 collective-permute-start.8
  126.8 11.8 %collective-permute-done.4 = bf16[2,32,4096]{2,1,0:T(8,128)(2,1)S(1)} collective-permute-done((bf16[2,32,4096]{2,1,0:T(8,128)(2,1)S(1)}, bf16[2,32,4096]{2,1,0:T(8,128)(2,1)S(1)}, u32[]{:S(2)}, u32[]{:S(2)}) %collective-permute-start.4) | collective-permute-done | bytes 524320 | tf_op jit(solution)/shard_map/ppermute | solution.py:59
  138.8 1.5 collective-permute-start.5
  140.3 8.8 %collective-permute-done.8 = bf16[2,32,4096]{2,1,0:T(8,128)(2,1)S(1)} collective-permute-done((bf16[2,32,4096]{2,1,0:T(8,128)(2,1)S(1)}, bf16[2,32,4096]{2,1,0:T(8,128)(2,1)S(1)}, u32[]{:S(2)}, u32[]{:S(2)}) %collective-permute-start.8) | collective-permute-done | bytes 524320 | tf_op jit(solution)/shard_map/ppermute | solution.py:59
  149.2 1.3 collective-permute-start.10
  150.5 1.3 collective-permute-start.9
  151.9 2.0 %fusion = bf16[1,128,4096]{2,1,0:T(8,128)(2,1)} fusion(bf16[32,4096]{1,0:T(8,128)(2,1)S(1)} %collective-permute-done.5, bf16[2,32,4096]{2,1,0:T(8,128)(2,1)S(1)} %fusion.5, pred[16,128]{1,0:T(8,128)(4,1)S(1)} %copy-done.6, pred[16,128]{1,0:T(8,128)(4,1)S(1)} %copy-done.4), kind=kOutput, calls=%fused_computation.2 | convolution fusion | flops 202248192 | bytes 1576960 | tf_op jit(solution)/shard_map/dot_general | solution.py:84
  153.9 7.4 %collective-permute-done.10 = bf16[32,4096]{1,0:T(8,128)(2,1)S(1)} collective-permute-done((bf16[32,4096]{1,0:T(8,128)(2,1)S(1)}, bf16[32,4096]{1,0:T(8,128)(2,1)S(1)}, u32[]{:S(2)}, u32[]{:S(2)}) %collective-permute-start.10) | collective-permute-done | bytes 262176 | tf_op jit(solution)/shard_map/ppermute | solution.py:79
  161.3 3.9 %collective-permute-done.9 = bf16[32,4096]{1,0:T(8,128)(2,1)S(1)} collective-permute-done((bf16[32,4096]{1,0:T(8,128)(2,1)S(1)}, bf16[32,4096]{1,0:T(8,128)(2,1)S(1)}, u32[]{:S(2)}, u32[]{:S(2)}) %collective-permute-start.9) | collective-permute-done | bytes 262176 | tf_op jit(solution)/shard_map/ppermute | solution.py:78
  165.2 2.0 %fusion.1 = bf16[1,128,4096]{2,1,0:T(8,128)(2,1)} fusion(bf16[32,4096]{1,0:T(8,128)(2,1)S(1)} %collective-permute-done.10, bf16[32,4096]{1,0:T(8,128)(2,1)S(1)} %collective-permute-done.9, pred[16,128]{1,0:T(8,128)(4,1)S(1)} %get-tuple-element.21, pred[16,128]{1,0:T(8,128)(4,1)S(1)} %get-tuple-element.20), kind=kOutput, calls=%fused_computation.3 | convolution fusion | flops 202248192 | bytes 1576960 | tf_op jit(solution)/shard_map/dot_general | solution.py:84
  (69 shorter events, 7.9 us)
Async XLA Ops:
  0.6 3.5 %copy-start.7 = (s32[1,128,2]{1,2,0:T(2,128)S(1)}, s32[1,128,2]{1,2,0:T(2,128)}, u32[]{:S(2)}) copy-start(s32[1,128,2]{1,2,0:T(2,128)} %param.9) | copy-start | bytes 3076
  0.6 3.2 %copy-start.2 = (bf16[1,128,4096]{2,1,0:T(8,128)(2,1)S(1)}, bf16[1,128,4096]{2,1,0:T(8,128)(2,1)}, u32[]{:S(2)}) copy-start(bf16[1,128,4096]{2,1,0:T(8,128)(2,1)} %param.10) | copy-start | bytes 3145732
  0.7 3.4 %copy-start.13 = (bf16[1,128,2]{1,2,0:T(2,128)(2,1)S(1)}, bf16[1,128,2]{1,2,0:T(2,128)(2,1)}, u32[]{:S(2)}) copy-start(bf16[1,128,2]{1,2,0:T(2,128)(2,1)} %param.8) | copy-start | bytes 1540
  2.3 2.0 %copy-start.3 = (pred[16,128]{1,0:T(8,128)(4,1)}, pred[16,128]{1,0:T(8,128)(4,1)S(1)}, u32[]{:S(2)}) copy-start(pred[16,128]{1,0:T(8,128)(4,1)S(1)} %get-tuple-element.18) | copy-start | bytes 6148
  2.3 2.0 %copy-start.5 = (pred[16,128]{1,0:T(8,128)(4,1)}, pred[16,128]{1,0:T(8,128)(4,1)S(1)}, u32[]{:S(2)}) copy-start(pred[16,128]{1,0:T(8,128)(4,1)S(1)} %get-tuple-element.19) | copy-start | bytes 6148
  4.5 2.1 %collective-permute-start = (bf16[1,32,8320]{2,1,0:T(8,128)(2,1)S(1)}, bf16[1,32,8320]{2,1,0:T(8,128)(2,1)S(1)}, u32[]{:S(2)}, u32[]{:S(2)}) collective-permute-start(bf16[1,32,8320]{2,1,0:T(8,128)(2,1)S(1)} %get-tuple-element.13), channel_id=1, source_target_pairs={{0,1},{1,0},{2,3},{3,2},{4,5},{5,4},{6,7},{7,6},{8,9},{9,8},{10,11... | collective-permute-start | bytes 1597448 | tf_op jit(solution)/shard_map/ppermute | solution.py:47
  6.7 26.7 %collective-permute-start.1 = (bf16[2,32,8320]{2,1,0:T(8,128)(2,1)S(1)}, bf16[2,32,8320]{2,1,0:T(8,128)(2,1)S(1)}, u32[]{:S(2)}, u32[]{:S(2)}) collective-permute-start(bf16[2,32,8320]{2,1,0:T(8,128)(2,1)S(1)} %pad_maximum_fusion.2), channel_id=1, source_target_pairs={{0,2},{1,3},{2,0},{3,1},{4,6},{5,7},{6,4},{7,5},{8,10},{9,11},{10,... | collective-permute-start | bytes 3194888 | tf_op jit(solution)/shard_map/ppermute | solution.py:47
  35.0 48.2 %collective-permute-start.2 = (bf16[4,32,8320]{2,1,0:T(8,128)(2,1)}, bf16[4,32,8320]{2,1,0:T(8,128)(2,1)}, u32[]{:S(2)}, u32[]{:S(2)}) collective-permute-start(bf16[4,32,8320]{2,1,0:T(8,128)(2,1)} %pad_maximum_fusion.1), channel_id=1, source_target_pairs={{0,4},{1,5},{2,6},{3,7},{4,0},{5,1},{6,2},{7,3},{8,12},{9,13},{10,... | collective-permute-start | bytes 6389768 | tf_op jit(solution)/shard_map/ppermute | solution.py:47
  36.8 5.5 %collective-permute-start.6 = (s32[128,2]{0,1:T(2,128)S(1)}, s32[128,2]{0,1:T(2,128)S(1)}, u32[]{:S(2)}, u32[]{:S(2)}) collective-permute-start(s32[128,2]{0,1:T(2,128)S(1)} %bitcast.102), channel_id=1, source_target_pairs={{8,0},{16,8},{24,16},{9,1},{17,9},{25,17},{10,2},{18,10},{26,18},{... | collective-permute-start | bytes 3080 | tf_op jit(solution)/shard_map/ppermute | solution.py:16
  42.3 44.4 %copy-start.9 = (pred[128]{0:T(512)(128)(4,1)}, pred[128]{0:T(512)(128)(4,1)S(1)}, u32[]{:S(2)}) copy-start(pred[128]{0:T(512)(128)(4,1)S(1)} %get-tuple-element.8) | copy-start | bytes 388
  119.3 2.5 %copy-start = (bf16[8,2,16,4096]{3,2,1,0:T(8,128)(2,1)S(1)}, bf16[8,2,16,4096]{3,2,1,0:T(8,128)(2,1)}, u32[]{:S(2)}) copy-start(bf16[8,2,16,4096]{3,2,1,0:T(8,128)(2,1)} %get-tuple-element.5) | copy-start | bytes 6291460
  119.3 4.2 %copy-start.1 = (bf16[8,2,16,4096]{3,2,1,0:T(8,128)(2,1)S(1)}, bf16[8,2,16,4096]{3,2,1,0:T(8,128)(2,1)}, u32[]{:S(2)}) copy-start(bf16[8,2,16,4096]{3,2,1,0:T(8,128)(2,1)} %get-tuple-element.4) | copy-start | bytes 6291460
  120.8 2.7 %collective-permute-start.3 = (bf16[4,32,4096]{2,1,0:T(8,128)(2,1)S(1)}, bf16[4,32,4096]{2,1,0:T(8,128)(2,1)S(1)}, u32[]{:S(2)}, u32[]{:S(2)}) collective-permute-start(bf16[4,32,4096]{2,1,0:T(8,128)(2,1)S(1)} %slice_bitcast_fusion.2), channel_id=1, source_target_pairs={{0,1},{1,0},{2,3},{3,2},{4,5},{5,4},{6,7},{7,6},{8,9},{9,8},{10,11... | collective-permute-start | bytes 3145736 | tf_op jit(solution)/shard_map/ppermute | solution.py:59
  121.9 3.3 %collective-permute-start.7 = (bf16[4,32,4096]{2,1,0:T(8,128)(2,1)S(1)}, bf16[4,32,4096]{2,1,0:T(8,128)(2,1)S(1)}, u32[]{:S(2)}, u32[]{:S(2)}) collective-permute-start(bf16[4,32,4096]{2,1,0:T(8,128)(2,1)S(1)} %slice_bitcast_fusion), channel_id=1, source_target_pairs={{0,1},{1,0},{2,3},{3,2},{4,5},{5,4},{6,7},{7,6},{8,9},{9,8},{10,11... | collective-permute-start | bytes 3145736 | tf_op jit(solution)/shard_map/ppermute | solution.py:59
  123.8 14.8 %collective-permute-start.4 = (bf16[2,32,4096]{2,1,0:T(8,128)(2,1)S(1)}, bf16[2,32,4096]{2,1,0:T(8,128)(2,1)S(1)}, u32[]{:S(2)}, u32[]{:S(2)}) collective-permute-start(bf16[2,32,4096]{2,1,0:T(8,128)(2,1)S(1)} %slice_bitcast_fusion.6), channel_id=1, source_target_pairs={{0,2},{1,3},{2,0},{3,1},{4,6},{5,7},{6,4},{7,5},{8,10},{9,11},{10,... | collective-permute-start | bytes 1572872 | tf_op jit(solution)/shard_map/ppermute | solution.py:59
  125.6 26.3 %copy-start.8 = (s32[128]{0:T(128)S(1)}, s32[128]{0:T(128)}, u32[]{:S(2)}) copy-start(s32[128]{0:T(128)} %add_reduce_fusion) | copy-start | bytes 1540
  125.6 26.3 %copy-start.10 = (pred[128]{0:T(512)(128)(4,1)S(1)}, pred[128]{0:T(512)(128)(4,1)}, u32[]{:S(2)}) copy-start(pred[128]{0:T(512)(128)(4,1)} %copy-done.9) | copy-start | bytes 388
  125.6 26.3 %copy-start.12 = (pred[128]{0:T(512)(128)(4,1)S(1)}, pred[128]{0:T(512)(128)(4,1)}, u32[]{:S(2)}) copy-start(pred[128]{0:T(512)(128)(4,1)} %copy-done.11) | copy-start | bytes 388
  125.6 26.3 %copy-start.4 = (pred[16,128]{1,0:T(8,128)(4,1)S(1)}, pred[16,128]{1,0:T(8,128)(4,1)}, u32[]{:S(2)}) copy-start(pred[16,128]{1,0:T(8,128)(4,1)} %copy-done.3) | copy-start | bytes 6148
  125.6 26.3 %copy-start.6 = (pred[16,128]{1,0:T(8,128)(4,1)S(1)}, pred[16,128]{1,0:T(8,128)(4,1)}, u32[]{:S(2)}) copy-start(pred[16,128]{1,0:T(8,128)(4,1)} %copy-done.5) | copy-start | bytes 6148
  125.6 23.4 %collective-permute-start.8 = (bf16[2,32,4096]{2,1,0:T(8,128)(2,1)S(1)}, bf16[2,32,4096]{2,1,0:T(8,128)(2,1)S(1)}, u32[]{:S(2)}, u32[]{:S(2)}) collective-permute-start(bf16[2,32,4096]{2,1,0:T(8,128)(2,1)S(1)} %slice_bitcast_fusion.4), channel_id=1, source_target_pairs={{0,2},{1,3},{2,0},{3,1},{4,6},{5,7},{6,4},{7,5},{8,10},{9,11},{10,... | collective-permute-start | bytes 1572872 | tf_op jit(solution)/shard_map/ppermute | solution.py:59
  138.8 13.1 %collective-permute-start.5 = (bf16[32,4096]{1,0:T(8,128)(2,1)S(1)}, bf16[32,4096]{1,0:T(8,128)(2,1)S(1)}, u32[]{:S(2)}, u32[]{:S(2)}) collective-permute-start(bf16[32,4096]{1,0:T(8,128)(2,1)S(1)} %slice_bitcast_fusion.10), channel_id=1, source_target_pairs={{0,4},{1,5},{2,6},{3,7},{4,0},{5,1},{6,2},{7,3},{8,12},{9,13},{10,... | collective-permute-start | bytes 786440 | tf_op jit(solution)/shard_map/ppermute | solution.py:68
  149.2 12.0 %collective-permute-start.10 = (bf16[32,4096]{1,0:T(8,128)(2,1)S(1)}, bf16[32,4096]{1,0:T(8,128)(2,1)S(1)}, u32[]{:S(2)}, u32[]{:S(2)}) collective-permute-start(bf16[32,4096]{1,0:T(8,128)(2,1)S(1)} %get-tuple-element.15), channel_id=1, source_target_pairs={{8,4},{9,5},{10,6},{11,7},{12,0},{13,1},{14,2},{15,3},{16,12},{17,... | collective-permute-start | bytes 786440 | tf_op jit(solution)/shard_map/ppermute | solution.py:79
  150.5 14.6 %collective-permute-start.9 = (bf16[32,4096]{1,0:T(8,128)(2,1)S(1)}, bf16[32,4096]{1,0:T(8,128)(2,1)S(1)}, u32[]{:S(2)}, u32[]{:S(2)}) collective-permute-start(bf16[32,4096]{1,0:T(8,128)(2,1)S(1)} %get-tuple-element.14), channel_id=1, source_target_pairs={{8,0},{9,1},{10,2},{11,3},{12,4},{13,5},{14,6},{15,7},{16,8},{17,9... | collective-permute-start | bytes 786440 | tf_op jit(solution)/shard_map/ppermute | solution.py:78
  (1 other events, 0.6 us)

commit v10 on v7

--- a/solution.py
+++ b/solution.py
@@ -39,34 +39,46 @@
     return jnp.dot(select.astype(rows.dtype), rows, preferred_element_type=jnp.float32).astype(rows.dtype)
 
 
-def halve_over_et(parts):
+def halve_over_et(parts, order, hook):
     n = lax.axis_size("et")
     me = lax.axis_index("et")
+    remaining = sorted(order)
     held = parts
-    bit = 1
-    while 2 * bit < n:
-        halves = held.reshape((held.shape[0] // 2, 2) + held.shape[1:])
+    for bit in order[:-1]:
+        lower = 1 << remaining.index(bit)
+        count = held.shape[0]
+        halves = held.reshape((count // (2 * lower), 2, lower) + held.shape[1:])
         side = (me // bit) % 2
-        keep = jnp.take(halves, side, axis=1)
-        give = jnp.take(halves, 1 - side, axis=1)
+        keep = jnp.take(halves, side, axis=1).reshape((count // 2,) + held.shape[1:])
+        give = jnp.take(halves, 1 - side, axis=1).reshape((count // 2,) + held.shape[1:])
         got = lax.ppermute(give, "et", [(i, i ^ bit) for i in range(n)])
         held = (keep.astype(jnp.float32) + got.astype(jnp.float32)).astype(jnp.bfloat16)
-        bit *= 2
+        held = hook(held)
+        hook = lambda value: value
+        remaining.remove(bit)
+    bit = order[-1]
     side = (me // bit) % 2
     return jnp.take(held, side, axis=0), jnp.take(held, 1 - side, axis=0), bit
 
 
-def reduce_to_owner(parts):
-    n = lax.axis_size("et")
-    keep, give, bit = halve_over_et(parts)
+def round_order(n, late):
+    bits = [1 << k for k in range(n.bit_length() - 1)]
+    if late in bits:
+        bits = [bit for bit in bits if bit != late] + [late]
+    return bits
+
+
+def reduce_to_owner(parts, order, hook):
+    n = lax.axis_size("et")
+    keep, give, bit = halve_over_et(parts, order, hook)
     got = lax.ppermute(give, "et", [(i, i ^ bit) for i in range(n)])
     return keep.astype(jnp.float32) + got.astype(jnp.float32)
 
 
-def reduce_to_previous(parts):
+def reduce_to_previous(parts, order, hook):
     n = lax.axis_size("et")
     stages = lax.axis_size("pipe")
-    keep, give, bit = halve_over_et(parts)
+    keep, give, bit = halve_over_et(parts, order, hook)
     to_same = [(stage * n + i, (stage - 1) * n + i) for stage in range(1, stages) for i in range(n)]
     to_other = [(stage * n + i, (stage - 1) * n + (i ^ bit)) for stage in range(1, stages) for i in range(n)]
     first = lax.ppermute(keep, ("pipe", "et"), to_same)
@@ -170,8 +182,11 @@
     )
     gathered = lax.all_gather(packed, "et", axis=0, tiled=True).reshape(n, E_WIN, MOST, 2 * width + TAIL)
     out_parts, grad_parts = expert_pass(gathered, gate_mats, up_mats, down_mats)
-    out_sums = reduce_to_owner(out_parts.reshape(n, E_WIN * MOST, width))
-    received = unpack(reduce_to_previous(grad_parts.reshape(n, E_WIN * MOST, width)), next_select)
+    same = lambda value: value
+    out_sums = reduce_to_owner(out_parts.reshape(n, E_WIN * MOST, width), round_order(n, n // 2), same)
+    received = unpack(
+        reduce_to_previous(grad_parts.reshape(n, E_WIN * MOST, width), round_order(n, 2), same), next_select
+    )
     out_share = unpack(out_sums, select)
     return (out_share[None], received[None])
 

time: 141 us -> 132 us (0.936)
  waiting for transfers between devices: 71.4 us -> 61.9 us
    ppermute x4, waiting for transfers between devices: 22.3 us -> 12.9 us  [halve_over_et(): got = lax.ppermute(give, 'et', [(i, i ^ bit) for i in range(n)])]
    ppermute x1, waiting for transfers between devices: 0.01 us -> 3.41 us  [reduce_to_owner(): got = lax.ppermute(give, 'et', [(i, i ^ bit) for i in range(n)])]
    ppermute x1, waiting for transfers between devices: 7.38 us -> 4 us  [reduce_to_previous(): second = lax.ppermute(give, ('pipe', 'et'), to_other)]
    select_n x4 -> x0, other arithmetic: 2.69 us -> none  [halve_over_et(): give = jnp.take(halves, 1 - side, axis=1)]
    reshape x0 -> x4, other arithmetic: none -> 2.69 us  [halve_over_et(): jnp.take(halves, 1 - side, axis=1).reshape((count // 2,) + held.shape[1:])]
  transfers between devices with their start and end apart: 9 -> 9, of which waited for: 7 -> 8; matrix products, arithmetic and copies ran while one was open for 3% -> 4% of each run, Pallas kernels for 0% -> 0%
where the time goes in v10:
time: 132 us; the launch traced here: 131 us
  waiting for transfers between devices  61.9 us (47%)
  Pallas kernels  32.6 us (25%)
  between operations  14.4 us (11%)
  starting transfers between devices  8.12 us (6%)
  other arithmetic  7.98 us (6%)
  matrix products  5.75 us (4%)
    all_gather x1, waiting for transfers between devices, per_device(): lax.all_gather(packed, 'et', axis=0, tiled=True)  32.8 us
    pallas_call x1, Pallas kernels, expert_pass(): pl.pallas_call(_expert_body, grid=(experts, steps), in_specs=[pl.BlockSpe...  32.6 us
    ppermute x4, waiting for transfers between devices, halve_over_et(): got = lax.ppermute(give, 'et', [(i, i ^ bit) for i in range(n)])  12.9 us
    ppermute x1, waiting for transfers between devices, shifted(): lax.ppermute(value, axis, [(source, source + steps) for source in range(f...  5.06 us
    ppermute x1, waiting for transfers between devices, reduce_to_previous(): second = lax.ppermute(give, ('pipe', 'et'), to_other)  4 us
    dot_general x2, matrix products, unpack(): lax.dot_general(select.astype(jnp.float32), slot_sums, (((0,), (0,)), (()...  4 us
    ppermute x1, waiting for transfers between devices, reduce_to_previous(): first = lax.ppermute(keep, ('pipe', 'et'), to_same)  3.68 us
    ppermute x1, waiting for transfers between devices, reduce_to_owner(): got = lax.ppermute(give, 'et', [(i, i ^ bit) for i in range(n)])  3.41 us
  transfers between devices with their start and end apart: 9, of which 8 were waited for; matrix products, arithmetic and copies ran while one was open for 4% of the time, Pallas kernels for 0%

profile of v10, /device:TPU:0, one launch (start us, length us, event | category | flops | bytes accessed | tf_op | source)
XLA Modules:
  0.0 131.3 jit_solution(7299568958478148525)
XLA Ops:
  7.2 0.8 fusion.32
  8.0 0.7 fusion.30
  9.6 1.5 %convolution_convert_fusion.2 = bf16[32,4096]{1,0:T(8,128)(2,1)S(1)} fusion(bf16[1,128,4096]{2,1,0:T(8,128)(2,1)} %param.18, pred[16,128]{1,0:T(8,128)(4,1)S(1)} %get-tuple-element.65, pred[16,128]{1,0:T(8,128)(4,1)S(1)} %get-tuple-element.64), kind=kOutput, calls=%fused_computation.4 | convolution fusion | flops 33689600 | bytes 1314816 | tf_op jit(solution)/shard_map/dot_general | solution.py:39
  11.7 0.8 pad_maximum_fusion
  12.5 1.3 collective-permute-start.3
  13.9 5.1 %collective-permute-done.3 = s32[128,2]{0,1:T(2,128)S(1)} collective-permute-done((s32[128,2]{0,1:T(2,128)S(1)}, s32[128,2]{0,1:T(2,128)S(1)}, u32[]{:S(2)}, u32[]{:S(2)}) %collective-permute-start.3) | collective-permute-done | bytes 1056 | tf_op jit(solution)/shard_map/ppermute | solution.py:16
  19.0 0.6 compare_reduce_fusion.1
  19.6 32.8 %all-gather.2.cloned.1.call-done = bf16[256,8320]{1,0:T(8,128)(2,1)} async-done(((bf16[32,8320]{1,0:T(8,128)(2,1)}), bf16[256,8320]{1,0:T(8,128)(2,1)}) %all-gather.2.cloned.1.call-update) | async-done | bytes 4259856 | tf_op jit(solution)/shard_map/all_gather | solution.py:183
  52.4 32.6 %shard_map.86 = (bf16[8,2,16,4096]{3,2,1,0:T(8,128)(2,1)}, bf16[8,2,16,4096]{3,2,1,0:T(8,128)(2,1)}) custom-call(bf16[8,2,16,8320]{3,2,1,0:T(8,128)(2,1)} %bitcast.106, bf16[8,2,16,8320]{3,2,1,0:T(8,128)(2,1)} %bitcast.107, bf16[8,2,16,8320]{3,2,1,0:T(8,128)(2,1)} %bitcast.108, bf16[2,4096,896]{2,1,0:T(8,128)(2,1)} %bitcast.109, ...), custom_call_target="tpu_custom_call" | custom-call | tf_op jit(solution)/shard_map/pallas_call | solution.py:142
  85.0 2.5 %select_bitcast_fusion.1 = bf16[4,32,4096]{2,1,0:T(8,128)(2,1)} fusion(bf16[4,2,1,32,4096]{4,3,1,0,2:T(8,128)(2,1)} %bitcast.118, s32[]{:T(128)S(6)} %select_n.139, pred[]{:T(512)S(6)} %and.109), kind=kLoop, calls=%fused_computation.21 | loop fusion | flops 524288 | bytes 2097157 | tf_op jit(solution)/shard_map/reshape | solution.py:53
  88.6 0.3 collective-permute-start.4
  88.9 1.4 %collective-permute-done = bf16[4,32,4096]{2,1,0:T(8,128)(2,1)S(1)} collective-permute-done((bf16[4,32,4096]{2,1,0:T(8,128)(2,1)}, bf16[4,32,4096]{2,1,0:T(8,128)(2,1)S(1)}, u32[]{:S(2)}, u32[]{:S(2)}) %collective-permute-start) | collective-permute-done | bytes 1048608 | tf_op jit(solution)/shard_map/ppermute | solution.py:54
  90.7 1.5 %collective-permute-start.1 = (bf16[2,32,4096]{2,1,0:T(8,128)(2,1)S(1)}, bf16[2,32,4096]{2,1,0:T(8,128)(2,1)S(1)}, u32[]{:S(2)}, u32[]{:S(2)}) collective-permute-start(bf16[2,32,4096]{2,1,0:T(8,128)(2,1)S(1)} %select_bitcast_fusion.3), channel_id=1, source_target_pairs={{0,2},{1,3},{2,0},{3,1},{4,6},{5,7},{6,4},{7,5},{8,10},{9,11},{10,... | collective-permute-start | bytes 1572872 | tf_op jit(solution)/shard_map/ppermute | solution.py:54
  92.2 0.3 fusion.2
  92.6 0.7 collective-permute-start.5
  93.4 11.5 %collective-permute-done.1 = bf16[2,32,4096]{2,1,0:T(8,128)(2,1)S(1)} collective-permute-done((bf16[2,32,4096]{2,1,0:T(8,128)(2,1)S(1)}, bf16[2,32,4096]{2,1,0:T(8,128)(2,1)S(1)}, u32[]{:S(2)}, u32[]{:S(2)}) %collective-permute-start.1) | collective-permute-done | bytes 524320 | tf_op jit(solution)/shard_map/ppermute | solution.py:54
  105.0 1.4 %collective-permute-start.2 = (bf16[32,4096]{1,0:T(8,128)(2,1)S(1)}, bf16[32,4096]{1,0:T(8,128)(2,1)S(1)}, u32[]{:S(2)}, u32[]{:S(2)}) collective-permute-start(bf16[32,4096]{1,0:T(8,128)(2,1)S(1)} %select_bitcast_fusion.6), channel_id=1, source_target_pairs={{0,4},{1,5},{2,6},{3,7},{4,0},{5,1},{6,2},{7,3},{8,12},{9,13},{10,... | collective-permute-start | bytes 786440 | tf_op jit(solution)/shard_map/ppermute | solution.py:74
  106.7 1.3 collective-permute-start.7
  108.0 1.3 collective-permute-start.6
  109.4 3.4 %collective-permute-done.2 = bf16[32,4096]{1,0:T(8,128)(2,1)S(1)} collective-permute-done((bf16[32,4096]{1,0:T(8,128)(2,1)S(1)}, bf16[32,4096]{1,0:T(8,128)(2,1)S(1)}, u32[]{:S(2)}, u32[]{:S(2)}) %collective-permute-start.2) | collective-permute-done | bytes 262176 | tf_op jit(solution)/shard_map/ppermute | solution.py:74
  112.8 2.0 %fusion = bf16[1,128,4096]{2,1,0:T(8,128)(2,1)} fusion(bf16[32,4096]{1,0:T(8,128)(2,1)S(1)} %collective-permute-done.2, bf16[2,32,4096]{2,1,0:T(8,128)(2,1)S(1)} %fusion.7, s32[]{:T(128)S(6)} %select_n.145, pred[]{:T(512)S(6)} %and.112, pred[16,128]{1,0:T(8,128)(4,1)S(1)} %copy-done.6, pred[16,128]{1,0:T(8,128)(4,1)S(1)} %copy-done.4), kind=kOutput, calls=%fused_computation.2 | convolution fusion | flops 202379264 | bytes 1576965 | tf_op jit(solution)/shard_map/dot_general | solution.py:90
  114.8 4.0 %collective-permute-done.7 = bf16[32,4096]{1,0:T(8,128)(2,1)S(1)} collective-permute-done((bf16[32,4096]{1,0:T(8,128)(2,1)S(1)}, bf16[32,4096]{1,0:T(8,128)(2,1)S(1)}, u32[]{:S(2)}, u32[]{:S(2)}) %collective-permute-start.7) | collective-permute-done | bytes 262176 | tf_op jit(solution)/shard_map/ppermute | solution.py:85
  118.8 3.7 %collective-permute-done.6 = bf16[32,4096]{1,0:T(8,128)(2,1)S(1)} collective-permute-done((bf16[32,4096]{1,0:T(8,128)(2,1)S(1)}, bf16[32,4096]{1,0:T(8,128)(2,1)S(1)}, u32[]{:S(2)}, u32[]{:S(2)}) %collective-permute-start.6) | collective-permute-done | bytes 262176 | tf_op jit(solution)/shard_map/ppermute | solution.py:84
  122.5 2.0 %fusion.1 = bf16[1,128,4096]{2,1,0:T(8,128)(2,1)} fusion(bf16[32,4096]{1,0:T(8,128)(2,1)S(1)} %collective-permute-done.7, bf16[32,4096]{1,0:T(8,128)(2,1)S(1)} %collective-permute-done.6, pred[16,128]{1,0:T(8,128)(4,1)S(1)} %get-tuple-element.67, pred[16,128]{1,0:T(8,128)(4,1)S(1)} %get-tuple-element.66), kind=kOutput, calls=%fused_computation.3 | convolution fusion | flops 202248192 | bytes 1576960 | tf_op jit(solution)/shard_map/dot_general | solution.py:90
  (55 shorter events, 3.6 us)
Async XLA Ops:
  7.2 3.9 %copy-start.2 = (bf16[1,128,4096]{2,1,0:T(8,128)(2,1)S(1)}, bf16[1,128,4096]{2,1,0:T(8,128)(2,1)}, u32[]{:S(2)}) copy-start(bf16[1,128,4096]{2,1,0:T(8,128)(2,1)} %param.15) | copy-start | bytes 3145732
  7.2 45.2 %all-gather.2.cloned.1.call-start = ((), (), s32[]{:S(2)}) async-start(), calls=%async_computation | async-start | bytes 4792320 | tf_op jit(solution)/shard_map/all_gather | solution.py:183
  9.5 1.8 %copy-start.3 = (pred[16,128]{1,0:T(8,128)(4,1)}, pred[16,128]{1,0:T(8,128)(4,1)S(1)}, u32[]{:S(2)}) copy-start(pred[16,128]{1,0:T(8,128)(4,1)S(1)} %get-tuple-element.64) | copy-start | bytes 6148
  9.5 1.8 %copy-start.5 = (pred[16,128]{1,0:T(8,128)(4,1)}, pred[16,128]{1,0:T(8,128)(4,1)S(1)}, u32[]{:S(2)}) copy-start(pred[16,128]{1,0:T(8,128)(4,1)S(1)} %get-tuple-element.65) | copy-start | bytes 6148
  9.6 3.0 %copy-start.7 = (s32[1,128,2]{1,2,0:T(2,128)S(1)}, s32[1,128,2]{1,2,0:T(2,128)}, u32[]{:S(2)}) copy-start(s32[1,128,2]{1,2,0:T(2,128)} %param.17) | copy-start | bytes 3076
  12.5 6.5 %collective-permute-start.3 = (s32[128,2]{0,1:T(2,128)S(1)}, s32[128,2]{0,1:T(2,128)S(1)}, u32[]{:S(2)}, u32[]{:S(2)}) collective-permute-start(s32[128,2]{0,1:T(2,128)S(1)} %bitcast.120), channel_id=1, source_target_pairs={{8,0},{16,8},{24,16},{9,1},{17,9},{25,17},{10,2},{18,10},{26,18},{... | collective-permute-start | bytes 3080 | tf_op jit(solution)/shard_map/ppermute | solution.py:16
  85.0 2.7 %copy-start.8 = (pred[128]{0:T(512)(128)(4,1)S(1)}, pred[128]{0:T(512)(128)(4,1)}, u32[]{:S(2)}) copy-start(pred[128]{0:T(512)(128)(4,1)} %get-tuple-element.56) | copy-start | bytes 388
  85.0 3.0 %copy-start.9 = (pred[128]{0:T(512)(128)(4,1)S(1)}, pred[128]{0:T(512)(128)(4,1)}, u32[]{:S(2)}) copy-start(pred[128]{0:T(512)(128)(4,1)} %get-tuple-element.57) | copy-start | bytes 388
  85.0 3.5 %copy-start = (bf16[8,2,16,4096]{3,2,1,0:T(8,128)(2,1)S(1)}, bf16[8,2,16,4096]{3,2,1,0:T(8,128)(2,1)}, u32[]{:S(2)}) copy-start(bf16[8,2,16,4096]{3,2,1,0:T(8,128)(2,1)} %get-tuple-element.9) | copy-start | bytes 6291460
  87.4 2.9 %collective-permute-start = (bf16[4,32,4096]{2,1,0:T(8,128)(2,1)}, bf16[4,32,4096]{2,1,0:T(8,128)(2,1)S(1)}, u32[]{:S(2)}, u32[]{:S(2)}) collective-permute-start(bf16[4,32,4096]{2,1,0:T(8,128)(2,1)} %select_bitcast_fusion.1), channel_id=1, source_target_pairs={{0,1},{1,0},{2,3},{3,2},{4,5},{5,4},{6,7},{7,6},{8,9},{9,8},{10,11... | collective-permute-start | bytes 3145736 | tf_op jit(solution)/shard_map/ppermute | solution.py:54
  88.3 2.0 %copy-start.1 = (bf16[8,2,16,4096]{3,2,1,0:T(8,128)(2,1)S(1)}, bf16[8,2,16,4096]{3,2,1,0:T(8,128)(2,1)}, u32[]{:S(2)}) copy-start(bf16[8,2,16,4096]{3,2,1,0:T(8,128)(2,1)} %get-tuple-element.8) | copy-start | bytes 6291460
  88.6 3.6 %collective-permute-start.4 = (bf16[4,32,4096]{2,1,0:T(8,128)(2,1)S(1)}, bf16[4,32,4096]{2,1,0:T(8,128)(2,1)S(1)}, u32[]{:S(2)}, u32[]{:S(2)}) collective-permute-start(bf16[4,32,4096]{2,1,0:T(8,128)(2,1)S(1)} %select_bitcast_fusion), channel_id=1, source_target_pairs={{0,1},{1,0},{2,3},{3,2},{4,5},{5,4},{6,7},{7,6},{8,9},{9,8},{10,11... | collective-permute-start | bytes 3145736 | tf_op jit(solution)/shard_map/ppermute | solution.py:54
  90.7 14.2 %collective-permute-start.1 = (bf16[2,32,4096]{2,1,0:T(8,128)(2,1)S(1)}, bf16[2,32,4096]{2,1,0:T(8,128)(2,1)S(1)}, u32[]{:S(2)}, u32[]{:S(2)}) collective-permute-start(bf16[2,32,4096]{2,1,0:T(8,128)(2,1)S(1)} %select_bitcast_fusion.3), channel_id=1, source_target_pairs={{0,2},{1,3},{2,0},{3,1},{4,6},{5,7},{6,4},{7,5},{8,10},{9,11},{10,... | collective-permute-start | bytes 1572872 | tf_op jit(solution)/shard_map/ppermute | solution.py:54
  92.6 20.2 %copy-start.4 = (pred[16,128]{1,0:T(8,128)(4,1)S(1)}, pred[16,128]{1,0:T(8,128)(4,1)}, u32[]{:S(2)}) copy-start(pred[16,128]{1,0:T(8,128)(4,1)} %copy-done.3) | copy-start | bytes 6148
  92.6 20.2 %copy-start.6 = (pred[16,128]{1,0:T(8,128)(4,1)S(1)}, pred[16,128]{1,0:T(8,128)(4,1)}, u32[]{:S(2)}) copy-start(pred[16,128]{1,0:T(8,128)(4,1)} %copy-done.5) | copy-start | bytes 6148
  92.6 13.9 %collective-permute-start.5 = (bf16[2,32,4096]{2,1,0:T(8,128)(2,1)S(1)}, bf16[2,32,4096]{2,1,0:T(8,128)(2,1)S(1)}, u32[]{:S(2)}, u32[]{:S(2)}) collective-permute-start(bf16[2,32,4096]{2,1,0:T(8,128)(2,1)S(1)} %select_bitcast_fusion.2), channel_id=1, source_target_pairs={{0,4},{1,5},{2,6},{3,7},{4,0},{5,1},{6,2},{7,3},{8,12},{9,13},{10,... | collective-permute-start | bytes 1572872 | tf_op jit(solution)/shard_map/ppermute | solution.py:54
  105.0 7.7 %collective-permute-start.2 = (bf16[32,4096]{1,0:T(8,128)(2,1)S(1)}, bf16[32,4096]{1,0:T(8,128)(2,1)S(1)}, u32[]{:S(2)}, u32[]{:S(2)}) collective-permute-start(bf16[32,4096]{1,0:T(8,128)(2,1)S(1)} %select_bitcast_fusion.6), channel_id=1, source_target_pairs={{0,4},{1,5},{2,6},{3,7},{4,0},{5,1},{6,2},{7,3},{8,12},{9,13},{10,... | collective-permute-start | bytes 786440 | tf_op jit(solution)/shard_map/ppermute | solution.py:74
  106.7 12.0 %collective-permute-start.7 = (bf16[32,4096]{1,0:T(8,128)(2,1)S(1)}, bf16[32,4096]{1,0:T(8,128)(2,1)S(1)}, u32[]{:S(2)}, u32[]{:S(2)}) collective-permute-start(bf16[32,4096]{1,0:T(8,128)(2,1)S(1)} %get-tuple-element.61), channel_id=1, source_target_pairs={{8,2},{9,3},{10,0},{11,1},{12,6},{13,7},{14,4},{15,5},{16,10},{17,... | collective-permute-start | bytes 786440 | tf_op jit(solution)/shard_map/ppermute | solution.py:85
  108.0 14.4 %collective-permute-start.6 = (bf16[32,4096]{1,0:T(8,128)(2,1)S(1)}, bf16[32,4096]{1,0:T(8,128)(2,1)S(1)}, u32[]{:S(2)}, u32[]{:S(2)}) collective-permute-start(bf16[32,4096]{1,0:T(8,128)(2,1)S(1)} %get-tuple-element.60), channel_id=1, source_target_pairs={{8,0},{9,1},{10,2},{11,3},{12,4},{13,5},{14,6},{15,7},{16,8},{17,9... | collective-permute-start | bytes 786440 | tf_op jit(solution)/shard_map/ppermute | solution.py:84
Sparse Core Ops, SparseCore 0:
  12.6 39.6 all-gather.1

commit v11 on v10

--- a/solution.py
+++ b/solution.py
@@ -136,7 +136,7 @@
     n, experts, most, packed_width = gathered.shape
     width = gate_mats.shape[1]
     shard = gate_mats.shape[2]
-    tile = 128 if shard % 128 == 0 else shard
+    tile = shard
     steps = shard // tile
     rows = n * most
     return pl.pallas_call(

time: 132 us -> 129 us (0.977)
  Pallas kernels: 32.6 us -> 30.1 us
    pallas_call x1, Pallas kernels: 32.6 us -> 30.1 us  [expert_pass(): pl.pallas_call(_expert_body, grid=(experts, steps), in_specs=[pl.BlockSpe...]
where the time goes in v11:
time: 129 us
  waiting for transfers between devices  61.9 us (48%)
  Pallas kernels  30.1 us (23%)
  between operations  14.4 us (11%)
  starting transfers between devices  8.11 us (6%)
  other arithmetic  7.98 us (6%)
  matrix products  5.75 us (4%)
    all_gather x1, waiting for transfers between devices, per_device(): lax.all_gather(packed, 'et', axis=0, tiled=True)  32.8 us
    pallas_call x1, Pallas kernels, expert_pass(): pl.pallas_call(_expert_body, grid=(experts, steps), in_specs=[pl.BlockSpe...  30.1 us
    ppermute x4, waiting for transfers between devices, halve_over_et(): got = lax.ppermute(give, 'et', [(i, i ^ bit) for i in range(n)])  12.9 us
    ppermute x1, waiting for transfers between devices, shifted(): lax.ppermute(value, axis, [(source, source + steps) for source in range(f...  5.06 us
    ppermute x1, waiting for transfers between devices, reduce_to_previous(): second = lax.ppermute(give, ('pipe', 'et'), to_other)  4 us
    dot_general x2, matrix products, unpack(): lax.dot_general(select.astype(jnp.float32), slot_sums, (((0,), (0,)), (()...  4 us
    ppermute x1, waiting for transfers between devices, reduce_to_previous(): first = lax.ppermute(keep, ('pipe', 'et'), to_same)  3.68 us
    ppermute x1, waiting for transfers between devices, reduce_to_owner(): got = lax.ppermute(give, 'et', [(i, i ^ bit) for i in range(n)])  3.41 us
  transfers between devices with their start and end apart: 9, of which 8 were waited for; matrix products, arithmetic and copies ran while one was open for 4% of the time, Pallas kernels for 0%

profile of v11, /device:TPU:0, one launch (start us, length us, event | category | flops | bytes accessed | tf_op | source)
XLA Modules:
  0.0 128.8 jit_solution(14204813449300003080)
XLA Ops:
  7.2 0.8 fusion.32
  8.0 0.7 fusion.30
  9.6 1.5 %convolution_convert_fusion.2 = bf16[32,4096]{1,0:T(8,128)(2,1)S(1)} fusion(bf16[1,128,4096]{2,1,0:T(8,128)(2,1)} %param.18, pred[16,128]{1,0:T(8,128)(4,1)S(1)} %get-tuple-element.65, pred[16,128]{1,0:T(8,128)(4,1)S(1)} %get-tuple-element.64), kind=kOutput, calls=%fused_computation.4 | convolution fusion | flops 33689600 | bytes 1314816 | tf_op jit(solution)/shard_map/dot_general | solution.py:39
  11.7 0.8 pad_maximum_fusion
  12.5 1.3 %collective-permute-start.3 = (s32[128,2]{0,1:T(2,128)S(1)}, s32[128,2]{0,1:T(2,128)S(1)}, u32[]{:S(2)}, u32[]{:S(2)}) collective-permute-start(s32[128,2]{0,1:T(2,128)S(1)} %bitcast.120), channel_id=1, source_target_pairs={{8,0},{16,8},{24,16},{9,1},{17,9},{25,17},{10,2},{18,10},{26,18},{... | collective-permute-start | bytes 3080 | tf_op jit(solution)/shard_map/ppermute | solution.py:16
  13.9 5.1 %collective-permute-done.3 = s32[128,2]{0,1:T(2,128)S(1)} collective-permute-done((s32[128,2]{0,1:T(2,128)S(1)}, s32[128,2]{0,1:T(2,128)S(1)}, u32[]{:S(2)}, u32[]{:S(2)}) %collective-permute-start.3) | collective-permute-done | bytes 1056 | tf_op jit(solution)/shard_map/ppermute | solution.py:16
  19.0 0.6 compare_reduce_fusion.1
  19.6 32.8 %all-gather.2.cloned.1.call-done = bf16[256,8320]{1,0:T(8,128)(2,1)} async-done(((bf16[32,8320]{1,0:T(8,128)(2,1)}), bf16[256,8320]{1,0:T(8,128)(2,1)}) %all-gather.2.cloned.1.call-update) | async-done | bytes 4259856 | tf_op jit(solution)/shard_map/all_gather | solution.py:183
  52.4 30.1 %shard_map.86 = (bf16[8,2,16,4096]{3,2,1,0:T(8,128)(2,1)}, bf16[8,2,16,4096]{3,2,1,0:T(8,128)(2,1)}) custom-call(bf16[8,2,16,8320]{3,2,1,0:T(8,128)(2,1)} %bitcast.106, bf16[8,2,16,8320]{3,2,1,0:T(8,128)(2,1)} %bitcast.107, bf16[8,2,16,8320]{3,2,1,0:T(8,128)(2,1)} %bitcast.108, bf16[2,4096,896]{2,1,0:T(8,128)(2,1)} %bitcast.109, ...), custom_call_target="tpu_custom_call" | custom-call | tf_op jit(solution)/shard_map/pallas_call | solution.py:142
  82.5 2.5 %select_bitcast_fusion.1 = bf16[4,32,4096]{2,1,0:T(8,128)(2,1)} fusion(bf16[4,2,1,32,4096]{4,3,1,0,2:T(8,128)(2,1)} %bitcast.118, s32[]{:T(128)S(6)} %select_n.139, pred[]{:T(512)S(6)} %and.109), kind=kLoop, calls=%fused_computation.21 | loop fusion | flops 524288 | bytes 2097157 | tf_op jit(solution)/shard_map/reshape | solution.py:53
  86.2 0.3 collective-permute-start.4
  86.5 1.4 %collective-permute-done = bf16[4,32,4096]{2,1,0:T(8,128)(2,1)S(1)} collective-permute-done((bf16[4,32,4096]{2,1,0:T(8,128)(2,1)}, bf16[4,32,4096]{2,1,0:T(8,128)(2,1)S(1)}, u32[]{:S(2)}, u32[]{:S(2)}) %collective-permute-start) | collective-permute-done | bytes 1048608 | tf_op jit(solution)/shard_map/ppermute | solution.py:54
  87.8 0.3 fusion.3
  88.2 1.5 %collective-permute-start.1 = (bf16[2,32,4096]{2,1,0:T(8,128)(2,1)S(1)}, bf16[2,32,4096]{2,1,0:T(8,128)(2,1)S(1)}, u32[]{:S(2)}, u32[]{:S(2)}) collective-permute-start(bf16[2,32,4096]{2,1,0:T(8,128)(2,1)S(1)} %select_bitcast_fusion.3), channel_id=1, source_target_pairs={{0,2},{1,3},{2,0},{3,1},{4,6},{5,7},{6,4},{7,5},{8,10},{9,11},{10,... | collective-permute-start | bytes 1572872 | tf_op jit(solution)/shard_map/ppermute | solution.py:54
  90.2 0.7 collective-permute-start.5
  90.9 11.5 %collective-permute-done.1 = bf16[2,32,4096]{2,1,0:T(8,128)(2,1)S(1)} collective-permute-done((bf16[2,32,4096]{2,1,0:T(8,128)(2,1)S(1)}, bf16[2,32,4096]{2,1,0:T(8,128)(2,1)S(1)}, u32[]{:S(2)}, u32[]{:S(2)}) %collective-permute-start.1) | collective-permute-done | bytes 524320 | tf_op jit(solution)/shard_map/ppermute | solution.py:54
  102.6 1.4 %collective-permute-start.2 = (bf16[32,4096]{1,0:T(8,128)(2,1)S(1)}, bf16[32,4096]{1,0:T(8,128)(2,1)S(1)}, u32[]{:S(2)}, u32[]{:S(2)}) collective-permute-start(bf16[32,4096]{1,0:T(8,128)(2,1)S(1)} %select_bitcast_fusion.6), channel_id=1, source_target_pairs={{0,4},{1,5},{2,6},{3,7},{4,0},{5,1},{6,2},{7,3},{8,12},{9,13},{10,... | collective-permute-start | bytes 786440 | tf_op jit(solution)/shard_map/ppermute | solution.py:74
  104.3 1.3 %collective-permute-start.7 = (bf16[32,4096]{1,0:T(8,128)(2,1)S(1)}, bf16[32,4096]{1,0:T(8,128)(2,1)S(1)}, u32[]{:S(2)}, u32[]{:S(2)}) collective-permute-start(bf16[32,4096]{1,0:T(8,128)(2,1)S(1)} %get-tuple-element.61), channel_id=1, source_target_pairs={{8,2},{9,3},{10,0},{11,1},{12,6},{13,7},{14,4},{15,5},{16,10},{17,... | collective-permute-start | bytes 786440 | tf_op jit(solution)/shard_map/ppermute | solution.py:85
  105.6 1.3 %collective-permute-start.6 = (bf16[32,4096]{1,0:T(8,128)(2,1)S(1)}, bf16[32,4096]{1,0:T(8,128)(2,1)S(1)}, u32[]{:S(2)}, u32[]{:S(2)}) collective-permute-start(bf16[32,4096]{1,0:T(8,128)(2,1)S(1)} %get-tuple-element.60), channel_id=1, source_target_pairs={{8,0},{9,1},{10,2},{11,3},{12,4},{13,5},{14,6},{15,7},{16,8},{17,9... | collective-permute-start | bytes 786440 | tf_op jit(solution)/shard_map/ppermute | solution.py:84
  106.9 3.4 %collective-permute-done.2 = bf16[32,4096]{1,0:T(8,128)(2,1)S(1)} collective-permute-done((bf16[32,4096]{1,0:T(8,128)(2,1)S(1)}, bf16[32,4096]{1,0:T(8,128)(2,1)S(1)}, u32[]{:S(2)}, u32[]{:S(2)}) %collective-permute-start.2) | collective-permute-done | bytes 262176 | tf_op jit(solution)/shard_map/ppermute | solution.py:74
  110.3 2.0 %fusion = bf16[1,128,4096]{2,1,0:T(8,128)(2,1)} fusion(bf16[32,4096]{1,0:T(8,128)(2,1)S(1)} %collective-permute-done.2, bf16[2,32,4096]{2,1,0:T(8,128)(2,1)S(1)} %fusion.7, s32[]{:T(128)S(6)} %select_n.145, pred[]{:T(512)S(6)} %and.112, pred[16,128]{1,0:T(8,128)(4,1)S(1)} %copy-done.6, pred[16,128]{1,0:T(8,128)(4,1)S(1)} %copy-done.4), kind=kOutput, calls=%fused_computation.2 | convolution fusion | flops 202379264 | bytes 1576965 | tf_op jit(solution)/shard_map/dot_general | solution.py:90
  112.3 4.0 %collective-permute-done.7 = bf16[32,4096]{1,0:T(8,128)(2,1)S(1)} collective-permute-done((bf16[32,4096]{1,0:T(8,128)(2,1)S(1)}, bf16[32,4096]{1,0:T(8,128)(2,1)S(1)}, u32[]{:S(2)}, u32[]{:S(2)}) %collective-permute-start.7) | collective-permute-done | bytes 262176 | tf_op jit(solution)/shard_map/ppermute | solution.py:85
  116.3 3.7 %collective-permute-done.6 = bf16[32,4096]{1,0:T(8,128)(2,1)S(1)} collective-permute-done((bf16[32,4096]{1,0:T(8,128)(2,1)S(1)}, bf16[32,4096]{1,0:T(8,128)(2,1)S(1)}, u32[]{:S(2)}, u32[]{:S(2)}) %collective-permute-start.6) | collective-permute-done | bytes 262176 | tf_op jit(solution)/shard_map/ppermute | solution.py:84
  120.0 2.0 %fusion.1 = bf16[1,128,4096]{2,1,0:T(8,128)(2,1)} fusion(bf16[32,4096]{1,0:T(8,128)(2,1)S(1)} %collective-permute-done.7, bf16[32,4096]{1,0:T(8,128)(2,1)S(1)} %collective-permute-done.6, pred[16,128]{1,0:T(8,128)(4,1)S(1)} %get-tuple-element.67, pred[16,128]{1,0:T(8,128)(4,1)S(1)} %get-tuple-element.66), kind=kOutput, calls=%fused_computation.3 | convolution fusion | flops 202248192 | bytes 1576960 | tf_op jit(solution)/shard_map/dot_general | solution.py:90
  (55 shorter events, 3.6 us)
Async XLA Ops:
  7.2 3.9 %copy-start.2 = (bf16[1,128,4096]{2,1,0:T(8,128)(2,1)S(1)}, bf16[1,128,4096]{2,1,0:T(8,128)(2,1)}, u32[]{:S(2)}) copy-start(bf16[1,128,4096]{2,1,0:T(8,128)(2,1)} %param.15) | copy-start | bytes 3145732
  7.2 45.2 %all-gather.2.cloned.1.call-start = ((), (), s32[]{:S(2)}) async-start(), calls=%async_computation | async-start | bytes 4792320 | tf_op jit(solution)/shard_map/all_gather | solution.py:183
  9.5 1.8 %copy-start.3 = (pred[16,128]{1,0:T(8,128)(4,1)}, pred[16,128]{1,0:T(8,128)(4,1)S(1)}, u32[]{:S(2)}) copy-start(pred[16,128]{1,0:T(8,128)(4,1)S(1)} %get-tuple-element.64) | copy-start | bytes 6148
  9.5 1.8 %copy-start.5 = (pred[16,128]{1,0:T(8,128)(4,1)}, pred[16,128]{1,0:T(8,128)(4,1)S(1)}, u32[]{:S(2)}) copy-start(pred[16,128]{1,0:T(8,128)(4,1)S(1)} %get-tuple-element.65) | copy-start | bytes 6148
  9.6 3.0 %copy-start.7 = (s32[1,128,2]{1,2,0:T(2,128)S(1)}, s32[1,128,2]{1,2,0:T(2,128)}, u32[]{:S(2)}) copy-start(s32[1,128,2]{1,2,0:T(2,128)} %param.17) | copy-start | bytes 3076
  12.5 6.5 %collective-permute-start.3 = (s32[128,2]{0,1:T(2,128)S(1)}, s32[128,2]{0,1:T(2,128)S(1)}, u32[]{:S(2)}, u32[]{:S(2)}) collective-permute-start(s32[128,2]{0,1:T(2,128)S(1)} %bitcast.120), channel_id=1, source_target_pairs={{8,0},{16,8},{24,16},{9,1},{17,9},{25,17},{10,2},{18,10},{26,18},{... | collective-permute-start | bytes 3080 | tf_op jit(solution)/shard_map/ppermute | solution.py:16
  82.5 2.7 %copy-start.8 = (pred[128]{0:T(512)(128)(4,1)S(1)}, pred[128]{0:T(512)(128)(4,1)}, u32[]{:S(2)}) copy-start(pred[128]{0:T(512)(128)(4,1)} %get-tuple-element.56) | copy-start | bytes 388
  82.5 3.0 %copy-start.9 = (pred[128]{0:T(512)(128)(4,1)S(1)}, pred[128]{0:T(512)(128)(4,1)}, u32[]{:S(2)}) copy-start(pred[128]{0:T(512)(128)(4,1)} %get-tuple-element.57) | copy-start | bytes 388
  82.5 3.5 %copy-start = (bf16[8,2,16,4096]{3,2,1,0:T(8,128)(2,1)S(1)}, bf16[8,2,16,4096]{3,2,1,0:T(8,128)(2,1)}, u32[]{:S(2)}) copy-start(bf16[8,2,16,4096]{3,2,1,0:T(8,128)(2,1)} %get-tuple-element.9) | copy-start | bytes 6291460
  85.0 2.9 %collective-permute-start = (bf16[4,32,4096]{2,1,0:T(8,128)(2,1)}, bf16[4,32,4096]{2,1,0:T(8,128)(2,1)S(1)}, u32[]{:S(2)}, u32[]{:S(2)}) collective-permute-start(bf16[4,32,4096]{2,1,0:T(8,128)(2,1)} %select_bitcast_fusion.1), channel_id=1, source_target_pairs={{0,1},{1,0},{2,3},{3,2},{4,5},{5,4},{6,7},{7,6},{8,9},{9,8},{10,11... | collective-permute-start | bytes 3145736 | tf_op jit(solution)/shard_map/ppermute | solution.py:54
  85.8 2.0 %copy-start.1 = (bf16[8,2,16,4096]{3,2,1,0:T(8,128)(2,1)S(1)}, bf16[8,2,16,4096]{3,2,1,0:T(8,128)(2,1)}, u32[]{:S(2)}) copy-start(bf16[8,2,16,4096]{3,2,1,0:T(8,128)(2,1)} %get-tuple-element.8) | copy-start | bytes 6291460
  86.2 3.6 %collective-permute-start.4 = (bf16[4,32,4096]{2,1,0:T(8,128)(2,1)S(1)}, bf16[4,32,4096]{2,1,0:T(8,128)(2,1)S(1)}, u32[]{:S(2)}, u32[]{:S(2)}) collective-permute-start(bf16[4,32,4096]{2,1,0:T(8,128)(2,1)S(1)} %select_bitcast_fusion), channel_id=1, source_target_pairs={{0,1},{1,0},{2,3},{3,2},{4,5},{5,4},{6,7},{7,6},{8,9},{9,8},{10,11... | collective-permute-start | bytes 3145736 | tf_op jit(solution)/shard_map/ppermute | solution.py:54
  88.2 14.2 %collective-permute-start.1 = (bf16[2,32,4096]{2,1,0:T(8,128)(2,1)S(1)}, bf16[2,32,4096]{2,1,0:T(8,128)(2,1)S(1)}, u32[]{:S(2)}, u32[]{:S(2)}) collective-permute-start(bf16[2,32,4096]{2,1,0:T(8,128)(2,1)S(1)} %select_bitcast_fusion.3), channel_id=1, source_target_pairs={{0,2},{1,3},{2,0},{3,1},{4,6},{5,7},{6,4},{7,5},{8,10},{9,11},{10,... | collective-permute-start | bytes 1572872 | tf_op jit(solution)/shard_map/ppermute | solution.py:54
  90.2 20.2 %copy-start.4 = (pred[16,128]{1,0:T(8,128)(4,1)S(1)}, pred[16,128]{1,0:T(8,128)(4,1)}, u32[]{:S(2)}) copy-start(pred[16,128]{1,0:T(8,128)(4,1)} %copy-done.3) | copy-start | bytes 6148
  90.2 20.1 %copy-start.6 = (pred[16,128]{1,0:T(8,128)(4,1)S(1)}, pred[16,128]{1,0:T(8,128)(4,1)}, u32[]{:S(2)}) copy-start(pred[16,128]{1,0:T(8,128)(4,1)} %copy-done.5) | copy-start | bytes 6148
  90.2 13.9 %collective-permute-start.5 = (bf16[2,32,4096]{2,1,0:T(8,128)(2,1)S(1)}, bf16[2,32,4096]{2,1,0:T(8,128)(2,1)S(1)}, u32[]{:S(2)}, u32[]{:S(2)}) collective-permute-start(bf16[2,32,4096]{2,1,0:T(8,128)(2,1)S(1)} %select_bitcast_fusion.2), channel_id=1, source_target_pairs={{0,4},{1,5},{2,6},{3,7},{4,0},{5,1},{6,2},{7,3},{8,12},{9,13},{10,... | collective-permute-start | bytes 1572872 | tf_op jit(solution)/shard_map/ppermute | solution.py:54
  102.6 7.7 %collective-permute-start.2 = (bf16[32,4096]{1,0:T(8,128)(2,1)S(1)}, bf16[32,4096]{1,0:T(8,128)(2,1)S(1)}, u32[]{:S(2)}, u32[]{:S(2)}) collective-permute-start(bf16[32,4096]{1,0:T(8,128)(2,1)S(1)} %select_bitcast_fusion.6), channel_id=1, source_target_pairs={{0,4},{1,5},{2,6},{3,7},{4,0},{5,1},{6,2},{7,3},{8,12},{9,13},{10,... | collective-permute-start | bytes 786440 | tf_op jit(solution)/shard_map/ppermute | solution.py:74
  104.3 12.0 %collective-permute-start.7 = (bf16[32,4096]{1,0:T(8,128)(2,1)S(1)}, bf16[32,4096]{1,0:T(8,128)(2,1)S(1)}, u32[]{:S(2)}, u32[]{:S(2)}) collective-permute-start(bf16[32,4096]{1,0:T(8,128)(2,1)S(1)} %get-tuple-element.61), channel_id=1, source_target_pairs={{8,2},{9,3},{10,0},{11,1},{12,6},{13,7},{14,4},{15,5},{16,10},{17,... | collective-permute-start | bytes 786440 | tf_op jit(solution)/shard_map/ppermute | solution.py:85
  105.6 14.4 %collective-permute-start.6 = (bf16[32,4096]{1,0:T(8,128)(2,1)S(1)}, bf16[32,4096]{1,0:T(8,128)(2,1)S(1)}, u32[]{:S(2)}, u32[]{:S(2)}) collective-permute-start(bf16[32,4096]{1,0:T(8,128)(2,1)S(1)} %get-tuple-element.60), channel_id=1, source_target_pairs={{8,0},{9,1},{10,2},{11,3},{12,4},{13,5},{14,6},{15,7},{16,8},{17,9... | collective-permute-start | bytes 786440 | tf_op jit(solution)/shard_map/ppermute | solution.py:84
Sparse Core Ops, SparseCore 0:
  12.6 39.6 all-gather.1

commit v12 on v11

--- a/solution.py
+++ b/solution.py
@@ -39,6 +39,28 @@
     return jnp.dot(select.astype(rows.dtype), rows, preferred_element_type=jnp.float32).astype(rows.dtype)
 
 
+def swap(value, bit):
+    n = lax.axis_size("et")
+    return lax.ppermute(value, "et", [(i, i ^ bit) for i in range(n)])
+
+
+def gather_over_et(packed):
+    n = lax.axis_size("et")
+    if n == 8:
+        pair = jnp.stack([packed, swap(packed, 1)])
+        across_x = swap(pair, 2)
+        across_y = swap(pair, 4)
+        last_x = swap(across_y[0], 2)
+        last_y = swap(across_x[1], 4)
+        return jnp.concatenate([pair, across_x, across_y, last_x[None], last_y[None]], axis=0)
+    held = packed[None]
+    bit = 1
+    while bit < n:
+        held = jnp.concatenate([held, swap(held, bit)], axis=0)
+        bit *= 2
+    return held
+
+
 def halve_over_et(parts, order, hook):
     n = lax.axis_size("et")
     me = lax.axis_index("et")
@@ -48,17 +70,15 @@
         lower = 1 << remaining.index(bit)
         count = held.shape[0]
         halves = held.reshape((count // (2 * lower), 2, lower) + held.shape[1:])
-        side = (me // bit) % 2
-        keep = jnp.take(halves, side, axis=1).reshape((count // 2,) + held.shape[1:])
-        give = jnp.take(halves, 1 - side, axis=1).reshape((count // 2,) + held.shape[1:])
+        keep = halves[:, 0].reshape((count // 2,) + held.shape[1:])
+        give = halves[:, 1].reshape((count // 2,) + held.shape[1:])
         got = lax.ppermute(give, "et", [(i, i ^ bit) for i in range(n)])
         held = (keep.astype(jnp.float32) + got.astype(jnp.float32)).astype(jnp.bfloat16)
         held = hook(held)
         hook = lambda value: value
         remaining.remove(bit)
     bit = order[-1]
-    side = (me // bit) % 2
-    return jnp.take(held, side, axis=0), jnp.take(held, 1 - side, axis=0), bit
+    return held[0], held[1], bit
 
 
 def round_order(n, late):
@@ -180,7 +200,7 @@
     packed = jnp.concatenate(
         [pick_rows(select, local_rows), pick_rows(select, local_grads), weight_cols], axis=1
     )
-    gathered = lax.all_gather(packed, "et", axis=0, tiled=True).reshape(n, E_WIN, MOST, 2 * width + TAIL)
+    gathered = gather_over_et(packed).reshape(n, E_WIN, MOST, 2 * width + TAIL)
     out_parts, grad_parts = expert_pass(gathered, gate_mats, up_mats, down_mats)
     same = lambda value: value
     out_sums = reduce_to_owner(out_parts.reshape(n, E_WIN * MOST, width), round_order(n, n // 2), same)

time: 129 us -> 122 us (0.946)
  between operations: 14.4 us -> 1.01 us
  local copies, waits for them, and re-layouts: 0.58 us -> 8.4 us
  starting transfers between devices: 8.11 us -> 13.1 us
  waiting for transfers between devices: 61.9 us -> 58 us
  other arithmetic: 7.98 us -> 5.12 us
    all_gather x1 -> x0, waiting for transfers between devices: 32.8 us -> none  [per_device(): lax.all_gather(packed, 'et', axis=0, tiled=True)]
    ppermute x0 -> x5, waiting for transfers between devices: none -> 29.5 us  [swap(): return lax.ppermute(value, 'et', [(i, i ^ bit) for i in range(n)])]
    ppermute x0 -> x5, starting transfers between devices: none -> 5.82 us  [swap(): return lax.ppermute(value, 'et', [(i, i ^ bit) for i in range(n)])]
    unnamed x20 -> x33, local copies, waits for them, and re-layouts: 0.05 us -> 5.3 us
    reshape x4 -> x0, other arithmetic: 2.69 us -> none  [halve_over_et(): jnp.take(halves, 1 - side, axis=1).reshape((count // 2,) + held.shape[1:])]
    another operation x0 -> x4, local copies, waits for them, and re-layouts: none -> 1.61 us  [halve_over_et(): give = halves[:, 1].reshape((count // 2,) + held.shape[1:])]
    sub x4, other arithmetic: 0.42 us -> 1.83 us  [local_slots(): positions = jnp.cumsum(routed.astype(jnp.int32), dtype=jnp.int32) - 1]
  transfers between devices with their start and end apart: 9 -> 13, of which waited for: 8 -> 10; matrix products, arithmetic and copies ran while one was open for 4% -> 9% of each run, Pallas kernels for 0% -> 0%
where the time goes in v12:
time: 122 us
  waiting for transfers between devices  58 us (48%)
  Pallas kernels  30.1 us (25%)
  starting transfers between devices  13.1 us (11%)
  local copies, waits for them, and re-layouts  8.4 us (7%)
  matrix products  5.75 us (5%)
  other arithmetic  5.12 us (4%)
    pallas_call x1, Pallas kernels, expert_pass(): pl.pallas_call(_expert_body, grid=(experts, steps), in_specs=[pl.BlockSpe...  30.1 us
    ppermute x5, waiting for transfers between devices, swap(): return lax.ppermute(value, 'et', [(i, i ^ bit) for i in range(n)])  29.5 us
    ppermute x4, waiting for transfers between devices, halve_over_et(): got = lax.ppermute(give, 'et', [(i, i ^ bit) for i in range(n)])  13.3 us
    ppermute x5, starting transfers between devices, swap(): return lax.ppermute(value, 'et', [(i, i ^ bit) for i in range(n)])  5.82 us
    unnamed x33, local copies, waits for them, and re-layouts  5.3 us
    ppermute x1, waiting for transfers between devices, reduce_to_previous(): second = lax.ppermute(give, ('pipe', 'et'), to_other)  4.74 us
    dot_general x2, matrix products, unpack(): lax.dot_general(select.astype(jnp.float32), slot_sums, (((0,), (0,)), (()...  4 us
    ppermute x1, waiting for transfers between devices, shifted(): lax.ppermute(value, axis, [(source, source + steps) for source in range(f...  3.92 us
  transfers between devices with their start and end apart: 13, of which 10 were waited for; matrix products, arithmetic and copies ran while one was open for 9% of the time, Pallas kernels for 0%

profile of v12, /device:TPU:0, one launch (start us, length us, event | category | flops | bytes accessed | tf_op | source)
XLA Modules:
  0.0 121.5 jit_solution(310654476435901483)
XLA Ops:
  2.3 1.5 %convolution_convert_fusion.3 = bf16[32,4096]{1,0:T(8,128)(2,1)S(1)} fusion(bf16[1,128,4096]{2,1,0:T(8,128)(2,1)} %param.7, pred[16,128]{1,0:T(8,128)(4,1)S(1)} %get-tuple-element.19, pred[16,128]{1,0:T(8,128)(4,1)S(1)} %get-tuple-element.18), kind=kOutput, calls=%fused_computation.5 | convolution fusion | flops 33689600 | bytes 1314816 | tf_op jit(solution)/shard_map/dot_general | solution.py:39
  5.0 1.3 %collective-permute-start.8 = (s32[128,2]{0,1:T(2,128)S(1)}, s32[128,2]{0,1:T(2,128)S(1)}, u32[]{:S(2)}, u32[]{:S(2)}) collective-permute-start(s32[128,2]{0,1:T(2,128)S(1)} %bitcast.111), channel_id=1, source_target_pairs={{8,0},{16,8},{24,16},{9,1},{17,9},{25,17},{10,2},{18,10},{26,18},{... | collective-permute-start | bytes 3080 | tf_op jit(solution)/shard_map/ppermute | solution.py:16
  7.1 3.9 %collective-permute-done.8 = s32[128,2]{0,1:T(2,128)S(1)} collective-permute-done((s32[128,2]{0,1:T(2,128)S(1)}, s32[128,2]{0,1:T(2,128)S(1)}, u32[]{:S(2)}, u32[]{:S(2)}) %collective-permute-start.8) | collective-permute-done | bytes 1056 | tf_op jit(solution)/shard_map/ppermute | solution.py:16
  12.1 2.0 %collective-permute-start.2 = (bf16[2,32,8320]{2,1,0:T(8,128)(2,1)S(1)}, bf16[2,32,8320]{2,1,0:T(8,128)(2,1)S(1)}, u32[]{:S(2)}, u32[]{:S(2)}) collective-permute-start(bf16[2,32,8320]{2,1,0:T(8,128)(2,1)S(1)} %pad_maximum_fusion), channel_id=1, source_target_pairs={{0,4},{1,5},{2,6},{3,7},{4,0},{5,1},{6,2},{7,3},{8,12},{9,13},{10,... | collective-permute-start | bytes 3194888 | tf_op jit(solution)/shard_map/ppermute | solution.py:44
  15.6 1.5 %collective-permute-start.1 = (bf16[2,32,8320]{2,1,0:T(8,128)(2,1)S(1)}, bf16[2,32,8320]{2,1,0:T(8,128)(2,1)S(1)}, u32[]{:S(2)}, u32[]{:S(2)}) collective-permute-start(bf16[2,32,8320]{2,1,0:T(8,128)(2,1)S(1)} %pad_maximum_fusion), channel_id=1, source_target_pairs={{0,2},{1,3},{2,0},{3,1},{4,6},{5,7},{6,4},{7,5},{8,10},{9,11},{10,... | collective-permute-start | bytes 3194888 | tf_op jit(solution)/shard_map/ppermute | solution.py:44
  18.0 19.2 %collective-permute-done.2 = bf16[2,32,8320]{2,1,0:T(8,128)(2,1)S(1)} collective-permute-done((bf16[2,32,8320]{2,1,0:T(8,128)(2,1)S(1)}, bf16[2,32,8320]{2,1,0:T(8,128)(2,1)S(1)}, u32[]{:S(2)}, u32[]{:S(2)}) %collective-permute-start.2) | collective-permute-done | bytes 1064992 | tf_op jit(solution)/shard_map/ppermute | solution.py:44
  37.2 1.7 %collective-permute-start.3 = (bf16[32,8320]{1,0:T(8,128)(2,1)S(1)}, bf16[32,8320]{1,0:T(8,128)(2,1)S(1)}, u32[]{:S(2)}, u32[]{:S(2)}) collective-permute-start(bf16[32,8320]{1,0:T(8,128)(2,1)S(1)} %slice_bitcast_fusion.5), channel_id=1, source_target_pairs={{0,2},{1,3},{2,0},{3,1},{4,6},{5,7},{6,4},{7,5},{8,10},{9,11},{10,... | collective-permute-start | bytes 1597448 | tf_op jit(solution)/shard_map/ppermute | solution.py:44
  38.9 2.6 %collective-permute-done.1 = bf16[2,32,8320]{2,1,0:T(8,128)(2,1)S(1)} collective-permute-done((bf16[2,32,8320]{2,1,0:T(8,128)(2,1)S(1)}, bf16[2,32,8320]{2,1,0:T(8,128)(2,1)S(1)}, u32[]{:S(2)}, u32[]{:S(2)}) %collective-permute-start.1) | collective-permute-done | bytes 1064992 | tf_op jit(solution)/shard_map/ppermute | solution.py:44
  41.7 1.1 constant_dynamic-update-slice_fusion.3
  42.8 1.1 constant_dynamic-update-slice_fusion.2
  43.8 7.7 %collective-permute-done.3 = bf16[32,8320]{1,0:T(8,128)(2,1)S(1)} collective-permute-done((bf16[32,8320]{1,0:T(8,128)(2,1)S(1)}, bf16[32,8320]{1,0:T(8,128)(2,1)S(1)}, u32[]{:S(2)}, u32[]{:S(2)}) %collective-permute-start.3) | collective-permute-done | bytes 532512 | tf_op jit(solution)/shard_map/ppermute | solution.py:44
  53.2 30.1 %shard_map.86 = (bf16[8,2,16,4096]{3,2,1,0:T(8,128)(2,1)}, bf16[8,2,16,4096]{3,2,1,0:T(8,128)(2,1)}) custom-call(bf16[8,2,16,8320]{3,2,1,0:T(8,128)(2,1)} %constant_dynamic-update-slice_fusion.x_ref.g_ref.w_ref, bf16[8,2,16,8320]{3,2,1,0:T(8,128)(2,1)} %constant_dynamic-update-slice_fusion.x_ref.g_ref.w_ref, ...), custom_call_target="tpu_custom_call" | custom-call | tf_op jit(solution)/shard_map/pallas_call | solution.py:162
  83.3 1.4 %slice_bitcast_fusion.2 = bf16[4,32,4096]{2,1,0:T(8,128)(2,1)S(1)} fusion(bf16[4,2,1,32,4096]{4,3,1,0,2:T(8,128)(2,1)} %bitcast.107), kind=kLoop, calls=%fused_computation.13 | loop fusion | bytes 2097152 | tf_op jit(solution)/shard_map/reshape;squeeze | solution.py:74
  84.8 1.0 add_reduce_fusion.1
  86.5 1.0 collective-permute-done.5
  87.8 1.6 %collective-permute-start.6 = (bf16[2,32,4096]{2,1,0:T(8,128)(2,1)S(1)}, bf16[2,32,4096]{2,1,0:T(8,128)(2,1)S(1)}, u32[]{:S(2)}, u32[]{:S(2)}) collective-permute-start(bf16[2,32,4096]{2,1,0:T(8,128)(2,1)S(1)} %slice_bitcast_fusion.8), channel_id=1, source_target_pairs={{0,2},{1,3},{2,0},{3,1},{4,6},{5,7},{6,4},{7,5},{8,10},{9,11},{10,... | collective-permute-start | bytes 1572872 | tf_op jit(solution)/shard_map/ppermute | solution.py:75
  90.3 11.5 %collective-permute-done.6 = bf16[2,32,4096]{2,1,0:T(8,128)(2,1)S(1)} collective-permute-done((bf16[2,32,4096]{2,1,0:T(8,128)(2,1)S(1)}, bf16[2,32,4096]{2,1,0:T(8,128)(2,1)S(1)}, u32[]{:S(2)}, u32[]{:S(2)}) %collective-permute-start.6) | collective-permute-done | bytes 524320 | tf_op jit(solution)/shard_map/ppermute | solution.py:75
  103.6 1.3 %collective-permute-start.11 = (bf16[32,4096]{1,0:T(8,128)(2,1)S(1)}, bf16[32,4096]{1,0:T(8,128)(2,1)S(1)}, u32[]{:S(2)}, u32[]{:S(2)}) collective-permute-start(bf16[32,4096]{1,0:T(8,128)(2,1)S(1)} %get-tuple-element.14), channel_id=1, source_target_pairs={{8,0},{9,1},{10,2},{11,3},{12,4},{13,5},{14,6},{15,7},{16,8},{17,9... | collective-permute-start | bytes 786440 | tf_op jit(solution)/shard_map/ppermute | solution.py:104
  104.9 1.3 %collective-permute-start.12 = (bf16[32,4096]{1,0:T(8,128)(2,1)S(1)}, bf16[32,4096]{1,0:T(8,128)(2,1)S(1)}, u32[]{:S(2)}, u32[]{:S(2)}) collective-permute-start(bf16[32,4096]{1,0:T(8,128)(2,1)S(1)} %get-tuple-element.15), channel_id=1, source_target_pairs={{8,2},{9,3},{10,0},{11,1},{12,6},{13,7},{14,4},{15,5},{16,10},{17,... | collective-permute-start | bytes 786440 | tf_op jit(solution)/shard_map/ppermute | solution.py:105
  106.3 3.3 %collective-permute-done.7 = bf16[32,4096]{1,0:T(8,128)(2,1)S(1)} collective-permute-done((bf16[32,4096]{1,0:T(8,128)(2,1)S(1)}, bf16[32,4096]{1,0:T(8,128)(2,1)S(1)}, u32[]{:S(2)}, u32[]{:S(2)}) %collective-permute-start.7) | collective-permute-done | bytes 262176 | tf_op jit(solution)/shard_map/ppermute | solution.py:94
  109.6 2.0 %fusion = bf16[1,128,4096]{2,1,0:T(8,128)(2,1)} fusion(bf16[32,4096]{1,0:T(8,128)(2,1)S(1)} %collective-permute-done.7, bf16[2,32,4096]{2,1,0:T(8,128)(2,1)S(1)} %fusion.5, pred[16,128]{1,0:T(8,128)(4,1)S(1)} %copy-done.6, pred[16,128]{1,0:T(8,128)(4,1)S(1)} %copy-done.4), kind=kOutput, calls=%fused_computation.2 | convolution fusion | flops 202248192 | bytes 1576960 | tf_op jit(solution)/shard_map/dot_general | solution.py:110
  111.6 3.2 %collective-permute-done.11 = bf16[32,4096]{1,0:T(8,128)(2,1)S(1)} collective-permute-done((bf16[32,4096]{1,0:T(8,128)(2,1)S(1)}, bf16[32,4096]{1,0:T(8,128)(2,1)S(1)}, u32[]{:S(2)}, u32[]{:S(2)}) %collective-permute-start.11) | collective-permute-done | bytes 262176 | tf_op jit(solution)/shard_map/ppermute | solution.py:104
  114.8 4.7 %collective-permute-done.12 = bf16[32,4096]{1,0:T(8,128)(2,1)S(1)} collective-permute-done((bf16[32,4096]{1,0:T(8,128)(2,1)S(1)}, bf16[32,4096]{1,0:T(8,128)(2,1)S(1)}, u32[]{:S(2)}, u32[]{:S(2)}) %collective-permute-start.12) | collective-permute-done | bytes 262176 | tf_op jit(solution)/shard_map/ppermute | solution.py:105
  119.5 2.0 %fusion.1 = bf16[1,128,4096]{2,1,0:T(8,128)(2,1)} fusion(bf16[32,4096]{1,0:T(8,128)(2,1)S(1)} %collective-permute-done.12, bf16[32,4096]{1,0:T(8,128)(2,1)S(1)} %collective-permute-done.11, pred[16,128]{1,0:T(8,128)(4,1)S(1)} %get-tuple-element.21, pred[16,128]{1,0:T(8,128)(4,1)S(1)} %get-tuple-element.20), kind=kOutput, calls=%fused_computation.3 | convolution fusion | flops 202248192 | bytes 1576960 | tf_op jit(solution)/shard_map/dot_general | solution.py:110
  (79 shorter events, 12.4 us)
Async XLA Ops:
  0.6 3.5 %copy-start.7 = (s32[1,128,2]{1,2,0:T(2,128)S(1)}, s32[1,128,2]{1,2,0:T(2,128)}, u32[]{:S(2)}) copy-start(s32[1,128,2]{1,2,0:T(2,128)} %param.9) | copy-start | bytes 3076
  0.6 3.2 %copy-start.2 = (bf16[1,128,4096]{2,1,0:T(8,128)(2,1)S(1)}, bf16[1,128,4096]{2,1,0:T(8,128)(2,1)}, u32[]{:S(2)}) copy-start(bf16[1,128,4096]{2,1,0:T(8,128)(2,1)} %param.10) | copy-start | bytes 3145732
  0.7 3.4 %copy-start.13 = (bf16[1,128,2]{1,2,0:T(2,128)(2,1)S(1)}, bf16[1,128,2]{1,2,0:T(2,128)(2,1)}, u32[]{:S(2)}) copy-start(bf16[1,128,2]{1,2,0:T(2,128)(2,1)} %param.8) | copy-start | bytes 1540
  2.3 2.0 %copy-start.3 = (pred[16,128]{1,0:T(8,128)(4,1)}, pred[16,128]{1,0:T(8,128)(4,1)S(1)}, u32[]{:S(2)}) copy-start(pred[16,128]{1,0:T(8,128)(4,1)S(1)} %get-tuple-element.18) | copy-start | bytes 6148
  4.5 7.4 %collective-permute-start = (bf16[32,8320]{1,0:T(8,128)(2,1)S(1)}, bf16[32,8320]{1,0:T(8,128)(2,1)S(1)}, u32[]{:S(2)}, u32[]{:S(2)}) collective-permute-start(bf16[32,8320]{1,0:T(8,128)(2,1)S(1)} %get-tuple-element.13), channel_id=1, source_target_pairs={{0,1},{1,0},{2,3},{3,2},{4,5},{5,4},{6,7},{7,6},{8,9},{9,8},{10,11... | collective-permute-start | bytes 1597448 | tf_op jit(solution)/shard_map/ppermute | solution.py:44
  5.0 6.0 %collective-permute-start.8 = (s32[128,2]{0,1:T(2,128)S(1)}, s32[128,2]{0,1:T(2,128)S(1)}, u32[]{:S(2)}, u32[]{:S(2)}) collective-permute-start(s32[128,2]{0,1:T(2,128)S(1)} %bitcast.111), channel_id=1, source_target_pairs={{8,0},{16,8},{24,16},{9,1},{17,9},{25,17},{10,2},{18,10},{26,18},{... | collective-permute-start | bytes 3080 | tf_op jit(solution)/shard_map/ppermute | solution.py:16
  12.1 25.1 %collective-permute-start.2 = (bf16[2,32,8320]{2,1,0:T(8,128)(2,1)S(1)}, bf16[2,32,8320]{2,1,0:T(8,128)(2,1)S(1)}, u32[]{:S(2)}, u32[]{:S(2)}) collective-permute-start(bf16[2,32,8320]{2,1,0:T(8,128)(2,1)S(1)} %pad_maximum_fusion), channel_id=1, source_target_pairs={{0,4},{1,5},{2,6},{3,7},{4,0},{5,1},{6,2},{7,3},{8,12},{9,13},{10,... | collective-permute-start | bytes 3194888 | tf_op jit(solution)/shard_map/ppermute | solution.py:44
  15.6 25.9 %collective-permute-start.1 = (bf16[2,32,8320]{2,1,0:T(8,128)(2,1)S(1)}, bf16[2,32,8320]{2,1,0:T(8,128)(2,1)S(1)}, u32[]{:S(2)}, u32[]{:S(2)}) collective-permute-start(bf16[2,32,8320]{2,1,0:T(8,128)(2,1)S(1)} %pad_maximum_fusion), channel_id=1, source_target_pairs={{0,2},{1,3},{2,0},{3,1},{4,6},{5,7},{6,4},{7,5},{8,10},{9,11},{10,... | collective-permute-start | bytes 3194888 | tf_op jit(solution)/shard_map/ppermute | solution.py:44
  37.2 14.3 %collective-permute-start.3 = (bf16[32,8320]{1,0:T(8,128)(2,1)S(1)}, bf16[32,8320]{1,0:T(8,128)(2,1)S(1)}, u32[]{:S(2)}, u32[]{:S(2)}) collective-permute-start(bf16[32,8320]{1,0:T(8,128)(2,1)S(1)} %slice_bitcast_fusion.5), channel_id=1, source_target_pairs={{0,2},{1,3},{2,0},{3,1},{4,6},{5,7},{6,4},{7,5},{8,10},{9,11},{10,... | collective-permute-start | bytes 1597448 | tf_op jit(solution)/shard_map/ppermute | solution.py:44
  41.6 10.7 %collective-permute-start.4 = (bf16[32,8320]{1,0:T(8,128)(2,1)S(1)}, bf16[32,8320]{1,0:T(8,128)(2,1)S(1)}, u32[]{:S(2)}, u32[]{:S(2)}) collective-permute-start(bf16[32,8320]{1,0:T(8,128)(2,1)S(1)} %slice_bitcast_fusion.4), channel_id=1, source_target_pairs={{0,4},{1,5},{2,6},{3,7},{4,0},{5,1},{6,2},{7,3},{8,12},{9,13},{10,... | collective-permute-start | bytes 1597448 | tf_op jit(solution)/shard_map/ppermute | solution.py:44
  83.3 2.5 %copy-start = (bf16[8,2,16,4096]{3,2,1,0:T(8,128)(2,1)S(1)}, bf16[8,2,16,4096]{3,2,1,0:T(8,128)(2,1)}, u32[]{:S(2)}) copy-start(bf16[8,2,16,4096]{3,2,1,0:T(8,128)(2,1)} %get-tuple-element.5) | copy-start | bytes 6291460
  83.3 4.2 %copy-start.1 = (bf16[8,2,16,4096]{3,2,1,0:T(8,128)(2,1)S(1)}, bf16[8,2,16,4096]{3,2,1,0:T(8,128)(2,1)}, u32[]{:S(2)}) copy-start(bf16[8,2,16,4096]{3,2,1,0:T(8,128)(2,1)} %get-tuple-element.4) | copy-start | bytes 6291460
  84.8 2.7 %collective-permute-start.5 = (bf16[4,32,4096]{2,1,0:T(8,128)(2,1)S(1)}, bf16[4,32,4096]{2,1,0:T(8,128)(2,1)S(1)}, u32[]{:S(2)}, u32[]{:S(2)}) collective-permute-start(bf16[4,32,4096]{2,1,0:T(8,128)(2,1)S(1)} %slice_bitcast_fusion.2), channel_id=1, source_target_pairs={{0,1},{1,0},{2,3},{3,2},{4,5},{5,4},{6,7},{7,6},{8,9},{9,8},{10,11... | collective-permute-start | bytes 3145736 | tf_op jit(solution)/shard_map/ppermute | solution.py:75
  85.9 3.4 %collective-permute-start.9 = (bf16[4,32,4096]{2,1,0:T(8,128)(2,1)S(1)}, bf16[4,32,4096]{2,1,0:T(8,128)(2,1)S(1)}, u32[]{:S(2)}, u32[]{:S(2)}) collective-permute-start(bf16[4,32,4096]{2,1,0:T(8,128)(2,1)S(1)} %slice_bitcast_fusion), channel_id=1, source_target_pairs={{0,1},{1,0},{2,3},{3,2},{4,5},{5,4},{6,7},{7,6},{8,9},{9,8},{10,11... | collective-permute-start | bytes 3145736 | tf_op jit(solution)/shard_map/ppermute | solution.py:75
  87.8 14.0 %collective-permute-start.6 = (bf16[2,32,4096]{2,1,0:T(8,128)(2,1)S(1)}, bf16[2,32,4096]{2,1,0:T(8,128)(2,1)S(1)}, u32[]{:S(2)}, u32[]{:S(2)}) collective-permute-start(bf16[2,32,4096]{2,1,0:T(8,128)(2,1)S(1)} %slice_bitcast_fusion.8), channel_id=1, source_target_pairs={{0,2},{1,3},{2,0},{3,1},{4,6},{5,7},{6,4},{7,5},{8,10},{9,11},{10,... | collective-permute-start | bytes 1572872 | tf_op jit(solution)/shard_map/ppermute | solution.py:75
  89.7 16.6 %copy-start.8 = (s32[128]{0:T(128)S(1)}, s32[128]{0:T(128)}, u32[]{:S(2)}) copy-start(s32[128]{0:T(128)} %add_reduce_fusion) | copy-start | bytes 1540
  89.7 16.6 %copy-start.10 = (pred[128]{0:T(512)(128)(4,1)S(1)}, pred[128]{0:T(512)(128)(4,1)}, u32[]{:S(2)}) copy-start(pred[128]{0:T(512)(128)(4,1)} %copy-done.9) | copy-start | bytes 388
  89.7 16.6 %copy-start.12 = (pred[128]{0:T(512)(128)(4,1)S(1)}, pred[128]{0:T(512)(128)(4,1)}, u32[]{:S(2)}) copy-start(pred[128]{0:T(512)(128)(4,1)} %copy-done.11) | copy-start | bytes 388
  89.7 19.9 %copy-start.4 = (pred[16,128]{1,0:T(8,128)(4,1)S(1)}, pred[16,128]{1,0:T(8,128)(4,1)}, u32[]{:S(2)}) copy-start(pred[16,128]{1,0:T(8,128)(4,1)} %copy-done.3) | copy-start | bytes 6148
  89.7 19.9 %copy-start.6 = (pred[16,128]{1,0:T(8,128)(4,1)S(1)}, pred[16,128]{1,0:T(8,128)(4,1)}, u32[]{:S(2)}) copy-start(pred[16,128]{1,0:T(8,128)(4,1)} %copy-done.5) | copy-start | bytes 6148
  89.7 13.8 %collective-permute-start.10 = (bf16[2,32,4096]{2,1,0:T(8,128)(2,1)S(1)}, bf16[2,32,4096]{2,1,0:T(8,128)(2,1)S(1)}, u32[]{:S(2)}, u32[]{:S(2)}) collective-permute-start(bf16[2,32,4096]{2,1,0:T(8,128)(2,1)S(1)} %slice_bitcast_fusion.6), channel_id=1, source_target_pairs={{0,4},{1,5},{2,6},{3,7},{4,0},{5,1},{6,2},{7,3},{8,12},{9,13},{10,... | collective-permute-start | bytes 1572872 | tf_op jit(solution)/shard_map/ppermute | solution.py:75
  102.0 7.6 %collective-permute-start.7 = (bf16[32,4096]{1,0:T(8,128)(2,1)S(1)}, bf16[32,4096]{1,0:T(8,128)(2,1)S(1)}, u32[]{:S(2)}, u32[]{:S(2)}) collective-permute-start(bf16[32,4096]{1,0:T(8,128)(2,1)S(1)} %slice_bitcast_fusion.12), channel_id=1, source_target_pairs={{0,4},{1,5},{2,6},{3,7},{4,0},{5,1},{6,2},{7,3},{8,12},{9,13},{10,... | collective-permute-start | bytes 786440 | tf_op jit(solution)/shard_map/ppermute | solution.py:94
  103.6 11.1 %collective-permute-start.11 = (bf16[32,4096]{1,0:T(8,128)(2,1)S(1)}, bf16[32,4096]{1,0:T(8,128)(2,1)S(1)}, u32[]{:S(2)}, u32[]{:S(2)}) collective-permute-start(bf16[32,4096]{1,0:T(8,128)(2,1)S(1)} %get-tuple-element.14), channel_id=1, source_target_pairs={{8,0},{9,1},{10,2},{11,3},{12,4},{13,5},{14,6},{15,7},{16,8},{17,9... | collective-permute-start | bytes 786440 | tf_op jit(solution)/shard_map/ppermute | solution.py:104
  104.9 14.6 %collective-permute-start.12 = (bf16[32,4096]{1,0:T(8,128)(2,1)S(1)}, bf16[32,4096]{1,0:T(8,128)(2,1)S(1)}, u32[]{:S(2)}, u32[]{:S(2)}) collective-permute-start(bf16[32,4096]{1,0:T(8,128)(2,1)S(1)} %get-tuple-element.15), channel_id=1, source_target_pairs={{8,2},{9,3},{10,0},{11,1},{12,6},{13,7},{14,4},{15,5},{16,10},{17,... | collective-permute-start | bytes 786440 | tf_op jit(solution)/shard_map/ppermute | solution.py:105
  (3 other events, 3.5 us)

commit v13 on v12

--- a/solution.py
+++ b/solution.py
@@ -47,12 +47,14 @@
 def gather_over_et(packed):
     n = lax.axis_size("et")
     if n == 8:
-        pair = jnp.stack([packed, swap(packed, 1)])
-        across_x = swap(pair, 2)
-        across_y = swap(pair, 4)
-        last_x = swap(across_y[0], 2)
-        last_y = swap(across_x[1], 4)
-        return jnp.concatenate([pair, across_x, across_y, last_x[None], last_y[None]], axis=0)
+        core = swap(packed, 1)
+        near_x = swap(packed, 2)
+        near_y = swap(packed, 4)
+        third = swap(core, 2)
+        fifth = swap(core, 4)
+        sixth = swap(near_y, 2)
+        seventh = swap(sixth, 1)
+        return jnp.stack([packed, core, near_x, third, near_y, fifth, sixth, seventh])
     held = packed[None]
     bit = 1
     while bit < n:

time: 122 us -> 118 us (0.967)
  waiting for transfers between devices: 58 us -> 48 us
  local copies, waits for them, and re-layouts: 8.4 us -> 10.7 us
  starting transfers between devices: 13.1 us -> 15.3 us
  matrix products: 5.75 us -> 6.98 us
    ppermute x5 -> x7, waiting for transfers between devices: 29.5 us -> 22.4 us  [swap(): return lax.ppermute(value, 'et', [(i, i ^ bit) for i in range(n)])]
    ppermute x4, waiting for transfers between devices: 13.3 us -> 10.8 us  [halve_over_et(): got = lax.ppermute(give, 'et', [(i, i ^ bit) for i in range(n)])]
    ppermute x4, starting transfers between devices: 2.73 us -> 4.33 us  [halve_over_et(): got = lax.ppermute(give, 'et', [(i, i ^ bit) for i in range(n)])]
    dot_general x2, matrix products: 1.75 us -> 2.99 us  [pick_rows(): jnp.dot(select.astype(rows.dtype), rows, preferred_element_type=jnp.float32)]
    unnamed x33 -> x31, local copies, waits for them, and re-layouts: 5.3 us -> 6.46 us
    ppermute x5 -> x7, starting transfers between devices: 5.82 us -> 5.25 us  [swap(): return lax.ppermute(value, 'et', [(i, i ^ bit) for i in range(n)])]
  transfers between devices with their start and end apart: 13 -> 15, of which waited for: 10 -> 11; matrix products, arithmetic and copies ran while one was open for 9% -> 11% of each run, Pallas kernels for 0% -> 0%
where the time goes in v13:
time: 118 us
  waiting for transfers between devices  48 us (41%)
  Pallas kernels  30.1 us (26%)
  starting transfers between devices  15.3 us (13%)
  local copies, waits for them, and re-layouts  10.7 us (9%)
  matrix products  6.98 us (6%)
  other arithmetic  5.61 us (5%)
    pallas_call x1, Pallas kernels, expert_pass(): pl.pallas_call(_expert_body, grid=(experts, steps), in_specs=[pl.BlockSpe...  30.1 us
    ppermute x7, waiting for transfers between devices, swap(): return lax.ppermute(value, 'et', [(i, i ^ bit) for i in range(n)])  22.4 us
    ppermute x4, waiting for transfers between devices, halve_over_et(): got = lax.ppermute(give, 'et', [(i, i ^ bit) for i in range(n)])  10.8 us
    unnamed x31, local copies, waits for them, and re-layouts  6.46 us
    ppermute x7, starting transfers between devices, swap(): return lax.ppermute(value, 'et', [(i, i ^ bit) for i in range(n)])  5.25 us
    ppermute x1, waiting for transfers between devices, reduce_to_previous(): second = lax.ppermute(give, ('pipe', 'et'), to_other)  5.01 us
    ppermute x4, starting transfers between devices, halve_over_et(): got = lax.ppermute(give, 'et', [(i, i ^ bit) for i in range(n)])  4.33 us
    dot_general x2, matrix products, unpack(): lax.dot_general(select.astype(jnp.float32), slot_sums, (((0,), (0,)), (()...  3.99 us
  transfers between devices with their start and end apart: 15, of which 11 were waited for; matrix products, arithmetic and copies ran while one was open for 11% of the time, Pallas kernels for 0%

profile of v13, /device:TPU:0, one launch (start us, length us, event | category | flops | bytes accessed | tf_op | source)
XLA Modules:
  0.0 117.7 jit_solution(12202674968023818627)
XLA Ops:
  2.3 1.5 %convolution_convert_fusion.3 = bf16[32,4096]{1,0:T(8,128)(2,1)S(1)} fusion(bf16[1,128,4096]{2,1,0:T(8,128)(2,1)} %param.7, pred[16,128]{1,0:T(8,128)(4,1)S(1)} %get-tuple-element.17, pred[16,128]{1,0:T(8,128)(4,1)S(1)} %get-tuple-element.16), kind=kOutput, calls=%fused_computation.5 | convolution fusion | flops 33689600 | bytes 1314816 | tf_op jit(solution)/shard_map/dot_general | solution.py:39
  3.8 1.5 %convolution_convert_fusion.2 = bf16[32,4096]{1,0:T(8,128)(2,1)S(1)} fusion(bf16[1,128,4096]{2,1,0:T(8,128)(2,1)} %param.10, pred[16,128]{1,0:T(8,128)(4,1)S(1)} %get-tuple-element.17, pred[16,128]{1,0:T(8,128)(4,1)S(1)} %get-tuple-element.16), kind=kOutput, calls=%fused_computation.4 | convolution fusion | flops 33689600 | bytes 1314816 | tf_op jit(solution)/shard_map/dot_general | solution.py:39
  6.8 2.6 %collective-permute-start.1 = (bf16[32,8320]{1,0:T(8,128)(2,1)S(1)}, bf16[32,8320]{1,0:T(8,128)(2,1)S(1)}, u32[]{:S(2)}, u32[]{:S(2)}) collective-permute-start(bf16[32,8320]{1,0:T(8,128)(2,1)S(1)} %pad_maximum_fusion), channel_id=1, source_target_pairs={{0,2},{1,3},{2,0},{3,1},{4,6},{5,7},{6,4},{7,5},{8,10},{9,11},{10,... | collective-permute-start | bytes 1597448 | tf_op jit(solution)/shard_map/ppermute | solution.py:44
  9.4 1.5 %collective-permute-start.3 = (bf16[32,8320]{1,0:T(8,128)(2,1)S(1)}, bf16[32,8320]{1,0:T(8,128)(2,1)S(1)}, u32[]{:S(2)}, u32[]{:S(2)}) collective-permute-start(bf16[32,8320]{1,0:T(8,128)(2,1)S(1)} %pad_maximum_fusion), channel_id=1, source_target_pairs={{0,4},{1,5},{2,6},{3,7},{4,0},{5,1},{6,2},{7,3},{8,12},{9,13},{10,... | collective-permute-start | bytes 1597448 | tf_op jit(solution)/shard_map/ppermute | solution.py:44
  10.9 1.3 %collective-permute-start.10 = (s32[128,2]{0,1:T(2,128)S(1)}, s32[128,2]{0,1:T(2,128)S(1)}, u32[]{:S(2)}, u32[]{:S(2)}) collective-permute-start(s32[128,2]{0,1:T(2,128)S(1)} %bitcast.107), channel_id=1, source_target_pairs={{8,0},{16,8},{24,16},{9,1},{17,9},{25,17},{10,2},{18,10},{26,18},{... | collective-permute-start | bytes 3080 | tf_op jit(solution)/shard_map/ppermute | solution.py:16
  13.0 3.3 %collective-permute-done.10 = s32[128,2]{0,1:T(2,128)S(1)} collective-permute-done((s32[128,2]{0,1:T(2,128)S(1)}, s32[128,2]{0,1:T(2,128)S(1)}, u32[]{:S(2)}, u32[]{:S(2)}) %collective-permute-start.10) | collective-permute-done | bytes 1056 | tf_op jit(solution)/shard_map/ppermute | solution.py:16
  19.4 4.9 %collective-permute-done.3 = bf16[32,8320]{1,0:T(8,128)(2,1)S(1)} collective-permute-done((bf16[32,8320]{1,0:T(8,128)(2,1)S(1)}, bf16[32,8320]{1,0:T(8,128)(2,1)S(1)}, u32[]{:S(2)}, u32[]{:S(2)}) %collective-permute-start.3) | collective-permute-done | bytes 532512 | tf_op jit(solution)/shard_map/ppermute | solution.py:44
  26.1 7.7 %collective-permute-done.2 = bf16[32,8320]{1,0:T(8,128)(2,1)S(1)} collective-permute-done((bf16[32,8320]{1,0:T(8,128)(2,1)S(1)}, bf16[32,8320]{1,0:T(8,128)(2,1)S(1)}, u32[]{:S(2)}, u32[]{:S(2)}) %collective-permute-start.2) | collective-permute-done | bytes 532512 | tf_op jit(solution)/shard_map/ppermute | solution.py:44
  36.3 8.6 %collective-permute-done.5 = bf16[32,8320]{1,0:T(8,128)(2,1)S(1)} collective-permute-done((bf16[32,8320]{1,0:T(8,128)(2,1)S(1)}, bf16[32,8320]{1,0:T(8,128)(2,1)S(1)}, u32[]{:S(2)}, u32[]{:S(2)}) %collective-permute-start.5) | collective-permute-done | bytes 532512 | tf_op jit(solution)/shard_map/ppermute | solution.py:44
  45.7 1.1 collective-permute-done.6
  47.7 30.1 %shard_map.86 = (bf16[8,2,16,4096]{3,2,1,0:T(8,128)(2,1)}, bf16[8,2,16,4096]{3,2,1,0:T(8,128)(2,1)}) custom-call(bf16[8,2,16,8320]{3,2,1,0:T(8,128)(2,1)} %constant_dynamic-update-slice_fusion.x_ref.g_ref.w_ref, bf16[8,2,16,8320]{3,2,1,0:T(8,128)(2,1)} %constant_dynamic-update-slice_fusion.x_ref.g_ref.w_ref, ...), custom_call_target="tpu_custom_call" | custom-call | tf_op jit(solution)/shard_map/pallas_call | solution.py:164
  77.8 1.4 %slice_bitcast_fusion.2 = bf16[4,32,4096]{2,1,0:T(8,128)(2,1)S(1)} fusion(bf16[4,2,1,32,4096]{4,3,1,0,2:T(8,128)(2,1)} %bitcast.98), kind=kLoop, calls=%fused_computation.12 | loop fusion | bytes 2097152 | tf_op jit(solution)/shard_map/reshape;squeeze | solution.py:76
  80.4 1.3 %slice_bitcast_fusion = bf16[4,32,4096]{2,1,0:T(8,128)(2,1)S(1)} fusion(bf16[4,2,1,32,4096]{4,3,1,0,2:T(8,128)(2,1)} %bitcast.96), kind=kLoop, calls=%fused_computation.10 | loop fusion | bytes 2097152 | tf_op jit(solution)/shard_map/reshape;squeeze | solution.py:76
  82.5 1.8 %collective-permute-start.8 = (bf16[2,32,4096]{2,1,0:T(8,128)(2,1)S(1)}, bf16[2,32,4096]{2,1,0:T(8,128)(2,1)S(1)}, u32[]{:S(2)}, u32[]{:S(2)}) collective-permute-start(bf16[2,32,4096]{2,1,0:T(8,128)(2,1)S(1)} %slice_bitcast_fusion.6), channel_id=1, source_target_pairs={{0,2},{1,3},{2,0},{3,1},{4,6},{5,7},{6,4},{7,5},{8,10},{9,11},{10,... | collective-permute-start | bytes 1572872 | tf_op jit(solution)/shard_map/ppermute | solution.py:77
  84.7 1.9 %collective-permute-start.12 = (bf16[2,32,4096]{2,1,0:T(8,128)(2,1)S(1)}, bf16[2,32,4096]{2,1,0:T(8,128)(2,1)S(1)}, u32[]{:S(2)}, u32[]{:S(2)}) collective-permute-start(bf16[2,32,4096]{2,1,0:T(8,128)(2,1)S(1)} %slice_bitcast_fusion.4), channel_id=1, source_target_pairs={{0,4},{1,5},{2,6},{3,7},{4,0},{5,1},{6,2},{7,3},{8,12},{9,13},{10,... | collective-permute-start | bytes 1572872 | tf_op jit(solution)/shard_map/ppermute | solution.py:77
  86.6 9.9 %collective-permute-done.8 = bf16[2,32,4096]{2,1,0:T(8,128)(2,1)S(1)} collective-permute-done((bf16[2,32,4096]{2,1,0:T(8,128)(2,1)S(1)}, bf16[2,32,4096]{2,1,0:T(8,128)(2,1)S(1)}, u32[]{:S(2)}, u32[]{:S(2)}) %collective-permute-start.8) | collective-permute-done | bytes 524320 | tf_op jit(solution)/shard_map/ppermute | solution.py:77
  96.7 1.8 %collective-permute-start.9 = (bf16[32,4096]{1,0:T(8,128)(2,1)S(1)}, bf16[32,4096]{1,0:T(8,128)(2,1)S(1)}, u32[]{:S(2)}, u32[]{:S(2)}) collective-permute-start(bf16[32,4096]{1,0:T(8,128)(2,1)S(1)} %slice_bitcast_fusion.10), channel_id=1, source_target_pairs={{0,4},{1,5},{2,6},{3,7},{4,0},{5,1},{6,2},{7,3},{8,12},{9,13},{10,... | collective-permute-start | bytes 786440 | tf_op jit(solution)/shard_map/ppermute | solution.py:96
  99.5 1.3 %collective-permute-start.13 = (bf16[32,4096]{1,0:T(8,128)(2,1)S(1)}, bf16[32,4096]{1,0:T(8,128)(2,1)S(1)}, u32[]{:S(2)}, u32[]{:S(2)}) collective-permute-start(bf16[32,4096]{1,0:T(8,128)(2,1)S(1)} %get-tuple-element.12), channel_id=1, source_target_pairs={{8,0},{9,1},{10,2},{11,3},{12,4},{13,5},{14,6},{15,7},{16,8},{17,9... | collective-permute-start | bytes 786440 | tf_op jit(solution)/shard_map/ppermute | solution.py:106
  100.8 1.3 %collective-permute-start.14 = (bf16[32,4096]{1,0:T(8,128)(2,1)S(1)}, bf16[32,4096]{1,0:T(8,128)(2,1)S(1)}, u32[]{:S(2)}, u32[]{:S(2)}) collective-permute-start(bf16[32,4096]{1,0:T(8,128)(2,1)S(1)} %get-tuple-element.13), channel_id=1, source_target_pairs={{8,2},{9,3},{10,0},{11,1},{12,6},{13,7},{14,4},{15,5},{16,10},{17,... | collective-permute-start | bytes 786440 | tf_op jit(solution)/shard_map/ppermute | solution.py:107
  102.2 2.5 %collective-permute-done.9 = bf16[32,4096]{1,0:T(8,128)(2,1)S(1)} collective-permute-done((bf16[32,4096]{1,0:T(8,128)(2,1)S(1)}, bf16[32,4096]{1,0:T(8,128)(2,1)S(1)}, u32[]{:S(2)}, u32[]{:S(2)}) %collective-permute-start.9) | collective-permute-done | bytes 262176 | tf_op jit(solution)/shard_map/ppermute | solution.py:96
  104.7 2.0 %fusion = bf16[1,128,4096]{2,1,0:T(8,128)(2,1)} fusion(bf16[32,4096]{1,0:T(8,128)(2,1)S(1)} %collective-permute-done.9, bf16[2,32,4096]{2,1,0:T(8,128)(2,1)S(1)} %fusion.5, pred[16,128]{1,0:T(8,128)(4,1)S(1)} %copy-done.5, pred[16,128]{1,0:T(8,128)(4,1)S(1)} %copy-done.3), kind=kOutput, calls=%fused_computation.2 | convolution fusion | flops 202248192 | bytes 1576960 | tf_op jit(solution)/shard_map/dot_general | solution.py:112
  106.7 4.0 %collective-permute-done.13 = bf16[32,4096]{1,0:T(8,128)(2,1)S(1)} collective-permute-done((bf16[32,4096]{1,0:T(8,128)(2,1)S(1)}, bf16[32,4096]{1,0:T(8,128)(2,1)S(1)}, u32[]{:S(2)}, u32[]{:S(2)}) %collective-permute-start.13) | collective-permute-done | bytes 262176 | tf_op jit(solution)/shard_map/ppermute | solution.py:106
  110.7 5.0 %collective-permute-done.14 = bf16[32,4096]{1,0:T(8,128)(2,1)S(1)} collective-permute-done((bf16[32,4096]{1,0:T(8,128)(2,1)S(1)}, bf16[32,4096]{1,0:T(8,128)(2,1)S(1)}, u32[]{:S(2)}, u32[]{:S(2)}) %collective-permute-start.14) | collective-permute-done | bytes 262176 | tf_op jit(solution)/shard_map/ppermute | solution.py:107
  115.7 2.0 %fusion.1 = bf16[1,128,4096]{2,1,0:T(8,128)(2,1)} fusion(bf16[32,4096]{1,0:T(8,128)(2,1)S(1)} %collective-permute-done.14, bf16[32,4096]{1,0:T(8,128)(2,1)S(1)} %collective-permute-done.13, pred[16,128]{1,0:T(8,128)(4,1)S(1)} %get-tuple-element.19, pred[16,128]{1,0:T(8,128)(4,1)S(1)} %get-tuple-element.18), kind=kOutput, calls=%fused_computation.3 | convolution fusion | flops 202248192 | bytes 1576960 | tf_op jit(solution)/shard_map/dot_general | solution.py:112
  (78 shorter events, 16.3 us)
Async XLA Ops:
  0.6 10.3 %copy-start.6 = (s32[1,128,2]{1,2,0:T(2,128)S(1)}, s32[1,128,2]{1,2,0:T(2,128)}, u32[]{:S(2)}) copy-start(s32[1,128,2]{1,2,0:T(2,128)} %param.9) | copy-start | bytes 3076
  6.3 12.5 %collective-permute-start = (bf16[32,8320]{1,0:T(8,128)(2,1)S(1)}, bf16[32,8320]{1,0:T(8,128)(2,1)S(1)}, u32[]{:S(2)}, u32[]{:S(2)}) collective-permute-start(bf16[32,8320]{1,0:T(8,128)(2,1)S(1)} %pad_maximum_fusion), channel_id=1, source_target_pairs={{0,1},{1,0},{2,3},{3,2},{4,5},{5,4},{6,7},{7,6},{8,9},{9,8},{10,11... | collective-permute-start | bytes 1597448 | tf_op jit(solution)/shard_map/ppermute | solution.py:44
  6.8 18.4 %collective-permute-start.1 = (bf16[32,8320]{1,0:T(8,128)(2,1)S(1)}, bf16[32,8320]{1,0:T(8,128)(2,1)S(1)}, u32[]{:S(2)}, u32[]{:S(2)}) collective-permute-start(bf16[32,8320]{1,0:T(8,128)(2,1)S(1)} %pad_maximum_fusion), channel_id=1, source_target_pairs={{0,2},{1,3},{2,0},{3,1},{4,6},{5,7},{6,4},{7,5},{8,10},{9,11},{10,... | collective-permute-start | bytes 1597448 | tf_op jit(solution)/shard_map/ppermute | solution.py:44
  9.4 14.9 %collective-permute-start.3 = (bf16[32,8320]{1,0:T(8,128)(2,1)S(1)}, bf16[32,8320]{1,0:T(8,128)(2,1)S(1)}, u32[]{:S(2)}, u32[]{:S(2)}) collective-permute-start(bf16[32,8320]{1,0:T(8,128)(2,1)S(1)} %pad_maximum_fusion), channel_id=1, source_target_pairs={{0,4},{1,5},{2,6},{3,7},{4,0},{5,1},{6,2},{7,3},{8,12},{9,13},{10,... | collective-permute-start | bytes 1597448 | tf_op jit(solution)/shard_map/ppermute | solution.py:44
  10.9 5.5 %collective-permute-start.10 = (s32[128,2]{0,1:T(2,128)S(1)}, s32[128,2]{0,1:T(2,128)S(1)}, u32[]{:S(2)}, u32[]{:S(2)}) collective-permute-start(s32[128,2]{0,1:T(2,128)S(1)} %bitcast.107), channel_id=1, source_target_pairs={{8,0},{16,8},{24,16},{9,1},{17,9},{25,17},{10,2},{18,10},{26,18},{... | collective-permute-start | bytes 3080 | tf_op jit(solution)/shard_map/ppermute | solution.py:16
  16.4 31.3 %copy-start.8 = (pred[128]{0:T(512)(128)(4,1)}, pred[128]{0:T(512)(128)(4,1)S(1)}, u32[]{:S(2)}) copy-start(pred[128]{0:T(512)(128)(4,1)S(1)} %get-tuple-element.8) | copy-start | bytes 388
  18.8 15.0 %collective-permute-start.2 = (bf16[32,8320]{1,0:T(8,128)(2,1)S(1)}, bf16[32,8320]{1,0:T(8,128)(2,1)S(1)}, u32[]{:S(2)}, u32[]{:S(2)}) collective-permute-start(bf16[32,8320]{1,0:T(8,128)(2,1)S(1)} %collective-permute-done), channel_id=1, source_target_pairs={{0,2},{1,3},{2,0},{3,1},{4,6},{5,7},{6,4},{7,5},{8,10},{9,11},{10,... | collective-permute-start | bytes 1597448 | tf_op jit(solution)/shard_map/ppermute | solution.py:44
  19.3 16.2 %collective-permute-start.4 = (bf16[32,8320]{1,0:T(8,128)(2,1)S(1)}, bf16[32,8320]{1,0:T(8,128)(2,1)S(1)}, u32[]{:S(2)}, u32[]{:S(2)}) collective-permute-start(bf16[32,8320]{1,0:T(8,128)(2,1)S(1)} %collective-permute-done), channel_id=1, source_target_pairs={{0,4},{1,5},{2,6},{3,7},{4,0},{5,1},{6,2},{7,3},{8,12},{9,13},{10,... | collective-permute-start | bytes 1597448 | tf_op jit(solution)/shard_map/ppermute | solution.py:44
  24.3 20.6 %collective-permute-start.5 = (bf16[32,8320]{1,0:T(8,128)(2,1)S(1)}, bf16[32,8320]{1,0:T(8,128)(2,1)S(1)}, u32[]{:S(2)}, u32[]{:S(2)}) collective-permute-start(bf16[32,8320]{1,0:T(8,128)(2,1)S(1)} %collective-permute-done.3), channel_id=1, source_target_pairs={{0,2},{1,3},{2,0},{3,1},{4,6},{5,7},{6,4},{7,5},{8,10},{9,11},{10,... | collective-permute-start | bytes 1597448 | tf_op jit(solution)/shard_map/ppermute | solution.py:44
  44.9 1.9 %collective-permute-start.6 = (bf16[32,8320]{1,0:T(8,128)(2,1)S(1)}, bf16[32,8320]{1,0:T(8,128)(2,1)S(1)}, u32[]{:S(2)}, u32[]{:S(2)}) collective-permute-start(bf16[32,8320]{1,0:T(8,128)(2,1)S(1)} %collective-permute-done.5), channel_id=1, source_target_pairs={{0,1},{1,0},{2,3},{3,2},{4,5},{5,4},{6,7},{7,6},{8,9},{9,8},{10,11... | collective-permute-start | bytes 1597448 | tf_op jit(solution)/shard_map/ppermute | solution.py:44
  77.8 4.4 %copy-start.1 = (bf16[8,2,16,4096]{3,2,1,0:T(8,128)(2,1)S(1)}, bf16[8,2,16,4096]{3,2,1,0:T(8,128)(2,1)}, u32[]{:S(2)}) copy-start(bf16[8,2,16,4096]{3,2,1,0:T(8,128)(2,1)} %get-tuple-element.4) | copy-start | bytes 6291460
  77.8 6.6 %copy-start = (bf16[8,2,16,4096]{3,2,1,0:T(8,128)(2,1)S(1)}, bf16[8,2,16,4096]{3,2,1,0:T(8,128)(2,1)}, u32[]{:S(2)}) copy-start(bf16[8,2,16,4096]{3,2,1,0:T(8,128)(2,1)} %get-tuple-element.5) | copy-start | bytes 6291460
  79.3 2.9 %collective-permute-start.7 = (bf16[4,32,4096]{2,1,0:T(8,128)(2,1)S(1)}, bf16[4,32,4096]{2,1,0:T(8,128)(2,1)S(1)}, u32[]{:S(2)}, u32[]{:S(2)}) collective-permute-start(bf16[4,32,4096]{2,1,0:T(8,128)(2,1)S(1)} %slice_bitcast_fusion.2), channel_id=1, source_target_pairs={{0,1},{1,0},{2,3},{3,2},{4,5},{5,4},{6,7},{7,6},{8,9},{9,8},{10,11... | collective-permute-start | bytes 3145736 | tf_op jit(solution)/shard_map/ppermute | solution.py:77
  81.7 2.7 %collective-permute-start.11 = (bf16[4,32,4096]{2,1,0:T(8,128)(2,1)S(1)}, bf16[4,32,4096]{2,1,0:T(8,128)(2,1)S(1)}, u32[]{:S(2)}, u32[]{:S(2)}) collective-permute-start(bf16[4,32,4096]{2,1,0:T(8,128)(2,1)S(1)} %slice_bitcast_fusion), channel_id=1, source_target_pairs={{0,1},{1,0},{2,3},{3,2},{4,5},{5,4},{6,7},{7,6},{8,9},{9,8},{10,11... | collective-permute-start | bytes 3145736 | tf_op jit(solution)/shard_map/ppermute | solution.py:77
  82.5 19.7 %copy-start.7 = (s32[128]{0:T(128)S(1)}, s32[128]{0:T(128)}, u32[]{:S(2)}) copy-start(s32[128]{0:T(128)} %add_reduce_fusion) | copy-start | bytes 1540
  82.5 19.7 %copy-start.9 = (pred[128]{0:T(512)(128)(4,1)S(1)}, pred[128]{0:T(512)(128)(4,1)}, u32[]{:S(2)}) copy-start(pred[128]{0:T(512)(128)(4,1)} %copy-done.8) | copy-start | bytes 388
  82.5 19.7 %copy-start.11 = (pred[128]{0:T(512)(128)(4,1)S(1)}, pred[128]{0:T(512)(128)(4,1)}, u32[]{:S(2)}) copy-start(pred[128]{0:T(512)(128)(4,1)} %copy-done.10) | copy-start | bytes 388
  82.5 22.2 %copy-start.3 = (pred[16,128]{1,0:T(8,128)(4,1)S(1)}, pred[16,128]{1,0:T(8,128)(4,1)}, u32[]{:S(2)}) copy-start(pred[16,128]{1,0:T(8,128)(4,1)} %copy-done.2) | copy-start | bytes 6148
  82.5 22.2 %copy-start.5 = (pred[16,128]{1,0:T(8,128)(4,1)S(1)}, pred[16,128]{1,0:T(8,128)(4,1)}, u32[]{:S(2)}) copy-start(pred[16,128]{1,0:T(8,128)(4,1)} %copy-done.4) | copy-start | bytes 6148
  82.5 14.1 %collective-permute-start.8 = (bf16[2,32,4096]{2,1,0:T(8,128)(2,1)S(1)}, bf16[2,32,4096]{2,1,0:T(8,128)(2,1)S(1)}, u32[]{:S(2)}, u32[]{:S(2)}) collective-permute-start(bf16[2,32,4096]{2,1,0:T(8,128)(2,1)S(1)} %slice_bitcast_fusion.6), channel_id=1, source_target_pairs={{0,2},{1,3},{2,0},{3,1},{4,6},{5,7},{6,4},{7,5},{8,10},{9,11},{10,... | collective-permute-start | bytes 1572872 | tf_op jit(solution)/shard_map/ppermute | solution.py:77
  84.7 14.6 %collective-permute-start.12 = (bf16[2,32,4096]{2,1,0:T(8,128)(2,1)S(1)}, bf16[2,32,4096]{2,1,0:T(8,128)(2,1)S(1)}, u32[]{:S(2)}, u32[]{:S(2)}) collective-permute-start(bf16[2,32,4096]{2,1,0:T(8,128)(2,1)S(1)} %slice_bitcast_fusion.4), channel_id=1, source_target_pairs={{0,4},{1,5},{2,6},{3,7},{4,0},{5,1},{6,2},{7,3},{8,12},{9,13},{10,... | collective-permute-start | bytes 1572872 | tf_op jit(solution)/shard_map/ppermute | solution.py:77
  96.7 8.0 %collective-permute-start.9 = (bf16[32,4096]{1,0:T(8,128)(2,1)S(1)}, bf16[32,4096]{1,0:T(8,128)(2,1)S(1)}, u32[]{:S(2)}, u32[]{:S(2)}) collective-permute-start(bf16[32,4096]{1,0:T(8,128)(2,1)S(1)} %slice_bitcast_fusion.10), channel_id=1, source_target_pairs={{0,4},{1,5},{2,6},{3,7},{4,0},{5,1},{6,2},{7,3},{8,12},{9,13},{10,... | collective-permute-start | bytes 786440 | tf_op jit(solution)/shard_map/ppermute | solution.py:96
  99.5 11.1 %collective-permute-start.13 = (bf16[32,4096]{1,0:T(8,128)(2,1)S(1)}, bf16[32,4096]{1,0:T(8,128)(2,1)S(1)}, u32[]{:S(2)}, u32[]{:S(2)}) collective-permute-start(bf16[32,4096]{1,0:T(8,128)(2,1)S(1)} %get-tuple-element.12), channel_id=1, source_target_pairs={{8,0},{9,1},{10,2},{11,3},{12,4},{13,5},{14,6},{15,7},{16,8},{17,9... | collective-permute-start | bytes 786440 | tf_op jit(solution)/shard_map/ppermute | solution.py:106
  100.8 14.9 %collective-permute-start.14 = (bf16[32,4096]{1,0:T(8,128)(2,1)S(1)}, bf16[32,4096]{1,0:T(8,128)(2,1)S(1)}, u32[]{:S(2)}, u32[]{:S(2)}) collective-permute-start(bf16[32,4096]{1,0:T(8,128)(2,1)S(1)} %get-tuple-element.13), channel_id=1, source_target_pairs={{8,2},{9,3},{10,0},{11,1},{12,6},{13,7},{14,4},{15,5},{16,10},{17,... | collective-permute-start | bytes 786440 | tf_op jit(solution)/shard_map/ppermute | solution.py:107
  (3 other events, 8.4 us)

commit v14 on v13

--- a/solution.py
+++ b/solution.py
@@ -52,7 +52,8 @@
         near_y = swap(packed, 4)
         third = swap(core, 2)
         fifth = swap(core, 4)
-        sixth = swap(near_y, 2)
+        half = packed.shape[0] // 2
+        sixth = jnp.concatenate([swap(near_y[:half], 2), swap(near_x[half:], 4)], axis=0)
         seventh = swap(sixth, 1)
         return jnp.stack([packed, core, near_x, third, near_y, fifth, sixth, seventh])
     held = packed[None]

time: 118 us -> 116 us (0.983)
  waiting for transfers between devices: 48 us -> 44.1 us
  starting transfers between devices: 15.3 us -> 17.1 us
    ppermute x7 -> x8, waiting for transfers between devices: 22.4 us -> 17.9 us  [swap(): return lax.ppermute(value, 'et', [(i, i ^ bit) for i in range(n)])]
    ppermute x7 -> x8, starting transfers between devices: 5.25 us -> 8.85 us  [swap(): return lax.ppermute(value, 'et', [(i, i ^ bit) for i in range(n)])]
    ppermute x4, waiting for transfers between devices: 10.8 us -> 12.7 us  [halve_over_et(): got = lax.ppermute(give, 'et', [(i, i ^ bit) for i in range(n)])]
    ppermute x4, starting transfers between devices: 4.33 us -> 2.83 us  [halve_over_et(): got = lax.ppermute(give, 'et', [(i, i ^ bit) for i in range(n)])]
    ppermute x1, waiting for transfers between devices: 5.01 us -> 3.67 us  [reduce_to_previous(): second = lax.ppermute(give, ('pipe', 'et'), to_other)]
    unnamed x31 -> x32, local copies, waits for them, and re-layouts: 6.46 us -> 6.47 us
  transfers between devices with their start and end apart: 15 -> 16, of which waited for: 11 -> 11; matrix products, arithmetic and copies ran while one was open for 11% -> 11% of each run, Pallas kernels for 0% -> 0%
where the time goes in v14:
time: 116 us
  waiting for transfers between devices  44.1 us (38%)
  Pallas kernels  30.1 us (26%)
  starting transfers between devices  17.1 us (15%)
  local copies, waits for them, and re-layouts  10.8 us (9%)
  matrix products  6.98 us (6%)
  other arithmetic  5.64 us (5%)
    pallas_call x1, Pallas kernels, expert_pass(): pl.pallas_call(_expert_body, grid=(experts, steps), in_specs=[pl.BlockSpe...  30.1 us
    ppermute x8, waiting for transfers between devices, swap(): return lax.ppermute(value, 'et', [(i, i ^ bit) for i in range(n)])  17.9 us
    ppermute x4, waiting for transfers between devices, halve_over_et(): got = lax.ppermute(give, 'et', [(i, i ^ bit) for i in range(n)])  12.7 us
    ppermute x8, starting transfers between devices, swap(): return lax.ppermute(value, 'et', [(i, i ^ bit) for i in range(n)])  8.85 us
    unnamed x32, local copies, waits for them, and re-layouts  6.47 us
    ppermute x1, waiting for transfers between devices, reduce_to_previous(): first = lax.ppermute(keep, ('pipe', 'et'), to_same)  4.17 us
    dot_general x2, matrix products, unpack(): lax.dot_general(select.astype(jnp.float32), slot_sums, (((0,), (0,)), (()...  3.99 us
    ppermute x1, waiting for transfers between devices, reduce_to_previous(): second = lax.ppermute(give, ('pipe', 'et'), to_other)  3.67 us
  transfers between devices with their start and end apart: 16, of which 11 were waited for; matrix products, arithmetic and copies ran while one was open for 11% of the time, Pallas kernels for 0%

profile of v14, /device:TPU:0, one launch (start us, length us, event | category | flops | bytes accessed | tf_op | source)
XLA Modules:
  0.0 115.7 jit_solution(6001370714961684735)
XLA Ops:
  2.3 1.5 %convolution_convert_fusion.3 = bf16[32,4096]{1,0:T(8,128)(2,1)S(1)} fusion(bf16[1,128,4096]{2,1,0:T(8,128)(2,1)} %param.7, pred[16,128]{1,0:T(8,128)(4,1)S(1)} %get-tuple-element.17, pred[16,128]{1,0:T(8,128)(4,1)S(1)} %get-tuple-element.16), kind=kOutput, calls=%fused_computation.5 | convolution fusion | flops 33689600 | bytes 1314816 | tf_op jit(solution)/shard_map/dot_general | solution.py:39
  3.8 1.5 %convolution_convert_fusion.2 = bf16[32,4096]{1,0:T(8,128)(2,1)S(1)} fusion(bf16[1,128,4096]{2,1,0:T(8,128)(2,1)} %param.10, pred[16,128]{1,0:T(8,128)(4,1)S(1)} %get-tuple-element.17, pred[16,128]{1,0:T(8,128)(4,1)S(1)} %get-tuple-element.16), kind=kOutput, calls=%fused_computation.4 | convolution fusion | flops 33689600 | bytes 1314816 | tf_op jit(solution)/shard_map/dot_general | solution.py:39
  6.8 2.6 %collective-permute-start.1 = (bf16[32,8320]{1,0:T(8,128)(2,1)S(1)}, bf16[32,8320]{1,0:T(8,128)(2,1)S(1)}, u32[]{:S(2)}, u32[]{:S(2)}) collective-permute-start(bf16[32,8320]{1,0:T(8,128)(2,1)S(1)} %pad_maximum_fusion), channel_id=1, source_target_pairs={{0,2},{1,3},{2,0},{3,1},{4,6},{5,7},{6,4},{7,5},{8,10},{9,11},{10,... | collective-permute-start | bytes 1597448 | tf_op jit(solution)/shard_map/ppermute | solution.py:44
  9.4 1.5 %collective-permute-start.3 = (bf16[32,8320]{1,0:T(8,128)(2,1)S(1)}, bf16[32,8320]{1,0:T(8,128)(2,1)S(1)}, u32[]{:S(2)}, u32[]{:S(2)}) collective-permute-start(bf16[32,8320]{1,0:T(8,128)(2,1)S(1)} %pad_maximum_fusion), channel_id=1, source_target_pairs={{0,4},{1,5},{2,6},{3,7},{4,0},{5,1},{6,2},{7,3},{8,12},{9,13},{10,... | collective-permute-start | bytes 1597448 | tf_op jit(solution)/shard_map/ppermute | solution.py:44
  13.0 3.3 %collective-permute-done.11 = s32[128,2]{0,1:T(2,128)S(1)} collective-permute-done((s32[128,2]{0,1:T(2,128)S(1)}, s32[128,2]{0,1:T(2,128)S(1)}, u32[]{:S(2)}, u32[]{:S(2)}) %collective-permute-start.11) | collective-permute-done | bytes 1056 | tf_op jit(solution)/shard_map/ppermute | solution.py:16
  18.8 4.8 %collective-permute-done.3 = bf16[32,8320]{1,0:T(8,128)(2,1)S(1)} collective-permute-done((bf16[32,8320]{1,0:T(8,128)(2,1)S(1)}, bf16[32,8320]{1,0:T(8,128)(2,1)S(1)}, u32[]{:S(2)}, u32[]{:S(2)}) %collective-permute-start.3) | collective-permute-done | bytes 532512 | tf_op jit(solution)/shard_map/ppermute | solution.py:44
  24.0 1.8 %collective-permute-start.6 = (bf16[16,8320]{1,0:T(8,128)(2,1)S(1)}, bf16[16,8320]{1,0:T(8,128)(2,1)S(1)}, u32[]{:S(2)}, u32[]{:S(2)}) collective-permute-start(bf16[16,8320]{1,0:T(8,128)(2,1)S(1)} %slice.57), channel_id=1, source_target_pairs={{0,4},{1,5},{2,6},{3,7},{4,0},{5,1},{6,2},{7,3},{8,12},{9,13},{10,... | collective-permute-start | bytes 798728 | tf_op jit(solution)/shard_map/ppermute | solution.py:44
  27.5 1.5 %collective-permute-start.2 = (bf16[32,8320]{1,0:T(8,128)(2,1)S(1)}, bf16[32,8320]{1,0:T(8,128)(2,1)S(1)}, u32[]{:S(2)}, u32[]{:S(2)}) collective-permute-start(bf16[32,8320]{1,0:T(8,128)(2,1)S(1)} %collective-permute-done), channel_id=1, source_target_pairs={{0,2},{1,3},{2,0},{3,1},{4,6},{5,7},{6,4},{7,5},{8,10},{9,11},{10,... | collective-permute-start | bytes 1597448 | tf_op jit(solution)/shard_map/ppermute | solution.py:44
  29.5 3.5 %collective-permute-done.5 = bf16[16,8320]{1,0:T(8,128)(2,1)S(1)} collective-permute-done((bf16[16,8320]{1,0:T(8,128)(2,1)S(1)}, bf16[16,8320]{1,0:T(8,128)(2,1)S(1)}, u32[]{:S(2)}, u32[]{:S(2)}) %collective-permute-start.5) | collective-permute-done | bytes 266272 | tf_op jit(solution)/shard_map/ppermute | solution.py:44
  33.3 9.4 %collective-permute-done.2 = bf16[32,8320]{1,0:T(8,128)(2,1)S(1)} collective-permute-done((bf16[32,8320]{1,0:T(8,128)(2,1)S(1)}, bf16[32,8320]{1,0:T(8,128)(2,1)S(1)}, u32[]{:S(2)}, u32[]{:S(2)}) %collective-permute-start.2) | collective-permute-done | bytes 532512 | tf_op jit(solution)/shard_map/ppermute | solution.py:44
  46.9 30.1 %shard_map.86 = (bf16[8,2,16,4096]{3,2,1,0:T(8,128)(2,1)}, bf16[8,2,16,4096]{3,2,1,0:T(8,128)(2,1)}) custom-call(bf16[8,2,16,8320]{3,2,1,0:T(8,128)(2,1)} %constant_dynamic-update-slice_fusion.2.x_ref.g_ref.w_ref, bf16[8,2,16,8320]{3,2,1,0:T(8,128)(2,1)} %constant_dynamic-update-slice_fusion.2.x_ref.g_ref.w_ref, ...), custom_call_target="tpu_custom_call" | custom-call | tf_op jit(solution)/shard_map/pallas_call | solution.py:165
  77.0 1.4 %slice_bitcast_fusion.2 = bf16[4,32,4096]{2,1,0:T(8,128)(2,1)S(1)} fusion(bf16[4,2,1,32,4096]{4,3,1,0,2:T(8,128)(2,1)} %bitcast.98), kind=kLoop, calls=%fused_computation.12 | loop fusion | bytes 2097152 | tf_op jit(solution)/shard_map/reshape;squeeze | solution.py:77
  79.5 1.3 %slice_bitcast_fusion = bf16[4,32,4096]{2,1,0:T(8,128)(2,1)S(1)} fusion(bf16[4,2,1,32,4096]{4,3,1,0,2:T(8,128)(2,1)} %bitcast.96), kind=kLoop, calls=%fused_computation.10 | loop fusion | bytes 2097152 | tf_op jit(solution)/shard_map/reshape;squeeze | solution.py:77
  82.4 1.3 %collective-permute-done.12 = bf16[4,32,4096]{2,1,0:T(8,128)(2,1)S(1)} collective-permute-done((bf16[4,32,4096]{2,1,0:T(8,128)(2,1)S(1)}, bf16[4,32,4096]{2,1,0:T(8,128)(2,1)S(1)}, u32[]{:S(2)}, u32[]{:S(2)}) %collective-permute-start.12) | collective-permute-done | bytes 1048608 | tf_op jit(solution)/shard_map/ppermute | solution.py:78
  83.9 1.6 %collective-permute-start.13 = (bf16[2,32,4096]{2,1,0:T(8,128)(2,1)S(1)}, bf16[2,32,4096]{2,1,0:T(8,128)(2,1)S(1)}, u32[]{:S(2)}, u32[]{:S(2)}) collective-permute-start(bf16[2,32,4096]{2,1,0:T(8,128)(2,1)S(1)} %slice_bitcast_fusion.4), channel_id=1, source_target_pairs={{0,4},{1,5},{2,6},{3,7},{4,0},{5,1},{6,2},{7,3},{8,12},{9,13},{10,... | collective-permute-start | bytes 1572872 | tf_op jit(solution)/shard_map/ppermute | solution.py:78
  85.5 10.1 %collective-permute-done.9 = bf16[2,32,4096]{2,1,0:T(8,128)(2,1)S(1)} collective-permute-done((bf16[2,32,4096]{2,1,0:T(8,128)(2,1)S(1)}, bf16[2,32,4096]{2,1,0:T(8,128)(2,1)S(1)}, u32[]{:S(2)}, u32[]{:S(2)}) %collective-permute-start.9) | collective-permute-done | bytes 524320 | tf_op jit(solution)/shard_map/ppermute | solution.py:78
  95.8 1.6 %collective-permute-start.10 = (bf16[32,4096]{1,0:T(8,128)(2,1)S(1)}, bf16[32,4096]{1,0:T(8,128)(2,1)S(1)}, u32[]{:S(2)}, u32[]{:S(2)}) collective-permute-start(bf16[32,4096]{1,0:T(8,128)(2,1)S(1)} %slice_bitcast_fusion.10), channel_id=1, source_target_pairs={{0,4},{1,5},{2,6},{3,7},{4,0},{5,1},{6,2},{7,3},{8,12},{9,13},{10,... | collective-permute-start | bytes 786440 | tf_op jit(solution)/shard_map/ppermute | solution.py:97
  97.4 1.3 %collective-permute-done.13 = bf16[2,32,4096]{2,1,0:T(8,128)(2,1)S(1)} collective-permute-done((bf16[2,32,4096]{2,1,0:T(8,128)(2,1)S(1)}, bf16[2,32,4096]{2,1,0:T(8,128)(2,1)S(1)}, u32[]{:S(2)}, u32[]{:S(2)}) %collective-permute-start.13) | collective-permute-done | bytes 524320 | tf_op jit(solution)/shard_map/ppermute | solution.py:78
  98.9 1.3 %collective-permute-start.14 = (bf16[32,4096]{1,0:T(8,128)(2,1)S(1)}, bf16[32,4096]{1,0:T(8,128)(2,1)S(1)}, u32[]{:S(2)}, u32[]{:S(2)}) collective-permute-start(bf16[32,4096]{1,0:T(8,128)(2,1)S(1)} %get-tuple-element.12), channel_id=1, source_target_pairs={{8,0},{9,1},{10,2},{11,3},{12,4},{13,5},{14,6},{15,7},{16,8},{17,9... | collective-permute-start | bytes 786440 | tf_op jit(solution)/shard_map/ppermute | solution.py:107
  101.5 2.3 %collective-permute-done.10 = bf16[32,4096]{1,0:T(8,128)(2,1)S(1)} collective-permute-done((bf16[32,4096]{1,0:T(8,128)(2,1)S(1)}, bf16[32,4096]{1,0:T(8,128)(2,1)S(1)}, u32[]{:S(2)}, u32[]{:S(2)}) %collective-permute-start.10) | collective-permute-done | bytes 262176 | tf_op jit(solution)/shard_map/ppermute | solution.py:97
  103.8 2.0 %fusion = bf16[1,128,4096]{2,1,0:T(8,128)(2,1)} fusion(bf16[32,4096]{1,0:T(8,128)(2,1)S(1)} %collective-permute-done.10, bf16[2,32,4096]{2,1,0:T(8,128)(2,1)S(1)} %fusion.5, pred[16,128]{1,0:T(8,128)(4,1)S(1)} %copy-done.5, pred[16,128]{1,0:T(8,128)(4,1)S(1)} %copy-done.3), kind=kOutput, calls=%fused_computation.2 | convolution fusion | flops 202248192 | bytes 1576960 | tf_op jit(solution)/shard_map/dot_general | solution.py:113
  105.8 4.2 %collective-permute-done.14 = bf16[32,4096]{1,0:T(8,128)(2,1)S(1)} collective-permute-done((bf16[32,4096]{1,0:T(8,128)(2,1)S(1)}, bf16[32,4096]{1,0:T(8,128)(2,1)S(1)}, u32[]{:S(2)}, u32[]{:S(2)}) %collective-permute-start.14) | collective-permute-done | bytes 262176 | tf_op jit(solution)/shard_map/ppermute | solution.py:107
  110.0 3.7 %collective-permute-done.15 = bf16[32,4096]{1,0:T(8,128)(2,1)S(1)} collective-permute-done((bf16[32,4096]{1,0:T(8,128)(2,1)S(1)}, bf16[32,4096]{1,0:T(8,128)(2,1)S(1)}, u32[]{:S(2)}, u32[]{:S(2)}) %collective-permute-start.15) | collective-permute-done | bytes 262176 | tf_op jit(solution)/shard_map/ppermute | solution.py:108
  113.7 2.0 %fusion.1 = bf16[1,128,4096]{2,1,0:T(8,128)(2,1)} fusion(bf16[32,4096]{1,0:T(8,128)(2,1)S(1)} %collective-permute-done.15, bf16[32,4096]{1,0:T(8,128)(2,1)S(1)} %collective-permute-done.14, pred[16,128]{1,0:T(8,128)(4,1)S(1)} %get-tuple-element.19, pred[16,128]{1,0:T(8,128)(4,1)S(1)} %get-tuple-element.18), kind=kOutput, calls=%fused_computation.3 | convolution fusion | flops 202248192 | bytes 1576960 | tf_op jit(solution)/shard_map/dot_general | solution.py:113
  (84 shorter events, 19.1 us)
Async XLA Ops:
  0.6 10.3 %copy-start.6 = (s32[1,128,2]{1,2,0:T(2,128)S(1)}, s32[1,128,2]{1,2,0:T(2,128)}, u32[]{:S(2)}) copy-start(s32[1,128,2]{1,2,0:T(2,128)} %param.9) | copy-start | bytes 3076
  6.3 19.5 %collective-permute-start = (bf16[32,8320]{1,0:T(8,128)(2,1)S(1)}, bf16[32,8320]{1,0:T(8,128)(2,1)S(1)}, u32[]{:S(2)}, u32[]{:S(2)}) collective-permute-start(bf16[32,8320]{1,0:T(8,128)(2,1)S(1)} %pad_maximum_fusion), channel_id=1, source_target_pairs={{0,1},{1,0},{2,3},{3,2},{4,5},{5,4},{6,7},{7,6},{8,9},{9,8},{10,11... | collective-permute-start | bytes 1597448 | tf_op jit(solution)/shard_map/ppermute | solution.py:44
  6.8 17.1 %collective-permute-start.1 = (bf16[32,8320]{1,0:T(8,128)(2,1)S(1)}, bf16[32,8320]{1,0:T(8,128)(2,1)S(1)}, u32[]{:S(2)}, u32[]{:S(2)}) collective-permute-start(bf16[32,8320]{1,0:T(8,128)(2,1)S(1)} %pad_maximum_fusion), channel_id=1, source_target_pairs={{0,2},{1,3},{2,0},{3,1},{4,6},{5,7},{6,4},{7,5},{8,10},{9,11},{10,... | collective-permute-start | bytes 1597448 | tf_op jit(solution)/shard_map/ppermute | solution.py:44
  9.4 14.2 %collective-permute-start.3 = (bf16[32,8320]{1,0:T(8,128)(2,1)S(1)}, bf16[32,8320]{1,0:T(8,128)(2,1)S(1)}, u32[]{:S(2)}, u32[]{:S(2)}) collective-permute-start(bf16[32,8320]{1,0:T(8,128)(2,1)S(1)} %pad_maximum_fusion), channel_id=1, source_target_pairs={{0,4},{1,5},{2,6},{3,7},{4,0},{5,1},{6,2},{7,3},{8,12},{9,13},{10,... | collective-permute-start | bytes 1597448 | tf_op jit(solution)/shard_map/ppermute | solution.py:44
  10.9 5.5 %collective-permute-start.11 = (s32[128,2]{0,1:T(2,128)S(1)}, s32[128,2]{0,1:T(2,128)S(1)}, u32[]{:S(2)}, u32[]{:S(2)}) collective-permute-start(s32[128,2]{0,1:T(2,128)S(1)} %bitcast.107), channel_id=1, source_target_pairs={{8,0},{16,8},{24,16},{9,1},{17,9},{25,17},{10,2},{18,10},{26,18},{... | collective-permute-start | bytes 3080 | tf_op jit(solution)/shard_map/ppermute | solution.py:16
  16.4 29.6 %copy-start.8 = (pred[128]{0:T(512)(128)(4,1)}, pred[128]{0:T(512)(128)(4,1)S(1)}, u32[]{:S(2)}) copy-start(pred[128]{0:T(512)(128)(4,1)S(1)} %get-tuple-element.8) | copy-start | bytes 388
  23.6 9.4 %collective-permute-start.5 = (bf16[16,8320]{1,0:T(8,128)(2,1)S(1)}, bf16[16,8320]{1,0:T(8,128)(2,1)S(1)}, u32[]{:S(2)}, u32[]{:S(2)}) collective-permute-start(bf16[16,8320]{1,0:T(8,128)(2,1)S(1)} %slice.56), channel_id=1, source_target_pairs={{0,2},{1,3},{2,0},{3,1},{4,6},{5,7},{6,4},{7,5},{8,10},{9,11},{10,... | collective-permute-start | bytes 798728 | tf_op jit(solution)/shard_map/ppermute | solution.py:44
  24.0 9.2 %collective-permute-start.6 = (bf16[16,8320]{1,0:T(8,128)(2,1)S(1)}, bf16[16,8320]{1,0:T(8,128)(2,1)S(1)}, u32[]{:S(2)}, u32[]{:S(2)}) collective-permute-start(bf16[16,8320]{1,0:T(8,128)(2,1)S(1)} %slice.57), channel_id=1, source_target_pairs={{0,4},{1,5},{2,6},{3,7},{4,0},{5,1},{6,2},{7,3},{8,12},{9,13},{10,... | collective-permute-start | bytes 798728 | tf_op jit(solution)/shard_map/ppermute | solution.py:44
  27.5 15.2 %collective-permute-start.2 = (bf16[32,8320]{1,0:T(8,128)(2,1)S(1)}, bf16[32,8320]{1,0:T(8,128)(2,1)S(1)}, u32[]{:S(2)}, u32[]{:S(2)}) collective-permute-start(bf16[32,8320]{1,0:T(8,128)(2,1)S(1)} %collective-permute-done), channel_id=1, source_target_pairs={{0,2},{1,3},{2,0},{3,1},{4,6},{5,7},{6,4},{7,5},{8,10},{9,11},{10,... | collective-permute-start | bytes 1597448 | tf_op jit(solution)/shard_map/ppermute | solution.py:44
  29.0 15.4 %collective-permute-start.4 = (bf16[32,8320]{1,0:T(8,128)(2,1)S(1)}, bf16[32,8320]{1,0:T(8,128)(2,1)S(1)}, u32[]{:S(2)}, u32[]{:S(2)}) collective-permute-start(bf16[32,8320]{1,0:T(8,128)(2,1)S(1)} %collective-permute-done), channel_id=1, source_target_pairs={{0,4},{1,5},{2,6},{3,7},{4,0},{5,1},{6,2},{7,3},{8,12},{9,13},{10,... | collective-permute-start | bytes 1597448 | tf_op jit(solution)/shard_map/ppermute | solution.py:44
  33.2 12.8 %collective-permute-start.7 = (bf16[32,8320]{1,0:T(8,128)(2,1)S(1)}, bf16[32,8320]{1,0:T(8,128)(2,1)S(1)}, u32[]{:S(2)}, u32[]{:S(2)}) collective-permute-start(bf16[32,8320]{1,0:T(8,128)(2,1)S(1)} %constant_dynamic-update-slice_fusion), channel_id=1, source_target_pairs={{0,1},{1,0},{2,3},{3,2},{4,5},{5,4},{6,7},{7,6},{8,9},{9,8},{10,11... | collective-permute-start | bytes 1597448 | tf_op jit(solution)/shard_map/ppermute | solution.py:44
  77.0 6.6 %copy-start = (bf16[8,2,16,4096]{3,2,1,0:T(8,128)(2,1)S(1)}, bf16[8,2,16,4096]{3,2,1,0:T(8,128)(2,1)}, u32[]{:S(2)}) copy-start(bf16[8,2,16,4096]{3,2,1,0:T(8,128)(2,1)} %get-tuple-element.5) | copy-start | bytes 6291460
  78.5 2.9 %collective-permute-start.8 = (bf16[4,32,4096]{2,1,0:T(8,128)(2,1)S(1)}, bf16[4,32,4096]{2,1,0:T(8,128)(2,1)S(1)}, u32[]{:S(2)}, u32[]{:S(2)}) collective-permute-start(bf16[4,32,4096]{2,1,0:T(8,128)(2,1)S(1)} %slice_bitcast_fusion.2), channel_id=1, source_target_pairs={{0,1},{1,0},{2,3},{3,2},{4,5},{5,4},{6,7},{7,6},{8,9},{9,8},{10,11... | collective-permute-start | bytes 3145736 | tf_op jit(solution)/shard_map/ppermute | solution.py:78
  80.8 2.8 %collective-permute-start.12 = (bf16[4,32,4096]{2,1,0:T(8,128)(2,1)S(1)}, bf16[4,32,4096]{2,1,0:T(8,128)(2,1)S(1)}, u32[]{:S(2)}, u32[]{:S(2)}) collective-permute-start(bf16[4,32,4096]{2,1,0:T(8,128)(2,1)S(1)} %slice_bitcast_fusion), channel_id=1, source_target_pairs={{0,1},{1,0},{2,3},{3,2},{4,5},{5,4},{6,7},{7,6},{8,9},{9,8},{10,11... | collective-permute-start | bytes 3145736 | tf_op jit(solution)/shard_map/ppermute | solution.py:78
  81.7 19.8 %copy-start.7 = (s32[128]{0:T(128)S(1)}, s32[128]{0:T(128)}, u32[]{:S(2)}) copy-start(s32[128]{0:T(128)} %add_reduce_fusion) | copy-start | bytes 1540
  81.7 19.8 %copy-start.9 = (pred[128]{0:T(512)(128)(4,1)S(1)}, pred[128]{0:T(512)(128)(4,1)}, u32[]{:S(2)}) copy-start(pred[128]{0:T(512)(128)(4,1)} %copy-done.8) | copy-start | bytes 388
  81.7 19.8 %copy-start.11 = (pred[128]{0:T(512)(128)(4,1)S(1)}, pred[128]{0:T(512)(128)(4,1)}, u32[]{:S(2)}) copy-start(pred[128]{0:T(512)(128)(4,1)} %copy-done.10) | copy-start | bytes 388
  81.7 22.1 %copy-start.3 = (pred[16,128]{1,0:T(8,128)(4,1)S(1)}, pred[16,128]{1,0:T(8,128)(4,1)}, u32[]{:S(2)}) copy-start(pred[16,128]{1,0:T(8,128)(4,1)} %copy-done.2) | copy-start | bytes 6148
  81.7 22.1 %copy-start.5 = (pred[16,128]{1,0:T(8,128)(4,1)S(1)}, pred[16,128]{1,0:T(8,128)(4,1)}, u32[]{:S(2)}) copy-start(pred[16,128]{1,0:T(8,128)(4,1)} %copy-done.4) | copy-start | bytes 6148
  81.7 13.9 %collective-permute-start.9 = (bf16[2,32,4096]{2,1,0:T(8,128)(2,1)S(1)}, bf16[2,32,4096]{2,1,0:T(8,128)(2,1)S(1)}, u32[]{:S(2)}, u32[]{:S(2)}) collective-permute-start(bf16[2,32,4096]{2,1,0:T(8,128)(2,1)S(1)} %slice_bitcast_fusion.6), channel_id=1, source_target_pairs={{0,2},{1,3},{2,0},{3,1},{4,6},{5,7},{6,4},{7,5},{8,10},{9,11},{10,... | collective-permute-start | bytes 1572872 | tf_op jit(solution)/shard_map/ppermute | solution.py:78
  83.9 14.7 %collective-permute-start.13 = (bf16[2,32,4096]{2,1,0:T(8,128)(2,1)S(1)}, bf16[2,32,4096]{2,1,0:T(8,128)(2,1)S(1)}, u32[]{:S(2)}, u32[]{:S(2)}) collective-permute-start(bf16[2,32,4096]{2,1,0:T(8,128)(2,1)S(1)} %slice_bitcast_fusion.4), channel_id=1, source_target_pairs={{0,4},{1,5},{2,6},{3,7},{4,0},{5,1},{6,2},{7,3},{8,12},{9,13},{10,... | collective-permute-start | bytes 1572872 | tf_op jit(solution)/shard_map/ppermute | solution.py:78
  95.8 8.0 %collective-permute-start.10 = (bf16[32,4096]{1,0:T(8,128)(2,1)S(1)}, bf16[32,4096]{1,0:T(8,128)(2,1)S(1)}, u32[]{:S(2)}, u32[]{:S(2)}) collective-permute-start(bf16[32,4096]{1,0:T(8,128)(2,1)S(1)} %slice_bitcast_fusion.10), channel_id=1, source_target_pairs={{0,4},{1,5},{2,6},{3,7},{4,0},{5,1},{6,2},{7,3},{8,12},{9,13},{10,... | collective-permute-start | bytes 786440 | tf_op jit(solution)/shard_map/ppermute | solution.py:97
  98.9 11.1 %collective-permute-start.14 = (bf16[32,4096]{1,0:T(8,128)(2,1)S(1)}, bf16[32,4096]{1,0:T(8,128)(2,1)S(1)}, u32[]{:S(2)}, u32[]{:S(2)}) collective-permute-start(bf16[32,4096]{1,0:T(8,128)(2,1)S(1)} %get-tuple-element.12), channel_id=1, source_target_pairs={{8,0},{9,1},{10,2},{11,3},{12,4},{13,5},{14,6},{15,7},{16,8},{17,9... | collective-permute-start | bytes 786440 | tf_op jit(solution)/shard_map/ppermute | solution.py:107
  100.2 13.5 %collective-permute-start.15 = (bf16[32,4096]{1,0:T(8,128)(2,1)S(1)}, bf16[32,4096]{1,0:T(8,128)(2,1)S(1)}, u32[]{:S(2)}, u32[]{:S(2)}) collective-permute-start(bf16[32,4096]{1,0:T(8,128)(2,1)S(1)} %get-tuple-element.13), channel_id=1, source_target_pairs={{8,2},{9,3},{10,0},{11,1},{12,6},{13,7},{14,4},{15,5},{16,10},{17,... | collective-permute-start | bytes 786440 | tf_op jit(solution)/shard_map/ppermute | solution.py:108
  (4 other events, 12.8 us)

commit v15 on v14

--- a/solution.py
+++ b/solution.py
@@ -206,10 +206,16 @@
     gathered = gather_over_et(packed).reshape(n, E_WIN, MOST, 2 * width + TAIL)
     out_parts, grad_parts = expert_pass(gathered, gate_mats, up_mats, down_mats)
     same = lambda value: value
-    out_sums = reduce_to_owner(out_parts.reshape(n, E_WIN * MOST, width), round_order(n, n // 2), same)
-    received = unpack(
-        reduce_to_previous(grad_parts.reshape(n, E_WIN * MOST, width), round_order(n, 2), same), next_select
-    )
+    slots = E_WIN * MOST
+    both = jnp.concatenate(
+        [out_parts.reshape(n, slots, width), grad_parts.reshape(n, slots, width)], axis=1
+    ).reshape(n // 2, 2, 2 * slots, width)
+    merged = swap(both[:, 1], 1)
+    held = (both[:, 0].astype(jnp.float32) + merged.astype(jnp.float32)).astype(jnp.bfloat16)
+    out_order = [bit for bit in round_order(n, n // 2) if bit != 1]
+    grad_order = [bit for bit in round_order(n, 2) if bit != 1]
+    out_sums = reduce_to_owner(held[:, :slots], out_order, same)
+    received = unpack(reduce_to_previous(held[:, slots:], grad_order, same), next_select)
     out_share = unpack(out_sums, select)
     return (out_share[None], received[None])
 

time: 116 us -> 121 us (1.043)
  waiting for transfers between devices: 44.1 us -> 49.2 us
  other arithmetic: 5.64 us -> 8.91 us
  local copies, waits for them, and re-layouts: 10.8 us -> 7.59 us
    ppermute x8 -> x9, waiting for transfers between devices: 17.9 us -> 24.9 us  [swap(): return lax.ppermute(value, 'et', [(i, i ^ bit) for i in range(n)])]
    squeeze x0 -> x1, other arithmetic: none -> 3.21 us  [per_device(): merged = swap(both[:, 1], 1)]
    another operation x4 -> x2, local copies, waits for them, and re-layouts: 2.82 us -> 0.07 us  [halve_over_et(): give = halves[:, 1].reshape((count // 2,) + held.shape[1:])]
    convert_element_type x0 -> x1, other arithmetic: none -> 2.63 us  [per_device(): (both[:, 0].astype(jnp.float32) + merged.astype(jnp.float32)).astype(jnp....]
    ppermute x4 -> x2, waiting for transfers between devices: 12.7 us -> 11 us  [halve_over_et(): got = lax.ppermute(give, 'et', [(i, i ^ bit) for i in range(n)])]
    sub x4, other arithmetic: 1.83 us -> 0.42 us  [local_slots(): positions = jnp.cumsum(routed.astype(jnp.int32), dtype=jnp.int32) - 1]
    ppermute x4 -> x2, starting transfers between devices: 2.83 us -> 2.19 us  [halve_over_et(): got = lax.ppermute(give, 'et', [(i, i ^ bit) for i in range(n)])]
    unnamed x32 -> x20, local copies, waits for them, and re-layouts: 6.47 us -> 5.9 us
  transfers between devices with their start and end apart: 16 -> 15, of which waited for: 11 -> 9; matrix products, arithmetic and copies ran while one was open for 11% -> 8% of each run, Pallas kernels for 0% -> 0%
where the time goes in v15:
time: 121 us; the launch traced here: 120 us
  waiting for transfers between devices  49.2 us (41%)
  Pallas kernels  30.1 us (25%)
  starting transfers between devices  16.7 us (14%)
  other arithmetic  8.91 us (7%)
  local copies, waits for them, and re-layouts  7.59 us (6%)
  matrix products  6.98 us (6%)
    pallas_call x1, Pallas kernels, expert_pass(): pl.pallas_call(_expert_body, grid=(experts, steps), in_specs=[pl.BlockSpe...  30.1 us
    ppermute x9, waiting for transfers between devices, swap(): return lax.ppermute(value, 'et', [(i, i ^ bit) for i in range(n)])  24.9 us
    ppermute x2, waiting for transfers between devices, halve_over_et(): got = lax.ppermute(give, 'et', [(i, i ^ bit) for i in range(n)])  11 us
    ppermute x9, starting transfers between devices, swap(): return lax.ppermute(value, 'et', [(i, i ^ bit) for i in range(n)])  8.86 us
    unnamed x20, local copies, waits for them, and re-layouts  5.9 us
    ppermute x1, waiting for transfers between devices, reduce_to_previous(): first = lax.ppermute(keep, ('pipe', 'et'), to_same)  4.1 us
    dot_general x2, matrix products, unpack(): lax.dot_general(select.astype(jnp.float32), slot_sums, (((0,), (0,)), (()...  3.99 us
    ppermute x1, waiting for transfers between devices, shifted(): lax.ppermute(value, axis, [(source, source + steps) for source in range(f...  3.98 us
  transfers between devices with their start and end apart: 15, of which 9 were waited for; matrix products, arithmetic and copies ran while one was open for 8% of the time, Pallas kernels for 0%

profile of v15, /device:TPU:0, one launch (start us, length us, event | category | flops | bytes accessed | tf_op | source)
XLA Modules:
  0.0 120.3 jit_solution(7452714570972913587)
XLA Ops:
  2.2 1.5 %convolution_convert_fusion.3 = bf16[32,4096]{1,0:T(8,128)(2,1)S(1)} fusion(bf16[1,128,4096]{2,1,0:T(8,128)(2,1)} %param.7, pred[16,128]{1,0:T(8,128)(4,1)S(1)} %get-tuple-element.19, pred[16,128]{1,0:T(8,128)(4,1)S(1)} %get-tuple-element.18), kind=kOutput, calls=%fused_computation.5 | convolution fusion | flops 33689600 | bytes 1314816 | tf_op jit(solution)/shard_map/dot_general | solution.py:39
  3.7 1.5 %convolution_convert_fusion.2 = bf16[32,4096]{1,0:T(8,128)(2,1)S(1)} fusion(bf16[1,128,4096]{2,1,0:T(8,128)(2,1)} %param.10, pred[16,128]{1,0:T(8,128)(4,1)S(1)} %get-tuple-element.19, pred[16,128]{1,0:T(8,128)(4,1)S(1)} %get-tuple-element.18), kind=kOutput, calls=%fused_computation.4 | convolution fusion | flops 33689600 | bytes 1314816 | tf_op jit(solution)/shard_map/dot_general | solution.py:39
  6.7 2.6 %collective-permute-start.1 = (bf16[32,8320]{1,0:T(8,128)(2,1)S(1)}, bf16[32,8320]{1,0:T(8,128)(2,1)S(1)}, u32[]{:S(2)}, u32[]{:S(2)}) collective-permute-start(bf16[32,8320]{1,0:T(8,128)(2,1)S(1)} %pad_maximum_fusion.1), channel_id=1, source_target_pairs={{0,2},{1,3},{2,0},{3,1},{4,6},{5,7},{6,4},{7,5},{8,10},{9,11},{10,... | collective-permute-start | bytes 1597448 | tf_op jit(solution)/shard_map/ppermute | solution.py:44
  9.3 1.5 %collective-permute-start.3 = (bf16[32,8320]{1,0:T(8,128)(2,1)S(1)}, bf16[32,8320]{1,0:T(8,128)(2,1)S(1)}, u32[]{:S(2)}, u32[]{:S(2)}) collective-permute-start(bf16[32,8320]{1,0:T(8,128)(2,1)S(1)} %pad_maximum_fusion.1), channel_id=1, source_target_pairs={{0,4},{1,5},{2,6},{3,7},{4,0},{5,1},{6,2},{7,3},{8,12},{9,13},{10,... | collective-permute-start | bytes 1597448 | tf_op jit(solution)/shard_map/ppermute | solution.py:44
  11.7 11.8 %collective-permute-done.3 = bf16[32,8320]{1,0:T(8,128)(2,1)S(1)} collective-permute-done((bf16[32,8320]{1,0:T(8,128)(2,1)S(1)}, bf16[32,8320]{1,0:T(8,128)(2,1)S(1)}, u32[]{:S(2)}, u32[]{:S(2)}) %collective-permute-start.3) | collective-permute-done | bytes 532512 | tf_op jit(solution)/shard_map/ppermute | solution.py:44
  23.9 1.8 %collective-permute-start.6 = (bf16[16,8320]{1,0:T(8,128)(2,1)S(1)}, bf16[16,8320]{1,0:T(8,128)(2,1)S(1)}, u32[]{:S(2)}, u32[]{:S(2)}) collective-permute-start(bf16[16,8320]{1,0:T(8,128)(2,1)S(1)} %slice.57), channel_id=1, source_target_pairs={{0,4},{1,5},{2,6},{3,7},{4,0},{5,1},{6,2},{7,3},{8,12},{9,13},{10,... | collective-permute-start | bytes 798728 | tf_op jit(solution)/shard_map/ppermute | solution.py:44
  27.4 1.5 %collective-permute-start.2 = (bf16[32,8320]{1,0:T(8,128)(2,1)S(1)}, bf16[32,8320]{1,0:T(8,128)(2,1)S(1)}, u32[]{:S(2)}, u32[]{:S(2)}) collective-permute-start(bf16[32,8320]{1,0:T(8,128)(2,1)S(1)} %collective-permute-done), channel_id=1, source_target_pairs={{0,2},{1,3},{2,0},{3,1},{4,6},{5,7},{6,4},{7,5},{8,10},{9,11},{10,... | collective-permute-start | bytes 1597448 | tf_op jit(solution)/shard_map/ppermute | solution.py:44
  29.4 3.5 %collective-permute-done.5 = bf16[16,8320]{1,0:T(8,128)(2,1)S(1)} collective-permute-done((bf16[16,8320]{1,0:T(8,128)(2,1)S(1)}, bf16[16,8320]{1,0:T(8,128)(2,1)S(1)}, u32[]{:S(2)}, u32[]{:S(2)}) %collective-permute-start.5) | collective-permute-done | bytes 266272 | tf_op jit(solution)/shard_map/ppermute | solution.py:44
  33.2 9.4 %collective-permute-done.2 = bf16[32,8320]{1,0:T(8,128)(2,1)S(1)} collective-permute-done((bf16[32,8320]{1,0:T(8,128)(2,1)S(1)}, bf16[32,8320]{1,0:T(8,128)(2,1)S(1)}, u32[]{:S(2)}, u32[]{:S(2)}) %collective-permute-start.2) | collective-permute-done | bytes 532512 | tf_op jit(solution)/shard_map/ppermute | solution.py:44
  46.8 30.1 %shard_map.86 = (bf16[8,2,16,4096]{3,2,1,0:T(8,128)(2,1)}, bf16[8,2,16,4096]{3,2,1,0:T(8,128)(2,1)}) custom-call(bf16[8,2,16,8320]{3,2,1,0:T(8,128)(2,1)} %constant_dynamic-update-slice_fusion.2.x_ref.g_ref.w_ref, bf16[8,2,16,8320]{3,2,1,0:T(8,128)(2,1)} %constant_dynamic-update-slice_fusion.2.x_ref.g_ref.w_ref, ...), custom_call_target="tpu_custom_call" | custom-call | tf_op jit(solution)/shard_map/pallas_call | solution.py:165
  76.9 3.2 %fusion.5 = bf16[4,64,4096]{2,1,0:T(8,128)(2,1)} fusion(bf16[4,2,32,4096]{3,2,1,0:T(8,128)(2,1)} %bitcast.84, bf16[4,2,32,4096]{3,2,1,0:T(8,128)(2,1)} %bitcast.82), kind=kLoop, calls=%fused_computation.13 | loop fusion | flops 4194304 | bytes 6291456 | tf_op jit(solution)/shard_map/squeeze | solution.py:213
  80.1 1.5 %collective-permute-start.11 = (s32[128,2]{0,1:T(2,128)S(1)}, s32[128,2]{0,1:T(2,128)S(1)}, u32[]{:S(2)}, u32[]{:S(2)}) collective-permute-start(s32[128,2]{0,1:T(2,128)S(1)} %bitcast.98), channel_id=1, source_target_pairs={{8,0},{16,8},{24,16},{9,1},{17,9},{25,17},{10,2},{18,10},{26,18},{... | collective-permute-start | bytes 3080 | tf_op jit(solution)/shard_map/ppermute | solution.py:16
  81.6 4.0 %collective-permute-done.11 = s32[128,2]{0,1:T(2,128)S(1)} collective-permute-done((s32[128,2]{0,1:T(2,128)S(1)}, s32[128,2]{0,1:T(2,128)S(1)}, u32[]{:S(2)}, u32[]{:S(2)}) %collective-permute-start.11) | collective-permute-done | bytes 1056 | tf_op jit(solution)/shard_map/ppermute | solution.py:16
  86.4 2.6 %fusion.2 = bf16[4,64,4096]{2,1,0:T(8,128)(2,1)S(1)} fusion(bf16[4,64,4096]{2,1,0:T(8,128)(2,1)} %collective-permute-done.8, bf16[4,2,32,4096]{3,2,1,0:T(8,128)(2,1)S(1)} %bitcast.83, bf16[4,2,32,4096]{3,2,1,0:T(8,128)(2,1)} %bitcast.85), kind=kLoop, calls=%fused_computation.9 | loop fusion | flops 8388608 | bytes 8388608 | tf_op jit(solution)/shard_map/convert_element_type | solution.py:214
  90.0 1.6 %collective-permute-start.12 = (bf16[2,32,4096]{2,1,0:T(8,128)(2,1)S(1)}, bf16[2,32,4096]{2,1,0:T(8,128)(2,1)S(1)}, u32[]{:S(2)}, u32[]{:S(2)}) collective-permute-start(bf16[2,32,4096]{2,1,0:T(8,128)(2,1)S(1)} %slice_bitcast_fusion), channel_id=1, source_target_pairs={{0,4},{1,5},{2,6},{3,7},{4,0},{5,1},{6,2},{7,3},{8,12},{9,13},{10,... | collective-permute-start | bytes 1572872 | tf_op jit(solution)/shard_map/ppermute | solution.py:78
  91.5 11.0 %collective-permute-done.9 = bf16[2,32,4096]{2,1,0:T(8,128)(2,1)S(1)} collective-permute-done((bf16[2,32,4096]{2,1,0:T(8,128)(2,1)S(1)}, bf16[2,32,4096]{2,1,0:T(8,128)(2,1)S(1)}, u32[]{:S(2)}, u32[]{:S(2)}) %collective-permute-start.9) | collective-permute-done | bytes 524320 | tf_op jit(solution)/shard_map/ppermute | solution.py:78
  102.7 1.6 %collective-permute-start.10 = (bf16[32,4096]{1,0:T(8,128)(2,1)S(1)}, bf16[32,4096]{1,0:T(8,128)(2,1)S(1)}, u32[]{:S(2)}, u32[]{:S(2)}) collective-permute-start(bf16[32,4096]{1,0:T(8,128)(2,1)S(1)} %slice_bitcast_fusion.6), channel_id=1, source_target_pairs={{0,4},{1,5},{2,6},{3,7},{4,0},{5,1},{6,2},{7,3},{8,12},{9,13},{10,... | collective-permute-start | bytes 786440 | tf_op jit(solution)/shard_map/ppermute | solution.py:97
  104.5 1.3 %collective-permute-start.13 = (bf16[32,4096]{1,0:T(8,128)(2,1)S(1)}, bf16[32,4096]{1,0:T(8,128)(2,1)S(1)}, u32[]{:S(2)}, u32[]{:S(2)}) collective-permute-start(bf16[32,4096]{1,0:T(8,128)(2,1)S(1)} %get-tuple-element.14), channel_id=1, source_target_pairs={{8,0},{9,1},{10,2},{11,3},{12,4},{13,5},{14,6},{15,7},{16,8},{17,9... | collective-permute-start | bytes 786440 | tf_op jit(solution)/shard_map/ppermute | solution.py:107
  105.8 1.3 %collective-permute-start.14 = (bf16[32,4096]{1,0:T(8,128)(2,1)S(1)}, bf16[32,4096]{1,0:T(8,128)(2,1)S(1)}, u32[]{:S(2)}, u32[]{:S(2)}) collective-permute-start(bf16[32,4096]{1,0:T(8,128)(2,1)S(1)} %get-tuple-element.15), channel_id=1, source_target_pairs={{8,2},{9,3},{10,0},{11,1},{12,6},{13,7},{14,4},{15,5},{16,10},{17,... | collective-permute-start | bytes 786440 | tf_op jit(solution)/shard_map/ppermute | solution.py:108
  107.1 2.3 %collective-permute-done.10 = bf16[32,4096]{1,0:T(8,128)(2,1)S(1)} collective-permute-done((bf16[32,4096]{1,0:T(8,128)(2,1)S(1)}, bf16[32,4096]{1,0:T(8,128)(2,1)S(1)}, u32[]{:S(2)}, u32[]{:S(2)}) %collective-permute-start.10) | collective-permute-done | bytes 262176 | tf_op jit(solution)/shard_map/ppermute | solution.py:97
  109.4 2.0 %fusion = bf16[1,128,4096]{2,1,0:T(8,128)(2,1)} fusion(bf16[32,4096]{1,0:T(8,128)(2,1)S(1)} %collective-permute-done.10, bf16[2,32,4096]{2,1,0:T(8,128)(2,1)S(1)} %fusion.7, pred[16,128]{1,0:T(8,128)(4,1)S(1)} %copy-done.4, pred[16,128]{1,0:T(8,128)(4,1)S(1)} %copy-done.2), kind=kOutput, calls=%fused_computation.2 | convolution fusion | flops 202248192 | bytes 1576960 | tf_op jit(solution)/shard_map/dot_general | solution.py:113
  111.4 4.1 %collective-permute-done.13 = bf16[32,4096]{1,0:T(8,128)(2,1)S(1)} collective-permute-done((bf16[32,4096]{1,0:T(8,128)(2,1)S(1)}, bf16[32,4096]{1,0:T(8,128)(2,1)S(1)}, u32[]{:S(2)}, u32[]{:S(2)}) %collective-permute-start.13) | collective-permute-done | bytes 262176 | tf_op jit(solution)/shard_map/ppermute | solution.py:107
  115.5 2.8 %collective-permute-done.14 = bf16[32,4096]{1,0:T(8,128)(2,1)S(1)} collective-permute-done((bf16[32,4096]{1,0:T(8,128)(2,1)S(1)}, bf16[32,4096]{1,0:T(8,128)(2,1)S(1)}, u32[]{:S(2)}, u32[]{:S(2)}) %collective-permute-start.14) | collective-permute-done | bytes 262176 | tf_op jit(solution)/shard_map/ppermute | solution.py:108
  118.3 2.0 %fusion.1 = bf16[1,128,4096]{2,1,0:T(8,128)(2,1)} fusion(bf16[32,4096]{1,0:T(8,128)(2,1)S(1)} %collective-permute-done.14, bf16[32,4096]{1,0:T(8,128)(2,1)S(1)} %collective-permute-done.13, pred[16,128]{1,0:T(8,128)(4,1)S(1)} %get-tuple-element.21, pred[16,128]{1,0:T(8,128)(4,1)S(1)} %get-tuple-element.20), kind=kOutput, calls=%fused_computation.3 | convolution fusion | flops 202248192 | bytes 1576960 | tf_op jit(solution)/shard_map/dot_general | solution.py:113
  (69 shorter events, 13.0 us)
Async XLA Ops:
  2.2 3.9 %copy-start.1 = (pred[16,128]{1,0:T(8,128)(4,1)}, pred[16,128]{1,0:T(8,128)(4,1)S(1)}, u32[]{:S(2)}) copy-start(pred[16,128]{1,0:T(8,128)(4,1)S(1)} %get-tuple-element.18) | copy-start | bytes 6148
  2.2 3.9 %copy-start.3 = (pred[16,128]{1,0:T(8,128)(4,1)}, pred[16,128]{1,0:T(8,128)(4,1)S(1)}, u32[]{:S(2)}) copy-start(pred[16,128]{1,0:T(8,128)(4,1)S(1)} %get-tuple-element.19) | copy-start | bytes 6148
  6.2 19.5 %collective-permute-start = (bf16[32,8320]{1,0:T(8,128)(2,1)S(1)}, bf16[32,8320]{1,0:T(8,128)(2,1)S(1)}, u32[]{:S(2)}, u32[]{:S(2)}) collective-permute-start(bf16[32,8320]{1,0:T(8,128)(2,1)S(1)} %pad_maximum_fusion.1), channel_id=1, source_target_pairs={{0,1},{1,0},{2,3},{3,2},{4,5},{5,4},{6,7},{7,6},{8,9},{9,8},{10,11... | collective-permute-start | bytes 1597448 | tf_op jit(solution)/shard_map/ppermute | solution.py:44
  6.7 17.1 %collective-permute-start.1 = (bf16[32,8320]{1,0:T(8,128)(2,1)S(1)}, bf16[32,8320]{1,0:T(8,128)(2,1)S(1)}, u32[]{:S(2)}, u32[]{:S(2)}) collective-permute-start(bf16[32,8320]{1,0:T(8,128)(2,1)S(1)} %pad_maximum_fusion.1), channel_id=1, source_target_pairs={{0,2},{1,3},{2,0},{3,1},{4,6},{5,7},{6,4},{7,5},{8,10},{9,11},{10,... | collective-permute-start | bytes 1597448 | tf_op jit(solution)/shard_map/ppermute | solution.py:44
  9.3 14.2 %collective-permute-start.3 = (bf16[32,8320]{1,0:T(8,128)(2,1)S(1)}, bf16[32,8320]{1,0:T(8,128)(2,1)S(1)}, u32[]{:S(2)}, u32[]{:S(2)}) collective-permute-start(bf16[32,8320]{1,0:T(8,128)(2,1)S(1)} %pad_maximum_fusion.1), channel_id=1, source_target_pairs={{0,4},{1,5},{2,6},{3,7},{4,0},{5,1},{6,2},{7,3},{8,12},{9,13},{10,... | collective-permute-start | bytes 1597448 | tf_op jit(solution)/shard_map/ppermute | solution.py:44
  23.5 9.4 %collective-permute-start.5 = (bf16[16,8320]{1,0:T(8,128)(2,1)S(1)}, bf16[16,8320]{1,0:T(8,128)(2,1)S(1)}, u32[]{:S(2)}, u32[]{:S(2)}) collective-permute-start(bf16[16,8320]{1,0:T(8,128)(2,1)S(1)} %slice.56), channel_id=1, source_target_pairs={{0,2},{1,3},{2,0},{3,1},{4,6},{5,7},{6,4},{7,5},{8,10},{9,11},{10,... | collective-permute-start | bytes 798728 | tf_op jit(solution)/shard_map/ppermute | solution.py:44
  23.9 9.2 %collective-permute-start.6 = (bf16[16,8320]{1,0:T(8,128)(2,1)S(1)}, bf16[16,8320]{1,0:T(8,128)(2,1)S(1)}, u32[]{:S(2)}, u32[]{:S(2)}) collective-permute-start(bf16[16,8320]{1,0:T(8,128)(2,1)S(1)} %slice.57), channel_id=1, source_target_pairs={{0,4},{1,5},{2,6},{3,7},{4,0},{5,1},{6,2},{7,3},{8,12},{9,13},{10,... | collective-permute-start | bytes 798728 | tf_op jit(solution)/shard_map/ppermute | solution.py:44
  27.4 15.2 %collective-permute-start.2 = (bf16[32,8320]{1,0:T(8,128)(2,1)S(1)}, bf16[32,8320]{1,0:T(8,128)(2,1)S(1)}, u32[]{:S(2)}, u32[]{:S(2)}) collective-permute-start(bf16[32,8320]{1,0:T(8,128)(2,1)S(1)} %collective-permute-done), channel_id=1, source_target_pairs={{0,2},{1,3},{2,0},{3,1},{4,6},{5,7},{6,4},{7,5},{8,10},{9,11},{10,... | collective-permute-start | bytes 1597448 | tf_op jit(solution)/shard_map/ppermute | solution.py:44
  28.9 15.4 %collective-permute-start.4 = (bf16[32,8320]{1,0:T(8,128)(2,1)S(1)}, bf16[32,8320]{1,0:T(8,128)(2,1)S(1)}, u32[]{:S(2)}, u32[]{:S(2)}) collective-permute-start(bf16[32,8320]{1,0:T(8,128)(2,1)S(1)} %collective-permute-done), channel_id=1, source_target_pairs={{0,4},{1,5},{2,6},{3,7},{4,0},{5,1},{6,2},{7,3},{8,12},{9,13},{10,... | collective-permute-start | bytes 1597448 | tf_op jit(solution)/shard_map/ppermute | solution.py:44
  33.1 12.8 %collective-permute-start.7 = (bf16[32,8320]{1,0:T(8,128)(2,1)S(1)}, bf16[32,8320]{1,0:T(8,128)(2,1)S(1)}, u32[]{:S(2)}, u32[]{:S(2)}) collective-permute-start(bf16[32,8320]{1,0:T(8,128)(2,1)S(1)} %constant_dynamic-update-slice_fusion), channel_id=1, source_target_pairs={{0,1},{1,0},{2,3},{3,2},{4,5},{5,4},{6,7},{7,6},{8,9},{9,8},{10,11... | collective-permute-start | bytes 1597448 | tf_op jit(solution)/shard_map/ppermute | solution.py:44
  76.9 3.2 %copy-start.5 = (s32[1,128,2]{1,2,0:T(2,128)S(1)}, s32[1,128,2]{1,2,0:T(2,128)}, u32[]{:S(2)}) copy-start(s32[1,128,2]{1,2,0:T(2,128)} %param.9) | copy-start | bytes 3076
  76.9 9.5 %copy-start = (bf16[8,2,16,4096]{3,2,1,0:T(8,128)(2,1)S(1)}, bf16[8,2,16,4096]{3,2,1,0:T(8,128)(2,1)}, u32[]{:S(2)}) copy-start(bf16[8,2,16,4096]{3,2,1,0:T(8,128)(2,1)} %get-tuple-element.4) | copy-start | bytes 6291460
  80.1 6.3 %collective-permute-start.8 = (bf16[4,64,4096]{2,1,0:T(8,128)(2,1)}, bf16[4,64,4096]{2,1,0:T(8,128)(2,1)}, u32[]{:S(2)}, u32[]{:S(2)}) collective-permute-start(bf16[4,64,4096]{2,1,0:T(8,128)(2,1)} %fusion.5), channel_id=1, source_target_pairs={{0,1},{1,0},{2,3},{3,2},{4,5},{5,4},{6,7},{7,6},{8,9},{9,8},{10,11... | collective-permute-start | bytes 6291464 | tf_op jit(solution)/shard_map/ppermute | solution.py:44
  80.1 5.5 %collective-permute-start.11 = (s32[128,2]{0,1:T(2,128)S(1)}, s32[128,2]{0,1:T(2,128)S(1)}, u32[]{:S(2)}, u32[]{:S(2)}) collective-permute-start(s32[128,2]{0,1:T(2,128)S(1)} %bitcast.98), channel_id=1, source_target_pairs={{8,0},{16,8},{24,16},{9,1},{17,9},{25,17},{10,2},{18,10},{26,18},{... | collective-permute-start | bytes 3080 | tf_op jit(solution)/shard_map/ppermute | solution.py:16
  89.2 20.2 %copy-start.2 = (pred[16,128]{1,0:T(8,128)(4,1)S(1)}, pred[16,128]{1,0:T(8,128)(4,1)}, u32[]{:S(2)}) copy-start(pred[16,128]{1,0:T(8,128)(4,1)} %copy-done.1) | copy-start | bytes 6148
  89.2 20.2 %copy-start.4 = (pred[16,128]{1,0:T(8,128)(4,1)S(1)}, pred[16,128]{1,0:T(8,128)(4,1)}, u32[]{:S(2)}) copy-start(pred[16,128]{1,0:T(8,128)(4,1)} %copy-done.3) | copy-start | bytes 6148
  89.3 13.3 %collective-permute-start.9 = (bf16[2,32,4096]{2,1,0:T(8,128)(2,1)S(1)}, bf16[2,32,4096]{2,1,0:T(8,128)(2,1)S(1)}, u32[]{:S(2)}, u32[]{:S(2)}) collective-permute-start(bf16[2,32,4096]{2,1,0:T(8,128)(2,1)S(1)} %slice_bitcast_fusion.2), channel_id=1, source_target_pairs={{0,2},{1,3},{2,0},{3,1},{4,6},{5,7},{6,4},{7,5},{8,10},{9,11},{10,... | collective-permute-start | bytes 1572872 | tf_op jit(solution)/shard_map/ppermute | solution.py:78
  90.0 14.3 %collective-permute-start.12 = (bf16[2,32,4096]{2,1,0:T(8,128)(2,1)S(1)}, bf16[2,32,4096]{2,1,0:T(8,128)(2,1)S(1)}, u32[]{:S(2)}, u32[]{:S(2)}) collective-permute-start(bf16[2,32,4096]{2,1,0:T(8,128)(2,1)S(1)} %slice_bitcast_fusion), channel_id=1, source_target_pairs={{0,4},{1,5},{2,6},{3,7},{4,0},{5,1},{6,2},{7,3},{8,12},{9,13},{10,... | collective-permute-start | bytes 1572872 | tf_op jit(solution)/shard_map/ppermute | solution.py:78
  102.7 6.7 %collective-permute-start.10 = (bf16[32,4096]{1,0:T(8,128)(2,1)S(1)}, bf16[32,4096]{1,0:T(8,128)(2,1)S(1)}, u32[]{:S(2)}, u32[]{:S(2)}) collective-permute-start(bf16[32,4096]{1,0:T(8,128)(2,1)S(1)} %slice_bitcast_fusion.6), channel_id=1, source_target_pairs={{0,4},{1,5},{2,6},{3,7},{4,0},{5,1},{6,2},{7,3},{8,12},{9,13},{10,... | collective-permute-start | bytes 786440 | tf_op jit(solution)/shard_map/ppermute | solution.py:97
  104.5 11.1 %collective-permute-start.13 = (bf16[32,4096]{1,0:T(8,128)(2,1)S(1)}, bf16[32,4096]{1,0:T(8,128)(2,1)S(1)}, u32[]{:S(2)}, u32[]{:S(2)}) collective-permute-start(bf16[32,4096]{1,0:T(8,128)(2,1)S(1)} %get-tuple-element.14), channel_id=1, source_target_pairs={{8,0},{9,1},{10,2},{11,3},{12,4},{13,5},{14,6},{15,7},{16,8},{17,9... | collective-permute-start | bytes 786440 | tf_op jit(solution)/shard_map/ppermute | solution.py:107
  105.8 12.6 %collective-permute-start.14 = (bf16[32,4096]{1,0:T(8,128)(2,1)S(1)}, bf16[32,4096]{1,0:T(8,128)(2,1)S(1)}, u32[]{:S(2)}, u32[]{:S(2)}) collective-permute-start(bf16[32,4096]{1,0:T(8,128)(2,1)S(1)} %get-tuple-element.15), channel_id=1, source_target_pairs={{8,2},{9,3},{10,0},{11,1},{12,6},{13,7},{14,4},{15,5},{16,10},{17,... | collective-permute-start | bytes 786440 | tf_op jit(solution)/shard_map/ppermute | solution.py:108

commit v16 on v14

--- a/solution.py
+++ b/solution.py
@@ -206,9 +206,9 @@
     gathered = gather_over_et(packed).reshape(n, E_WIN, MOST, 2 * width + TAIL)
     out_parts, grad_parts = expert_pass(gathered, gate_mats, up_mats, down_mats)
     same = lambda value: value
-    out_sums = reduce_to_owner(out_parts.reshape(n, E_WIN * MOST, width), round_order(n, n // 2), same)
+    out_sums = reduce_to_owner(out_parts.reshape(n, E_WIN * MOST, width), round_order(n, 2), same)
     received = unpack(
-        reduce_to_previous(grad_parts.reshape(n, E_WIN * MOST, width), round_order(n, 2), same), next_select
+        reduce_to_previous(grad_parts.reshape(n, E_WIN * MOST, width), round_order(n, n // 2), same), next_select
     )
     out_share = unpack(out_sums, select)
     return (out_share[None], received[None])

time: 116 us -> 117 us (level)
  waiting for transfers between devices: 44.1 us -> 46 us
where the time goes in v16:
time: 117 us
  waiting for transfers between devices  46 us (39%)
  Pallas kernels  30.1 us (26%)
  starting transfers between devices  16.2 us (14%)
  local copies, waits for them, and re-layouts  10.8 us (9%)
  matrix products  6.98 us (6%)
  other arithmetic  5.64 us (5%)
    pallas_call x1, Pallas kernels, expert_pass(): pl.pallas_call(_expert_body, grid=(experts, steps), in_specs=[pl.BlockSpe...  30.1 us
    ppermute x8, waiting for transfers between devices, swap(): return lax.ppermute(value, 'et', [(i, i ^ bit) for i in range(n)])  17.9 us
    ppermute x4, waiting for transfers between devices, halve_over_et(): got = lax.ppermute(give, 'et', [(i, i ^ bit) for i in range(n)])  13.7 us
    ppermute x8, starting transfers between devices, swap(): return lax.ppermute(value, 'et', [(i, i ^ bit) for i in range(n)])  8.85 us
    unnamed x32, local copies, waits for them, and re-layouts  6.47 us
    ppermute x1, waiting for transfers between devices, reduce_to_previous(): second = lax.ppermute(give, ('pipe', 'et'), to_other)  4.62 us
    ppermute x1, waiting for transfers between devices, reduce_to_previous(): first = lax.ppermute(keep, ('pipe', 'et'), to_same)  4.17 us
    dot_general x2, matrix products, unpack(): lax.dot_general(select.astype(jnp.float32), slot_sums, (((0,), (0,)), (()...  4 us
  transfers between devices with their start and end apart: 16, of which 11 were waited for; matrix products, arithmetic and copies ran while one was open for 11% of the time, Pallas kernels for 0%

profile of v16, /device:TPU:0, one launch (start us, length us, event | category | flops | bytes accessed | tf_op | source)
XLA Modules:
  0.0 116.6 jit_solution(15295203846707071722)
XLA Ops:
  2.3 1.5 %convolution_convert_fusion.3 = bf16[32,4096]{1,0:T(8,128)(2,1)S(1)} fusion(bf16[1,128,4096]{2,1,0:T(8,128)(2,1)} %param.7, pred[16,128]{1,0:T(8,128)(4,1)S(1)} %get-tuple-element.17, pred[16,128]{1,0:T(8,128)(4,1)S(1)} %get-tuple-element.16), kind=kOutput, calls=%fused_computation.5 | convolution fusion | flops 33689600 | bytes 1314816 | tf_op jit(solution)/shard_map/dot_general | solution.py:39
  3.8 1.5 %convolution_convert_fusion.2 = bf16[32,4096]{1,0:T(8,128)(2,1)S(1)} fusion(bf16[1,128,4096]{2,1,0:T(8,128)(2,1)} %param.10, pred[16,128]{1,0:T(8,128)(4,1)S(1)} %get-tuple-element.17, pred[16,128]{1,0:T(8,128)(4,1)S(1)} %get-tuple-element.16), kind=kOutput, calls=%fused_computation.4 | convolution fusion | flops 33689600 | bytes 1314816 | tf_op jit(solution)/shard_map/dot_general | solution.py:39
  6.8 2.6 %collective-permute-start.1 = (bf16[32,8320]{1,0:T(8,128)(2,1)S(1)}, bf16[32,8320]{1,0:T(8,128)(2,1)S(1)}, u32[]{:S(2)}, u32[]{:S(2)}) collective-permute-start(bf16[32,8320]{1,0:T(8,128)(2,1)S(1)} %pad_maximum_fusion), channel_id=1, source_target_pairs={{0,2},{1,3},{2,0},{3,1},{4,6},{5,7},{6,4},{7,5},{8,10},{9,11},{10,... | collective-permute-start | bytes 1597448 | tf_op jit(solution)/shard_map/ppermute | solution.py:44
  9.4 1.5 %collective-permute-start.3 = (bf16[32,8320]{1,0:T(8,128)(2,1)S(1)}, bf16[32,8320]{1,0:T(8,128)(2,1)S(1)}, u32[]{:S(2)}, u32[]{:S(2)}) collective-permute-start(bf16[32,8320]{1,0:T(8,128)(2,1)S(1)} %pad_maximum_fusion), channel_id=1, source_target_pairs={{0,4},{1,5},{2,6},{3,7},{4,0},{5,1},{6,2},{7,3},{8,12},{9,13},{10,... | collective-permute-start | bytes 1597448 | tf_op jit(solution)/shard_map/ppermute | solution.py:44
  10.9 1.3 %collective-permute-start.11 = (s32[128,2]{0,1:T(2,128)S(1)}, s32[128,2]{0,1:T(2,128)S(1)}, u32[]{:S(2)}, u32[]{:S(2)}) collective-permute-start(s32[128,2]{0,1:T(2,128)S(1)} %bitcast.107), channel_id=1, source_target_pairs={{8,0},{16,8},{24,16},{9,1},{17,9},{25,17},{10,2},{18,10},{26,18},{... | collective-permute-start | bytes 3080 | tf_op jit(solution)/shard_map/ppermute | solution.py:16
  13.0 3.3 %collective-permute-done.11 = s32[128,2]{0,1:T(2,128)S(1)} collective-permute-done((s32[128,2]{0,1:T(2,128)S(1)}, s32[128,2]{0,1:T(2,128)S(1)}, u32[]{:S(2)}, u32[]{:S(2)}) %collective-permute-start.11) | collective-permute-done | bytes 1056 | tf_op jit(solution)/shard_map/ppermute | solution.py:16
  18.8 4.8 %collective-permute-done.3 = bf16[32,8320]{1,0:T(8,128)(2,1)S(1)} collective-permute-done((bf16[32,8320]{1,0:T(8,128)(2,1)S(1)}, bf16[32,8320]{1,0:T(8,128)(2,1)S(1)}, u32[]{:S(2)}, u32[]{:S(2)}) %collective-permute-start.3) | collective-permute-done | bytes 532512 | tf_op jit(solution)/shard_map/ppermute | solution.py:44
  24.0 1.8 %collective-permute-start.6 = (bf16[16,8320]{1,0:T(8,128)(2,1)S(1)}, bf16[16,8320]{1,0:T(8,128)(2,1)S(1)}, u32[]{:S(2)}, u32[]{:S(2)}) collective-permute-start(bf16[16,8320]{1,0:T(8,128)(2,1)S(1)} %slice.57), channel_id=1, source_target_pairs={{0,4},{1,5},{2,6},{3,7},{4,0},{5,1},{6,2},{7,3},{8,12},{9,13},{10,... | collective-permute-start | bytes 798728 | tf_op jit(solution)/shard_map/ppermute | solution.py:44
  27.5 1.5 %collective-permute-start.2 = (bf16[32,8320]{1,0:T(8,128)(2,1)S(1)}, bf16[32,8320]{1,0:T(8,128)(2,1)S(1)}, u32[]{:S(2)}, u32[]{:S(2)}) collective-permute-start(bf16[32,8320]{1,0:T(8,128)(2,1)S(1)} %collective-permute-done), channel_id=1, source_target_pairs={{0,2},{1,3},{2,0},{3,1},{4,6},{5,7},{6,4},{7,5},{8,10},{9,11},{10,... | collective-permute-start | bytes 1597448 | tf_op jit(solution)/shard_map/ppermute | solution.py:44
  29.5 3.5 %collective-permute-done.5 = bf16[16,8320]{1,0:T(8,128)(2,1)S(1)} collective-permute-done((bf16[16,8320]{1,0:T(8,128)(2,1)S(1)}, bf16[16,8320]{1,0:T(8,128)(2,1)S(1)}, u32[]{:S(2)}, u32[]{:S(2)}) %collective-permute-start.5) | collective-permute-done | bytes 266272 | tf_op jit(solution)/shard_map/ppermute | solution.py:44
  33.3 9.4 %collective-permute-done.2 = bf16[32,8320]{1,0:T(8,128)(2,1)S(1)} collective-permute-done((bf16[32,8320]{1,0:T(8,128)(2,1)S(1)}, bf16[32,8320]{1,0:T(8,128)(2,1)S(1)}, u32[]{:S(2)}, u32[]{:S(2)}) %collective-permute-start.2) | collective-permute-done | bytes 532512 | tf_op jit(solution)/shard_map/ppermute | solution.py:44
  46.9 30.1 %shard_map.86 = (bf16[8,2,16,4096]{3,2,1,0:T(8,128)(2,1)}, bf16[8,2,16,4096]{3,2,1,0:T(8,128)(2,1)}) custom-call(bf16[8,2,16,8320]{3,2,1,0:T(8,128)(2,1)} %constant_dynamic-update-slice_fusion.2.x_ref.g_ref.w_ref, bf16[8,2,16,8320]{3,2,1,0:T(8,128)(2,1)} %constant_dynamic-update-slice_fusion.2.x_ref.g_ref.w_ref, ...), custom_call_target="tpu_custom_call" | custom-call | tf_op jit(solution)/shard_map/pallas_call | solution.py:165
  77.0 1.4 %slice_bitcast_fusion.2 = bf16[4,32,4096]{2,1,0:T(8,128)(2,1)S(1)} fusion(bf16[4,2,1,32,4096]{4,3,1,0,2:T(8,128)(2,1)} %bitcast.98), kind=kLoop, calls=%fused_computation.12 | loop fusion | bytes 2097152 | tf_op jit(solution)/shard_map/reshape;squeeze | solution.py:77
  79.5 1.3 %slice_bitcast_fusion = bf16[4,32,4096]{2,1,0:T(8,128)(2,1)S(1)} fusion(bf16[4,2,1,32,4096]{4,3,1,0,2:T(8,128)(2,1)} %bitcast.96), kind=kLoop, calls=%fused_computation.10 | loop fusion | bytes 2097152 | tf_op jit(solution)/shard_map/reshape;squeeze | solution.py:77
  81.7 1.6 %collective-permute-start.9 = (bf16[2,32,4096]{2,1,0:T(8,128)(2,1)S(1)}, bf16[2,32,4096]{2,1,0:T(8,128)(2,1)S(1)}, u32[]{:S(2)}, u32[]{:S(2)}) collective-permute-start(bf16[2,32,4096]{2,1,0:T(8,128)(2,1)S(1)} %slice_bitcast_fusion.6), channel_id=1, source_target_pairs={{0,4},{1,5},{2,6},{3,7},{4,0},{5,1},{6,2},{7,3},{8,12},{9,13},{10,... | collective-permute-start | bytes 1572872 | tf_op jit(solution)/shard_map/ppermute | solution.py:78
  84.6 11.1 %collective-permute-done.9 = bf16[2,32,4096]{2,1,0:T(8,128)(2,1)S(1)} collective-permute-done((bf16[2,32,4096]{2,1,0:T(8,128)(2,1)S(1)}, bf16[2,32,4096]{2,1,0:T(8,128)(2,1)S(1)}, u32[]{:S(2)}, u32[]{:S(2)}) %collective-permute-start.9) | collective-permute-done | bytes 524320 | tf_op jit(solution)/shard_map/ppermute | solution.py:78
  96.4 2.2 %collective-permute-done.13 = bf16[2,32,4096]{2,1,0:T(8,128)(2,1)S(1)} collective-permute-done((bf16[2,32,4096]{2,1,0:T(8,128)(2,1)S(1)}, bf16[2,32,4096]{2,1,0:T(8,128)(2,1)S(1)}, u32[]{:S(2)}, u32[]{:S(2)}) %collective-permute-start.13) | collective-permute-done | bytes 524320 | tf_op jit(solution)/shard_map/ppermute | solution.py:78
  98.9 1.3 %collective-permute-start.14 = (bf16[32,4096]{1,0:T(8,128)(2,1)S(1)}, bf16[32,4096]{1,0:T(8,128)(2,1)S(1)}, u32[]{:S(2)}, u32[]{:S(2)}) collective-permute-start(bf16[32,4096]{1,0:T(8,128)(2,1)S(1)} %get-tuple-element.12), channel_id=1, source_target_pairs={{8,0},{9,1},{10,2},{11,3},{12,4},{13,5},{14,6},{15,7},{16,8},{17,9... | collective-permute-start | bytes 786440 | tf_op jit(solution)/shard_map/ppermute | solution.py:107
  100.2 1.3 %collective-permute-start.15 = (bf16[32,4096]{1,0:T(8,128)(2,1)S(1)}, bf16[32,4096]{1,0:T(8,128)(2,1)S(1)}, u32[]{:S(2)}, u32[]{:S(2)}) collective-permute-start(bf16[32,4096]{1,0:T(8,128)(2,1)S(1)} %get-tuple-element.13), channel_id=1, source_target_pairs={{8,4},{9,5},{10,6},{11,7},{12,0},{13,1},{14,2},{15,3},{16,12},{17,... | collective-permute-start | bytes 786440 | tf_op jit(solution)/shard_map/ppermute | solution.py:108
  101.5 2.3 %collective-permute-done.10 = bf16[32,4096]{1,0:T(8,128)(2,1)S(1)} collective-permute-done((bf16[32,4096]{1,0:T(8,128)(2,1)S(1)}, bf16[32,4096]{1,0:T(8,128)(2,1)S(1)}, u32[]{:S(2)}, u32[]{:S(2)}) %collective-permute-start.10) | collective-permute-done | bytes 262176 | tf_op jit(solution)/shard_map/ppermute | solution.py:97
  103.8 2.0 %fusion = bf16[1,128,4096]{2,1,0:T(8,128)(2,1)} fusion(bf16[32,4096]{1,0:T(8,128)(2,1)S(1)} %collective-permute-done.10, bf16[2,32,4096]{2,1,0:T(8,128)(2,1)S(1)} %fusion.5, pred[16,128]{1,0:T(8,128)(4,1)S(1)} %copy-done.5, pred[16,128]{1,0:T(8,128)(4,1)S(1)} %copy-done.3), kind=kOutput, calls=%fused_computation.2 | convolution fusion | flops 202248192 | bytes 1576960 | tf_op jit(solution)/shard_map/dot_general | solution.py:113
  105.8 4.2 %collective-permute-done.14 = bf16[32,4096]{1,0:T(8,128)(2,1)S(1)} collective-permute-done((bf16[32,4096]{1,0:T(8,128)(2,1)S(1)}, bf16[32,4096]{1,0:T(8,128)(2,1)S(1)}, u32[]{:S(2)}, u32[]{:S(2)}) %collective-permute-start.14) | collective-permute-done | bytes 262176 | tf_op jit(solution)/shard_map/ppermute | solution.py:107
  110.0 4.6 %collective-permute-done.15 = bf16[32,4096]{1,0:T(8,128)(2,1)S(1)} collective-permute-done((bf16[32,4096]{1,0:T(8,128)(2,1)S(1)}, bf16[32,4096]{1,0:T(8,128)(2,1)S(1)}, u32[]{:S(2)}, u32[]{:S(2)}) %collective-permute-start.15) | collective-permute-done | bytes 262176 | tf_op jit(solution)/shard_map/ppermute | solution.py:108
  114.6 2.0 %fusion.1 = bf16[1,128,4096]{2,1,0:T(8,128)(2,1)} fusion(bf16[32,4096]{1,0:T(8,128)(2,1)S(1)} %collective-permute-done.15, bf16[32,4096]{1,0:T(8,128)(2,1)S(1)} %collective-permute-done.14, pred[16,128]{1,0:T(8,128)(4,1)S(1)} %get-tuple-element.19, pred[16,128]{1,0:T(8,128)(4,1)S(1)} %get-tuple-element.18), kind=kOutput, calls=%fused_computation.3 | convolution fusion | flops 202248192 | bytes 1576960 | tf_op jit(solution)/shard_map/dot_general | solution.py:113
  (84 shorter events, 17.6 us)
Async XLA Ops:
  0.6 10.3 %copy-start.6 = (s32[1,128,2]{1,2,0:T(2,128)S(1)}, s32[1,128,2]{1,2,0:T(2,128)}, u32[]{:S(2)}) copy-start(s32[1,128,2]{1,2,0:T(2,128)} %param.9) | copy-start | bytes 3076
  6.3 19.5 %collective-permute-start = (bf16[32,8320]{1,0:T(8,128)(2,1)S(1)}, bf16[32,8320]{1,0:T(8,128)(2,1)S(1)}, u32[]{:S(2)}, u32[]{:S(2)}) collective-permute-start(bf16[32,8320]{1,0:T(8,128)(2,1)S(1)} %pad_maximum_fusion), channel_id=1, source_target_pairs={{0,1},{1,0},{2,3},{3,2},{4,5},{5,4},{6,7},{7,6},{8,9},{9,8},{10,11... | collective-permute-start | bytes 1597448 | tf_op jit(solution)/shard_map/ppermute | solution.py:44
  6.8 17.1 %collective-permute-start.1 = (bf16[32,8320]{1,0:T(8,128)(2,1)S(1)}, bf16[32,8320]{1,0:T(8,128)(2,1)S(1)}, u32[]{:S(2)}, u32[]{:S(2)}) collective-permute-start(bf16[32,8320]{1,0:T(8,128)(2,1)S(1)} %pad_maximum_fusion), channel_id=1, source_target_pairs={{0,2},{1,3},{2,0},{3,1},{4,6},{5,7},{6,4},{7,5},{8,10},{9,11},{10,... | collective-permute-start | bytes 1597448 | tf_op jit(solution)/shard_map/ppermute | solution.py:44
  9.4 14.2 %collective-permute-start.3 = (bf16[32,8320]{1,0:T(8,128)(2,1)S(1)}, bf16[32,8320]{1,0:T(8,128)(2,1)S(1)}, u32[]{:S(2)}, u32[]{:S(2)}) collective-permute-start(bf16[32,8320]{1,0:T(8,128)(2,1)S(1)} %pad_maximum_fusion), channel_id=1, source_target_pairs={{0,4},{1,5},{2,6},{3,7},{4,0},{5,1},{6,2},{7,3},{8,12},{9,13},{10,... | collective-permute-start | bytes 1597448 | tf_op jit(solution)/shard_map/ppermute | solution.py:44
  10.9 5.5 %collective-permute-start.11 = (s32[128,2]{0,1:T(2,128)S(1)}, s32[128,2]{0,1:T(2,128)S(1)}, u32[]{:S(2)}, u32[]{:S(2)}) collective-permute-start(s32[128,2]{0,1:T(2,128)S(1)} %bitcast.107), channel_id=1, source_target_pairs={{8,0},{16,8},{24,16},{9,1},{17,9},{25,17},{10,2},{18,10},{26,18},{... | collective-permute-start | bytes 3080 | tf_op jit(solution)/shard_map/ppermute | solution.py:16
  16.4 29.6 %copy-start.8 = (pred[128]{0:T(512)(128)(4,1)}, pred[128]{0:T(512)(128)(4,1)S(1)}, u32[]{:S(2)}) copy-start(pred[128]{0:T(512)(128)(4,1)S(1)} %get-tuple-element.8) | copy-start | bytes 388
  23.6 9.4 %collective-permute-start.5 = (bf16[16,8320]{1,0:T(8,128)(2,1)S(1)}, bf16[16,8320]{1,0:T(8,128)(2,1)S(1)}, u32[]{:S(2)}, u32[]{:S(2)}) collective-permute-start(bf16[16,8320]{1,0:T(8,128)(2,1)S(1)} %slice.56), channel_id=1, source_target_pairs={{0,2},{1,3},{2,0},{3,1},{4,6},{5,7},{6,4},{7,5},{8,10},{9,11},{10,... | collective-permute-start | bytes 798728 | tf_op jit(solution)/shard_map/ppermute | solution.py:44
  24.0 9.2 %collective-permute-start.6 = (bf16[16,8320]{1,0:T(8,128)(2,1)S(1)}, bf16[16,8320]{1,0:T(8,128)(2,1)S(1)}, u32[]{:S(2)}, u32[]{:S(2)}) collective-permute-start(bf16[16,8320]{1,0:T(8,128)(2,1)S(1)} %slice.57), channel_id=1, source_target_pairs={{0,4},{1,5},{2,6},{3,7},{4,0},{5,1},{6,2},{7,3},{8,12},{9,13},{10,... | collective-permute-start | bytes 798728 | tf_op jit(solution)/shard_map/ppermute | solution.py:44
  27.5 15.2 %collective-permute-start.2 = (bf16[32,8320]{1,0:T(8,128)(2,1)S(1)}, bf16[32,8320]{1,0:T(8,128)(2,1)S(1)}, u32[]{:S(2)}, u32[]{:S(2)}) collective-permute-start(bf16[32,8320]{1,0:T(8,128)(2,1)S(1)} %collective-permute-done), channel_id=1, source_target_pairs={{0,2},{1,3},{2,0},{3,1},{4,6},{5,7},{6,4},{7,5},{8,10},{9,11},{10,... | collective-permute-start | bytes 1597448 | tf_op jit(solution)/shard_map/ppermute | solution.py:44
  29.0 15.4 %collective-permute-start.4 = (bf16[32,8320]{1,0:T(8,128)(2,1)S(1)}, bf16[32,8320]{1,0:T(8,128)(2,1)S(1)}, u32[]{:S(2)}, u32[]{:S(2)}) collective-permute-start(bf16[32,8320]{1,0:T(8,128)(2,1)S(1)} %collective-permute-done), channel_id=1, source_target_pairs={{0,4},{1,5},{2,6},{3,7},{4,0},{5,1},{6,2},{7,3},{8,12},{9,13},{10,... | collective-permute-start | bytes 1597448 | tf_op jit(solution)/shard_map/ppermute | solution.py:44
  33.2 12.8 %collective-permute-start.7 = (bf16[32,8320]{1,0:T(8,128)(2,1)S(1)}, bf16[32,8320]{1,0:T(8,128)(2,1)S(1)}, u32[]{:S(2)}, u32[]{:S(2)}) collective-permute-start(bf16[32,8320]{1,0:T(8,128)(2,1)S(1)} %constant_dynamic-update-slice_fusion), channel_id=1, source_target_pairs={{0,1},{1,0},{2,3},{3,2},{4,5},{5,4},{6,7},{7,6},{8,9},{9,8},{10,11... | collective-permute-start | bytes 1597448 | tf_op jit(solution)/shard_map/ppermute | solution.py:44
  77.0 6.6 %copy-start = (bf16[8,2,16,4096]{3,2,1,0:T(8,128)(2,1)S(1)}, bf16[8,2,16,4096]{3,2,1,0:T(8,128)(2,1)}, u32[]{:S(2)}) copy-start(bf16[8,2,16,4096]{3,2,1,0:T(8,128)(2,1)} %get-tuple-element.5) | copy-start | bytes 6291460
  78.5 2.9 %collective-permute-start.8 = (bf16[4,32,4096]{2,1,0:T(8,128)(2,1)S(1)}, bf16[4,32,4096]{2,1,0:T(8,128)(2,1)S(1)}, u32[]{:S(2)}, u32[]{:S(2)}) collective-permute-start(bf16[4,32,4096]{2,1,0:T(8,128)(2,1)S(1)} %slice_bitcast_fusion.2), channel_id=1, source_target_pairs={{0,1},{1,0},{2,3},{3,2},{4,5},{5,4},{6,7},{7,6},{8,9},{9,8},{10,11... | collective-permute-start | bytes 3145736 | tf_op jit(solution)/shard_map/ppermute | solution.py:78
  80.8 2.8 %collective-permute-start.12 = (bf16[4,32,4096]{2,1,0:T(8,128)(2,1)S(1)}, bf16[4,32,4096]{2,1,0:T(8,128)(2,1)S(1)}, u32[]{:S(2)}, u32[]{:S(2)}) collective-permute-start(bf16[4,32,4096]{2,1,0:T(8,128)(2,1)S(1)} %slice_bitcast_fusion), channel_id=1, source_target_pairs={{0,1},{1,0},{2,3},{3,2},{4,5},{5,4},{6,7},{7,6},{8,9},{9,8},{10,11... | collective-permute-start | bytes 3145736 | tf_op jit(solution)/shard_map/ppermute | solution.py:78
  81.7 19.8 %copy-start.7 = (s32[128]{0:T(128)S(1)}, s32[128]{0:T(128)}, u32[]{:S(2)}) copy-start(s32[128]{0:T(128)} %add_reduce_fusion) | copy-start | bytes 1540
  81.7 19.8 %copy-start.9 = (pred[128]{0:T(512)(128)(4,1)S(1)}, pred[128]{0:T(512)(128)(4,1)}, u32[]{:S(2)}) copy-start(pred[128]{0:T(512)(128)(4,1)} %copy-done.8) | copy-start | bytes 388
  81.7 19.8 %copy-start.11 = (pred[128]{0:T(512)(128)(4,1)S(1)}, pred[128]{0:T(512)(128)(4,1)}, u32[]{:S(2)}) copy-start(pred[128]{0:T(512)(128)(4,1)} %copy-done.10) | copy-start | bytes 388
  81.7 22.1 %copy-start.3 = (pred[16,128]{1,0:T(8,128)(4,1)S(1)}, pred[16,128]{1,0:T(8,128)(4,1)}, u32[]{:S(2)}) copy-start(pred[16,128]{1,0:T(8,128)(4,1)} %copy-done.2) | copy-start | bytes 6148
  81.7 22.1 %copy-start.5 = (pred[16,128]{1,0:T(8,128)(4,1)S(1)}, pred[16,128]{1,0:T(8,128)(4,1)}, u32[]{:S(2)}) copy-start(pred[16,128]{1,0:T(8,128)(4,1)} %copy-done.4) | copy-start | bytes 6148
  81.7 13.9 %collective-permute-start.9 = (bf16[2,32,4096]{2,1,0:T(8,128)(2,1)S(1)}, bf16[2,32,4096]{2,1,0:T(8,128)(2,1)S(1)}, u32[]{:S(2)}, u32[]{:S(2)}) collective-permute-start(bf16[2,32,4096]{2,1,0:T(8,128)(2,1)S(1)} %slice_bitcast_fusion.6), channel_id=1, source_target_pairs={{0,4},{1,5},{2,6},{3,7},{4,0},{5,1},{6,2},{7,3},{8,12},{9,13},{10,... | collective-permute-start | bytes 1572872 | tf_op jit(solution)/shard_map/ppermute | solution.py:78
  83.9 14.7 %collective-permute-start.13 = (bf16[2,32,4096]{2,1,0:T(8,128)(2,1)S(1)}, bf16[2,32,4096]{2,1,0:T(8,128)(2,1)S(1)}, u32[]{:S(2)}, u32[]{:S(2)}) collective-permute-start(bf16[2,32,4096]{2,1,0:T(8,128)(2,1)S(1)} %slice_bitcast_fusion.4), channel_id=1, source_target_pairs={{0,2},{1,3},{2,0},{3,1},{4,6},{5,7},{6,4},{7,5},{8,10},{9,11},{10,... | collective-permute-start | bytes 1572872 | tf_op jit(solution)/shard_map/ppermute | solution.py:78
  95.8 8.0 %collective-permute-start.10 = (bf16[32,4096]{1,0:T(8,128)(2,1)S(1)}, bf16[32,4096]{1,0:T(8,128)(2,1)S(1)}, u32[]{:S(2)}, u32[]{:S(2)}) collective-permute-start(bf16[32,4096]{1,0:T(8,128)(2,1)S(1)} %slice_bitcast_fusion.10), channel_id=1, source_target_pairs={{0,2},{1,3},{2,0},{3,1},{4,6},{5,7},{6,4},{7,5},{8,10},{9,11},{10,... | collective-permute-start | bytes 786440 | tf_op jit(solution)/shard_map/ppermute | solution.py:97
  98.9 11.1 %collective-permute-start.14 = (bf16[32,4096]{1,0:T(8,128)(2,1)S(1)}, bf16[32,4096]{1,0:T(8,128)(2,1)S(1)}, u32[]{:S(2)}, u32[]{:S(2)}) collective-permute-start(bf16[32,4096]{1,0:T(8,128)(2,1)S(1)} %get-tuple-element.12), channel_id=1, source_target_pairs={{8,0},{9,1},{10,2},{11,3},{12,4},{13,5},{14,6},{15,7},{16,8},{17,9... | collective-permute-start | bytes 786440 | tf_op jit(solution)/shard_map/ppermute | solution.py:107
  100.2 14.5 %collective-permute-start.15 = (bf16[32,4096]{1,0:T(8,128)(2,1)S(1)}, bf16[32,4096]{1,0:T(8,128)(2,1)S(1)}, u32[]{:S(2)}, u32[]{:S(2)}) collective-permute-start(bf16[32,4096]{1,0:T(8,128)(2,1)S(1)} %get-tuple-element.13), channel_id=1, source_target_pairs={{8,4},{9,5},{10,6},{11,7},{12,0},{13,1},{14,2},{15,3},{16,12},{17,... | collective-permute-start | bytes 786440 | tf_op jit(solution)/shard_map/ppermute | solution.py:108
  (4 other events, 12.8 us)

commit v17 on v14

--- a/solution.py
+++ b/solution.py
@@ -114,7 +114,7 @@
         select.astype(jnp.float32),
         slot_sums,
         (((0,), (0,)), ((), ())),
-        precision=lax.Precision.HIGHEST,
+        precision=lax.Precision.HIGH,
         preferred_element_type=jnp.float32,
     ).astype(jnp.bfloat16)
 

time: 116 us -> 116 us (level)
  no operation moved by 1% of the time
where the time goes in v17:
time: 116 us; the launch traced here: 115 us
  waiting for transfers between devices  44.3 us (38%)
  Pallas kernels  30.1 us (26%)
  starting transfers between devices  17.1 us (15%)
  local copies, waits for them, and re-layouts  10.8 us (9%)
  matrix products  6.44 us (6%)
  other arithmetic  5.64 us (5%)
    pallas_call x1, Pallas kernels, expert_pass(): pl.pallas_call(_expert_body, grid=(experts, steps), in_specs=[pl.BlockSpe...  30.1 us
    ppermute x8, waiting for transfers between devices, swap(): return lax.ppermute(value, 'et', [(i, i ^ bit) for i in range(n)])  17.9 us
    ppermute x4, waiting for transfers between devices, halve_over_et(): got = lax.ppermute(give, 'et', [(i, i ^ bit) for i in range(n)])  12.7 us
    ppermute x8, starting transfers between devices, swap(): return lax.ppermute(value, 'et', [(i, i ^ bit) for i in range(n)])  8.85 us
    unnamed x32, local copies, waits for them, and re-layouts  6.47 us
    ppermute x1, waiting for transfers between devices, reduce_to_previous(): first = lax.ppermute(keep, ('pipe', 'et'), to_same)  4.45 us
    ppermute x1, waiting for transfers between devices, reduce_to_previous(): second = lax.ppermute(give, ('pipe', 'et'), to_other)  3.67 us
    dot_general x2, matrix products, unpack(): lax.dot_general(select.astype(jnp.float32), slot_sums, (((0,), (0,)), (()...  3.45 us
  transfers between devices with their start and end apart: 16, of which 11 were waited for; matrix products, arithmetic and copies ran while one was open for 11% of the time, Pallas kernels for 0%

profile of v17, /device:TPU:0, one launch (start us, length us, event | category | flops | bytes accessed | tf_op | source)
XLA Modules:
  0.0 115.4 jit_solution(11455769398181157951)
XLA Ops:
  2.3 1.5 %convolution_convert_fusion.3 = bf16[32,4096]{1,0:T(8,128)(2,1)S(1)} fusion(bf16[1,128,4096]{2,1,0:T(8,128)(2,1)} %param.7, pred[16,128]{1,0:T(8,128)(4,1)S(1)} %get-tuple-element.17, pred[16,128]{1,0:T(8,128)(4,1)S(1)} %get-tuple-element.16), kind=kOutput, calls=%fused_computation.5 | convolution fusion | flops 33689600 | bytes 1314816 | tf_op jit(solution)/shard_map/dot_general | solution.py:39
  3.8 1.5 %convolution_convert_fusion.2 = bf16[32,4096]{1,0:T(8,128)(2,1)S(1)} fusion(bf16[1,128,4096]{2,1,0:T(8,128)(2,1)} %param.10, pred[16,128]{1,0:T(8,128)(4,1)S(1)} %get-tuple-element.17, pred[16,128]{1,0:T(8,128)(4,1)S(1)} %get-tuple-element.16), kind=kOutput, calls=%fused_computation.4 | convolution fusion | flops 33689600 | bytes 1314816 | tf_op jit(solution)/shard_map/dot_general | solution.py:39
  6.8 2.6 %collective-permute-start.1 = (bf16[32,8320]{1,0:T(8,128)(2,1)S(1)}, bf16[32,8320]{1,0:T(8,128)(2,1)S(1)}, u32[]{:S(2)}, u32[]{:S(2)}) collective-permute-start(bf16[32,8320]{1,0:T(8,128)(2,1)S(1)} %pad_maximum_fusion), channel_id=1, source_target_pairs={{0,2},{1,3},{2,0},{3,1},{4,6},{5,7},{6,4},{7,5},{8,10},{9,11},{10,... | collective-permute-start | bytes 1597448 | tf_op jit(solution)/shard_map/ppermute | solution.py:44
  9.4 1.5 %collective-permute-start.3 = (bf16[32,8320]{1,0:T(8,128)(2,1)S(1)}, bf16[32,8320]{1,0:T(8,128)(2,1)S(1)}, u32[]{:S(2)}, u32[]{:S(2)}) collective-permute-start(bf16[32,8320]{1,0:T(8,128)(2,1)S(1)} %pad_maximum_fusion), channel_id=1, source_target_pairs={{0,4},{1,5},{2,6},{3,7},{4,0},{5,1},{6,2},{7,3},{8,12},{9,13},{10,... | collective-permute-start | bytes 1597448 | tf_op jit(solution)/shard_map/ppermute | solution.py:44
  13.0 3.3 %collective-permute-done.11 = s32[128,2]{0,1:T(2,128)S(1)} collective-permute-done((s32[128,2]{0,1:T(2,128)S(1)}, s32[128,2]{0,1:T(2,128)S(1)}, u32[]{:S(2)}, u32[]{:S(2)}) %collective-permute-start.11) | collective-permute-done | bytes 1056 | tf_op jit(solution)/shard_map/ppermute | solution.py:16
  18.8 4.8 %collective-permute-done.3 = bf16[32,8320]{1,0:T(8,128)(2,1)S(1)} collective-permute-done((bf16[32,8320]{1,0:T(8,128)(2,1)S(1)}, bf16[32,8320]{1,0:T(8,128)(2,1)S(1)}, u32[]{:S(2)}, u32[]{:S(2)}) %collective-permute-start.3) | collective-permute-done | bytes 532512 | tf_op jit(solution)/shard_map/ppermute | solution.py:44
  24.0 1.8 %collective-permute-start.6 = (bf16[16,8320]{1,0:T(8,128)(2,1)S(1)}, bf16[16,8320]{1,0:T(8,128)(2,1)S(1)}, u32[]{:S(2)}, u32[]{:S(2)}) collective-permute-start(bf16[16,8320]{1,0:T(8,128)(2,1)S(1)} %slice.57), channel_id=1, source_target_pairs={{0,4},{1,5},{2,6},{3,7},{4,0},{5,1},{6,2},{7,3},{8,12},{9,13},{10,... | collective-permute-start | bytes 798728 | tf_op jit(solution)/shard_map/ppermute | solution.py:44
  27.5 1.5 %collective-permute-start.2 = (bf16[32,8320]{1,0:T(8,128)(2,1)S(1)}, bf16[32,8320]{1,0:T(8,128)(2,1)S(1)}, u32[]{:S(2)}, u32[]{:S(2)}) collective-permute-start(bf16[32,8320]{1,0:T(8,128)(2,1)S(1)} %collective-permute-done), channel_id=1, source_target_pairs={{0,2},{1,3},{2,0},{3,1},{4,6},{5,7},{6,4},{7,5},{8,10},{9,11},{10,... | collective-permute-start | bytes 1597448 | tf_op jit(solution)/shard_map/ppermute | solution.py:44
  29.5 3.5 %collective-permute-done.5 = bf16[16,8320]{1,0:T(8,128)(2,1)S(1)} collective-permute-done((bf16[16,8320]{1,0:T(8,128)(2,1)S(1)}, bf16[16,8320]{1,0:T(8,128)(2,1)S(1)}, u32[]{:S(2)}, u32[]{:S(2)}) %collective-permute-start.5) | collective-permute-done | bytes 266272 | tf_op jit(solution)/shard_map/ppermute | solution.py:44
  33.3 9.4 %collective-permute-done.2 = bf16[32,8320]{1,0:T(8,128)(2,1)S(1)} collective-permute-done((bf16[32,8320]{1,0:T(8,128)(2,1)S(1)}, bf16[32,8320]{1,0:T(8,128)(2,1)S(1)}, u32[]{:S(2)}, u32[]{:S(2)}) %collective-permute-start.2) | collective-permute-done | bytes 532512 | tf_op jit(solution)/shard_map/ppermute | solution.py:44
  46.9 30.1 %shard_map.86 = (bf16[8,2,16,4096]{3,2,1,0:T(8,128)(2,1)}, bf16[8,2,16,4096]{3,2,1,0:T(8,128)(2,1)}) custom-call(bf16[8,2,16,8320]{3,2,1,0:T(8,128)(2,1)} %constant_dynamic-update-slice_fusion.2.x_ref.g_ref.w_ref, bf16[8,2,16,8320]{3,2,1,0:T(8,128)(2,1)} %constant_dynamic-update-slice_fusion.2.x_ref.g_ref.w_ref, ...), custom_call_target="tpu_custom_call" | custom-call | tf_op jit(solution)/shard_map/pallas_call | solution.py:165
  77.0 1.4 %slice_bitcast_fusion.2 = bf16[4,32,4096]{2,1,0:T(8,128)(2,1)S(1)} fusion(bf16[4,2,1,32,4096]{4,3,1,0,2:T(8,128)(2,1)} %bitcast.98), kind=kLoop, calls=%fused_computation.12 | loop fusion | bytes 2097152 | tf_op jit(solution)/shard_map/reshape;squeeze | solution.py:77
  79.5 1.3 %slice_bitcast_fusion = bf16[4,32,4096]{2,1,0:T(8,128)(2,1)S(1)} fusion(bf16[4,2,1,32,4096]{4,3,1,0,2:T(8,128)(2,1)} %bitcast.96), kind=kLoop, calls=%fused_computation.10 | loop fusion | bytes 2097152 | tf_op jit(solution)/shard_map/reshape;squeeze | solution.py:77
  82.4 1.3 %collective-permute-done.12 = bf16[4,32,4096]{2,1,0:T(8,128)(2,1)S(1)} collective-permute-done((bf16[4,32,4096]{2,1,0:T(8,128)(2,1)S(1)}, bf16[4,32,4096]{2,1,0:T(8,128)(2,1)S(1)}, u32[]{:S(2)}, u32[]{:S(2)}) %collective-permute-start.12) | collective-permute-done | bytes 1048608 | tf_op jit(solution)/shard_map/ppermute | solution.py:78
  83.9 1.6 %collective-permute-start.13 = (bf16[2,32,4096]{2,1,0:T(8,128)(2,1)S(1)}, bf16[2,32,4096]{2,1,0:T(8,128)(2,1)S(1)}, u32[]{:S(2)}, u32[]{:S(2)}) collective-permute-start(bf16[2,32,4096]{2,1,0:T(8,128)(2,1)S(1)} %slice_bitcast_fusion.4), channel_id=1, source_target_pairs={{0,4},{1,5},{2,6},{3,7},{4,0},{5,1},{6,2},{7,3},{8,12},{9,13},{10,... | collective-permute-start | bytes 1572872 | tf_op jit(solution)/shard_map/ppermute | solution.py:78
  85.5 10.1 %collective-permute-done.9 = bf16[2,32,4096]{2,1,0:T(8,128)(2,1)S(1)} collective-permute-done((bf16[2,32,4096]{2,1,0:T(8,128)(2,1)S(1)}, bf16[2,32,4096]{2,1,0:T(8,128)(2,1)S(1)}, u32[]{:S(2)}, u32[]{:S(2)}) %collective-permute-start.9) | collective-permute-done | bytes 524320 | tf_op jit(solution)/shard_map/ppermute | solution.py:78
  95.8 1.6 %collective-permute-start.10 = (bf16[32,4096]{1,0:T(8,128)(2,1)S(1)}, bf16[32,4096]{1,0:T(8,128)(2,1)S(1)}, u32[]{:S(2)}, u32[]{:S(2)}) collective-permute-start(bf16[32,4096]{1,0:T(8,128)(2,1)S(1)} %slice_bitcast_fusion.10), channel_id=1, source_target_pairs={{0,4},{1,5},{2,6},{3,7},{4,0},{5,1},{6,2},{7,3},{8,12},{9,13},{10,... | collective-permute-start | bytes 786440 | tf_op jit(solution)/shard_map/ppermute | solution.py:97
  97.4 1.3 %collective-permute-done.13 = bf16[2,32,4096]{2,1,0:T(8,128)(2,1)S(1)} collective-permute-done((bf16[2,32,4096]{2,1,0:T(8,128)(2,1)S(1)}, bf16[2,32,4096]{2,1,0:T(8,128)(2,1)S(1)}, u32[]{:S(2)}, u32[]{:S(2)}) %collective-permute-start.13) | collective-permute-done | bytes 524320 | tf_op jit(solution)/shard_map/ppermute | solution.py:78
  98.9 1.3 %collective-permute-start.14 = (bf16[32,4096]{1,0:T(8,128)(2,1)S(1)}, bf16[32,4096]{1,0:T(8,128)(2,1)S(1)}, u32[]{:S(2)}, u32[]{:S(2)}) collective-permute-start(bf16[32,4096]{1,0:T(8,128)(2,1)S(1)} %get-tuple-element.12), channel_id=1, source_target_pairs={{8,0},{9,1},{10,2},{11,3},{12,4},{13,5},{14,6},{15,7},{16,8},{17,9... | collective-permute-start | bytes 786440 | tf_op jit(solution)/shard_map/ppermute | solution.py:107
  101.5 2.3 %collective-permute-done.10 = bf16[32,4096]{1,0:T(8,128)(2,1)S(1)} collective-permute-done((bf16[32,4096]{1,0:T(8,128)(2,1)S(1)}, bf16[32,4096]{1,0:T(8,128)(2,1)S(1)}, u32[]{:S(2)}, u32[]{:S(2)}) %collective-permute-start.10) | collective-permute-done | bytes 262176 | tf_op jit(solution)/shard_map/ppermute | solution.py:97
  103.8 1.7 %fusion = bf16[1,128,4096]{2,1,0:T(8,128)(2,1)} fusion(bf16[32,4096]{1,0:T(8,128)(2,1)S(1)} %collective-permute-done.10, bf16[2,32,4096]{2,1,0:T(8,128)(2,1)S(1)} %fusion.5, pred[16,128]{1,0:T(8,128)(4,1)S(1)} %copy-done.5, pred[16,128]{1,0:T(8,128)(4,1)S(1)} %copy-done.3), kind=kOutput, calls=%fused_computation.2 | convolution fusion | flops 101584896 | bytes 1576960 | tf_op jit(solution)/shard_map/dot_general | solution.py:113
  105.6 4.4 %collective-permute-done.14 = bf16[32,4096]{1,0:T(8,128)(2,1)S(1)} collective-permute-done((bf16[32,4096]{1,0:T(8,128)(2,1)S(1)}, bf16[32,4096]{1,0:T(8,128)(2,1)S(1)}, u32[]{:S(2)}, u32[]{:S(2)}) %collective-permute-start.14) | collective-permute-done | bytes 262176 | tf_op jit(solution)/shard_map/ppermute | solution.py:107
  110.0 3.7 %collective-permute-done.15 = bf16[32,4096]{1,0:T(8,128)(2,1)S(1)} collective-permute-done((bf16[32,4096]{1,0:T(8,128)(2,1)S(1)}, bf16[32,4096]{1,0:T(8,128)(2,1)S(1)}, u32[]{:S(2)}, u32[]{:S(2)}) %collective-permute-start.15) | collective-permute-done | bytes 262176 | tf_op jit(solution)/shard_map/ppermute | solution.py:108
  113.7 1.7 %fusion.1 = bf16[1,128,4096]{2,1,0:T(8,128)(2,1)} fusion(bf16[32,4096]{1,0:T(8,128)(2,1)S(1)} %collective-permute-done.15, bf16[32,4096]{1,0:T(8,128)(2,1)S(1)} %collective-permute-done.14, pred[16,128]{1,0:T(8,128)(4,1)S(1)} %get-tuple-element.19, pred[16,128]{1,0:T(8,128)(4,1)S(1)} %get-tuple-element.18), kind=kOutput, calls=%fused_computation.3 | convolution fusion | flops 101584896 | bytes 1576960 | tf_op jit(solution)/shard_map/dot_general | solution.py:113
  (84 shorter events, 19.1 us)
Async XLA Ops:
  0.6 10.3 %copy-start.6 = (s32[1,128,2]{1,2,0:T(2,128)S(1)}, s32[1,128,2]{1,2,0:T(2,128)}, u32[]{:S(2)}) copy-start(s32[1,128,2]{1,2,0:T(2,128)} %param.9) | copy-start | bytes 3076
  6.3 19.5 %collective-permute-start = (bf16[32,8320]{1,0:T(8,128)(2,1)S(1)}, bf16[32,8320]{1,0:T(8,128)(2,1)S(1)}, u32[]{:S(2)}, u32[]{:S(2)}) collective-permute-start(bf16[32,8320]{1,0:T(8,128)(2,1)S(1)} %pad_maximum_fusion), channel_id=1, source_target_pairs={{0,1},{1,0},{2,3},{3,2},{4,5},{5,4},{6,7},{7,6},{8,9},{9,8},{10,11... | collective-permute-start | bytes 1597448 | tf_op jit(solution)/shard_map/ppermute | solution.py:44
  6.8 17.1 %collective-permute-start.1 = (bf16[32,8320]{1,0:T(8,128)(2,1)S(1)}, bf16[32,8320]{1,0:T(8,128)(2,1)S(1)}, u32[]{:S(2)}, u32[]{:S(2)}) collective-permute-start(bf16[32,8320]{1,0:T(8,128)(2,1)S(1)} %pad_maximum_fusion), channel_id=1, source_target_pairs={{0,2},{1,3},{2,0},{3,1},{4,6},{5,7},{6,4},{7,5},{8,10},{9,11},{10,... | collective-permute-start | bytes 1597448 | tf_op jit(solution)/shard_map/ppermute | solution.py:44
  9.4 14.2 %collective-permute-start.3 = (bf16[32,8320]{1,0:T(8,128)(2,1)S(1)}, bf16[32,8320]{1,0:T(8,128)(2,1)S(1)}, u32[]{:S(2)}, u32[]{:S(2)}) collective-permute-start(bf16[32,8320]{1,0:T(8,128)(2,1)S(1)} %pad_maximum_fusion), channel_id=1, source_target_pairs={{0,4},{1,5},{2,6},{3,7},{4,0},{5,1},{6,2},{7,3},{8,12},{9,13},{10,... | collective-permute-start | bytes 1597448 | tf_op jit(solution)/shard_map/ppermute | solution.py:44
  10.9 5.5 %collective-permute-start.11 = (s32[128,2]{0,1:T(2,128)S(1)}, s32[128,2]{0,1:T(2,128)S(1)}, u32[]{:S(2)}, u32[]{:S(2)}) collective-permute-start(s32[128,2]{0,1:T(2,128)S(1)} %bitcast.107), channel_id=1, source_target_pairs={{8,0},{16,8},{24,16},{9,1},{17,9},{25,17},{10,2},{18,10},{26,18},{... | collective-permute-start | bytes 3080 | tf_op jit(solution)/shard_map/ppermute | solution.py:16
  16.4 29.6 %copy-start.8 = (pred[128]{0:T(512)(128)(4,1)}, pred[128]{0:T(512)(128)(4,1)S(1)}, u32[]{:S(2)}) copy-start(pred[128]{0:T(512)(128)(4,1)S(1)} %get-tuple-element.8) | copy-start | bytes 388
  23.6 9.4 %collective-permute-start.5 = (bf16[16,8320]{1,0:T(8,128)(2,1)S(1)}, bf16[16,8320]{1,0:T(8,128)(2,1)S(1)}, u32[]{:S(2)}, u32[]{:S(2)}) collective-permute-start(bf16[16,8320]{1,0:T(8,128)(2,1)S(1)} %slice.56), channel_id=1, source_target_pairs={{0,2},{1,3},{2,0},{3,1},{4,6},{5,7},{6,4},{7,5},{8,10},{9,11},{10,... | collective-permute-start | bytes 798728 | tf_op jit(solution)/shard_map/ppermute | solution.py:44
  24.0 9.2 %collective-permute-start.6 = (bf16[16,8320]{1,0:T(8,128)(2,1)S(1)}, bf16[16,8320]{1,0:T(8,128)(2,1)S(1)}, u32[]{:S(2)}, u32[]{:S(2)}) collective-permute-start(bf16[16,8320]{1,0:T(8,128)(2,1)S(1)} %slice.57), channel_id=1, source_target_pairs={{0,4},{1,5},{2,6},{3,7},{4,0},{5,1},{6,2},{7,3},{8,12},{9,13},{10,... | collective-permute-start | bytes 798728 | tf_op jit(solution)/shard_map/ppermute | solution.py:44
  27.5 15.2 %collective-permute-start.2 = (bf16[32,8320]{1,0:T(8,128)(2,1)S(1)}, bf16[32,8320]{1,0:T(8,128)(2,1)S(1)}, u32[]{:S(2)}, u32[]{:S(2)}) collective-permute-start(bf16[32,8320]{1,0:T(8,128)(2,1)S(1)} %collective-permute-done), channel_id=1, source_target_pairs={{0,2},{1,3},{2,0},{3,1},{4,6},{5,7},{6,4},{7,5},{8,10},{9,11},{10,... | collective-permute-start | bytes 1597448 | tf_op jit(solution)/shard_map/ppermute | solution.py:44
  29.0 15.4 %collective-permute-start.4 = (bf16[32,8320]{1,0:T(8,128)(2,1)S(1)}, bf16[32,8320]{1,0:T(8,128)(2,1)S(1)}, u32[]{:S(2)}, u32[]{:S(2)}) collective-permute-start(bf16[32,8320]{1,0:T(8,128)(2,1)S(1)} %collective-permute-done), channel_id=1, source_target_pairs={{0,4},{1,5},{2,6},{3,7},{4,0},{5,1},{6,2},{7,3},{8,12},{9,13},{10,... | collective-permute-start | bytes 1597448 | tf_op jit(solution)/shard_map/ppermute | solution.py:44
  33.2 12.8 %collective-permute-start.7 = (bf16[32,8320]{1,0:T(8,128)(2,1)S(1)}, bf16[32,8320]{1,0:T(8,128)(2,1)S(1)}, u32[]{:S(2)}, u32[]{:S(2)}) collective-permute-start(bf16[32,8320]{1,0:T(8,128)(2,1)S(1)} %constant_dynamic-update-slice_fusion), channel_id=1, source_target_pairs={{0,1},{1,0},{2,3},{3,2},{4,5},{5,4},{6,7},{7,6},{8,9},{9,8},{10,11... | collective-permute-start | bytes 1597448 | tf_op jit(solution)/shard_map/ppermute | solution.py:44
  77.0 6.6 %copy-start = (bf16[8,2,16,4096]{3,2,1,0:T(8,128)(2,1)S(1)}, bf16[8,2,16,4096]{3,2,1,0:T(8,128)(2,1)}, u32[]{:S(2)}) copy-start(bf16[8,2,16,4096]{3,2,1,0:T(8,128)(2,1)} %get-tuple-element.5) | copy-start | bytes 6291460
  78.5 2.9 %collective-permute-start.8 = (bf16[4,32,4096]{2,1,0:T(8,128)(2,1)S(1)}, bf16[4,32,4096]{2,1,0:T(8,128)(2,1)S(1)}, u32[]{:S(2)}, u32[]{:S(2)}) collective-permute-start(bf16[4,32,4096]{2,1,0:T(8,128)(2,1)S(1)} %slice_bitcast_fusion.2), channel_id=1, source_target_pairs={{0,1},{1,0},{2,3},{3,2},{4,5},{5,4},{6,7},{7,6},{8,9},{9,8},{10,11... | collective-permute-start | bytes 3145736 | tf_op jit(solution)/shard_map/ppermute | solution.py:78
  80.8 2.8 %collective-permute-start.12 = (bf16[4,32,4096]{2,1,0:T(8,128)(2,1)S(1)}, bf16[4,32,4096]{2,1,0:T(8,128)(2,1)S(1)}, u32[]{:S(2)}, u32[]{:S(2)}) collective-permute-start(bf16[4,32,4096]{2,1,0:T(8,128)(2,1)S(1)} %slice_bitcast_fusion), channel_id=1, source_target_pairs={{0,1},{1,0},{2,3},{3,2},{4,5},{5,4},{6,7},{7,6},{8,9},{9,8},{10,11... | collective-permute-start | bytes 3145736 | tf_op jit(solution)/shard_map/ppermute | solution.py:78
  81.7 19.8 %copy-start.7 = (s32[128]{0:T(128)S(1)}, s32[128]{0:T(128)}, u32[]{:S(2)}) copy-start(s32[128]{0:T(128)} %add_reduce_fusion) | copy-start | bytes 1540
  81.7 19.8 %copy-start.9 = (pred[128]{0:T(512)(128)(4,1)S(1)}, pred[128]{0:T(512)(128)(4,1)}, u32[]{:S(2)}) copy-start(pred[128]{0:T(512)(128)(4,1)} %copy-done.8) | copy-start | bytes 388
  81.7 19.8 %copy-start.11 = (pred[128]{0:T(512)(128)(4,1)S(1)}, pred[128]{0:T(512)(128)(4,1)}, u32[]{:S(2)}) copy-start(pred[128]{0:T(512)(128)(4,1)} %copy-done.10) | copy-start | bytes 388
  81.7 22.1 %copy-start.3 = (pred[16,128]{1,0:T(8,128)(4,1)S(1)}, pred[16,128]{1,0:T(8,128)(4,1)}, u32[]{:S(2)}) copy-start(pred[16,128]{1,0:T(8,128)(4,1)} %copy-done.2) | copy-start | bytes 6148
  81.7 22.1 %copy-start.5 = (pred[16,128]{1,0:T(8,128)(4,1)S(1)}, pred[16,128]{1,0:T(8,128)(4,1)}, u32[]{:S(2)}) copy-start(pred[16,128]{1,0:T(8,128)(4,1)} %copy-done.4) | copy-start | bytes 6148
  81.7 13.9 %collective-permute-start.9 = (bf16[2,32,4096]{2,1,0:T(8,128)(2,1)S(1)}, bf16[2,32,4096]{2,1,0:T(8,128)(2,1)S(1)}, u32[]{:S(2)}, u32[]{:S(2)}) collective-permute-start(bf16[2,32,4096]{2,1,0:T(8,128)(2,1)S(1)} %slice_bitcast_fusion.6), channel_id=1, source_target_pairs={{0,2},{1,3},{2,0},{3,1},{4,6},{5,7},{6,4},{7,5},{8,10},{9,11},{10,... | collective-permute-start | bytes 1572872 | tf_op jit(solution)/shard_map/ppermute | solution.py:78
  83.9 14.7 %collective-permute-start.13 = (bf16[2,32,4096]{2,1,0:T(8,128)(2,1)S(1)}, bf16[2,32,4096]{2,1,0:T(8,128)(2,1)S(1)}, u32[]{:S(2)}, u32[]{:S(2)}) collective-permute-start(bf16[2,32,4096]{2,1,0:T(8,128)(2,1)S(1)} %slice_bitcast_fusion.4), channel_id=1, source_target_pairs={{0,4},{1,5},{2,6},{3,7},{4,0},{5,1},{6,2},{7,3},{8,12},{9,13},{10,... | collective-permute-start | bytes 1572872 | tf_op jit(solution)/shard_map/ppermute | solution.py:78
  95.8 8.0 %collective-permute-start.10 = (bf16[32,4096]{1,0:T(8,128)(2,1)S(1)}, bf16[32,4096]{1,0:T(8,128)(2,1)S(1)}, u32[]{:S(2)}, u32[]{:S(2)}) collective-permute-start(bf16[32,4096]{1,0:T(8,128)(2,1)S(1)} %slice_bitcast_fusion.10), channel_id=1, source_target_pairs={{0,4},{1,5},{2,6},{3,7},{4,0},{5,1},{6,2},{7,3},{8,12},{9,13},{10,... | collective-permute-start | bytes 786440 | tf_op jit(solution)/shard_map/ppermute | solution.py:97
  98.9 11.1 %collective-permute-start.14 = (bf16[32,4096]{1,0:T(8,128)(2,1)S(1)}, bf16[32,4096]{1,0:T(8,128)(2,1)S(1)}, u32[]{:S(2)}, u32[]{:S(2)}) collective-permute-start(bf16[32,4096]{1,0:T(8,128)(2,1)S(1)} %get-tuple-element.12), channel_id=1, source_target_pairs={{8,0},{9,1},{10,2},{11,3},{12,4},{13,5},{14,6},{15,7},{16,8},{17,9... | collective-permute-start | bytes 786440 | tf_op jit(solution)/shard_map/ppermute | solution.py:107
  100.2 13.5 %collective-permute-start.15 = (bf16[32,4096]{1,0:T(8,128)(2,1)S(1)}, bf16[32,4096]{1,0:T(8,128)(2,1)S(1)}, u32[]{:S(2)}, u32[]{:S(2)}) collective-permute-start(bf16[32,4096]{1,0:T(8,128)(2,1)S(1)} %get-tuple-element.13), channel_id=1, source_target_pairs={{8,2},{9,3},{10,0},{11,1},{12,6},{13,7},{14,4},{15,5},{16,10},{17,... | collective-permute-start | bytes 786440 | tf_op jit(solution)/shard_map/ppermute | solution.py:108
  (4 other events, 12.8 us)

commit v18 on v17

--- a/solution.py
+++ b/solution.py
@@ -110,12 +110,13 @@
 
 
 def unpack(slot_sums, select):
-    return lax.dot_general(
-        select.astype(jnp.float32),
-        slot_sums,
-        (((0,), (0,)), ((), ())),
-        precision=lax.Precision.HIGH,
-        preferred_element_type=jnp.float32,
+    high = slot_sums.astype(jnp.bfloat16)
+    low = (slot_sums - high.astype(jnp.float32)).astype(jnp.bfloat16)
+    picks = select.astype(jnp.bfloat16)
+    dims = (((0,), (0,)), ((), ()))
+    return (
+        lax.dot_general(picks, high, dims, preferred_element_type=jnp.float32)
+        + lax.dot_general(picks, low, dims, preferred_element_type=jnp.float32)
     ).astype(jnp.bfloat16)
 
 

time: 116 us -> 115 us (level)
    ppermute x1, waiting for transfers between devices: 4.45 us -> 6.77 us  [reduce_to_previous(): first = lax.ppermute(keep, ('pipe', 'et'), to_same)]
    ppermute x1, waiting for transfers between devices: 2.31 us -> 0.01 us  [reduce_to_owner(): got = lax.ppermute(give, 'et', [(i, i ^ bit) for i in range(n)])]
    dot_general x2 -> x4, matrix products: 3.45 us -> 3.87 us  [the longest x2 2.91 us: unpack(): lax.dot_general(picks, high, dims, preferred_element_type=jnp.float32)]
    unnamed x32 -> x26, local copies, waits for them, and re-layouts: 6.47 us -> 6.43 us
  transfers between devices with their start and end apart: 16 -> 16, of which waited for: 11 -> 10; matrix products, arithmetic and copies ran while one was open for 11% -> 11% of each run, Pallas kernels for 0% -> 0%
where the time goes in v18:
time: 115 us
  waiting for transfers between devices  43.4 us (38%)
  Pallas kernels  30.1 us (26%)
  starting transfers between devices  17.2 us (15%)
  local copies, waits for them, and re-layouts  10.7 us (9%)
  matrix products  6.85 us (6%)
  other arithmetic  5.43 us (5%)
    pallas_call x1, Pallas kernels, expert_pass(): pl.pallas_call(_expert_body, grid=(experts, steps), in_specs=[pl.BlockSpe...  30.1 us
    ppermute x8, waiting for transfers between devices, swap(): return lax.ppermute(value, 'et', [(i, i ^ bit) for i in range(n)])  17.8 us
    ppermute x4, waiting for transfers between devices, halve_over_et(): got = lax.ppermute(give, 'et', [(i, i ^ bit) for i in range(n)])  11.6 us
    ppermute x8, starting transfers between devices, swap(): return lax.ppermute(value, 'et', [(i, i ^ bit) for i in range(n)])  8.85 us
    ppermute x1, waiting for transfers between devices, reduce_to_previous(): first = lax.ppermute(keep, ('pipe', 'et'), to_same)  6.77 us
    unnamed x26, local copies, waits for them, and re-layouts  6.43 us
    ppermute x1, waiting for transfers between devices, reduce_to_previous(): second = lax.ppermute(give, ('pipe', 'et'), to_other)  3.91 us
    ppermute x1, waiting for transfers between devices, shifted(): lax.ppermute(value, axis, [(source, source + steps) for source in range(f...  3.34 us
  transfers between devices with their start and end apart: 16, of which 10 were waited for; matrix products, arithmetic and copies ran while one was open for 11% of the time, Pallas kernels for 0%

profile of v18, /device:TPU:0, one launch (start us, length us, event | category | flops | bytes accessed | tf_op | source)
XLA Modules:
  0.0 114.6 jit_solution(18175729696951314332)
XLA Ops:
  2.3 1.5 %convolution_convert_fusion.1 = bf16[32,4096]{1,0:T(8,128)(2,1)S(1)} fusion(bf16[1,128,4096]{2,1,0:T(8,128)(2,1)} %param.7, pred[16,128]{1,0:T(8,128)(4,1)S(1)} %get-tuple-element.17, pred[16,128]{1,0:T(8,128)(4,1)S(1)} %get-tuple-element.16), kind=kOutput, calls=%fused_computation.7 | convolution fusion | flops 33689600 | bytes 1314816 | tf_op jit(solution)/shard_map/dot_general | solution.py:39
  3.8 1.5 %convolution_convert_fusion = bf16[32,4096]{1,0:T(8,128)(2,1)S(1)} fusion(bf16[1,128,4096]{2,1,0:T(8,128)(2,1)} %param.10, pred[16,128]{1,0:T(8,128)(4,1)S(1)} %get-tuple-element.17, pred[16,128]{1,0:T(8,128)(4,1)S(1)} %get-tuple-element.16), kind=kOutput, calls=%fused_computation.6 | convolution fusion | flops 33689600 | bytes 1314816 | tf_op jit(solution)/shard_map/dot_general | solution.py:39
  6.8 2.6 %collective-permute-start.1 = (bf16[32,8320]{1,0:T(8,128)(2,1)S(1)}, bf16[32,8320]{1,0:T(8,128)(2,1)S(1)}, u32[]{:S(2)}, u32[]{:S(2)}) collective-permute-start(bf16[32,8320]{1,0:T(8,128)(2,1)S(1)} %pad_maximum_fusion), channel_id=1, source_target_pairs={{0,2},{1,3},{2,0},{3,1},{4,6},{5,7},{6,4},{7,5},{8,10},{9,11},{10,... | collective-permute-start | bytes 1597448 | tf_op jit(solution)/shard_map/ppermute | solution.py:44
  9.4 1.5 %collective-permute-start.3 = (bf16[32,8320]{1,0:T(8,128)(2,1)S(1)}, bf16[32,8320]{1,0:T(8,128)(2,1)S(1)}, u32[]{:S(2)}, u32[]{:S(2)}) collective-permute-start(bf16[32,8320]{1,0:T(8,128)(2,1)S(1)} %pad_maximum_fusion), channel_id=1, source_target_pairs={{0,4},{1,5},{2,6},{3,7},{4,0},{5,1},{6,2},{7,3},{8,12},{9,13},{10,... | collective-permute-start | bytes 1597448 | tf_op jit(solution)/shard_map/ppermute | solution.py:44
  10.9 1.3 %collective-permute-start.11 = (s32[128,2]{0,1:T(2,128)S(1)}, s32[128,2]{0,1:T(2,128)S(1)}, u32[]{:S(2)}, u32[]{:S(2)}) collective-permute-start(s32[128,2]{0,1:T(2,128)S(1)} %bitcast.110), channel_id=1, source_target_pairs={{8,0},{16,8},{24,16},{9,1},{17,9},{25,17},{10,2},{18,10},{26,18},{... | collective-permute-start | bytes 3080 | tf_op jit(solution)/shard_map/ppermute | solution.py:16
  13.0 3.3 %collective-permute-done.11 = s32[128,2]{0,1:T(2,128)S(1)} collective-permute-done((s32[128,2]{0,1:T(2,128)S(1)}, s32[128,2]{0,1:T(2,128)S(1)}, u32[]{:S(2)}, u32[]{:S(2)}) %collective-permute-start.11) | collective-permute-done | bytes 1056 | tf_op jit(solution)/shard_map/ppermute | solution.py:16
  18.8 4.8 %collective-permute-done.3 = bf16[32,8320]{1,0:T(8,128)(2,1)S(1)} collective-permute-done((bf16[32,8320]{1,0:T(8,128)(2,1)S(1)}, bf16[32,8320]{1,0:T(8,128)(2,1)S(1)}, u32[]{:S(2)}, u32[]{:S(2)}) %collective-permute-start.3) | collective-permute-done | bytes 532512 | tf_op jit(solution)/shard_map/ppermute | solution.py:44
  24.0 1.8 %collective-permute-start.6 = (bf16[16,8320]{1,0:T(8,128)(2,1)S(1)}, bf16[16,8320]{1,0:T(8,128)(2,1)S(1)}, u32[]{:S(2)}, u32[]{:S(2)}) collective-permute-start(bf16[16,8320]{1,0:T(8,128)(2,1)S(1)} %slice.57), channel_id=1, source_target_pairs={{0,4},{1,5},{2,6},{3,7},{4,0},{5,1},{6,2},{7,3},{8,12},{9,13},{10,... | collective-permute-start | bytes 798728 | tf_op jit(solution)/shard_map/ppermute | solution.py:44
  26.6 0.8 constant_dynamic-update-slice_fusion.7
  27.5 1.5 %collective-permute-start.2 = (bf16[32,8320]{1,0:T(8,128)(2,1)S(1)}, bf16[32,8320]{1,0:T(8,128)(2,1)S(1)}, u32[]{:S(2)}, u32[]{:S(2)}) collective-permute-start(bf16[32,8320]{1,0:T(8,128)(2,1)S(1)} %collective-permute-done), channel_id=1, source_target_pairs={{0,2},{1,3},{2,0},{3,1},{4,6},{5,7},{6,4},{7,5},{8,10},{9,11},{10,... | collective-permute-start | bytes 1597448 | tf_op jit(solution)/shard_map/ppermute | solution.py:44
  29.5 3.5 %collective-permute-done.5 = bf16[16,8320]{1,0:T(8,128)(2,1)S(1)} collective-permute-done((bf16[16,8320]{1,0:T(8,128)(2,1)S(1)}, bf16[16,8320]{1,0:T(8,128)(2,1)S(1)}, u32[]{:S(2)}, u32[]{:S(2)}) %collective-permute-start.5) | collective-permute-done | bytes 266272 | tf_op jit(solution)/shard_map/ppermute | solution.py:44
  33.3 9.4 %collective-permute-done.2 = bf16[32,8320]{1,0:T(8,128)(2,1)S(1)} collective-permute-done((bf16[32,8320]{1,0:T(8,128)(2,1)S(1)}, bf16[32,8320]{1,0:T(8,128)(2,1)S(1)}, u32[]{:S(2)}, u32[]{:S(2)}) %collective-permute-start.2) | collective-permute-done | bytes 532512 | tf_op jit(solution)/shard_map/ppermute | solution.py:44
  46.9 30.1 %shard_map.86 = (bf16[8,2,16,4096]{3,2,1,0:T(8,128)(2,1)}, bf16[8,2,16,4096]{3,2,1,0:T(8,128)(2,1)}) custom-call(bf16[8,2,16,8320]{3,2,1,0:T(8,128)(2,1)} %constant_dynamic-update-slice_fusion.2.x_ref.g_ref.w_ref, bf16[8,2,16,8320]{3,2,1,0:T(8,128)(2,1)} %constant_dynamic-update-slice_fusion.2.x_ref.g_ref.w_ref, ...), custom_call_target="tpu_custom_call" | custom-call | tf_op jit(solution)/shard_map/pallas_call | solution.py:166
  77.0 1.4 %slice_bitcast_fusion = bf16[4,32,4096]{2,1,0:T(8,128)(2,1)S(1)} fusion(bf16[4,2,1,32,4096]{4,3,1,0,2:T(8,128)(2,1)} %bitcast.101), kind=kLoop, calls=%fused_computation.12 | loop fusion | bytes 2097152 | tf_op jit(solution)/shard_map/reshape;squeeze | solution.py:77
  79.3 1.3 %slice_bitcast_fusion.2 = bf16[4,32,4096]{2,1,0:T(8,128)(2,1)S(1)} fusion(bf16[4,2,1,32,4096]{4,3,1,0,2:T(8,128)(2,1)} %bitcast.99), kind=kLoop, calls=%fused_computation.14 | loop fusion | bytes 2097152 | tf_op jit(solution)/shard_map/reshape;squeeze | solution.py:77
  81.5 1.6 %collective-permute-start.13 = (bf16[2,32,4096]{2,1,0:T(8,128)(2,1)S(1)}, bf16[2,32,4096]{2,1,0:T(8,128)(2,1)S(1)}, u32[]{:S(2)}, u32[]{:S(2)}) collective-permute-start(bf16[2,32,4096]{2,1,0:T(8,128)(2,1)S(1)} %slice_bitcast_fusion.4), channel_id=1, source_target_pairs={{0,4},{1,5},{2,6},{3,7},{4,0},{5,1},{6,2},{7,3},{8,12},{9,13},{10,... | collective-permute-start | bytes 1572872 | tf_op jit(solution)/shard_map/ppermute | solution.py:78
  84.3 11.2 %collective-permute-done.13 = bf16[2,32,4096]{2,1,0:T(8,128)(2,1)S(1)} collective-permute-done((bf16[2,32,4096]{2,1,0:T(8,128)(2,1)S(1)}, bf16[2,32,4096]{2,1,0:T(8,128)(2,1)S(1)}, u32[]{:S(2)}, u32[]{:S(2)}) %collective-permute-start.13) | collective-permute-done | bytes 524320 | tf_op jit(solution)/shard_map/ppermute | solution.py:78
  95.7 1.3 %collective-permute-start.14 = (bf16[32,4096]{1,0:T(8,128)(2,1)S(1)}, bf16[32,4096]{1,0:T(8,128)(2,1)S(1)}, u32[]{:S(2)}, u32[]{:S(2)}) collective-permute-start(bf16[32,4096]{1,0:T(8,128)(2,1)S(1)} %get-tuple-element.12), channel_id=1, source_target_pairs={{8,0},{9,1},{10,2},{11,3},{12,4},{13,5},{14,6},{15,7},{16,8},{17,9... | collective-permute-start | bytes 786440 | tf_op jit(solution)/shard_map/ppermute | solution.py:107
  97.0 1.3 %collective-permute-start.15 = (bf16[32,4096]{1,0:T(8,128)(2,1)S(1)}, bf16[32,4096]{1,0:T(8,128)(2,1)S(1)}, u32[]{:S(2)}, u32[]{:S(2)}) collective-permute-start(bf16[32,4096]{1,0:T(8,128)(2,1)S(1)} %get-tuple-element.13), channel_id=1, source_target_pairs={{8,2},{9,3},{10,0},{11,1},{12,6},{13,7},{14,4},{15,5},{16,10},{17,... | collective-permute-start | bytes 786440 | tf_op jit(solution)/shard_map/ppermute | solution.py:108
  98.5 1.6 %collective-permute-start.10 = (bf16[32,4096]{1,0:T(8,128)(2,1)S(1)}, bf16[32,4096]{1,0:T(8,128)(2,1)S(1)}, u32[]{:S(2)}, u32[]{:S(2)}) collective-permute-start(bf16[32,4096]{1,0:T(8,128)(2,1)S(1)} %slice_bitcast_fusion.10), channel_id=1, source_target_pairs={{0,4},{1,5},{2,6},{3,7},{4,0},{5,1},{6,2},{7,3},{8,12},{9,13},{10,... | collective-permute-start | bytes 786440 | tf_op jit(solution)/shard_map/ppermute | solution.py:97
  100.1 6.8 %collective-permute-done.14 = bf16[32,4096]{1,0:T(8,128)(2,1)S(1)} collective-permute-done((bf16[32,4096]{1,0:T(8,128)(2,1)S(1)}, bf16[32,4096]{1,0:T(8,128)(2,1)S(1)}, u32[]{:S(2)}, u32[]{:S(2)}) %collective-permute-start.14) | collective-permute-done | bytes 262176 | tf_op jit(solution)/shard_map/ppermute | solution.py:107
  106.8 3.9 %collective-permute-done.15 = bf16[32,4096]{1,0:T(8,128)(2,1)S(1)} collective-permute-done((bf16[32,4096]{1,0:T(8,128)(2,1)S(1)}, bf16[32,4096]{1,0:T(8,128)(2,1)S(1)}, u32[]{:S(2)}, u32[]{:S(2)}) %collective-permute-start.15) | collective-permute-done | bytes 262176 | tf_op jit(solution)/shard_map/ppermute | solution.py:108
  111.2 1.5 %fusion.2 = bf16[1,128,4096]{2,1,0:T(8,128)(2,1)} fusion(f32[128,4096]{1,0:T(8,128)S(1)} %fusion.15, bf16[32,4096]{1,0:T(8,128)(2,1)S(1)} %collective-permute-done.15, bf16[32,4096]{1,0:T(8,128)(2,1)S(1)} %collective-permute-done.14, pred[16,128]{1,0:T(8,128)(4,1)S(1)} %get-tuple-element.19, pred[16,128]{1,0:T(8,128)(4,1)S(1)} %get-tuple-element.18), kind=kOutput, calls=%fused_computation.4 | convolution fusion | flops 35131392 | bytes 3674112 | tf_op jit(solution)/shard_map/dot_general | solution.py:118
  113.2 1.5 %fusion.3 = bf16[1,128,4096]{2,1,0:T(8,128)(2,1)} fusion(f32[128,4096]{1,0:T(8,128)S(1)} %fusion.14, bf16[32,4096]{1,0:T(8,128)(2,1)S(1)} %collective-permute-done.10, bf16[2,32,4096]{2,1,0:T(8,128)(2,1)S(1)} %fusion.7, pred[16,128]{1,0:T(8,128)(4,1)S(1)} %copy-done.5, pred[16,128]{1,0:T(8,128)(4,1)S(1)} %copy-done.3), kind=kOutput, calls=%fused_computation.5 | convolution fusion | flops 35131392 | bytes 3674112 | tf_op jit(solution)/shard_map/dot_general | solution.py:118
  (80 shorter events, 16.8 us)
Async XLA Ops:
  0.6 10.3 %copy-start.6 = (s32[1,128,2]{1,2,0:T(2,128)S(1)}, s32[1,128,2]{1,2,0:T(2,128)}, u32[]{:S(2)}) copy-start(s32[1,128,2]{1,2,0:T(2,128)} %param.9) | copy-start | bytes 3076
  2.2 3.9 %copy-start.2 = (pred[16,128]{1,0:T(8,128)(4,1)}, pred[16,128]{1,0:T(8,128)(4,1)S(1)}, u32[]{:S(2)}) copy-start(pred[16,128]{1,0:T(8,128)(4,1)S(1)} %get-tuple-element.16) | copy-start | bytes 6148
  2.2 3.9 %copy-start.4 = (pred[16,128]{1,0:T(8,128)(4,1)}, pred[16,128]{1,0:T(8,128)(4,1)S(1)}, u32[]{:S(2)}) copy-start(pred[16,128]{1,0:T(8,128)(4,1)S(1)} %get-tuple-element.17) | copy-start | bytes 6148
  6.3 19.5 %collective-permute-start = (bf16[32,8320]{1,0:T(8,128)(2,1)S(1)}, bf16[32,8320]{1,0:T(8,128)(2,1)S(1)}, u32[]{:S(2)}, u32[]{:S(2)}) collective-permute-start(bf16[32,8320]{1,0:T(8,128)(2,1)S(1)} %pad_maximum_fusion), channel_id=1, source_target_pairs={{0,1},{1,0},{2,3},{3,2},{4,5},{5,4},{6,7},{7,6},{8,9},{9,8},{10,11... | collective-permute-start | bytes 1597448 | tf_op jit(solution)/shard_map/ppermute | solution.py:44
  6.8 17.1 %collective-permute-start.1 = (bf16[32,8320]{1,0:T(8,128)(2,1)S(1)}, bf16[32,8320]{1,0:T(8,128)(2,1)S(1)}, u32[]{:S(2)}, u32[]{:S(2)}) collective-permute-start(bf16[32,8320]{1,0:T(8,128)(2,1)S(1)} %pad_maximum_fusion), channel_id=1, source_target_pairs={{0,2},{1,3},{2,0},{3,1},{4,6},{5,7},{6,4},{7,5},{8,10},{9,11},{10,... | collective-permute-start | bytes 1597448 | tf_op jit(solution)/shard_map/ppermute | solution.py:44
  9.4 14.2 %collective-permute-start.3 = (bf16[32,8320]{1,0:T(8,128)(2,1)S(1)}, bf16[32,8320]{1,0:T(8,128)(2,1)S(1)}, u32[]{:S(2)}, u32[]{:S(2)}) collective-permute-start(bf16[32,8320]{1,0:T(8,128)(2,1)S(1)} %pad_maximum_fusion), channel_id=1, source_target_pairs={{0,4},{1,5},{2,6},{3,7},{4,0},{5,1},{6,2},{7,3},{8,12},{9,13},{10,... | collective-permute-start | bytes 1597448 | tf_op jit(solution)/shard_map/ppermute | solution.py:44
  10.9 5.5 %collective-permute-start.11 = (s32[128,2]{0,1:T(2,128)S(1)}, s32[128,2]{0,1:T(2,128)S(1)}, u32[]{:S(2)}, u32[]{:S(2)}) collective-permute-start(s32[128,2]{0,1:T(2,128)S(1)} %bitcast.110), channel_id=1, source_target_pairs={{8,0},{16,8},{24,16},{9,1},{17,9},{25,17},{10,2},{18,10},{26,18},{... | collective-permute-start | bytes 3080 | tf_op jit(solution)/shard_map/ppermute | solution.py:16
  16.4 29.6 %copy-start.7 = (pred[128]{0:T(512)(128)(4,1)}, pred[128]{0:T(512)(128)(4,1)S(1)}, u32[]{:S(2)}) copy-start(pred[128]{0:T(512)(128)(4,1)S(1)} %get-tuple-element.8) | copy-start | bytes 388
  23.6 9.4 %collective-permute-start.5 = (bf16[16,8320]{1,0:T(8,128)(2,1)S(1)}, bf16[16,8320]{1,0:T(8,128)(2,1)S(1)}, u32[]{:S(2)}, u32[]{:S(2)}) collective-permute-start(bf16[16,8320]{1,0:T(8,128)(2,1)S(1)} %slice.56), channel_id=1, source_target_pairs={{0,2},{1,3},{2,0},{3,1},{4,6},{5,7},{6,4},{7,5},{8,10},{9,11},{10,... | collective-permute-start | bytes 798728 | tf_op jit(solution)/shard_map/ppermute | solution.py:44
  24.0 9.2 %collective-permute-start.6 = (bf16[16,8320]{1,0:T(8,128)(2,1)S(1)}, bf16[16,8320]{1,0:T(8,128)(2,1)S(1)}, u32[]{:S(2)}, u32[]{:S(2)}) collective-permute-start(bf16[16,8320]{1,0:T(8,128)(2,1)S(1)} %slice.57), channel_id=1, source_target_pairs={{0,4},{1,5},{2,6},{3,7},{4,0},{5,1},{6,2},{7,3},{8,12},{9,13},{10,... | collective-permute-start | bytes 798728 | tf_op jit(solution)/shard_map/ppermute | solution.py:44
  27.5 15.2 %collective-permute-start.2 = (bf16[32,8320]{1,0:T(8,128)(2,1)S(1)}, bf16[32,8320]{1,0:T(8,128)(2,1)S(1)}, u32[]{:S(2)}, u32[]{:S(2)}) collective-permute-start(bf16[32,8320]{1,0:T(8,128)(2,1)S(1)} %collective-permute-done), channel_id=1, source_target_pairs={{0,2},{1,3},{2,0},{3,1},{4,6},{5,7},{6,4},{7,5},{8,10},{9,11},{10,... | collective-permute-start | bytes 1597448 | tf_op jit(solution)/shard_map/ppermute | solution.py:44
  29.0 15.4 %collective-permute-start.4 = (bf16[32,8320]{1,0:T(8,128)(2,1)S(1)}, bf16[32,8320]{1,0:T(8,128)(2,1)S(1)}, u32[]{:S(2)}, u32[]{:S(2)}) collective-permute-start(bf16[32,8320]{1,0:T(8,128)(2,1)S(1)} %collective-permute-done), channel_id=1, source_target_pairs={{0,4},{1,5},{2,6},{3,7},{4,0},{5,1},{6,2},{7,3},{8,12},{9,13},{10,... | collective-permute-start | bytes 1597448 | tf_op jit(solution)/shard_map/ppermute | solution.py:44
  33.2 12.8 %collective-permute-start.7 = (bf16[32,8320]{1,0:T(8,128)(2,1)S(1)}, bf16[32,8320]{1,0:T(8,128)(2,1)S(1)}, u32[]{:S(2)}, u32[]{:S(2)}) collective-permute-start(bf16[32,8320]{1,0:T(8,128)(2,1)S(1)} %constant_dynamic-update-slice_fusion), channel_id=1, source_target_pairs={{0,1},{1,0},{2,3},{3,2},{4,5},{5,4},{6,7},{7,6},{8,9},{9,8},{10,11... | collective-permute-start | bytes 1597448 | tf_op jit(solution)/shard_map/ppermute | solution.py:44
  77.0 4.2 %copy-start.1 = (bf16[8,2,16,4096]{3,2,1,0:T(8,128)(2,1)S(1)}, bf16[8,2,16,4096]{3,2,1,0:T(8,128)(2,1)}, u32[]{:S(2)}) copy-start(bf16[8,2,16,4096]{3,2,1,0:T(8,128)(2,1)} %get-tuple-element.5) | copy-start | bytes 6291460
  77.0 6.4 %copy-start = (bf16[8,2,16,4096]{3,2,1,0:T(8,128)(2,1)S(1)}, bf16[8,2,16,4096]{3,2,1,0:T(8,128)(2,1)}, u32[]{:S(2)}) copy-start(bf16[8,2,16,4096]{3,2,1,0:T(8,128)(2,1)} %get-tuple-element.4) | copy-start | bytes 6291460
  78.4 2.7 %collective-permute-start.12 = (bf16[4,32,4096]{2,1,0:T(8,128)(2,1)S(1)}, bf16[4,32,4096]{2,1,0:T(8,128)(2,1)S(1)}, u32[]{:S(2)}, u32[]{:S(2)}) collective-permute-start(bf16[4,32,4096]{2,1,0:T(8,128)(2,1)S(1)} %slice_bitcast_fusion), channel_id=1, source_target_pairs={{0,1},{1,0},{2,3},{3,2},{4,5},{5,4},{6,7},{7,6},{8,9},{9,8},{10,11... | collective-permute-start | bytes 3145736 | tf_op jit(solution)/shard_map/ppermute | solution.py:78
  80.6 2.8 %collective-permute-start.8 = (bf16[4,32,4096]{2,1,0:T(8,128)(2,1)S(1)}, bf16[4,32,4096]{2,1,0:T(8,128)(2,1)S(1)}, u32[]{:S(2)}, u32[]{:S(2)}) collective-permute-start(bf16[4,32,4096]{2,1,0:T(8,128)(2,1)S(1)} %slice_bitcast_fusion.2), channel_id=1, source_target_pairs={{0,1},{1,0},{2,3},{3,2},{4,5},{5,4},{6,7},{7,6},{8,9},{9,8},{10,11... | collective-permute-start | bytes 3145736 | tf_op jit(solution)/shard_map/ppermute | solution.py:78
  81.5 14.0 %collective-permute-start.13 = (bf16[2,32,4096]{2,1,0:T(8,128)(2,1)S(1)}, bf16[2,32,4096]{2,1,0:T(8,128)(2,1)S(1)}, u32[]{:S(2)}, u32[]{:S(2)}) collective-permute-start(bf16[2,32,4096]{2,1,0:T(8,128)(2,1)S(1)} %slice_bitcast_fusion.4), channel_id=1, source_target_pairs={{0,4},{1,5},{2,6},{3,7},{4,0},{5,1},{6,2},{7,3},{8,12},{9,13},{10,... | collective-permute-start | bytes 1572872 | tf_op jit(solution)/shard_map/ppermute | solution.py:78
  83.7 14.6 %collective-permute-start.9 = (bf16[2,32,4096]{2,1,0:T(8,128)(2,1)S(1)}, bf16[2,32,4096]{2,1,0:T(8,128)(2,1)S(1)}, u32[]{:S(2)}, u32[]{:S(2)}) collective-permute-start(bf16[2,32,4096]{2,1,0:T(8,128)(2,1)S(1)} %slice_bitcast_fusion.6), channel_id=1, source_target_pairs={{0,2},{1,3},{2,0},{3,1},{4,6},{5,7},{6,4},{7,5},{8,10},{9,11},{10,... | collective-permute-start | bytes 1572872 | tf_op jit(solution)/shard_map/ppermute | solution.py:78
  95.7 17.0 %copy-start.3 = (pred[16,128]{1,0:T(8,128)(4,1)S(1)}, pred[16,128]{1,0:T(8,128)(4,1)}, u32[]{:S(2)}) copy-start(pred[16,128]{1,0:T(8,128)(4,1)} %copy-done.2) | copy-start | bytes 6148
  95.7 17.0 %copy-start.5 = (pred[16,128]{1,0:T(8,128)(4,1)S(1)}, pred[16,128]{1,0:T(8,128)(4,1)}, u32[]{:S(2)}) copy-start(pred[16,128]{1,0:T(8,128)(4,1)} %copy-done.4) | copy-start | bytes 6148
  95.7 11.1 %collective-permute-start.14 = (bf16[32,4096]{1,0:T(8,128)(2,1)S(1)}, bf16[32,4096]{1,0:T(8,128)(2,1)S(1)}, u32[]{:S(2)}, u32[]{:S(2)}) collective-permute-start(bf16[32,4096]{1,0:T(8,128)(2,1)S(1)} %get-tuple-element.12), channel_id=1, source_target_pairs={{8,0},{9,1},{10,2},{11,3},{12,4},{13,5},{14,6},{15,7},{16,8},{17,9... | collective-permute-start | bytes 786440 | tf_op jit(solution)/shard_map/ppermute | solution.py:107
  97.0 13.7 %collective-permute-start.15 = (bf16[32,4096]{1,0:T(8,128)(2,1)S(1)}, bf16[32,4096]{1,0:T(8,128)(2,1)S(1)}, u32[]{:S(2)}, u32[]{:S(2)}) collective-permute-start(bf16[32,4096]{1,0:T(8,128)(2,1)S(1)} %get-tuple-element.13), channel_id=1, source_target_pairs={{8,2},{9,3},{10,0},{11,1},{12,6},{13,7},{14,4},{15,5},{16,10},{17,... | collective-permute-start | bytes 786440 | tf_op jit(solution)/shard_map/ppermute | solution.py:108
  98.5 14.2 %collective-permute-start.10 = (bf16[32,4096]{1,0:T(8,128)(2,1)S(1)}, bf16[32,4096]{1,0:T(8,128)(2,1)S(1)}, u32[]{:S(2)}, u32[]{:S(2)}) collective-permute-start(bf16[32,4096]{1,0:T(8,128)(2,1)S(1)} %slice_bitcast_fusion.10), channel_id=1, source_target_pairs={{0,4},{1,5},{2,6},{3,7},{4,0},{5,1},{6,2},{7,3},{8,12},{9,13},{10,... | collective-permute-start | bytes 786440 | tf_op jit(solution)/shard_map/ppermute | solution.py:97
  (1 other events, 0.5 us)
